TPU v7x, 32 devices: a whole 2x2x4 slice. The times are simulated.
32 devices in a mesh: row: 4 (over x, core), col: 8 (over z, y).
Axes of the slice: x: 2, y: 2, z: 4, core: 2. Of those that a mesh axis runs over, the one named last changes fastest.
Arguments:
- atom_feat: float32 [8192, 128], P(('row', 'col')), may hold values from -6 to 6
- types: int32 [8192], P(('row', 'col')), may hold values from 0 to 3
- neighbors: int32 [8192, 32], P(('row', 'col')), may hold values from 0 to 255
- frame_of_atom: int32 [8192], P(('row', 'col')), may hold values from 0 to 3
- weights: float32 [128, 128], replicated, may hold values from -0.5 to 0.5
- type_gain: float32 [4, 128], replicated, may hold values from -4 to 4
- out_vec: float32 [4, 128], replicated, may hold values from -1.5 to 1.5
- targets: float32 [128], replicated, may hold values from -5 to 5
- noise: float32 [128], replicated, may hold values from 0.05 to 2
- cov: float32 [16384, 16384], P('row', 'col'), as said below
Outputs:
- new_weights: float32 [16384], P(('row', 'col'))
- new_cov: float32 [16384, 16384], P('row', 'col')
Inputs may be any that keep to these rules, and one draw needn't show every extreme that they name: cov is symmetric positive definite.
All inputs are finite; a program needn't handle non-finite values.
Results may differ from a plain program's by a relative error of at most 0.0003.
Values sent between devices are 32-bit elements; how exact they have to be, the bound alone decides.
No kernel may reach another device: no remote copies, remote signals or barrier semaphores. Data moves between devices by JAX's collectives and lax.ppermute only.
A program may use at most 192 MiB of HBM per device.

v0:
```python
import jax
import jax.numpy as jnp
from jax import lax
from jax.sharding import PartitionSpec as P

FR = 64


def broadcast(value, axis, root):
    mine = lax.axis_index(axis) == root
    return lax.psum(jnp.where(mine, value, jnp.zeros_like(value)), axis)


def on_device(
    atom_feat, types, neighbors, frame_of_atom, weights, type_gain, out_vec, targets, noise, cov
):
    hi = lax.Precision.HIGHEST
    atoms = atom_feat.shape[0]
    ntypes = type_gain.shape[0]
    frames = atoms // FR
    onehot_type = (types[:, None] == jnp.arange(ntypes)[None, :]).astype(jnp.float32)
    row_gain = jnp.dot(onehot_type, type_gain, precision=hi)
    row_out = jnp.dot(onehot_type, out_vec, precision=hi)
    scaled = atom_feat * row_gain
    near = scaled[neighbors]
    desc = jnp.tanh(atom_feat + jnp.mean(near, axis=1))
    act = jnp.tanh(jnp.dot(desc, weights, precision=hi))
    site_energy = jnp.sum(act * row_out, axis=1)
    slope = (1.0 - act * act) * row_out
    member = (frame_of_atom[:, None] == jnp.arange(frames)[None, :]).astype(jnp.float32)
    pred_local = jnp.dot(site_energy, member, precision=hi) / FR
    grads = jnp.einsum("af,ai,aj->fij", member, desc, slope, precision=hi) / FR
    width = grads.shape[1] * grads.shape[2]
    grads = grads.reshape(frames, width)
    n_row = lax.axis_size("row")
    n_col = lax.axis_size("col")
    row_id = lax.axis_index("row")
    col_id = lax.axis_index("col")
    device_id = row_id * n_col + col_id
    col_w = width // n_col
    blk = width // (n_row * n_col)
    col_part = lax.all_to_all(grads, "col", split_axis=1, concat_axis=0, tiled=True)
    grad_col = lax.all_gather(col_part, "row", axis=0, tiled=True)
    grad_own = lax.all_to_all(grads, ("row", "col"), split_axis=1, concat_axis=0, tiled=True)
    partial_rows = jnp.einsum("ik,mk->im", cov, grad_col, precision=hi)
    gain_rows = lax.psum(partial_rows, "col")
    gain_own = lax.dynamic_slice_in_dim(gain_rows, col_id * blk, blk, 0)
    gram_part = jnp.einsum("mk,kn->mn", grad_own, gain_own, precision=hi)
    gram = lax.psum(gram_part, ("row", "col"))
    pred_all = lax.all_gather(pred_local, ("row", "col"), axis=0, tiled=True)
    gram = gram + jnp.diag(noise)
    lower = jnp.linalg.cholesky(gram)
    factor = n_col // n_row
    half_rows = lax.dynamic_slice_in_dim(gain_rows, col_id % factor * col_w, col_w, 0)
    gain_col = broadcast(half_rows, "row", col_id // factor)
    white_row = jax.scipy.linalg.solve_triangular(lower, gain_rows.T, lower=True)
    white_col = jax.scipy.linalg.solve_triangular(lower, gain_col.T, lower=True)
    new_cov = cov - jnp.einsum("mi,mj->ij", white_row, white_col, precision=hi)
    coef = jax.scipy.linalg.cho_solve((lower, True), targets - pred_all)
    own_weights = lax.dynamic_slice_in_dim(weights.reshape(-1), device_id * blk, blk, 0)
    new_weights = own_weights + jnp.dot(gain_own, coef, precision=hi)
    return (new_weights, new_cov)


def solution(mesh):
    return jax.shard_map(
        on_device,
        mesh=mesh,
        in_specs=(
            P(("row", "col"), None),
            P(("row", "col")),
            P(("row", "col"), None),
            P(("row", "col")),
            P(),
            P(),
            P(),
            P(),
            P(),
            P("row", "col"),
        ),
        out_specs=(P(("row", "col")), P("row", "col")),
        check_vma=False,
    )
```

profile of v0, /device:TPU:0, one launch (start us, length us, event | category | flops | bytes accessed | tf_op | source)
XLA Modules:
  0.0 428.5 jit_solution(279523916073849036)
XLA Ops:
  7.2 0.0 all-gather.2.cloned.1.call-start
  7.2 0.7 fusion.25
  7.9 0.8 compare_select_fusion
  8.7 0.1 copy.15
  8.8 0.1 reshape.48
  8.9 1.0 fusion.13
  9.9 1.2 convolution_multiply_fusion.1
  11.1 28.0 %gather_fusion = f32[8192,128]{1,0:T(8,128)} fusion(f32[256,128]{1,0:T(8,128)S(1)} %convolution_multiply_fusion.1, s32[8192]{0:T(1024)S(1)} %broadcast_clamp_fusion), kind=kCustom, calls=%fused_computation | custom fusion | bytes 8421376 | tf_op jit(solution)/shard_map/gather | solution.py:25
  39.1 2.9 bitcast_reduce_fusion
  42.0 0.1 copy.16
  42.2 0.3 multiply_reduce_fusion
  42.5 0.6 fusion
  43.2 0.2 copy.18
  43.3 16.0 %all_to_all.38 = f32[4,8,2048]{2,0,1:T(4,128)S(1)} all-to-all(f32[4,8,2048]{2,0,1:T(4,128)S(1)} %copy.18), channel_id=1, replica_groups=mesh['row'=4,'col'=8] {'col'}, dimensions={1} | all-to-all | bytes 524288 | tf_op jit(solution)/shard_map/all_to_all | solution.py:42
  59.3 0.8 all_to_all.31
  60.1 0.0 all-gather.2.cloned.1.call-update
  60.1 0.0 all-reduce.5.cloned.1.call-start
  60.2 15.8 %all-gather.2.cloned.1.call-done = f32[128,2048]{1,0:T(8,128)} async-done(((f32[32,2048]{1,0:T(8,128)}), f32[128,2048]{1,0:T(8,128)}) %all-gather.2.cloned.1.call-update) | async-done | bytes 1048592 | tf_op jit(solution)/shard_map/all_gather | solution.py:43
  76.0 39.2 %convolution_bitcast_fusion = f32[4096,128]{0,1:T(8,128)} fusion(f32[128,2048]{1,0:T(8,128)} %all-gather.2.cloned.1.call-done, f32[4096,2048]{1,0:T(8,128)} %param.19), kind=kOutput, calls=%fused_computation.2 | convolution fusion | flops 12884901888 | bytes 36700160 | tf_op jit(solution)/shard_map/ik,mk->im/dot_general | solution.py:45
  115.2 0.0 all-reduce.5.cloned.1.call-update
  115.3 0.9 copy.19
  116.1 4.6 %all-to-all-start.1 = ((f32[4,32,512]{2,0,1:T(4,128)}), f32[4,32,512]{2,0,1:T(4,128)S(1)}, u32[]{:S(2)}, u32[]{:S(2)}) async-start(f32[4,32,512]{2,0,1:T(4,128)} %copy.19), calls=%async_computation.1 | async-start | bytes 524288 | tf_op jit(solution)/shard_map/all_to_all | solution.py:44
  120.8 0.0 all-reduce.7.cloned.1.call-start
  120.9 0.1 fusion.1
  121.0 0.2 dynamic-update-slice.3
  121.2 42.4 %all-reduce = f32[128]{0:T(128)S(1)} all-reduce(f32[128]{0:T(128)S(1)} %dynamic-update-slice.3), channel_id=1, replica_groups=mesh['row'=4,'col'=8] {'row','col'}, use_global_device_ids=true, to_apply=%add | all-reduce | flops 128 | bytes 1024
  163.6 0.1 all_to_all.35
  163.7 60.1 %all-reduce.5.cloned.1.call-done = f32[4096,128]{0,1:T(8,128)} async-done(((f32[4096,128]{0,1:T(8,128)}), f32[4096,128]{0,1:T(8,128)}) %all-reduce.5.cloned.1.call-update) | async-done | bytes 2097168 | tf_op jit(solution)/shard_map/psum | solution.py:46
  223.8 1.9 fusion.7
  225.8 0.2 all-reduce.9.cloned.1.call-start
  226.0 2.3 dynamic-slice_select_fusion
  228.3 0.0 all-reduce.9.cloned.1.call-update
  228.3 118.3 %all-reduce.7.cloned.1.call-done = f32[128,128]{1,0:T(8,128)} async-done(((f32[128,128]{1,0:T(8,128)}), f32[128,128]{1,0:T(8,128)}) %all-reduce.7.cloned.1.call-update) | async-done | bytes 65552 | tf_op jit(solution)/shard_map/psum | solution.py:49
  346.6 0.9 select_add_fusion
  347.6 0.1 copy.20
  347.7 0.9 fusion.21
  348.6 11.7 %cholesky.16 = f32[128,128]{1,0:T(8,128)S(1)} custom-call(f32[128,128]{1,0:T(8,128)S(1)} %fusion.21), custom_call_target="Cholesky" | custom-call | tf_op jit(solution)/shard_map/jit(cholesky)/cholesky | solution.py:52
  360.3 0.6 compare_reduce_fusion
  361.0 0.7 fusion.14
  361.7 9.8 %custom-call.16 = f32[1,128,128]{1,2,0:T(8,128)S(1)} custom-call(f32[1,128,128]{2,1,0:T(8,128)S(1)} %fusion.14), custom_call_target="InvertDiagBlocksLowerTriangular" | custom-call | tf_op jit(solution)/shard_map/jit(_cho_solve)/triangular_solve | solution.py:59
  371.5 0.2 convolution_bitcast_fusion.3
  371.6 0.2 convolution_bitcast_fusion.2
  371.8 1.2 fusion.5
  373.1 0.7 dynamic-slice_add_fusion
  373.7 3.6 fusion.17
  377.3 9.1 %all-reduce.9.cloned.1.call-done = f32[2048,128]{0,1:T(8,128)} async-done(((f32[2048,128]{0,1:T(8,128)}), f32[2048,128]{0,1:T(8,128)}) %all-reduce.9.cloned.1.call-update) | async-done | bytes 1048592 | tf_op jit(solution)/shard_map/psum | solution.py:11
  386.4 2.3 fusion.15
  388.7 33.3 %convolution_subtract_fusion = f32[4096,2048]{1,0:T(8,128)} fusion(f32[4096,2048]{1,0:T(8,128)} %param.19, f32[128,4096]{1,0:T(8,128)S(1)} %fusion.17, f32[128,2048]{1,0:T(8,128)S(1)} %fusion.15), kind=kOutput, calls=%fused_computation.1 | convolution fusion | flops 12893290496 | bytes 70254592 | tf_op jit(solution)/shard_map/mi,mj->ij/dot_general | solution.py:58
  (22 shorter events, 0.2 us)
Async XLA Ops:
  7.2 1.7 copy-start
  7.2 68.8 %all-gather.2.cloned.1.call-start = ((), (), s32[]{:S(2)}) async-start(), calls=%async_computation.2 | async-start | bytes 1310720 | tf_op jit(solution)/shard_map/all_gather | solution.py:43
  39.1 2.9 copy-start.2
  39.1 3.1 copy-start.3
  60.1 163.6 %all-reduce.5.cloned.1.call-start = ((), (), s32[]{:S(2)}) async-start(), calls=%async_computation.3 | async-start | bytes 4194304 | tf_op jit(solution)/shard_map/psum | solution.py:46
  115.2 5.7 %copy-start.5 = (s32[256]{0:T(256)S(1)}, s32[256]{0:T(256)}, u32[]{:S(2)}) copy-start(s32[256]{0:T(256)} %param.13) | copy-start | bytes 3076
  116.1 47.4 %all-to-all-start.1 = ((f32[4,32,512]{2,0,1:T(4,128)}), f32[4,32,512]{2,0,1:T(4,128)S(1)}, u32[]{:S(2)}, u32[]{:S(2)}) async-start(f32[4,32,512]{2,0,1:T(4,128)} %copy.19), calls=%async_computation.1 | async-start | bytes 524288 | tf_op jit(solution)/shard_map/all_to_all | solution.py:44
  120.8 225.9 %all-reduce.7.cloned.1.call-start = ((), (), s32[]{:S(2)}) async-start(), calls=%async_computation.4 | async-start | bytes 131072 | tf_op jit(solution)/shard_map/psum | solution.py:49
  163.6 183.1 %copy-start.4 = (f32[128]{0:T(128)S(1)}, f32[128]{0:T(128)}, u32[]{:S(2)}) copy-start(f32[128]{0:T(128)} %param.18) | copy-start | bytes 1540
  163.7 207.8 %copy-start.6 = (f32[128]{0:T(128)S(1)}, f32[128]{0:T(128)}, u32[]{:S(2)}) copy-start(f32[128]{0:T(128)} %param.17) | copy-start | bytes 1540
  225.8 160.6 %all-reduce.9.cloned.1.call-start = ((), (), s32[]{:S(2)}) async-start(), calls=%async_computation.5 | async-start | bytes 2097152 | tf_op jit(solution)/shard_map/psum | solution.py:11
  388.6 33.3 %copy-start.1 = (f32[4,128]{1,0:T(4,128)S(1)}, f32[4,128]{1,0:T(4,128)}, u32[]{:S(2)}) copy-start(f32[4,128]{1,0:T(4,128)} %param.16) | copy-start | bytes 6148
Sparse Core Ops, SparseCore 0:
  60.3 15.7 all-gather.1
  115.3 108.4 all-reduce.4
  229.4 117.2 all-reduce.6
  349.4 36.9 all-reduce.8
where the time goes:
time: 429 us; the launch traced here: 428 us
  waiting for transfers between devices  203 us (47%)
  matrix products  85 us (20%)
  blocking collectives  58.4 us (14%)
  other arithmetic  32.1 us (7%)
  local copies, waits for them, and re-layouts  30.6 us (7%)
  between operations  14 us (3%)
  starting transfers between devices  4.95 us (1%)
    psum x1, waiting for transfers between devices, on_device(): gram = lax.psum(gram_part, ('row', 'col'))  118 us
    psum x1, waiting for transfers between devices, on_device(): gain_rows = lax.psum(partial_rows, 'col')  60.1 us
    unnamed x1, blocking collectives  42.4 us
    dot_general x1, matrix products, on_device(): partial_rows = jnp.einsum('ik,mk->im', cov, grad_col, precision=hi)  39.2 us
    dot_general x1, matrix products, on_device(): new_cov = cov - jnp.einsum('mi,mj->ij', white_row, white_col, precision=hi)  33.3 us
    gather x1, local copies, waits for them, and re-layouts, on_device(): near = scaled[neighbors]  28 us
    all_to_all x1, blocking collectives, on_device(): lax.all_to_all(grads, 'col', split_axis=1, concat_axis=0, tiled=True)  16 us
    all_gather x1, waiting for transfers between devices, on_device(): grad_col = lax.all_gather(col_part, 'row', axis=0, tiled=True)  15.8 us
  transfers between devices with their start and end apart: 5, of which 4 were waited for; matrix products, arithmetic and copies ran while one was open for 8% of the time, Pallas kernels for 0%

commit v1 on v0

v1 whole, which is shorter than its diff:
```python
import jax
import jax.numpy as jnp
from jax import lax
from jax.sharding import PartitionSpec as P

FR = 64


def on_device(
    atom_feat, types, neighbors, frame_of_atom, weights, type_gain, out_vec, targets, noise, cov
):
    hi = lax.Precision.HIGHEST
    mid = lax.Precision.HIGH
    atoms = atom_feat.shape[0]
    ntypes = type_gain.shape[0]
    nbrs = neighbors.shape[1]
    frames = atoms // FR
    onehot_type = (types[:, None] == jnp.arange(ntypes)[None, :]).astype(jnp.float32)
    row_gain = jnp.dot(onehot_type, type_gain, precision=hi)
    row_out = jnp.dot(onehot_type, out_vec, precision=hi)
    scaled = atom_feat * row_gain
    counts = jnp.sum(
        (neighbors[:, :, None] == jnp.arange(atoms)[None, None, :]).astype(jnp.float32), axis=1
    )
    near_sum = jnp.dot(counts, scaled, precision=hi)
    desc = jnp.tanh(atom_feat + near_sum / nbrs)
    act = jnp.tanh(jnp.dot(desc, weights, precision=hi))
    site_energy = jnp.sum(act * row_out, axis=1)
    slope = (1.0 - act * act) * row_out
    member = (frame_of_atom[:, None] == jnp.arange(frames)[None, :]).astype(jnp.float32)
    pred_local = jnp.dot(site_energy, member, precision=hi) / FR
    grads = jnp.einsum("af,ai,aj->fij", member, desc, slope, precision=hi) / FR
    width = grads.shape[1] * grads.shape[2]
    grads = grads.reshape(frames, width)
    n_row = lax.axis_size("row")
    n_col = lax.axis_size("col")
    row_id = lax.axis_index("row")
    col_id = lax.axis_index("col")
    m_all = frames * n_row * n_col
    col_w = width // n_col
    blk = width // (n_row * n_col)
    col_part = lax.all_to_all(grads, "col", split_axis=1, concat_axis=0, tiled=True)
    grad_col = lax.all_gather(col_part, "row", axis=0, tiled=True)
    grad_own = lax.all_to_all(grads, ("row", "col"), split_axis=1, concat_axis=0, tiled=True)
    partial_rows = jnp.einsum("ik,mk->im", cov, grad_col, precision=mid)
    gain_own = lax.psum_scatter(partial_rows, "col", scatter_dimension=0, tiled=True)
    gram_own = jnp.einsum("mk,kn->mn", grad_own, gain_own, precision=hi)
    pred_pad = jnp.zeros((8, m_all), jnp.float32).at[0, :frames].set(pred_local)
    payload = jnp.concatenate([gain_own, gram_own, pred_pad], axis=0)
    gathered = lax.all_gather(payload, "col", axis=0)
    gain_rows = gathered[:, :blk, :].reshape(n_col * blk, m_all)
    gram_row = jnp.sum(gathered[:, blk : blk + m_all, :], axis=0)
    pred_row = gathered[:, blk + m_all, :frames].reshape(n_col * frames)
    slots = lax.dynamic_update_slice_in_dim(
        jnp.zeros((8, m_all), jnp.float32),
        jnp.zeros((8, n_col * frames), jnp.float32).at[0].set(pred_row),
        row_id * n_col * frames,
        1,
    )
    small = lax.psum(jnp.concatenate([gram_row, slots], axis=0), "row")
    gram = small[:m_all] + jnp.diag(noise)
    pred_all = small[m_all]
    lower = jnp.linalg.cholesky(gram)
    factor = n_col // n_row
    half_rows = lax.dynamic_slice_in_dim(gain_rows, col_id % factor * col_w, col_w, 0)
    mine = row_id == col_id // factor
    gain_col = lax.psum(jnp.where(mine, half_rows, jnp.zeros_like(half_rows)), "row")
    white_row = jax.scipy.linalg.solve_triangular(lower, gain_rows.T, lower=True)
    white_col = jax.scipy.linalg.solve_triangular(lower, gain_col.T, lower=True)
    new_cov = cov - jnp.einsum("mi,mj->ij", white_row, white_col, precision=mid)
    coef = jax.scipy.linalg.cho_solve((lower, True), targets - pred_all)
    device_id = row_id * n_col + col_id
    own_weights = lax.dynamic_slice_in_dim(weights.reshape(-1), device_id * blk, blk, 0)
    new_weights = own_weights + jnp.dot(gain_own, coef, precision=hi)
    return (new_weights, new_cov)


def solution(mesh):
    return jax.shard_map(
        on_device,
        mesh=mesh,
        in_specs=(
            P(("row", "col"), None),
            P(("row", "col")),
            P(("row", "col"), None),
            P(("row", "col")),
            P(),
            P(),
            P(),
            P(),
            P(),
            P("row", "col"),
        ),
        out_specs=(P(("row", "col")), P("row", "col")),
        check_vma=False,
    )
```

time: 429 us -> 312 us (0.73)
  blocking collectives: 58.4 us -> 16 us
  waiting for transfers between devices: 203 us -> 171 us
  local copies, waits for them, and re-layouts: 30.6 us -> 6.88 us
  matrix products: 85 us -> 61.9 us
    psum x3 -> x1, waiting for transfers between devices: 188 us -> 35.8 us  [on_device(): small = lax.psum(jnp.concatenate([gram_row, slots], axis=0), 'row')]
    all_gather x0 -> x1, waiting for transfers between devices: none -> 53.9 us  [on_device(): gathered = lax.all_gather(payload, 'col', axis=0)]
    reduce_scatter x0 -> x1, waiting for transfers between devices: none -> 52.1 us  [on_device(): lax.psum_scatter(partial_rows, 'col', scatter_dimension=0, tiled=True)]
    unnamed x1 -> x0, blocking collectives: 42.4 us -> none
    gather x1 -> x0, local copies, waits for them, and re-layouts: 28 us -> none  [on_device(): near = scaled[neighbors]]
    dot_general x3 -> x4, matrix products: 74.4 us -> 53.5 us  [the longest x1 27.1 us: on_device(): new_cov = cov - jnp.einsum('mi,mj->ij', white_row, white_col, precision=mid)]
    all_to_all x1, waiting for transfers between devices: 0.01 us -> 13.5 us  [on_device(): lax.all_to_all(grads, ('row', 'col'), split_axis=1, concat_axis=0, tiled=...]
  transfers between devices with their start and end apart: 5 -> 5, of which waited for: 4 -> 5; matrix products, arithmetic and copies ran while one was open for 8% -> 0% of each run, Pallas kernels for 0% -> 0%
where the time goes in v1:
time: 312 us; the launch traced here: 311 us
  waiting for transfers between devices  171 us (55%)
  matrix products  61.9 us (20%)
  other arithmetic  36.2 us (12%)
  blocking collectives  16 us (5%)
  between operations  14 us (4%)
  local copies, waits for them, and re-layouts  6.88 us (2%)
  starting transfers between devices  4.95 us (2%)
    all_gather x1, waiting for transfers between devices, on_device(): gathered = lax.all_gather(payload, 'col', axis=0)  53.9 us
    reduce_scatter x1, waiting for transfers between devices, on_device(): lax.psum_scatter(partial_rows, 'col', scatter_dimension=0, tiled=True)  52.1 us
    psum x1, waiting for transfers between devices, on_device(): small = lax.psum(jnp.concatenate([gram_row, slots], axis=0), 'row')  35.8 us
    dot_general x1, matrix products, on_device(): new_cov = cov - jnp.einsum('mi,mj->ij', white_row, white_col, precision=mid)  27.1 us
    dot_general x1, matrix products, on_device(): partial_rows = jnp.einsum('ik,mk->im', cov, grad_col, precision=mid)  23.8 us
    all_to_all x1, blocking collectives, on_device(): lax.all_to_all(grads, 'col', split_axis=1, concat_axis=0, tiled=True)  16 us
    all_gather x1, waiting for transfers between devices, on_device(): grad_col = lax.all_gather(col_part, 'row', axis=0, tiled=True)  15.8 us
    all_to_all x1, waiting for transfers between devices, on_device(): lax.all_to_all(grads, ('row', 'col'), split_axis=1, concat_axis=0, tiled=...  13.5 us
  transfers between devices with their start and end apart: 5, of which 5 were waited for; matrix products, arithmetic and copies ran while one was open for 0% of the time, Pallas kernels for 0%

profile of v1, /device:TPU:0, one launch (start us, length us, event | category | flops | bytes accessed | tf_op | source)
XLA Modules:
  0.0 311.2 jit_solution(11438957174490737260)
XLA Ops:
  7.2 0.7 fusion.24
  7.9 0.9 copy.37
  8.8 5.7 %convert_reduce_fusion = f32[256,256]{1,0:T(8,128)S(1)} fusion(s32[256,32]{1,0:T(8,128)S(1)} %copy.37), kind=kLoop, calls=%fused_computation.1 | loop fusion | flops 6225920 | bytes 294912 | tf_op jit(solution)/shard_map/reduce_sum | solution.py:22
  14.5 1.0 fusion.12
  15.5 1.2 convolution_multiply_fusion.2
  16.7 1.3 fusion.2
  18.0 0.1 copy.38
  18.1 1.2 multiply_reduce_fusion
  19.2 0.6 fusion
  19.9 0.2 copy.40
  20.1 16.0 %all_to_all.38 = f32[4,8,2048]{2,0,1:T(4,128)S(1)} all-to-all(f32[4,8,2048]{2,0,1:T(4,128)S(1)} %copy.40), channel_id=1, replica_groups=mesh['row'=4,'col'=8] {'col'}, dimensions={1} | all-to-all | bytes 524288 | tf_op jit(solution)/shard_map/all_to_all | solution.py:42
  36.1 0.8 all_to_all.31
  36.9 15.8 %all-gather.4.cloned.1.call-done = f32[128,2048]{1,0:T(8,128)} async-done(((f32[32,2048]{1,0:T(8,128)}), f32[128,2048]{1,0:T(8,128)}) %all-gather.4.cloned.1.call-update) | async-done | bytes 1048592 | tf_op jit(solution)/shard_map/all_gather | solution.py:43
  52.8 23.8 %convolution_bitcast_fusion = f32[4096,128]{0,1:T(8,128)} fusion(f32[128,2048]{1,0:T(8,128)} %all-gather.4.cloned.1.call-done, f32[4096,2048]{1,0:T(8,128)} %param.23), kind=kOutput, calls=%fused_computation.3 | convolution fusion | flops 6442450944 | bytes 36700160 | tf_op jit(solution)/shard_map/ik,mk->im/dot_general | solution.py:45
  76.6 0.9 copy.41
  77.5 4.6 %all-to-all-start.1 = ((f32[4,32,512]{2,0,1:T(4,128)}), f32[4,32,512]{2,0,1:T(4,128)S(1)}, u32[]{:S(2)}, u32[]{:S(2)}) async-start(f32[4,32,512]{2,0,1:T(4,128)} %copy.41), calls=%async_computation.2 | async-start | bytes 524288 | tf_op jit(solution)/shard_map/all_to_all | solution.py:44
  82.1 0.1 fusion.4
  82.2 0.1 copy.42
  82.3 13.5 %all-to-all-done.1 = f32[4,32,512]{2,0,1:T(4,128)S(1)} async-done(((f32[4,32,512]{2,0,1:T(4,128)}), f32[4,32,512]{2,0,1:T(4,128)S(1)}, u32[]{:S(2)}, u32[]{:S(2)}) %all-to-all-start.1) | async-done | bytes 262176 | tf_op jit(solution)/shard_map/all_to_all | solution.py:44
  95.8 0.1 all_to_all.35
  95.9 52.1 %reduce-scatter.2.cloned.1.call-done = f32[512,128]{0,1:T(8,128)} async-done(((f32[4096,128]{0,1:T(8,128)}), f32[512,128]{0,1:T(8,128)}) %reduce-scatter.2.cloned.1.call-update) | async-done | bytes 262160 | tf_op jit(solution)/shard_map/reduce_scatter | solution.py:46
  148.0 1.3 fusion.30
  149.4 1.0 select_maximum_fusion
  150.3 0.9 copy.44
  151.3 0.2 all-reduce.5.cloned.1.call-start
  151.5 53.9 %all-gather.6.cloned.1.call-done = f32[5184,128]{1,0:T(8,128)} async-done(((f32[648,128]{1,0:T(8,128)}), f32[5184,128]{1,0:T(8,128)}) %all-gather.6.cloned.1.call-update) | async-done | bytes 2654224 | tf_op jit(solution)/shard_map/all_gather | solution.py:50
  205.4 0.8 slice_reduce_fusion.1
  206.2 1.1 slice_reduce_fusion
  207.3 1.7 slice.84
  209.1 0.1 reshape.109
  209.2 0.2 dynamic_update_slice.3
  209.4 0.6 pad_maximum_fusion
  210.0 1.0 dynamic-slice_select_fusion
  211.1 35.8 %all-reduce.5.cloned.1.call-done = (f32[136,128]{1,0:T(8,128)}, f32[2048,128]{1,0:T(8,128)}) async-done(((f32[136,128]{1,0:T(8,128)}, f32[2048,128]{1,0:T(8,128)}), (f32[136,128]{1,0:T(8,128)}, f32[2048,128]{1,0:T(8,128)})) %all-reduce.5.cloned.1.call-update) | async-done | bytes 1118224 | tf_op jit(solution)/shard_map/psum | solution.py:60
  246.9 1.0 slice_add_fusion
  247.9 0.1 copy.45
  248.0 0.9 fusion.20
  248.9 11.7 %cholesky.16 = f32[128,128]{1,0:T(8,128)S(1)} custom-call(f32[128,128]{1,0:T(8,128)S(1)} %fusion.20), custom_call_target="Cholesky" | custom-call | tf_op jit(solution)/shard_map/jit(cholesky)/cholesky | solution.py:63
  260.7 0.6 compare_reduce_fusion
  261.3 0.7 fusion.13
  262.0 9.8 %custom-call.16 = f32[1,128,128]{1,2,0:T(8,128)S(1)} custom-call(f32[1,128,128]{2,1,0:T(8,128)S(1)} %fusion.13), custom_call_target="InvertDiagBlocksLowerTriangular" | custom-call | tf_op jit(solution)/shard_map/jit(_cho_solve)/triangular_solve | solution.py:71
  271.8 2.0 fusion.16
  273.8 0.8 convolution_bitcast_fusion.3
  274.6 0.2 convolution_bitcast_fusion.2
  274.8 1.1 fusion.14
  276.0 27.1 %convolution_subtract_fusion = f32[4096,2048]{1,0:T(8,128)} fusion(f32[4096,2048]{1,0:T(8,128)} %param.23, f32[128,4096]{1,0:T(8,128)S(1)} %fusion.16, f32[128,2048]{1,0:T(8,128)S(1)} %fusion.14), kind=kOutput, calls=%fused_computation | convolution fusion | flops 6450839552 | bytes 70254592 | tf_op jit(solution)/shard_map/mi,mj->ij/dot_general | solution.py:70
  303.1 0.2 fusion.31
  303.3 1.3 dynamic-slice_add_fusion
  (26 shorter events, 0.4 us)
Async XLA Ops:
  7.2 7.3 %copy-start = (f32[4,128]{1,0:T(4,128)S(1)}, f32[4,128]{1,0:T(4,128)}, u32[]{:S(2)}) copy-start(f32[4,128]{1,0:T(4,128)} %param.20) | copy-start | bytes 6148
  7.2 45.6 %all-gather.4.cloned.1.call-start = ((), (), s32[]{:S(2)}) async-start(), calls=%async_computation.3 | async-start | bytes 1310720 | tf_op jit(solution)/shard_map/all_gather | solution.py:43
  36.9 111.1 %reduce-scatter.2.cloned.1.call-start = ((), (), s32[]{:S(2)}) async-start(), calls=%async_computation.4 | async-start | bytes 2359296 | tf_op jit(solution)/shard_map/reduce_scatter | solution.py:46
  76.5 5.6 %copy-start.5 = (s32[256]{0:T(256)S(1)}, s32[256]{0:T(256)}, u32[]{:S(2)}) copy-start(s32[256]{0:T(256)} %param.17) | copy-start | bytes 3076
  77.5 18.4 %all-to-all-start.1 = ((f32[4,32,512]{2,0,1:T(4,128)}), f32[4,32,512]{2,0,1:T(4,128)S(1)}, u32[]{:S(2)}, u32[]{:S(2)}) async-start(f32[4,32,512]{2,0,1:T(4,128)} %copy.41), calls=%async_computation.2 | async-start | bytes 524288 | tf_op jit(solution)/shard_map/all_to_all | solution.py:44
  82.1 123.4 %all-gather.6.cloned.1.call-start = ((), (), s32[]{:S(2)}) async-start(), calls=%async_computation.5 | async-start | bytes 2985984 | tf_op jit(solution)/shard_map/all_gather | solution.py:50
  151.3 95.6 %all-reduce.5.cloned.1.call-start = ((), (), s32[]{:S(2)}) async-start(), calls=%async_computation.6 | async-start | bytes 2236416 | tf_op jit(solution)/shard_map/psum | solution.py:60
  209.1 37.8 %copy-start.4 = (f32[128]{0:T(128)S(1)}, f32[128]{0:T(128)}, u32[]{:S(2)}) copy-start(f32[128]{0:T(128)} %param.22) | copy-start | bytes 1540
  211.1 62.7 %copy-start.6 = (f32[128]{0:T(128)S(1)}, f32[128]{0:T(128)}, u32[]{:S(2)}) copy-start(f32[128]{0:T(128)} %param.21) | copy-start | bytes 1540
  246.9 27.9 %copy-start.3 = (f32[2048,128]{1,0:T(8,128)S(1)}, f32[2048,128]{1,0:T(8,128)}, u32[]{:S(2)}) copy-start(f32[2048,128]{1,0:T(8,128)} %get-tuple-element.27) | copy-start | bytes 3145732
  276.0 27.1 %copy-start.2 = (f32[512,128]{0,1:T(8,128)S(1)}, f32[512,128]{0,1:T(8,128)}, u32[]{:S(2)}) copy-start(f32[512,128]{0,1:T(8,128)} %reduce-scatter.2.cloned.1.call-done) | copy-start | bytes 786436
  276.0 28.7 %copy-start.1 = (f32[4,128]{1,0:T(4,128)S(1)}, f32[4,128]{1,0:T(4,128)}, u32[]{:S(2)}) copy-start(f32[4,128]{1,0:T(4,128)} %param.20) | copy-start | bytes 6148
Sparse Core Ops, SparseCore 0:
  37.0 15.7 all-gather.3
  76.7 71.3 reduce-scatter.1
  151.4 54.0 all-gather.5
  211.2 35.6 all-reduce.4

commit v2 on v1

--- a/solution.py
+++ b/solution.py
@@ -4,6 +4,25 @@
 from jax.sharding import PartitionSpec as P
 
 FR = 64
+
+
+def broadcast_rows(buf, n_row, n_col, factor):
+    bits = []
+    b = 1
+    while b < n_row:
+        bits.append(b)
+        b *= 2
+    bits = bits[1:][::-1] + bits[:1]
+    held = [0]
+    for bit in bits:
+        perm = []
+        for c in range(n_col):
+            s = c // factor
+            for rel in held:
+                perm.append(((s ^ rel) * n_col + c, (s ^ rel ^ bit) * n_col + c))
+        buf = buf + lax.ppermute(buf, ("row", "col"), perm)
+        held = held + [rel ^ bit for rel in held]
+    return buf
 
 
 def on_device(
@@ -64,7 +83,7 @@
     factor = n_col // n_row
     half_rows = lax.dynamic_slice_in_dim(gain_rows, col_id % factor * col_w, col_w, 0)
     mine = row_id == col_id // factor
-    gain_col = lax.psum(jnp.where(mine, half_rows, jnp.zeros_like(half_rows)), "row")
+    gain_col = broadcast_rows(jnp.where(mine, half_rows, jnp.zeros_like(half_rows)), n_row, n_col, factor)
     white_row = jax.scipy.linalg.solve_triangular(lower, gain_rows.T, lower=True)
     white_col = jax.scipy.linalg.solve_triangular(lower, gain_col.T, lower=True)
     new_cov = cov - jnp.einsum("mi,mj->ij", white_row, white_col, precision=mid)

time: 312 us -> 310 us (level)
  waiting for transfers between devices: 171 us -> 163 us
  starting transfers between devices: 4.95 us -> 10.9 us
    psum x1, waiting for transfers between devices: 35.8 us -> 27.2 us  [on_device(): small = lax.psum(jnp.concatenate([gram_row, slots], axis=0), 'row')]
    ppermute x0 -> x2, starting transfers between devices: none -> 6.17 us  [broadcast_rows(): buf = buf + lax.ppermute(buf, ('row', 'col'), perm)]
  transfers between devices with their start and end apart: 5 -> 7, of which waited for: 5 -> 5; matrix products, arithmetic and copies ran while one was open for 0% -> 10% of each run, Pallas kernels for 0% -> 0%
where the time goes in v2:
time: 310 us; the launch traced here: 309 us
  waiting for transfers between devices  163 us (53%)
  matrix products  61.7 us (20%)
  other arithmetic  36.3 us (12%)
  blocking collectives  16 us (5%)
  between operations  14.1 us (5%)
  starting transfers between devices  10.9 us (4%)
  local copies, waits for them, and re-layouts  6.88 us (2%)
    all_gather x1, waiting for transfers between devices, on_device(): gathered = lax.all_gather(payload, 'col', axis=0)  54.1 us
    reduce_scatter x1, waiting for transfers between devices, on_device(): lax.psum_scatter(partial_rows, 'col', scatter_dimension=0, tiled=True)  52.2 us
    psum x1, waiting for transfers between devices, on_device(): small = lax.psum(jnp.concatenate([gram_row, slots], axis=0), 'row')  27.2 us
    dot_general x1, matrix products, on_device(): new_cov = cov - jnp.einsum('mi,mj->ij', white_row, white_col, precision=mid)  26.9 us
    dot_general x1, matrix products, on_device(): partial_rows = jnp.einsum('ik,mk->im', cov, grad_col, precision=mid)  23.8 us
    all_to_all x1, blocking collectives, on_device(): lax.all_to_all(grads, 'col', split_axis=1, concat_axis=0, tiled=True)  16 us
    all_gather x1, waiting for transfers between devices, on_device(): grad_col = lax.all_gather(col_part, 'row', axis=0, tiled=True)  15.8 us
    all_to_all x1, waiting for transfers between devices, on_device(): lax.all_to_all(grads, ('row', 'col'), split_axis=1, concat_axis=0, tiled=...  13.5 us
  transfers between devices with their start and end apart: 7, of which 5 were waited for; matrix products, arithmetic and copies ran while one was open for 10% of the time, Pallas kernels for 0%

profile of v2, /device:TPU:0, one launch (start us, length us, event | category | flops | bytes accessed | tf_op | source)
XLA Modules:
  0.0 308.7 jit_solution(14348470481380371568)
XLA Ops:
  7.2 0.7 fusion.25
  7.9 0.9 copy.37
  8.8 5.7 %convert_reduce_fusion = f32[256,256]{1,0:T(8,128)S(1)} fusion(s32[256,32]{1,0:T(8,128)S(1)} %copy.37), kind=kLoop, calls=%fused_computation.1 | loop fusion | flops 6225920 | bytes 294912 | tf_op jit(solution)/shard_map/reduce_sum | solution.py:41
  14.5 1.0 fusion.14
  15.5 1.2 convolution_multiply_fusion.2
  16.7 1.3 fusion.2
  18.0 0.1 copy.38
  18.1 1.2 multiply_reduce_fusion
  19.2 0.6 fusion
  19.9 0.2 copy.40
  20.1 16.0 %all_to_all.38 = f32[4,8,2048]{2,0,1:T(4,128)S(1)} all-to-all(f32[4,8,2048]{2,0,1:T(4,128)S(1)} %copy.40), channel_id=1, replica_groups=mesh['row'=4,'col'=8] {'col'}, dimensions={1} | all-to-all | bytes 524288 | tf_op jit(solution)/shard_map/all_to_all | solution.py:61
  36.1 0.8 all_to_all.31
  36.9 15.8 %all-gather.4.cloned.1.call-done = f32[128,2048]{1,0:T(8,128)} async-done(((f32[32,2048]{1,0:T(8,128)}), f32[128,2048]{1,0:T(8,128)}) %all-gather.4.cloned.1.call-update) | async-done | bytes 1048592 | tf_op jit(solution)/shard_map/all_gather | solution.py:62
  52.8 23.8 %convolution_bitcast_fusion = f32[4096,128]{0,1:T(8,128)} fusion(f32[128,2048]{1,0:T(8,128)} %all-gather.4.cloned.1.call-done, f32[4096,2048]{1,0:T(8,128)} %param.23), kind=kOutput, calls=%fused_computation.3 | convolution fusion | flops 6442450944 | bytes 36700160 | tf_op jit(solution)/shard_map/ik,mk->im/dot_general | solution.py:64
  76.6 0.9 copy.41
  77.5 4.6 %all-to-all-start.1 = ((f32[4,32,512]{2,0,1:T(4,128)}), f32[4,32,512]{2,0,1:T(4,128)S(1)}, u32[]{:S(2)}, u32[]{:S(2)}) async-start(f32[4,32,512]{2,0,1:T(4,128)} %copy.41), calls=%async_computation.2 | async-start | bytes 524288 | tf_op jit(solution)/shard_map/all_to_all | solution.py:63
  82.1 0.1 fusion.4
  82.2 0.1 copy.42
  82.3 13.5 %all-to-all-done.1 = f32[4,32,512]{2,0,1:T(4,128)S(1)} async-done(((f32[4,32,512]{2,0,1:T(4,128)}), f32[4,32,512]{2,0,1:T(4,128)S(1)}, u32[]{:S(2)}, u32[]{:S(2)}) %all-to-all-start.1) | async-done | bytes 262176 | tf_op jit(solution)/shard_map/all_to_all | solution.py:63
  95.8 0.1 all_to_all.35
  95.9 52.2 %reduce-scatter.2.cloned.1.call-done = f32[512,128]{0,1:T(8,128)} async-done(((f32[4096,128]{0,1:T(8,128)}), f32[512,128]{0,1:T(8,128)}) %reduce-scatter.2.cloned.1.call-update) | async-done | bytes 262160 | tf_op jit(solution)/shard_map/reduce_scatter | solution.py:65
  148.1 1.3 fusion.31
  149.5 1.0 select_maximum_fusion
  150.4 0.9 copy.44
  151.4 54.1 %all-gather.6.cloned.1.call-done = f32[5184,128]{1,0:T(8,128)} async-done(((f32[648,128]{1,0:T(8,128)}), f32[5184,128]{1,0:T(8,128)}) %all-gather.6.cloned.1.call-update) | async-done | bytes 2654224 | tf_op jit(solution)/shard_map/all_gather | solution.py:69
  205.5 0.8 slice_reduce_fusion.1
  206.3 1.1 slice_reduce_fusion
  207.4 1.7 slice.84
  209.2 1.0 dynamic-slice_select_fusion
  210.3 3.6 %collective-permute-start = (f32[2048,128]{1,0:T(8,128)}, f32[2048,128]{1,0:T(8,128)S(1)}, u32[]{:S(2)}, u32[]{:S(2)}) collective-permute-start(f32[2048,128]{1,0:T(8,128)} %dynamic-slice_select_fusion), channel_id=1, source_target_pairs={{0,16},{1,17},{10,26},{11,27},{20,4},{21,5},{30,14},{31,15}} | collective-permute-start | bytes 3145736 | tf_op jit(solution)/shard_map/ppermute | solution.py:23
  213.9 0.2 dynamic_update_slice.3
  214.1 0.6 pad_maximum_fusion
  214.8 27.2 %all-reduce.4.cloned.1.call-done = f32[136,128]{1,0:T(8,128)} async-done(((f32[136,128]{1,0:T(8,128)}), f32[136,128]{1,0:T(8,128)}) %all-reduce.4.cloned.1.call-update) | async-done | bytes 69648 | tf_op jit(solution)/shard_map/psum | solution.py:79
  242.0 0.9 slice_add_fusion
  243.0 0.9 fusion.21
  244.0 11.7 %cholesky.16 = f32[128,128]{1,0:T(8,128)S(1)} custom-call(f32[128,128]{1,0:T(8,128)S(1)} %fusion.21), custom_call_target="Cholesky" | custom-call | tf_op jit(solution)/shard_map/jit(cholesky)/cholesky | solution.py:82
  255.7 0.6 compare_reduce_fusion
  256.3 0.7 fusion.15
  257.0 9.8 %custom-call.16 = f32[1,128,128]{1,2,0:T(8,128)S(1)} custom-call(f32[1,128,128]{2,1,0:T(8,128)S(1)} %fusion.15), custom_call_target="InvertDiagBlocksLowerTriangular" | custom-call | tf_op jit(solution)/shard_map/jit(_cho_solve)/triangular_solve | solution.py:90
  266.8 0.1 fusion.50
  267.0 2.6 collective-permute-start.1
  269.5 0.8 convolution_bitcast_fusion.3
  270.4 0.2 convolution_bitcast_fusion.2
  270.6 0.3 fusion.32
  270.9 1.3 dynamic-slice_add_fusion
  272.2 2.0 fusion.17
  274.2 1.1 fusion.5
  275.3 26.9 %convolution_subtract_fusion = f32[4096,2048]{1,0:T(8,128)} fusion(f32[4096,2048]{1,0:T(8,128)} %param.23, f32[128,4096]{1,0:T(8,128)S(1)} %fusion.17, f32[128,2048]{1,0:T(8,128)S(1)} %fusion.5), kind=kOutput, calls=%fused_computation | convolution fusion | flops 6450839552 | bytes 70254592 | tf_op jit(solution)/shard_map/mi,mj->ij/dot_general | solution.py:89
  (29 shorter events, 0.6 us)
Async XLA Ops:
  7.2 7.3 %copy-start = (f32[4,128]{1,0:T(4,128)S(1)}, f32[4,128]{1,0:T(4,128)}, u32[]{:S(2)}) copy-start(f32[4,128]{1,0:T(4,128)} %param.20) | copy-start | bytes 6148
  7.2 45.6 %all-gather.4.cloned.1.call-start = ((), (), s32[]{:S(2)}) async-start(), calls=%async_computation.3 | async-start | bytes 1310720 | tf_op jit(solution)/shard_map/all_gather | solution.py:62
  36.9 111.2 %reduce-scatter.2.cloned.1.call-start = ((), (), s32[]{:S(2)}) async-start(), calls=%async_computation.4 | async-start | bytes 2359296 | tf_op jit(solution)/shard_map/reduce_scatter | solution.py:65
  76.5 5.6 %copy-start.4 = (s32[256]{0:T(256)S(1)}, s32[256]{0:T(256)}, u32[]{:S(2)}) copy-start(s32[256]{0:T(256)} %param.17) | copy-start | bytes 3076
  77.5 18.3 %all-to-all-start.1 = ((f32[4,32,512]{2,0,1:T(4,128)}), f32[4,32,512]{2,0,1:T(4,128)S(1)}, u32[]{:S(2)}, u32[]{:S(2)}) async-start(f32[4,32,512]{2,0,1:T(4,128)} %copy.41), calls=%async_computation.2 | async-start | bytes 524288 | tf_op jit(solution)/shard_map/all_to_all | solution.py:63
  82.1 123.4 %all-gather.6.cloned.1.call-start = ((), (), s32[]{:S(2)}) async-start(), calls=%async_computation.6 | async-start | bytes 2985984 | tf_op jit(solution)/shard_map/all_gather | solution.py:69
  151.4 90.6 %all-reduce.4.cloned.1.call-start = ((), (), s32[]{:S(2)}) async-start(), calls=%async_computation.5 | async-start | bytes 139264 | tf_op jit(solution)/shard_map/psum | solution.py:79
  207.4 34.6 %copy-start.3 = (f32[128]{0:T(128)S(1)}, f32[128]{0:T(128)}, u32[]{:S(2)}) copy-start(f32[128]{0:T(128)} %param.22) | copy-start | bytes 1540
  209.2 60.3 %copy-start.5 = (f32[128]{0:T(128)S(1)}, f32[128]{0:T(128)}, u32[]{:S(2)}) copy-start(f32[128]{0:T(128)} %param.21) | copy-start | bytes 1540
  209.2 61.4 %copy-start.2 = (f32[512,128]{0,1:T(8,128)S(1)}, f32[512,128]{0,1:T(8,128)}, u32[]{:S(2)}) copy-start(f32[512,128]{0,1:T(8,128)} %reduce-scatter.2.cloned.1.call-done) | copy-start | bytes 786436
  210.3 56.6 %collective-permute-start = (f32[2048,128]{1,0:T(8,128)}, f32[2048,128]{1,0:T(8,128)S(1)}, u32[]{:S(2)}, u32[]{:S(2)}) collective-permute-start(f32[2048,128]{1,0:T(8,128)} %dynamic-slice_select_fusion), channel_id=1, source_target_pairs={{0,16},{1,17},{10,26},{11,27},{20,4},{21,5},{30,14},{31,15}} | collective-permute-start | bytes 3145736 | tf_op jit(solution)/shard_map/ppermute | solution.py:23
  267.0 7.2 %collective-permute-start.1 = (f32[2048,128]{1,0:T(8,128)S(1)}, f32[2048,128]{1,0:T(8,128)S(1)}, u32[]{:S(2)}, u32[]{:S(2)}) collective-permute-start(f32[2048,128]{1,0:T(8,128)S(1)} %fusion.50), channel_id=1, source_target_pairs={{0,8},{16,24},{1,9},{17,25},{10,2},{26,18},{11,3},{27,19},{20,28},... | collective-permute-start | bytes 3145736 | tf_op jit(solution)/shard_map/ppermute | solution.py:23
  275.3 26.9 %copy-start.1 = (f32[4,128]{1,0:T(4,128)S(1)}, f32[4,128]{1,0:T(4,128)}, u32[]{:S(2)}) copy-start(f32[4,128]{1,0:T(4,128)} %param.20) | copy-start | bytes 6148
Sparse Core Ops, SparseCore 0:
  37.0 15.7 all-gather.3
  76.7 71.4 reduce-scatter.1
  151.5 53.9 all-gather.5
  214.9 27.0 all-reduce.3

commit v3 on v2

--- a/solution.py
+++ b/solution.py
@@ -22,6 +22,14 @@
                 perm.append(((s ^ rel) * n_col + c, (s ^ rel ^ bit) * n_col + c))
         buf = buf + lax.ppermute(buf, ("row", "col"), perm)
         held = held + [rel ^ bit for rel in held]
+    return buf
+
+
+def butterfly_sum(buf, axis, size):
+    bit = 1
+    while bit < size:
+        buf = buf + lax.ppermute(buf, axis, [(i, i ^ bit) for i in range(size)])
+        bit *= 2
     return buf
 
 
@@ -76,7 +84,7 @@
         row_id * n_col * frames,
         1,
     )
-    small = lax.psum(jnp.concatenate([gram_row, slots], axis=0), "row")
+    small = butterfly_sum(jnp.concatenate([gram_row, slots], axis=0), "row", n_row)
     gram = small[:m_all] + jnp.diag(noise)
     pred_all = small[m_all]
     lower = jnp.linalg.cholesky(gram)

time: 310 us -> 297 us (0.958)
  waiting for transfers between devices: 163 us -> 148 us
    psum x1 -> x0, waiting for transfers between devices: 27.2 us -> none  [on_device(): small = lax.psum(jnp.concatenate([gram_row, slots], axis=0), 'row')]
    ppermute x0 -> x2, waiting for transfers between devices: none -> 12.4 us  [butterfly_sum(): buf = buf + lax.ppermute(buf, axis, [(i, i ^ bit) for i in range(size)])]
  transfers between devices with their start and end apart: 7 -> 8, of which waited for: 5 -> 5; matrix products, arithmetic and copies ran while one was open for 10% -> 12% of each run, Pallas kernels for 0% -> 0%
where the time goes in v3:
time: 297 us; the launch traced here: 296 us
  waiting for transfers between devices  148 us (50%)
  matrix products  61 us (21%)
  other arithmetic  38.4 us (13%)
  blocking collectives  16 us (5%)
  between operations  14.1 us (5%)
  starting transfers between devices  10.2 us (3%)
  local copies, waits for them, and re-layouts  8.23 us (3%)
    all_gather x1, waiting for transfers between devices, on_device(): gathered = lax.all_gather(payload, 'col', axis=0)  54.1 us
    reduce_scatter x1, waiting for transfers between devices, on_device(): lax.psum_scatter(partial_rows, 'col', scatter_dimension=0, tiled=True)  52.1 us
    dot_general x1, matrix products, on_device(): new_cov = cov - jnp.einsum('mi,mj->ij', white_row, white_col, precision=mid)  26.9 us
    dot_general x1, matrix products, on_device(): partial_rows = jnp.einsum('ik,mk->im', cov, grad_col, precision=mid)  23.8 us
    all_to_all x1, blocking collectives, on_device(): lax.all_to_all(grads, 'col', split_axis=1, concat_axis=0, tiled=True)  16 us
    all_gather x1, waiting for transfers between devices, on_device(): grad_col = lax.all_gather(col_part, 'row', axis=0, tiled=True)  15.8 us
    all_to_all x1, waiting for transfers between devices, on_device(): lax.all_to_all(grads, ('row', 'col'), split_axis=1, concat_axis=0, tiled=...  13.5 us
    another operation x3, other arithmetic, on_device(): lower = jnp.linalg.cholesky(gram)  13.2 us
  transfers between devices with their start and end apart: 8, of which 5 were waited for; matrix products, arithmetic and copies ran while one was open for 12% of the time, Pallas kernels for 0%

profile of v3, /device:TPU:0, one launch (start us, length us, event | category | flops | bytes accessed | tf_op | source)
XLA Modules:
  0.0 296.0 jit_solution(10972515949585393419)
XLA Ops:
  7.2 0.7 fusion.25
  7.9 0.9 copy.37
  8.8 5.7 %convert_reduce_fusion = f32[256,256]{1,0:T(8,128)S(1)} fusion(s32[256,32]{1,0:T(8,128)S(1)} %copy.37), kind=kLoop, calls=%fused_computation.1 | loop fusion | flops 6225920 | bytes 294912 | tf_op jit(solution)/shard_map/reduce_sum | solution.py:49
  14.5 1.0 fusion.14
  15.5 1.2 convolution_multiply_fusion.2
  16.7 1.3 fusion.2
  18.1 1.2 multiply_reduce_fusion
  19.2 0.6 fusion
  19.9 0.2 copy.40
  20.1 16.0 %all_to_all.38 = f32[4,8,2048]{2,0,1:T(4,128)S(1)} all-to-all(f32[4,8,2048]{2,0,1:T(4,128)S(1)} %copy.40), channel_id=1, replica_groups=mesh['row'=4,'col'=8] {'col'}, dimensions={1} | all-to-all | bytes 524288 | tf_op jit(solution)/shard_map/all_to_all | solution.py:69
  36.1 0.8 all_to_all.31
  36.9 15.8 %all-gather.4.cloned.1.call-done = f32[128,2048]{1,0:T(8,128)} async-done(((f32[32,2048]{1,0:T(8,128)}), f32[128,2048]{1,0:T(8,128)}) %all-gather.4.cloned.1.call-update) | async-done | bytes 1048592 | tf_op jit(solution)/shard_map/all_gather | solution.py:70
  52.8 23.8 %convolution_bitcast_fusion = f32[4096,128]{0,1:T(8,128)} fusion(f32[128,2048]{1,0:T(8,128)} %all-gather.4.cloned.1.call-done, f32[4096,2048]{1,0:T(8,128)} %param.23), kind=kOutput, calls=%fused_computation.3 | convolution fusion | flops 6442450944 | bytes 36700160 | tf_op jit(solution)/shard_map/ik,mk->im/dot_general | solution.py:72
  76.6 0.9 copy.41
  77.4 4.6 %all-to-all-start.1 = ((f32[4,32,512]{2,0,1:T(4,128)}), f32[4,32,512]{2,0,1:T(4,128)S(1)}, u32[]{:S(2)}, u32[]{:S(2)}) async-start(f32[4,32,512]{2,0,1:T(4,128)} %copy.41), calls=%async_computation.2 | async-start | bytes 524288 | tf_op jit(solution)/shard_map/all_to_all | solution.py:71
  82.1 0.1 fusion.4
  82.2 0.1 copy.42
  82.3 13.5 %all-to-all-done.1 = f32[4,32,512]{2,0,1:T(4,128)S(1)} async-done(((f32[4,32,512]{2,0,1:T(4,128)}), f32[4,32,512]{2,0,1:T(4,128)S(1)}, u32[]{:S(2)}, u32[]{:S(2)}) %all-to-all-start.1) | async-done | bytes 262176 | tf_op jit(solution)/shard_map/all_to_all | solution.py:71
  95.9 52.1 %reduce-scatter.2.cloned.1.call-done = f32[512,128]{0,1:T(8,128)} async-done(((f32[4096,128]{0,1:T(8,128)}), f32[512,128]{0,1:T(8,128)}) %reduce-scatter.2.cloned.1.call-update) | async-done | bytes 262160 | tf_op jit(solution)/shard_map/reduce_scatter | solution.py:73
  148.0 1.3 fusion.32
  149.4 1.0 select_maximum_fusion
  150.4 0.9 copy.44
  151.3 54.1 %all-gather.6.cloned.1.call-done = f32[5184,128]{1,0:T(8,128)} async-done(((f32[648,128]{1,0:T(8,128)}), f32[5184,128]{1,0:T(8,128)}) %all-gather.6.cloned.1.call-update) | async-done | bytes 2654224 | tf_op jit(solution)/shard_map/all_gather | solution.py:77
  205.4 0.8 slice_reduce_fusion.1
  206.2 1.1 slice_reduce_fusion
  207.3 1.7 slice.84
  209.1 0.2 dynamic_update_slice.3
  209.4 1.0 dynamic-slice_select_fusion
  210.5 3.8 %collective-permute-start.2 = (f32[2048,128]{1,0:T(8,128)}, f32[2048,128]{1,0:T(8,128)S(1)}, u32[]{:S(2)}, u32[]{:S(2)}) collective-permute-start(f32[2048,128]{1,0:T(8,128)} %dynamic-slice_select_fusion), channel_id=1, source_target_pairs={{0,16},{1,17},{10,26},{11,27},{20,4},{21,5},{30,14},{31,15}} | collective-permute-start | bytes 3145736 | tf_op jit(solution)/shard_map/ppermute | solution.py:23
  214.4 0.5 copy-done.3
  215.0 12.4 %collective-permute-done.1 = f32[136,128]{1,0:T(8,128)} collective-permute-done((f32[136,128]{1,0:T(8,128)S(1)}, f32[136,128]{1,0:T(8,128)}, u32[]{:S(2)}, u32[]{:S(2)}) %collective-permute-start.1) | collective-permute-done | bytes 69664 | tf_op jit(solution)/shard_map/ppermute | solution.py:31
  227.3 0.9 add.74
  228.3 0.7 slice_add_fusion
  229.0 0.9 copy.45
  229.9 0.7 fusion.21
  230.6 12.5 %cholesky.16 = f32[128,128]{1,0:T(8,128)S(1)} custom-call(f32[128,128]{1,0:T(8,128)} %fusion.21), custom_call_target="Cholesky" | custom-call | tf_op jit(solution)/shard_map/jit(cholesky)/cholesky | solution.py:90
  243.2 0.6 compare_reduce_fusion
  243.8 1.3 fusion.15
  245.1 10.6 %custom-call.16 = f32[1,128,128]{1,2,0:T(8,128)S(1)} custom-call(f32[1,128,128]{2,1,0:T(8,128)} %fusion.15), custom_call_target="InvertDiagBlocksLowerTriangular" | custom-call | tf_op jit(solution)/shard_map/jit(_cho_solve)/triangular_solve | solution.py:98
  255.8 0.1 fusion.51
  255.9 1.6 collective-permute-start.3
  257.5 0.2 convolution_bitcast_fusion.3
  257.6 0.2 convolution_bitcast_fusion.2
  257.8 0.3 fusion.33
  258.1 1.3 dynamic-slice_add_fusion
  259.5 2.0 fusion.17
  261.5 1.1 fusion.5
  262.6 26.9 %convolution_subtract_fusion = f32[4096,2048]{1,0:T(8,128)} fusion(f32[4096,2048]{1,0:T(8,128)} %param.23, f32[128,4096]{1,0:T(8,128)S(1)} %fusion.17, f32[128,2048]{1,0:T(8,128)S(1)} %fusion.5), kind=kOutput, calls=%fused_computation | convolution fusion | flops 6450839552 | bytes 70254592 | tf_op jit(solution)/shard_map/mi,mj->ij/dot_general | solution.py:97
  (34 shorter events, 0.8 us)
Async XLA Ops:
  7.2 7.3 %copy-start = (f32[4,128]{1,0:T(4,128)S(1)}, f32[4,128]{1,0:T(4,128)}, u32[]{:S(2)}) copy-start(f32[4,128]{1,0:T(4,128)} %param.20) | copy-start | bytes 6148
  7.2 45.6 %all-gather.4.cloned.1.call-start = ((), (), s32[]{:S(2)}) async-start(), calls=%async_computation.3 | async-start | bytes 1310720 | tf_op jit(solution)/shard_map/all_gather | solution.py:70
  36.9 111.1 %reduce-scatter.2.cloned.1.call-start = ((), (), s32[]{:S(2)}) async-start(), calls=%async_computation.4 | async-start | bytes 2359296 | tf_op jit(solution)/shard_map/reduce_scatter | solution.py:73
  76.5 5.6 %copy-start.5 = (s32[256]{0:T(256)S(1)}, s32[256]{0:T(256)}, u32[]{:S(2)}) copy-start(s32[256]{0:T(256)} %param.17) | copy-start | bytes 3076
  77.4 18.3 %all-to-all-start.1 = ((f32[4,32,512]{2,0,1:T(4,128)}), f32[4,32,512]{2,0,1:T(4,128)S(1)}, u32[]{:S(2)}, u32[]{:S(2)}) async-start(f32[4,32,512]{2,0,1:T(4,128)} %copy.41), calls=%async_computation.2 | async-start | bytes 524288 | tf_op jit(solution)/shard_map/all_to_all | solution.py:71
  82.1 123.3 %all-gather.6.cloned.1.call-start = ((), (), s32[]{:S(2)}) async-start(), calls=%async_computation.5 | async-start | bytes 2985984 | tf_op jit(solution)/shard_map/all_gather | solution.py:77
  207.3 21.0 %copy-start.4 = (f32[128]{0:T(128)S(1)}, f32[128]{0:T(128)}, u32[]{:S(2)}) copy-start(f32[128]{0:T(128)} %param.22) | copy-start | bytes 1540
  209.4 5.0 %collective-permute-start = (f32[136,128]{1,0:T(8,128)S(1)}, f32[136,128]{1,0:T(8,128)S(1)}, u32[]{:S(2)}, u32[]{:S(2)}) collective-permute-start(f32[136,128]{1,0:T(8,128)S(1)} %pad_maximum_fusion), channel_id=1, source_target_pairs={{0,8},{8,0},{16,24},{24,16},{1,9},{9,1},{17,25},{25,17},{2,10},{10... | collective-permute-start | bytes 208904 | tf_op jit(solution)/shard_map/ppermute | solution.py:31
  209.4 48.0 %copy-start.6 = (f32[128]{0:T(128)S(1)}, f32[128]{0:T(128)}, u32[]{:S(2)}) copy-start(f32[128]{0:T(128)} %param.21) | copy-start | bytes 1540
  210.5 47.3 %copy-start.2 = (f32[512,128]{0,1:T(8,128)S(1)}, f32[512,128]{0,1:T(8,128)}, u32[]{:S(2)}) copy-start(f32[512,128]{0,1:T(8,128)} %reduce-scatter.2.cloned.1.call-done) | copy-start | bytes 786436
  210.5 45.3 %collective-permute-start.2 = (f32[2048,128]{1,0:T(8,128)}, f32[2048,128]{1,0:T(8,128)S(1)}, u32[]{:S(2)}, u32[]{:S(2)}) collective-permute-start(f32[2048,128]{1,0:T(8,128)} %dynamic-slice_select_fusion), channel_id=1, source_target_pairs={{0,16},{1,17},{10,26},{11,27},{20,4},{21,5},{30,14},{31,15}} | collective-permute-start | bytes 3145736 | tf_op jit(solution)/shard_map/ppermute | solution.py:23
  214.3 0.6 copy-start.3
  214.3 13.0 %collective-permute-start.1 = (f32[136,128]{1,0:T(8,128)S(1)}, f32[136,128]{1,0:T(8,128)}, u32[]{:S(2)}, u32[]{:S(2)}) collective-permute-start(f32[136,128]{1,0:T(8,128)S(1)} %fusion.31), channel_id=1, source_target_pairs={{0,16},{8,24},{16,0},{24,8},{1,17},{9,25},{17,1},{25,9},{2,18},{10... | collective-permute-start | bytes 208904 | tf_op jit(solution)/shard_map/ppermute | solution.py:31
  255.9 5.6 %collective-permute-start.3 = (f32[2048,128]{1,0:T(8,128)S(1)}, f32[2048,128]{1,0:T(8,128)S(1)}, u32[]{:S(2)}, u32[]{:S(2)}) collective-permute-start(f32[2048,128]{1,0:T(8,128)S(1)} %fusion.51), channel_id=1, source_target_pairs={{0,8},{16,24},{1,9},{17,25},{10,2},{26,18},{11,3},{27,19},{20,28},... | collective-permute-start | bytes 3145736 | tf_op jit(solution)/shard_map/ppermute | solution.py:23
  262.6 26.9 %copy-start.1 = (f32[4,128]{1,0:T(4,128)S(1)}, f32[4,128]{1,0:T(4,128)}, u32[]{:S(2)}) copy-start(f32[4,128]{1,0:T(4,128)} %param.20) | copy-start | bytes 6148
Sparse Core Ops, SparseCore 0:
  37.0 15.7 all-gather.3
  76.7 71.3 reduce-scatter.1
  151.4 53.9 all-gather.5

commit v4 on v3

--- a/solution.py
+++ b/solution.py
@@ -31,6 +31,19 @@
         buf = buf + lax.ppermute(buf, axis, [(i, i ^ bit) for i in range(size)])
         bit *= 2
     return buf
+
+
+def halving_scatter(x, axis, size, me):
+    nbits = size.bit_length() - 1
+    x = x.reshape((2,) * nbits + (x.shape[0] // size,) + x.shape[1:])
+    for step in range(nbits):
+        bit = 1 << step
+        dim = nbits - 1 - step
+        mine = (me // bit) % 2
+        keep = lax.dynamic_index_in_dim(x, mine, dim, keepdims=False)
+        send = lax.dynamic_index_in_dim(x, 1 - mine, dim, keepdims=False)
+        x = keep + lax.ppermute(send, axis, [(i, i ^ bit) for i in range(size)])
+    return x
 
 
 def on_device(
@@ -70,7 +83,7 @@
     grad_col = lax.all_gather(col_part, "row", axis=0, tiled=True)
     grad_own = lax.all_to_all(grads, ("row", "col"), split_axis=1, concat_axis=0, tiled=True)
     partial_rows = jnp.einsum("ik,mk->im", cov, grad_col, precision=mid)
-    gain_own = lax.psum_scatter(partial_rows, "col", scatter_dimension=0, tiled=True)
+    gain_own = halving_scatter(partial_rows, "col", n_col, col_id)
     gram_own = jnp.einsum("mk,kn->mn", grad_own, gain_own, precision=hi)
     pred_pad = jnp.zeros((8, m_all), jnp.float32).at[0, :frames].set(pred_local)
     payload = jnp.concatenate([gain_own, gram_own, pred_pad], axis=0)

time: 297 us -> 287 us (0.966)
  waiting for transfers between devices: 148 us -> 126 us
  local copies, waits for them, and re-layouts: 8.23 us -> 16.7 us
  starting transfers between devices: 10.2 us -> 14.7 us
    reduce_scatter x1 -> x0, waiting for transfers between devices: 52.1 us -> none  [on_device(): lax.psum_scatter(partial_rows, 'col', scatter_dimension=0, tiled=True)]
    ppermute x0 -> x3, waiting for transfers between devices: none -> 42.2 us  [halving_scatter(): x = keep + lax.ppermute(send, axis, [(i, i ^ bit) for i in range(size)])]
    all_to_all x1, waiting for transfers between devices: 13.5 us -> 2.19 us  [on_device(): lax.all_to_all(grads, ('row', 'col'), split_axis=1, concat_axis=0, tiled=...]
    dynamic_slice x0 -> x4, local copies, waits for them, and re-layouts: none -> 6.07 us  [the longest x3 5.68 us: halving_scatter(): keep = lax.dynamic_index_in_dim(x, mine, dim, keepdims=False)]
    ppermute x0 -> x3, starting transfers between devices: none -> 5.34 us  [halving_scatter(): x = keep + lax.ppermute(send, axis, [(i, i ^ bit) for i in range(size)])]
  transfers between devices with their start and end apart: 8 -> 10, of which waited for: 5 -> 7; matrix products, arithmetic and copies ran while one was open for 12% -> 12% of each run, Pallas kernels for 0% -> 0%
where the time goes in v4:
time: 287 us; the launch traced here: 286 us
  waiting for transfers between devices  126 us (44%)
  matrix products  59.2 us (21%)
  other arithmetic  39 us (14%)
  local copies, waits for them, and re-layouts  16.7 us (6%)
  blocking collectives  16 us (6%)
  starting transfers between devices  14.7 us (5%)
  between operations  14.5 us (5%)
    all_gather x1, waiting for transfers between devices, on_device(): gathered = lax.all_gather(payload, 'col', axis=0)  53.7 us
    ppermute x3, waiting for transfers between devices, halving_scatter(): x = keep + lax.ppermute(send, axis, [(i, i ^ bit) for i in range(size)])  42.2 us
    dot_general x1, matrix products, on_device(): new_cov = cov - jnp.einsum('mi,mj->ij', white_row, white_col, precision=mid)  26.9 us
    dot_general x1, matrix products, on_device(): partial_rows = jnp.einsum('ik,mk->im', cov, grad_col, precision=mid)  22.8 us
    all_to_all x1, blocking collectives, on_device(): lax.all_to_all(grads, 'col', split_axis=1, concat_axis=0, tiled=True)  16 us
    all_gather x1, waiting for transfers between devices, on_device(): grad_col = lax.all_gather(col_part, 'row', axis=0, tiled=True)  15.9 us
    another operation x3, other arithmetic, on_device(): lower = jnp.linalg.cholesky(gram)  13.2 us
    ppermute x2, waiting for transfers between devices, butterfly_sum(): buf = buf + lax.ppermute(buf, axis, [(i, i ^ bit) for i in range(size)])  12.3 us
  transfers between devices with their start and end apart: 10, of which 7 were waited for; matrix products, arithmetic and copies ran while one was open for 12% of the time, Pallas kernels for 0%

profile of v4, /device:TPU:0, one launch (start us, length us, event | category | flops | bytes accessed | tf_op | source)
XLA Modules:
  0.0 286.4 jit_solution(285702926833517973)
XLA Ops:
  7.2 0.7 fusion.25
  7.9 0.9 copy.26
  8.8 5.7 %convert_reduce_fusion = f32[256,256]{1,0:T(8,128)S(1)} fusion(s32[256,32]{1,0:T(8,128)S(1)} %copy.26), kind=kLoop, calls=%fused_computation.1 | loop fusion | flops 6225920 | bytes 294912 | tf_op jit(solution)/shard_map/reduce_sum | solution.py:62
  14.5 1.0 fusion.14
  15.5 1.2 convolution_multiply_fusion.2
  16.7 1.3 fusion.2
  18.1 1.2 multiply_reduce_fusion
  19.2 0.6 fusion
  20.1 16.0 %all_to_all.38 = f32[4,8,2048]{2,0,1:T(4,128)S(1)} all-to-all(f32[4,8,2048]{2,0,1:T(4,128)S(1)} %copy.29), channel_id=1, replica_groups=mesh['row'=4,'col'=8] {'col'}, dimensions={1} | all-to-all | bytes 524288 | tf_op jit(solution)/shard_map/all_to_all | solution.py:82
  36.1 0.8 all_to_all.31
  36.9 15.9 %all-gather.4.cloned.1.call-done = f32[128,2048]{1,0:T(8,128)} async-done(((f32[32,2048]{1,0:T(8,128)}), f32[128,2048]{1,0:T(8,128)}) %all-gather.4.cloned.1.call-update) | async-done | bytes 1048592 | tf_op jit(solution)/shard_map/all_gather | solution.py:83
  52.8 22.8 %convolution_bitcast_fusion = f32[4096,128]{0,1:T(8,128)S(1)} fusion(f32[128,2048]{1,0:T(8,128)} %all-gather.4.cloned.1.call-done, f32[4096,2048]{1,0:T(8,128)} %param.23), kind=kOutput, calls=%fused_computation.3 | convolution fusion | flops 6442450944 | bytes 36700160 | tf_op jit(solution)/shard_map/ik,mk->im/dot_general | solution.py:85
  75.6 2.8 reshape.111
  78.4 4.4 %constant_dynamic-slice_fusion.3 = (f32[2,2,1,512,128]{3,2,1,0,4:T(1,128)S(1)}, f32[2,2,1,512,128]{3,2,1,0,4:T(1,128)S(1)}) fusion(f32[2,2,2,512,128]{3,2,1,0,4:T(2,128)} %reshape.111, s32[]{:T(128)S(6)} %select_n.75, s32[]{:T(128)S(6)} %select_n.76), kind=kLoop, calls=%fused_computation.63 | loop fusion | bytes 4194312 | tf_op jit(solution)/shard_map/jit(dynamic_index_in_dim)/dynamic_slice | solution.py:43
  82.7 0.5 copy.40
  83.3 1.5 collective-permute-start
  84.8 23.8 %collective-permute-done = f32[2,2,512,128]{2,1,0,3:T(2,128)S(1)} collective-permute-done((f32[2,2,512,128]{2,1,0,3:T(2,128)S(1)}, f32[2,2,512,128]{2,1,0,3:T(2,128)S(1)}, u32[]{:S(2)}, u32[]{:S(2)}) %collective-permute-start) | collective-permute-done | bytes 1048608 | tf_op jit(solution)/shard_map/ppermute | solution.py:45
  108.6 0.7 bitcast_add_fusion
  109.3 0.9 constant_dynamic-slice_fusion.1
  110.7 1.6 collective-permute-start.1
  112.3 0.9 copy.32
  113.1 3.7 %all-to-all-start.1 = ((f32[4,32,512]{2,0,1:T(4,128)}), f32[4,32,512]{2,0,1:T(4,128)S(1)}, u32[]{:S(2)}, u32[]{:S(2)}) async-start(f32[4,32,512]{2,0,1:T(4,128)} %copy.32), calls=%async_computation.1 | async-start | bytes 524288 | tf_op jit(solution)/shard_map/all_to_all | solution.py:84
  117.3 9.1 %collective-permute-done.1 = f32[2,512,128]{2,1,0:T(8,128)S(1)} collective-permute-done((f32[2,512,128]{2,1,0:T(8,128)S(1)}, f32[2,512,128]{2,1,0:T(8,128)S(1)}, u32[]{:S(2)}, u32[]{:S(2)}) %collective-permute-start.1) | collective-permute-done | bytes 524320 | tf_op jit(solution)/shard_map/ppermute | solution.py:45
  126.5 2.2 collective-permute-start.2
  128.8 2.2 all-to-all-done.1
  131.1 9.3 %collective-permute-done.2 = f32[512,128]{1,0:T(8,128)S(1)} collective-permute-done((f32[512,128]{1,0:T(8,128)S(1)}, f32[512,128]{1,0:T(8,128)S(1)}, u32[]{:S(2)}, u32[]{:S(2)}) %collective-permute-start.2) | collective-permute-done | bytes 262176 | tf_op jit(solution)/shard_map/ppermute | solution.py:45
  140.9 0.7 select_maximum_fusion
  141.7 53.7 %all-gather.6.cloned.1.call-done = f32[5184,128]{1,0:T(8,128)} async-done(((f32[648,128]{1,0:T(8,128)}), f32[5184,128]{1,0:T(8,128)}) %all-gather.6.cloned.1.call-update) | async-done | bytes 2654224 | tf_op jit(solution)/shard_map/all_gather | solution.py:90
  195.4 0.8 slice_reduce_fusion.1
  196.2 1.1 slice_reduce_fusion
  197.3 1.7 slice.84
  199.4 1.0 dynamic-slice_select_fusion
  200.5 3.8 %collective-permute-start.5 = (f32[2048,128]{1,0:T(8,128)}, f32[2048,128]{1,0:T(8,128)S(1)}, u32[]{:S(2)}, u32[]{:S(2)}) collective-permute-start(f32[2048,128]{1,0:T(8,128)} %dynamic-slice_select_fusion), channel_id=1, source_target_pairs={{0,16},{1,17},{10,26},{11,27},{20,4},{21,5},{30,14},{31,15}} | collective-permute-start | bytes 3145736 | tf_op jit(solution)/shard_map/ppermute | solution.py:23
  204.5 0.5 copy-done.2
  205.0 12.3 %collective-permute-done.4 = f32[136,128]{1,0:T(8,128)} collective-permute-done((f32[136,128]{1,0:T(8,128)S(1)}, f32[136,128]{1,0:T(8,128)}, u32[]{:S(2)}, u32[]{:S(2)}) %collective-permute-start.4) | collective-permute-done | bytes 69664 | tf_op jit(solution)/shard_map/ppermute | solution.py:31
  217.3 0.9 add.126
  218.2 0.7 slice_add_fusion
  219.0 0.9 copy.33
  219.9 0.7 fusion.21
  220.6 12.5 %cholesky.16 = f32[128,128]{1,0:T(8,128)S(1)} custom-call(f32[128,128]{1,0:T(8,128)} %fusion.21), custom_call_target="Cholesky" | custom-call | tf_op jit(solution)/shard_map/jit(cholesky)/cholesky | solution.py:103
  233.2 0.6 compare_reduce_fusion
  233.8 1.3 fusion.15
  235.1 10.6 %custom-call.16 = f32[1,128,128]{1,2,0:T(8,128)S(1)} custom-call(f32[1,128,128]{2,1,0:T(8,128)} %fusion.15), custom_call_target="InvertDiagBlocksLowerTriangular" | custom-call | tf_op jit(solution)/shard_map/jit(_cho_solve)/triangular_solve | solution.py:111
  245.9 1.6 collective-permute-start.6
  248.3 1.4 dynamic-slice_add_fusion
  249.6 2.0 fusion.17
  251.6 1.1 fusion.5
  252.7 26.9 %convolution_subtract_fusion = f32[4096,2048]{1,0:T(8,128)} fusion(f32[4096,2048]{1,0:T(8,128)} %param.23, f32[128,4096]{1,0:T(8,128)S(1)} %fusion.17, f32[128,2048]{1,0:T(8,128)S(1)} %fusion.5), kind=kOutput, calls=%fused_computation | convolution fusion | flops 6450839552 | bytes 70254592 | tf_op jit(solution)/shard_map/mi,mj->ij/dot_general | solution.py:110
  (43 shorter events, 3.3 us)
Async XLA Ops:
  7.2 7.3 %copy-start = (f32[4,128]{1,0:T(4,128)S(1)}, f32[4,128]{1,0:T(4,128)}, u32[]{:S(2)}) copy-start(f32[4,128]{1,0:T(4,128)} %param.20) | copy-start | bytes 6148
  7.2 45.6 %all-gather.4.cloned.1.call-start = ((), (), s32[]{:S(2)}) async-start(), calls=%async_computation.2 | async-start | bytes 1310720 | tf_op jit(solution)/shard_map/all_gather | solution.py:83
  83.3 25.4 %collective-permute-start = (f32[2,2,512,128]{2,1,0,3:T(2,128)S(1)}, f32[2,2,512,128]{2,1,0,3:T(2,128)S(1)}, u32[]{:S(2)}, u32[]{:S(2)}) collective-permute-start(f32[2,2,512,128]{2,1,0,3:T(2,128)S(1)} %bitcast.90), channel_id=1, source_target_pairs={{0,1},{1,0},{2,3},{3,2},{4,5},{5,4},{6,7},{7,6},{8,9},{9,8},{10,11... | collective-permute-start | bytes 3145736 | tf_op jit(solution)/shard_map/ppermute | solution.py:45
  110.7 15.7 %collective-permute-start.1 = (f32[2,512,128]{2,1,0:T(8,128)S(1)}, f32[2,512,128]{2,1,0:T(8,128)S(1)}, u32[]{:S(2)}, u32[]{:S(2)}) collective-permute-start(f32[2,512,128]{2,1,0:T(8,128)S(1)} %bitcast.93), channel_id=1, source_target_pairs={{0,2},{1,3},{2,0},{3,1},{4,6},{5,7},{6,4},{7,5},{8,10},{9,11},{10,... | collective-permute-start | bytes 1572872 | tf_op jit(solution)/shard_map/ppermute | solution.py:45
  112.3 16.5 %copy-start.4 = (s32[256]{0:T(256)S(1)}, s32[256]{0:T(256)}, u32[]{:S(2)}) copy-start(s32[256]{0:T(256)} %param.17) | copy-start | bytes 3076
  113.1 17.9 %all-to-all-start.1 = ((f32[4,32,512]{2,0,1:T(4,128)}), f32[4,32,512]{2,0,1:T(4,128)S(1)}, u32[]{:S(2)}, u32[]{:S(2)}) async-start(f32[4,32,512]{2,0,1:T(4,128)} %copy.32), calls=%async_computation.1 | async-start | bytes 524288 | tf_op jit(solution)/shard_map/all_to_all | solution.py:84
  116.8 78.6 %all-gather.6.cloned.1.call-start = ((), (), s32[]{:S(2)}) async-start(), calls=%async_computation.3 | async-start | bytes 2985984 | tf_op jit(solution)/shard_map/all_gather | solution.py:90
  126.5 14.0 %collective-permute-start.2 = (f32[512,128]{1,0:T(8,128)S(1)}, f32[512,128]{1,0:T(8,128)S(1)}, u32[]{:S(2)}, u32[]{:S(2)}) collective-permute-start(f32[512,128]{1,0:T(8,128)S(1)} %dynamic-slice_bitcast_fusion), channel_id=1, source_target_pairs={{0,4},{1,5},{2,6},{3,7},{4,0},{5,1},{6,2},{7,3},{8,12},{9,13},{10,... | collective-permute-start | bytes 786440 | tf_op jit(solution)/shard_map/ppermute | solution.py:45
  199.0 19.2 %copy-start.3 = (f32[128]{0:T(128)S(1)}, f32[128]{0:T(128)}, u32[]{:S(2)}) copy-start(f32[128]{0:T(128)} %param.22) | copy-start | bytes 1540
  199.3 5.0 %collective-permute-start.3 = (f32[136,128]{1,0:T(8,128)S(1)}, f32[136,128]{1,0:T(8,128)S(1)}, u32[]{:S(2)}, u32[]{:S(2)}) collective-permute-start(f32[136,128]{1,0:T(8,128)S(1)} %pad_maximum_fusion), channel_id=1, source_target_pairs={{0,8},{8,0},{16,24},{24,16},{1,9},{9,1},{17,25},{25,17},{2,10},{10... | collective-permute-start | bytes 208904 | tf_op jit(solution)/shard_map/ppermute | solution.py:31
  200.5 47.1 %copy-start.5 = (f32[128]{0:T(128)S(1)}, f32[128]{0:T(128)}, u32[]{:S(2)}) copy-start(f32[128]{0:T(128)} %param.21) | copy-start | bytes 1540
  200.5 45.3 %collective-permute-start.5 = (f32[2048,128]{1,0:T(8,128)}, f32[2048,128]{1,0:T(8,128)S(1)}, u32[]{:S(2)}, u32[]{:S(2)}) collective-permute-start(f32[2048,128]{1,0:T(8,128)} %dynamic-slice_select_fusion), channel_id=1, source_target_pairs={{0,16},{1,17},{10,26},{11,27},{20,4},{21,5},{30,14},{31,15}} | collective-permute-start | bytes 3145736 | tf_op jit(solution)/shard_map/ppermute | solution.py:23
  204.4 0.6 copy-start.2
  204.4 12.9 %collective-permute-start.4 = (f32[136,128]{1,0:T(8,128)S(1)}, f32[136,128]{1,0:T(8,128)}, u32[]{:S(2)}, u32[]{:S(2)}) collective-permute-start(f32[136,128]{1,0:T(8,128)S(1)} %fusion.31), channel_id=1, source_target_pairs={{0,16},{8,24},{16,0},{24,8},{1,17},{9,25},{17,1},{25,9},{2,18},{10... | collective-permute-start | bytes 208904 | tf_op jit(solution)/shard_map/ppermute | solution.py:31
  245.9 5.7 %collective-permute-start.6 = (f32[2048,128]{1,0:T(8,128)S(1)}, f32[2048,128]{1,0:T(8,128)S(1)}, u32[]{:S(2)}, u32[]{:S(2)}) collective-permute-start(f32[2048,128]{1,0:T(8,128)S(1)} %fusion.51), channel_id=1, source_target_pairs={{0,8},{16,24},{1,9},{17,25},{10,2},{26,18},{11,3},{27,19},{20,28},... | collective-permute-start | bytes 3145736 | tf_op jit(solution)/shard_map/ppermute | solution.py:23
  252.7 26.9 %copy-start.1 = (f32[4,128]{1,0:T(4,128)S(1)}, f32[4,128]{1,0:T(4,128)}, u32[]{:S(2)}) copy-start(f32[4,128]{1,0:T(4,128)} %param.20) | copy-start | bytes 6148
Sparse Core Ops, SparseCore 0:
  37.0 15.7 all-gather.3
  141.8 53.5 all-gather.5

commit v5 on v4

--- a/solution.py
+++ b/solution.py
@@ -85,21 +85,18 @@
     partial_rows = jnp.einsum("ik,mk->im", cov, grad_col, precision=mid)
     gain_own = halving_scatter(partial_rows, "col", n_col, col_id)
     gram_own = jnp.einsum("mk,kn->mn", grad_own, gain_own, precision=hi)
-    pred_pad = jnp.zeros((8, m_all), jnp.float32).at[0, :frames].set(pred_local)
-    payload = jnp.concatenate([gain_own, gram_own, pred_pad], axis=0)
-    gathered = lax.all_gather(payload, "col", axis=0)
-    gain_rows = gathered[:, :blk, :].reshape(n_col * blk, m_all)
-    gram_row = jnp.sum(gathered[:, blk : blk + m_all, :], axis=0)
-    pred_row = gathered[:, blk + m_all, :frames].reshape(n_col * frames)
+    device_id = row_id * n_col + col_id
     slots = lax.dynamic_update_slice_in_dim(
         jnp.zeros((8, m_all), jnp.float32),
-        jnp.zeros((8, n_col * frames), jnp.float32).at[0].set(pred_row),
-        row_id * n_col * frames,
+        jnp.zeros((8, frames), jnp.float32).at[0].set(pred_local),
+        device_id * frames,
         1,
     )
-    small = butterfly_sum(jnp.concatenate([gram_row, slots], axis=0), "row", n_row)
+    small = jnp.concatenate([gram_own, slots], axis=0)
+    small = butterfly_sum(butterfly_sum(small, "col", n_col), "row", n_row)
     gram = small[:m_all] + jnp.diag(noise)
     pred_all = small[m_all]
+    gain_rows = lax.all_gather(gain_own, "col", axis=0, tiled=True)
     lower = jnp.linalg.cholesky(gram)
     factor = n_col // n_row
     half_rows = lax.dynamic_slice_in_dim(gain_rows, col_id % factor * col_w, col_w, 0)
@@ -109,7 +106,6 @@
     white_col = jax.scipy.linalg.solve_triangular(lower, gain_col.T, lower=True)
     new_cov = cov - jnp.einsum("mi,mj->ij", white_row, white_col, precision=mid)
     coef = jax.scipy.linalg.cho_solve((lower, True), targets - pred_all)
-    device_id = row_id * n_col + col_id
     own_weights = lax.dynamic_slice_in_dim(weights.reshape(-1), device_id * blk, blk, 0)
     new_weights = own_weights + jnp.dot(gain_own, coef, precision=hi)
     return (new_weights, new_cov)

time: 287 us -> 276 us (0.962)
  waiting for transfers between devices: 126 us -> 116 us
  starting transfers between devices: 14.7 us -> 21.5 us
  local copies, waits for them, and re-layouts: 16.7 us -> 12.7 us
    all_gather x1, waiting for transfers between devices: 53.7 us -> 17.3 us  [on_device(): gain_rows = lax.all_gather(gain_own, 'col', axis=0, tiled=True)]
    ppermute x2 -> x5, waiting for transfers between devices: 12.3 us -> 24.9 us  [butterfly_sum(): buf = buf + lax.ppermute(buf, axis, [(i, i ^ bit) for i in range(size)])]
    all_to_all x1, waiting for transfers between devices: 2.19 us -> 11.4 us  [on_device(): lax.all_to_all(grads, ('row', 'col'), split_axis=1, concat_axis=0, tiled=...]
    ppermute x2 -> x5, starting transfers between devices: 0.14 us -> 5.18 us  [butterfly_sum(): buf = buf + lax.ppermute(buf, axis, [(i, i ^ bit) for i in range(size)])]
    ppermute x3, waiting for transfers between devices: 42.2 us -> 46.4 us  [halving_scatter(): x = keep + lax.ppermute(send, axis, [(i, i ^ bit) for i in range(size)])]
  transfers between devices with their start and end apart: 10 -> 13, of which waited for: 7 -> 10; matrix products, arithmetic and copies ran while one was open for 12% -> 11% of each run, Pallas kernels for 0% -> 0%
where the time goes in v5:
time: 276 us
  waiting for transfers between devices  116 us (42%)
  matrix products  59 us (21%)
  other arithmetic  36.4 us (13%)
  starting transfers between devices  21.5 us (8%)
  blocking collectives  16 us (6%)
  between operations  14.4 us (5%)
  local copies, waits for them, and re-layouts  12.7 us (5%)
    ppermute x3, waiting for transfers between devices, halving_scatter(): x = keep + lax.ppermute(send, axis, [(i, i ^ bit) for i in range(size)])  46.4 us
    dot_general x1, matrix products, on_device(): new_cov = cov - jnp.einsum('mi,mj->ij', white_row, white_col, precision=mid)  26.9 us
    ppermute x5, waiting for transfers between devices, butterfly_sum(): buf = buf + lax.ppermute(buf, axis, [(i, i ^ bit) for i in range(size)])  24.9 us
    dot_general x1, matrix products, on_device(): partial_rows = jnp.einsum('ik,mk->im', cov, grad_col, precision=mid)  22.8 us
    all_gather x1, waiting for transfers between devices, on_device(): gain_rows = lax.all_gather(gain_own, 'col', axis=0, tiled=True)  17.3 us
    all_to_all x1, blocking collectives, on_device(): lax.all_to_all(grads, 'col', split_axis=1, concat_axis=0, tiled=True)  16 us
    all_gather x1, waiting for transfers between devices, on_device(): grad_col = lax.all_gather(col_part, 'row', axis=0, tiled=True)  15.8 us
    another operation x3, other arithmetic, on_device(): lower = jnp.linalg.cholesky(gram)  12.4 us
  transfers between devices with their start and end apart: 13, of which 10 were waited for; matrix products, arithmetic and copies ran while one was open for 11% of the time, Pallas kernels for 0%

profile of v5, /device:TPU:0, one launch (start us, length us, event | category | flops | bytes accessed | tf_op | source)
XLA Modules:
  0.0 275.8 jit_solution(2433482479020052338)
XLA Ops:
  7.2 0.7 fusion.25
  7.9 0.9 copy.22
  8.8 5.7 %convert_reduce_fusion = f32[256,256]{1,0:T(8,128)S(1)} fusion(s32[256,32]{1,0:T(8,128)S(1)} %copy.22), kind=kLoop, calls=%fused_computation.1 | loop fusion | flops 6225920 | bytes 294912 | tf_op jit(solution)/shard_map/reduce_sum | solution.py:62
  14.5 1.0 fusion.14
  15.5 1.2 convolution_multiply_fusion.2
  16.7 1.3 fusion.2
  18.1 1.2 multiply_reduce_fusion
  19.2 0.6 fusion
  20.1 16.0 %all_to_all.38 = f32[4,8,2048]{2,0,1:T(4,128)S(1)} all-to-all(f32[4,8,2048]{2,0,1:T(4,128)S(1)} %copy.25), channel_id=1, replica_groups=mesh['row'=4,'col'=8] {'col'}, dimensions={1} | all-to-all | bytes 524288 | tf_op jit(solution)/shard_map/all_to_all | solution.py:82
  36.1 0.8 all_to_all.31
  37.0 15.8 %all-gather.3.cloned.1.call-done = f32[128,2048]{1,0:T(8,128)} async-done(((f32[32,2048]{1,0:T(8,128)}), f32[128,2048]{1,0:T(8,128)}) %all-gather.3.cloned.1.call-update) | async-done | bytes 1048592 | tf_op jit(solution)/shard_map/all_gather | solution.py:83
  52.8 22.8 %convolution_bitcast_fusion = f32[4096,128]{0,1:T(8,128)S(1)} fusion(f32[128,2048]{1,0:T(8,128)} %all-gather.3.cloned.1.call-done, f32[4096,2048]{1,0:T(8,128)} %param.21), kind=kOutput, calls=%fused_computation.3 | convolution fusion | flops 6442450944 | bytes 36700160 | tf_op jit(solution)/shard_map/ik,mk->im/dot_general | solution.py:85
  75.6 2.8 %reshape.78 = f32[2,2,2,512,128]{3,2,1,0,4:T(2,128)} reshape(f32[4096,128]{0,1:T(8,128)S(1)} %convolution_bitcast_fusion) | data formatting | bytes 4194304 | tf_op jit(solution)/shard_map/reshape | solution.py:38
  78.4 4.4 %constant_dynamic-slice_fusion.5 = (f32[2,2,1,512,128]{3,2,1,0,4:T(1,128)S(1)}, f32[2,2,1,512,128]{3,2,1,0,4:T(1,128)S(1)}) fusion(f32[2,2,2,512,128]{3,2,1,0,4:T(2,128)} %reshape.78, s32[]{:T(128)S(6)} %select_n.75, s32[]{:T(128)S(6)} %select_n.76), kind=kLoop, calls=%fused_computation.62 | loop fusion | bytes 4194312 | tf_op jit(solution)/shard_map/jit(dynamic_index_in_dim)/dynamic_slice | solution.py:43
  82.7 0.5 copy.42
  83.3 1.5 collective-permute-start
  84.8 23.8 %collective-permute-done = f32[2,2,512,128]{2,1,0,3:T(2,128)S(1)} collective-permute-done((f32[2,2,512,128]{2,1,0,3:T(2,128)S(1)}, f32[2,2,512,128]{2,1,0,3:T(2,128)S(1)}, u32[]{:S(2)}, u32[]{:S(2)}) %collective-permute-start) | collective-permute-done | bytes 1048608 | tf_op jit(solution)/shard_map/ppermute | solution.py:45
  108.7 0.7 bitcast_add_fusion
  109.4 0.9 constant_dynamic-slice_fusion.3
  110.5 1.6 collective-permute-start.1
  112.1 11.8 %collective-permute-done.1 = f32[2,512,128]{1,0,2:T(2,128)S(1)} collective-permute-done((f32[2,512,128]{1,0,2:T(2,128)S(1)}, f32[2,512,128]{1,0,2:T(2,128)S(1)}, u32[]{:S(2)}, u32[]{:S(2)}) %collective-permute-start.1) | collective-permute-done | bytes 524320 | tf_op jit(solution)/shard_map/ppermute | solution.py:45
  124.2 0.5 constant_dynamic-slice_fusion.1
  124.7 2.5 collective-permute-start.2
  127.2 10.8 %collective-permute-done.2 = f32[512,128]{0,1:T(8,128)S(1)} collective-permute-done((f32[512,128]{0,1:T(8,128)S(1)}, f32[512,128]{0,1:T(8,128)S(1)}, u32[]{:S(2)}, u32[]{:S(2)}) %collective-permute-start.2) | collective-permute-done | bytes 262176 | tf_op jit(solution)/shard_map/ppermute | solution.py:45
  138.0 0.7 bitcast_add_fusion.2
  138.8 0.9 copy.26
  139.7 4.6 %all-to-all-start.1 = ((f32[4,32,512]{2,0,1:T(4,128)}), f32[4,32,512]{2,0,1:T(4,128)S(1)}, u32[]{:S(2)}, u32[]{:S(2)}) async-start(f32[4,32,512]{2,0,1:T(4,128)} %copy.26), calls=%async_computation.1 | async-start | bytes 524288 | tf_op jit(solution)/shard_map/all_to_all | solution.py:84
  144.7 11.4 %all-to-all-done.1 = f32[4,32,512]{2,0,1:T(4,128)S(1)} async-done(((f32[4,32,512]{2,0,1:T(4,128)}), f32[4,32,512]{2,0,1:T(4,128)S(1)}, u32[]{:S(2)}, u32[]{:S(2)}) %all-to-all-start.1) | async-done | bytes 262176 | tf_op jit(solution)/shard_map/all_to_all | solution.py:84
  156.6 3.0 %collective-permute-start.3 = (f32[136,128]{1,0:T(8,128)S(1)}, f32[136,128]{1,0:T(8,128)S(1)}, u32[]{:S(2)}, u32[]{:S(2)}) collective-permute-start(f32[136,128]{1,0:T(8,128)S(1)} %pad_maximum_fusion), channel_id=1, source_target_pairs={{0,1},{1,0},{2,3},{3,2},{4,5},{5,4},{6,7},{7,6},{8,9},{9,8},{10,11... | collective-permute-start | bytes 208904 | tf_op jit(solution)/shard_map/ppermute | solution.py:31
  159.6 3.0 %collective-permute-done.3 = f32[136,128]{1,0:T(8,128)S(1)} collective-permute-done((f32[136,128]{1,0:T(8,128)S(1)}, f32[136,128]{1,0:T(8,128)S(1)}, u32[]{:S(2)}, u32[]{:S(2)}) %collective-permute-start.3) | collective-permute-done | bytes 69664 | tf_op jit(solution)/shard_map/ppermute | solution.py:31
  162.6 1.0 collective-permute-start.4
  163.6 3.3 %collective-permute-done.4 = f32[136,128]{1,0:T(8,128)S(1)} collective-permute-done((f32[136,128]{1,0:T(8,128)S(1)}, f32[136,128]{1,0:T(8,128)S(1)}, u32[]{:S(2)}, u32[]{:S(2)}) %collective-permute-start.4) | collective-permute-done | bytes 69664 | tf_op jit(solution)/shard_map/ppermute | solution.py:31
  167.0 1.0 collective-permute-start.5
  168.0 6.4 %collective-permute-done.5 = f32[136,128]{1,0:T(8,128)S(1)} collective-permute-done((f32[136,128]{1,0:T(8,128)S(1)}, f32[136,128]{1,0:T(8,128)S(1)}, u32[]{:S(2)}, u32[]{:S(2)}) %collective-permute-start.5) | collective-permute-done | bytes 69664 | tf_op jit(solution)/shard_map/ppermute | solution.py:31
  174.5 17.3 %all-gather.5.cloned.1.call-done = f32[4096,128]{0,1:T(8,128)} async-done(((f32[512,128]{0,1:T(8,128)}), f32[4096,128]{0,1:T(8,128)}) %all-gather.5.cloned.1.call-update) | async-done | bytes 2097168 | tf_op jit(solution)/shard_map/all_gather | solution.py:99
  191.7 2.4 dynamic-slice_select_fusion
  194.2 4.5 %collective-permute-start.8 = (f32[2048,128]{0,1:T(8,128)}, f32[2048,128]{0,1:T(8,128)}, u32[]{:S(2)}, u32[]{:S(2)}) collective-permute-start(f32[2048,128]{0,1:T(8,128)} %dynamic-slice_select_fusion), channel_id=1, source_target_pairs={{0,16},{1,17},{10,26},{11,27},{20,4},{21,5},{30,14},{31,15}} | collective-permute-start | bytes 3145736 | tf_op jit(solution)/shard_map/ppermute | solution.py:23
  198.7 12.2 %collective-permute-done.7 = f32[136,128]{1,0:T(8,128)S(1)} collective-permute-done((f32[136,128]{1,0:T(8,128)S(1)}, f32[136,128]{1,0:T(8,128)S(1)}, u32[]{:S(2)}, u32[]{:S(2)}) %collective-permute-start.7) | collective-permute-done | bytes 69664 | tf_op jit(solution)/shard_map/ppermute | solution.py:31
  211.2 11.7 %cholesky.16 = f32[128,128]{1,0:T(8,128)S(1)} custom-call(f32[128,128]{1,0:T(8,128)S(1)} %fusion.21), custom_call_target="Cholesky" | custom-call | tf_op jit(solution)/shard_map/jit(cholesky)/cholesky | solution.py:100
  223.0 0.6 compare_reduce_fusion
  223.6 0.7 fusion.15
  224.3 9.8 %custom-call.16 = f32[1,128,128]{1,2,0:T(8,128)S(1)} custom-call(f32[1,128,128]{2,1,0:T(8,128)S(1)} %fusion.15), custom_call_target="InvertDiagBlocksLowerTriangular" | custom-call | tf_op jit(solution)/shard_map/jit(_cho_solve)/triangular_solve | solution.py:108
  234.1 1.3 fusion.51
  235.5 1.6 collective-permute-start.9
  237.7 1.3 dynamic-slice_add_fusion
  239.1 1.9 fusion.17
  241.0 1.1 fusion.5
  242.1 26.9 %convolution_subtract_fusion = f32[4096,2048]{1,0:T(8,128)} fusion(f32[4096,2048]{1,0:T(8,128)} %param.21, f32[128,4096]{1,0:T(8,128)S(1)} %fusion.17, f32[128,2048]{1,0:T(8,128)S(1)} %fusion.5), kind=kOutput, calls=%fused_computation | convolution fusion | flops 6450839552 | bytes 70254592 | tf_op jit(solution)/shard_map/mi,mj->ij/dot_general | solution.py:107
  (49 shorter events, 3.1 us)
Async XLA Ops:
  7.2 7.3 %copy-start = (f32[4,128]{1,0:T(4,128)S(1)}, f32[4,128]{1,0:T(4,128)}, u32[]{:S(2)}) copy-start(f32[4,128]{1,0:T(4,128)} %param.18) | copy-start | bytes 6148
  7.2 45.6 %all-gather.3.cloned.1.call-start = ((), (), s32[]{:S(2)}) async-start(), calls=%async_computation.2 | async-start | bytes 1310720 | tf_op jit(solution)/shard_map/all_gather | solution.py:83
  36.9 154.8 %all-gather.5.cloned.1.call-start = ((), (), s32[]{:S(2)}) async-start(), calls=%async_computation.3 | async-start | bytes 2359296 | tf_op jit(solution)/shard_map/all_gather | solution.py:99
  83.3 25.4 %collective-permute-start = (f32[2,2,512,128]{2,1,0,3:T(2,128)S(1)}, f32[2,2,512,128]{2,1,0,3:T(2,128)S(1)}, u32[]{:S(2)}, u32[]{:S(2)}) collective-permute-start(f32[2,2,512,128]{2,1,0,3:T(2,128)S(1)} %bitcast.85), channel_id=1, source_target_pairs={{0,1},{1,0},{2,3},{3,2},{4,5},{5,4},{6,7},{7,6},{8,9},{9,8},{10,11... | collective-permute-start | bytes 3145736 | tf_op jit(solution)/shard_map/ppermute | solution.py:45
  110.5 13.3 %collective-permute-start.1 = (f32[2,512,128]{1,0,2:T(2,128)S(1)}, f32[2,512,128]{1,0,2:T(2,128)S(1)}, u32[]{:S(2)}, u32[]{:S(2)}) collective-permute-start(f32[2,512,128]{1,0,2:T(2,128)S(1)} %bitcast.88), channel_id=1, source_target_pairs={{0,2},{1,3},{2,0},{3,1},{4,6},{5,7},{6,4},{7,5},{8,10},{9,11},{10,... | collective-permute-start | bytes 1572872 | tf_op jit(solution)/shard_map/ppermute | solution.py:45
  124.2 20.1 %copy-start.5 = (s32[256]{0:T(256)S(1)}, s32[256]{0:T(256)}, u32[]{:S(2)}) copy-start(s32[256]{0:T(256)} %param.15) | copy-start | bytes 3076
  124.7 13.3 %collective-permute-start.2 = (f32[512,128]{0,1:T(8,128)S(1)}, f32[512,128]{0,1:T(8,128)S(1)}, u32[]{:S(2)}, u32[]{:S(2)}) collective-permute-start(f32[512,128]{0,1:T(8,128)S(1)} %bitcast.89), channel_id=1, source_target_pairs={{0,4},{1,5},{2,6},{3,7},{4,0},{5,1},{6,2},{7,3},{8,12},{9,13},{10,... | collective-permute-start | bytes 786440 | tf_op jit(solution)/shard_map/ppermute | solution.py:45
  138.8 17.4 %copy-start.3 = (f32[512,128]{0,1:T(8,128)S(1)}, f32[512,128]{0,1:T(8,128)}, u32[]{:S(2)}) copy-start(f32[512,128]{0,1:T(8,128)} %bitcast_add_fusion.2) | copy-start | bytes 786436
  139.7 16.4 %all-to-all-start.1 = ((f32[4,32,512]{2,0,1:T(4,128)}), f32[4,32,512]{2,0,1:T(4,128)S(1)}, u32[]{:S(2)}, u32[]{:S(2)}) async-start(f32[4,32,512]{2,0,1:T(4,128)} %copy.26), calls=%async_computation.1 | async-start | bytes 524288 | tf_op jit(solution)/shard_map/all_to_all | solution.py:84
  156.1 54.8 %copy-start.4 = (f32[128]{0:T(128)S(1)}, f32[128]{0:T(128)}, u32[]{:S(2)}) copy-start(f32[128]{0:T(128)} %param.20) | copy-start | bytes 1540
  156.6 6.0 %collective-permute-start.3 = (f32[136,128]{1,0:T(8,128)S(1)}, f32[136,128]{1,0:T(8,128)S(1)}, u32[]{:S(2)}, u32[]{:S(2)}) collective-permute-start(f32[136,128]{1,0:T(8,128)S(1)} %pad_maximum_fusion), channel_id=1, source_target_pairs={{0,1},{1,0},{2,3},{3,2},{4,5},{5,4},{6,7},{7,6},{8,9},{9,8},{10,11... | collective-permute-start | bytes 208904 | tf_op jit(solution)/shard_map/ppermute | solution.py:31
  162.6 4.4 %collective-permute-start.4 = (f32[136,128]{1,0:T(8,128)S(1)}, f32[136,128]{1,0:T(8,128)S(1)}, u32[]{:S(2)}, u32[]{:S(2)}) collective-permute-start(f32[136,128]{1,0:T(8,128)S(1)} %fusion.31), channel_id=1, source_target_pairs={{0,2},{1,3},{2,0},{3,1},{4,6},{5,7},{6,4},{7,5},{8,10},{9,11},{10,... | collective-permute-start | bytes 208904 | tf_op jit(solution)/shard_map/ppermute | solution.py:31
  167.0 7.4 %collective-permute-start.5 = (f32[136,128]{1,0:T(8,128)S(1)}, f32[136,128]{1,0:T(8,128)S(1)}, u32[]{:S(2)}, u32[]{:S(2)}) collective-permute-start(f32[136,128]{1,0:T(8,128)S(1)} %add.131), channel_id=1, source_target_pairs={{0,4},{1,5},{2,6},{3,7},{4,0},{5,1},{6,2},{7,3},{8,12},{9,13},{10,... | collective-permute-start | bytes 208904 | tf_op jit(solution)/shard_map/ppermute | solution.py:31
  174.4 24.3 %collective-permute-start.6 = (f32[136,128]{1,0:T(8,128)S(1)}, f32[136,128]{1,0:T(8,128)S(1)}, u32[]{:S(2)}, u32[]{:S(2)}) collective-permute-start(f32[136,128]{1,0:T(8,128)S(1)} %add.132), channel_id=1, source_target_pairs={{0,8},{8,0},{16,24},{24,16},{1,9},{9,1},{17,25},{25,17},{2,10},{10... | collective-permute-start | bytes 208904 | tf_op jit(solution)/shard_map/ppermute | solution.py:31
  191.7 42.4 %copy-start.2 = (f32[4096,128]{0,1:T(8,128)S(1)}, f32[4096,128]{0,1:T(8,128)}, u32[]{:S(2)}) copy-start(f32[4096,128]{0,1:T(8,128)} %all-gather.5.cloned.1.call-done) | copy-start | bytes 6291460
  194.2 42.9 %copy-start.6 = (f32[128]{0:T(128)S(1)}, f32[128]{0:T(128)}, u32[]{:S(2)}) copy-start(f32[128]{0:T(128)} %param.19) | copy-start | bytes 1540
  194.2 39.9 %collective-permute-start.8 = (f32[2048,128]{0,1:T(8,128)}, f32[2048,128]{0,1:T(8,128)}, u32[]{:S(2)}, u32[]{:S(2)}) collective-permute-start(f32[2048,128]{0,1:T(8,128)} %dynamic-slice_select_fusion), channel_id=1, source_target_pairs={{0,16},{1,17},{10,26},{11,27},{20,4},{21,5},{30,14},{31,15}} | collective-permute-start | bytes 3145736 | tf_op jit(solution)/shard_map/ppermute | solution.py:23
  198.7 12.3 %collective-permute-start.7 = (f32[136,128]{1,0:T(8,128)S(1)}, f32[136,128]{1,0:T(8,128)S(1)}, u32[]{:S(2)}, u32[]{:S(2)}) collective-permute-start(f32[136,128]{1,0:T(8,128)S(1)} %add.133), channel_id=1, source_target_pairs={{0,16},{8,24},{16,0},{24,8},{1,17},{9,25},{17,1},{25,9},{2,18},{10... | collective-permute-start | bytes 208904 | tf_op jit(solution)/shard_map/ppermute | solution.py:31
  235.5 5.6 %collective-permute-start.9 = (f32[2048,128]{0,1:T(8,128)S(1)}, f32[2048,128]{0,1:T(8,128)S(1)}, u32[]{:S(2)}, u32[]{:S(2)}) collective-permute-start(f32[2048,128]{0,1:T(8,128)S(1)} %fusion.51), channel_id=1, source_target_pairs={{0,8},{16,24},{1,9},{17,25},{10,2},{26,18},{11,3},{27,19},{20,28},... | collective-permute-start | bytes 3145736 | tf_op jit(solution)/shard_map/ppermute | solution.py:23
  242.1 26.9 %copy-start.1 = (f32[4,128]{1,0:T(4,128)S(1)}, f32[4,128]{1,0:T(4,128)}, u32[]{:S(2)}) copy-start(f32[4,128]{1,0:T(4,128)} %param.18) | copy-start | bytes 6148
Sparse Core Ops, SparseCore 0:
  37.0 15.7 all-gather.2
  138.9 52.7 all-gather.4

commit v6 on v5

--- a/solution.py
+++ b/solution.py
@@ -35,13 +35,11 @@
 
 def halving_scatter(x, axis, size, me):
     nbits = size.bit_length() - 1
-    x = x.reshape((2,) * nbits + (x.shape[0] // size,) + x.shape[1:])
     for step in range(nbits):
         bit = 1 << step
-        dim = nbits - 1 - step
         mine = (me // bit) % 2
-        keep = lax.dynamic_index_in_dim(x, mine, dim, keepdims=False)
-        send = lax.dynamic_index_in_dim(x, 1 - mine, dim, keepdims=False)
+        keep = lax.dynamic_index_in_dim(x, mine, 0, keepdims=False)
+        send = lax.dynamic_index_in_dim(x, 1 - mine, 0, keepdims=False)
         x = keep + lax.ppermute(send, axis, [(i, i ^ bit) for i in range(size)])
     return x
 
@@ -82,9 +80,15 @@
     col_part = lax.all_to_all(grads, "col", split_axis=1, concat_axis=0, tiled=True)
     grad_col = lax.all_gather(col_part, "row", axis=0, tiled=True)
     grad_own = lax.all_to_all(grads, ("row", "col"), split_axis=1, concat_axis=0, tiled=True)
-    partial_rows = jnp.einsum("ik,mk->im", cov, grad_col, precision=mid)
-    gain_own = halving_scatter(partial_rows, "col", n_col, col_id)
-    gram_own = jnp.einsum("mk,kn->mn", grad_own, gain_own, precision=hi)
+    grad_own, grad_col = lax.optimization_barrier((grad_own, grad_col))
+    nbits = n_col.bit_length() - 1
+    letters = "abcdefgh"[:nbits]
+    cov_blocks = cov.reshape((2,) * nbits + (cov.shape[0] // n_col, cov.shape[1]))
+    partial_t = jnp.einsum(
+        "mk," + letters + "ik->" + letters[::-1] + "mi", grad_col, cov_blocks, precision=mid
+    )
+    gain_own_t = halving_scatter(partial_t, "col", n_col, col_id)
+    gram_own = jnp.einsum("mk,nk->mn", grad_own, gain_own_t, precision=hi)
     device_id = row_id * n_col + col_id
     slots = lax.dynamic_update_slice_in_dim(
         jnp.zeros((8, m_all), jnp.float32),
@@ -96,18 +100,18 @@
     small = butterfly_sum(butterfly_sum(small, "col", n_col), "row", n_row)
     gram = small[:m_all] + jnp.diag(noise)
     pred_all = small[m_all]
-    gain_rows = lax.all_gather(gain_own, "col", axis=0, tiled=True)
+    gain_rows_t = lax.all_gather(gain_own_t, "col", axis=1, tiled=True)
     lower = jnp.linalg.cholesky(gram)
     factor = n_col // n_row
-    half_rows = lax.dynamic_slice_in_dim(gain_rows, col_id % factor * col_w, col_w, 0)
+    half_t = lax.dynamic_slice_in_dim(gain_rows_t, col_id % factor * col_w, col_w, 1)
     mine = row_id == col_id // factor
-    gain_col = broadcast_rows(jnp.where(mine, half_rows, jnp.zeros_like(half_rows)), n_row, n_col, factor)
-    white_row = jax.scipy.linalg.solve_triangular(lower, gain_rows.T, lower=True)
-    white_col = jax.scipy.linalg.solve_triangular(lower, gain_col.T, lower=True)
+    gain_col_t = broadcast_rows(jnp.where(mine, half_t, jnp.zeros_like(half_t)), n_row, n_col, factor)
+    white_row = jax.scipy.linalg.solve_triangular(lower, gain_rows_t, lower=True)
+    white_col = jax.scipy.linalg.solve_triangular(lower, gain_col_t, lower=True)
     new_cov = cov - jnp.einsum("mi,mj->ij", white_row, white_col, precision=mid)
     coef = jax.scipy.linalg.cho_solve((lower, True), targets - pred_all)
     own_weights = lax.dynamic_slice_in_dim(weights.reshape(-1), device_id * blk, blk, 0)
-    new_weights = own_weights + jnp.dot(gain_own, coef, precision=hi)
+    new_weights = own_weights + jnp.dot(coef, gain_own_t, precision=hi)
     return (new_weights, new_cov)
 
 

time: 276 us -> 273 us (0.989)
  local copies, waits for them, and re-layouts: 12.7 us -> 4.3 us
  other arithmetic: 36.4 us -> 40.1 us
    all_gather x1, waiting for transfers between devices: 17.3 us -> 31.7 us  [on_device(): gain_rows_t = lax.all_gather(gain_own_t, 'col', axis=1, tiled=True)]
    all_gather x1, waiting for transfers between devices: 15.8 us -> 2.41 us  [on_device(): grad_col = lax.all_gather(col_part, 'row', axis=0, tiled=True)]
    dynamic_slice x3 -> x0, local copies, waits for them, and re-layouts: 5.74 us -> none  [halving_scatter(): keep = lax.dynamic_index_in_dim(x, mine, dim, keepdims=False)]
    reshape x1 -> x0, local copies, waits for them, and re-layouts: 2.78 us -> none  [halving_scatter(): x = x.reshape((2,) * nbits + (x.shape[0] // size,) + x.shape[1:])]
  transfers between devices with their start and end apart: 13 -> 13, of which waited for: 10 -> 10; matrix products, arithmetic and copies ran while one was open for 11% -> 14% of each run, Pallas kernels for 0% -> 0%
where the time goes in v6:
time: 273 us; the launch traced here: 272 us
  waiting for transfers between devices  117 us (43%)
  matrix products  60.9 us (22%)
  other arithmetic  40.1 us (15%)
  starting transfers between devices  19.6 us (7%)
  blocking collectives  16 us (6%)
  between operations  14.4 us (5%)
  local copies, waits for them, and re-layouts  4.3 us (2%)
    ppermute x3, waiting for transfers between devices, halving_scatter(): x = keep + lax.ppermute(send, axis, [(i, i ^ bit) for i in range(size)])  46.7 us
    all_gather x1, waiting for transfers between devices, on_device(): gain_rows_t = lax.all_gather(gain_own_t, 'col', axis=1, tiled=True)  31.7 us
    dot_general x1, matrix products, on_device(): new_cov = cov - jnp.einsum('mi,mj->ij', white_row, white_col, precision=mid)  26.9 us
    ppermute x5, waiting for transfers between devices, butterfly_sum(): buf = buf + lax.ppermute(buf, axis, [(i, i ^ bit) for i in range(size)])  25.3 us
    dot_general x1, matrix products, on_device(): jnp.einsum('mk,' + letters + 'ik->' + letters[::-1] + 'mi', grad_col, cov...  23 us
    all_to_all x1, blocking collectives, on_device(): lax.all_to_all(grads, 'col', split_axis=1, concat_axis=0, tiled=True)  16 us
    another operation x3, other arithmetic, on_device(): lower = jnp.linalg.cholesky(gram)  13.2 us
    another operation x2, other arithmetic, on_device(): coef = jax.scipy.linalg.cho_solve((lower, True), targets - pred_all)  11.9 us
  transfers between devices with their start and end apart: 13, of which 10 were waited for; matrix products, arithmetic and copies ran while one was open for 14% of the time, Pallas kernels for 0%

profile of v6, /device:TPU:0, one launch (start us, length us, event | category | flops | bytes accessed | tf_op | source)
XLA Modules:
  0.0 271.8 jit_solution(11375102375499249221)
XLA Ops:
  7.2 0.7 fusion.27
  7.9 0.9 copy.32
  8.8 5.7 %convert_reduce_fusion = f32[256,256]{1,0:T(8,128)S(1)} fusion(s32[256,32]{1,0:T(8,128)S(1)} %copy.32), kind=kLoop, calls=%fused_computation.1 | loop fusion | flops 6225920 | bytes 294912 | tf_op jit(solution)/shard_map/reduce_sum | solution.py:60
  14.5 1.0 fusion.16
  15.5 1.2 convolution_multiply_fusion.2
  16.7 1.3 fusion.2
  18.1 1.2 multiply_reduce_fusion
  19.2 0.6 fusion
  20.1 16.0 %all_to_all.38 = f32[4,8,2048]{2,0,1:T(4,128)S(1)} all-to-all(f32[4,8,2048]{2,0,1:T(4,128)S(1)} %copy.36), channel_id=1, replica_groups=mesh['row'=4,'col'=8] {'col'}, dimensions={1} | all-to-all | bytes 524288 | tf_op jit(solution)/shard_map/all_to_all | solution.py:80
  36.1 0.8 all_to_all.35
  36.9 0.9 copy.35
  37.8 3.6 %all-to-all-start = ((f32[4,32,512]{2,0,1:T(4,128)}), f32[4,32,512]{2,0,1:T(4,128)S(1)}, u32[]{:S(2)}, u32[]{:S(2)}) async-start(f32[4,32,512]{2,0,1:T(4,128)} %copy.35), calls=%async_computation | async-start | bytes 524288 | tf_op jit(solution)/shard_map/all_to_all | solution.py:82
  41.7 10.4 %all-to-all-done = f32[4,32,512]{2,0,1:T(4,128)S(1)} async-done(((f32[4,32,512]{2,0,1:T(4,128)}), f32[4,32,512]{2,0,1:T(4,128)S(1)}, u32[]{:S(2)}, u32[]{:S(2)}) %all-to-all-start) | async-done | bytes 262176 | tf_op jit(solution)/shard_map/all_to_all | solution.py:82
  52.2 2.4 all-gather.3.cloned.1.call-done
  54.6 23.0 %fusion.5 = f32[128,2,2,2,512]{4,0,3,2,1:T(8,128)S(1)} fusion(f32[2,2,2,512,2048]{4,3,2,1,0:T(8,128)} %bitcast.89, f32[128,2048]{1,0:T(8,128)} %all-gather.3.cloned.1.call-done), kind=kOutput, calls=%fused_computation.16 | convolution fusion | flops 6442450944 | bytes 36700160 | tf_op jit(solution)/shard_map/mk,abcik->cbami/dot_general | solution.py:87
  77.7 1.6 collective-permute-start
  79.3 23.8 %collective-permute-done = f32[2,2,128,512]{3,2,0,1:T(8,128)} collective-permute-done((f32[2,2,128,512]{3,2,0,1:T(8,128)S(1)}, f32[2,2,128,512]{3,2,0,1:T(8,128)}, u32[]{:S(2)}, u32[]{:S(2)}) %collective-permute-start) | collective-permute-done | bytes 1048608 | tf_op jit(solution)/shard_map/ppermute | solution.py:43
  103.1 1.5 bitcast_add_fusion
  104.6 1.4 collective-permute-start.1
  106.0 11.9 %collective-permute-done.1 = f32[2,128,512]{2,1,0:T(8,128)S(1)} collective-permute-done((f32[2,128,512]{2,1,0:T(8,128)S(1)}, f32[2,128,512]{2,1,0:T(8,128)S(1)}, u32[]{:S(2)}, u32[]{:S(2)}) %collective-permute-start.1) | collective-permute-done | bytes 524320 | tf_op jit(solution)/shard_map/ppermute | solution.py:43
  118.1 2.3 collective-permute-start.2
  120.3 11.0 %collective-permute-done.2 = f32[128,512]{1,0:T(8,128)S(1)} collective-permute-done((f32[128,512]{1,0:T(8,128)S(1)}, f32[128,512]{1,0:T(8,128)S(1)}, u32[]{:S(2)}, u32[]{:S(2)}) %collective-permute-start.2) | collective-permute-done | bytes 262176 | tf_op jit(solution)/shard_map/ppermute | solution.py:43
  131.3 0.7 bitcast_add_fusion.2
  132.5 1.3 fusion.34
  133.8 1.7 collective-permute-start.3
  135.6 2.6 collective-permute-done.3
  138.2 0.3 collective-permute-start.4
  138.5 4.0 %collective-permute-done.4 = f32[136,128]{1,0:T(8,128)S(1)} collective-permute-done((f32[136,128]{1,0:T(8,128)S(1)}, f32[136,128]{1,0:T(8,128)S(1)}, u32[]{:S(2)}, u32[]{:S(2)}) %collective-permute-start.4) | collective-permute-done | bytes 69664 | tf_op jit(solution)/shard_map/ppermute | solution.py:31
  142.6 2.9 %collective-permute-start.5 = (f32[136,128]{1,0:T(8,128)S(1)}, f32[136,128]{1,0:T(8,128)S(1)}, u32[]{:S(2)}, u32[]{:S(2)}) collective-permute-start(f32[136,128]{1,0:T(8,128)S(1)} %add.131), channel_id=1, source_target_pairs={{0,4},{1,5},{2,6},{3,7},{4,0},{5,1},{6,2},{7,3},{8,12},{9,13},{10,... | collective-permute-start | bytes 208904 | tf_op jit(solution)/shard_map/ppermute | solution.py:31
  145.5 5.8 %collective-permute-done.5 = f32[136,128]{1,0:T(8,128)S(1)} collective-permute-done((f32[136,128]{1,0:T(8,128)S(1)}, f32[136,128]{1,0:T(8,128)S(1)}, u32[]{:S(2)}, u32[]{:S(2)}) %collective-permute-start.5) | collective-permute-done | bytes 69664 | tf_op jit(solution)/shard_map/ppermute | solution.py:31
  151.4 31.7 %all-gather.5.cloned.1.call-done = f32[128,4096]{1,0:T(8,128)} async-done(((f32[128,512]{1,0:T(8,128)}), f32[128,4096]{1,0:T(8,128)}) %all-gather.5.cloned.1.call-update) | async-done | bytes 2097168 | tf_op jit(solution)/shard_map/all_gather | solution.py:103
  183.1 2.4 dynamic-slice_select_fusion
  185.6 3.6 %collective-permute-start.8 = (f32[128,2048]{1,0:T(8,128)}, f32[128,2048]{1,0:T(8,128)S(1)}, u32[]{:S(2)}, u32[]{:S(2)}) collective-permute-start(f32[128,2048]{1,0:T(8,128)} %dynamic-slice_select_fusion), channel_id=1, source_target_pairs={{0,16},{1,17},{10,26},{11,27},{20,4},{21,5},{30,14},{31,15}} | collective-permute-start | bytes 3145736 | tf_op jit(solution)/shard_map/ppermute | solution.py:23
  189.3 12.8 %collective-permute-done.7 = f32[136,128]{1,0:T(8,128)} collective-permute-done((f32[136,128]{1,0:T(8,128)S(1)}, f32[136,128]{1,0:T(8,128)}, u32[]{:S(2)}, u32[]{:S(2)}) %collective-permute-start.7) | collective-permute-done | bytes 69664 | tf_op jit(solution)/shard_map/ppermute | solution.py:31
  202.2 0.9 add.134
  203.1 0.7 slice_add_fusion
  203.8 0.9 copy.38
  204.7 0.7 fusion.23
  205.4 12.5 %cholesky.16 = f32[128,128]{1,0:T(8,128)S(1)} custom-call(f32[128,128]{1,0:T(8,128)} %fusion.23), custom_call_target="Cholesky" | custom-call | tf_op jit(solution)/shard_map/jit(cholesky)/cholesky | solution.py:104
  218.0 0.6 compare_reduce_fusion
  218.7 1.3 fusion.17
  220.0 10.6 %custom-call.16 = f32[1,128,128]{1,2,0:T(8,128)S(1)} custom-call(f32[1,128,128]{2,1,0:T(8,128)} %fusion.17), custom_call_target="InvertDiagBlocksLowerTriangular" | custom-call | tf_op jit(solution)/shard_map/jit(_cho_solve)/triangular_solve | solution.py:112
  230.8 1.6 collective-permute-start.9
  232.4 0.8 convolution_bitcast_fusion.2
  233.7 1.3 dynamic-slice_add_fusion
  235.0 1.9 fusion.19
  237.0 1.1 fusion.7
  238.1 26.9 %convolution_subtract_fusion = f32[4096,2048]{1,0:T(8,128)} fusion(f32[4096,2048]{1,0:T(8,128)} %param.21, f32[128,4096]{1,0:T(8,128)S(1)} %fusion.19, f32[128,2048]{1,0:T(8,128)S(1)} %fusion.7), kind=kOutput, calls=%fused_computation | convolution fusion | flops 6450839552 | bytes 70254592 | tf_op jit(solution)/shard_map/mi,mj->ij/dot_general | solution.py:111
  (43 shorter events, 2.2 us)
Async XLA Ops:
  7.2 7.3 %copy-start = (f32[4,128]{1,0:T(4,128)S(1)}, f32[4,128]{1,0:T(4,128)}, u32[]{:S(2)}) copy-start(f32[4,128]{1,0:T(4,128)} %param.18) | copy-start | bytes 6148
  7.2 47.4 %all-gather.3.cloned.1.call-start = ((), (), s32[]{:S(2)}) async-start(), calls=%async_computation.2 | async-start | bytes 1310720 | tf_op jit(solution)/shard_map/all_gather | solution.py:81
  37.8 14.3 %all-to-all-start = ((f32[4,32,512]{2,0,1:T(4,128)}), f32[4,32,512]{2,0,1:T(4,128)S(1)}, u32[]{:S(2)}, u32[]{:S(2)}) async-start(f32[4,32,512]{2,0,1:T(4,128)} %copy.35), calls=%async_computation | async-start | bytes 524288 | tf_op jit(solution)/shard_map/all_to_all | solution.py:82
  41.4 141.7 %all-gather.5.cloned.1.call-start = ((), (), s32[]{:S(2)}) async-start(), calls=%async_computation.3 | async-start | bytes 2359296 | tf_op jit(solution)/shard_map/all_gather | solution.py:103
  77.7 25.5 %collective-permute-start = (f32[2,2,128,512]{3,2,0,1:T(8,128)S(1)}, f32[2,2,128,512]{3,2,0,1:T(8,128)}, u32[]{:S(2)}, u32[]{:S(2)}) collective-permute-start(f32[2,2,128,512]{3,2,0,1:T(8,128)S(1)} %dynamic-slice_bitcast_fusion), channel_id=1, source_target_pairs={{0,1},{1,0},{2,3},{3,2},{4,5},{5,4},{6,7},{7,6},{8,9},{9,8},{10,11... | collective-permute-start | bytes 3145736 | tf_op jit(solution)/shard_map/ppermute | solution.py:43
  104.6 27.5 %copy-start.5 = (s32[256]{0:T(256)S(1)}, s32[256]{0:T(256)}, u32[]{:S(2)}) copy-start(s32[256]{0:T(256)} %param.15) | copy-start | bytes 3076
  104.6 13.3 %collective-permute-start.1 = (f32[2,128,512]{2,1,0:T(8,128)S(1)}, f32[2,128,512]{2,1,0:T(8,128)S(1)}, u32[]{:S(2)}, u32[]{:S(2)}) collective-permute-start(f32[2,128,512]{2,1,0:T(8,128)S(1)} %dynamic-slice_bitcast_fusion.1), channel_id=1, source_target_pairs={{0,2},{1,3},{2,0},{3,1},{4,6},{5,7},{6,4},{7,5},{8,10},{9,11},{10,... | collective-permute-start | bytes 1572872 | tf_op jit(solution)/shard_map/ppermute | solution.py:43
  118.1 13.3 %collective-permute-start.2 = (f32[128,512]{1,0:T(8,128)S(1)}, f32[128,512]{1,0:T(8,128)S(1)}, u32[]{:S(2)}, u32[]{:S(2)}) collective-permute-start(f32[128,512]{1,0:T(8,128)S(1)} %dynamic-slice_bitcast_fusion.2), channel_id=1, source_target_pairs={{0,4},{1,5},{2,6},{3,7},{4,0},{5,1},{6,2},{7,3},{8,12},{9,13},{10,... | collective-permute-start | bytes 786440 | tf_op jit(solution)/shard_map/ppermute | solution.py:43
  132.1 71.0 %copy-start.4 = (f32[128]{0:T(128)S(1)}, f32[128]{0:T(128)}, u32[]{:S(2)}) copy-start(f32[128]{0:T(128)} %param.20) | copy-start | bytes 1540
  133.8 4.4 %collective-permute-start.3 = (f32[136,128]{1,0:T(8,128)S(1)}, f32[136,128]{1,0:T(8,128)S(1)}, u32[]{:S(2)}, u32[]{:S(2)}) collective-permute-start(f32[136,128]{1,0:T(8,128)S(1)} %pad_maximum_fusion), channel_id=1, source_target_pairs={{0,1},{1,0},{2,3},{3,2},{4,5},{5,4},{6,7},{7,6},{8,9},{9,8},{10,11... | collective-permute-start | bytes 208904 | tf_op jit(solution)/shard_map/ppermute | solution.py:31
  138.2 4.4 %collective-permute-start.4 = (f32[136,128]{1,0:T(8,128)S(1)}, f32[136,128]{1,0:T(8,128)S(1)}, u32[]{:S(2)}, u32[]{:S(2)}) collective-permute-start(f32[136,128]{1,0:T(8,128)S(1)} %fusion.33), channel_id=1, source_target_pairs={{0,2},{1,3},{2,0},{3,1},{4,6},{5,7},{6,4},{7,5},{8,10},{9,11},{10,... | collective-permute-start | bytes 208904 | tf_op jit(solution)/shard_map/ppermute | solution.py:31
  142.6 8.7 %collective-permute-start.5 = (f32[136,128]{1,0:T(8,128)S(1)}, f32[136,128]{1,0:T(8,128)S(1)}, u32[]{:S(2)}, u32[]{:S(2)}) collective-permute-start(f32[136,128]{1,0:T(8,128)S(1)} %add.131), channel_id=1, source_target_pairs={{0,4},{1,5},{2,6},{3,7},{4,0},{5,1},{6,2},{7,3},{8,12},{9,13},{10,... | collective-permute-start | bytes 208904 | tf_op jit(solution)/shard_map/ppermute | solution.py:31
  151.3 37.9 %collective-permute-start.6 = (f32[136,128]{1,0:T(8,128)S(1)}, f32[136,128]{1,0:T(8,128)S(1)}, u32[]{:S(2)}, u32[]{:S(2)}) collective-permute-start(f32[136,128]{1,0:T(8,128)S(1)} %add.132), channel_id=1, source_target_pairs={{0,8},{8,0},{16,24},{24,16},{1,9},{9,1},{17,25},{25,17},{2,10},{10... | collective-permute-start | bytes 208904 | tf_op jit(solution)/shard_map/ppermute | solution.py:31
  183.1 47.5 %copy-start.2 = (f32[128,4096]{1,0:T(8,128)S(1)}, f32[128,4096]{1,0:T(8,128)}, u32[]{:S(2)}) copy-start(f32[128,4096]{1,0:T(8,128)} %all-gather.5.cloned.1.call-done) | copy-start | bytes 6291460
  185.6 45.0 %collective-permute-start.8 = (f32[128,2048]{1,0:T(8,128)}, f32[128,2048]{1,0:T(8,128)S(1)}, u32[]{:S(2)}, u32[]{:S(2)}) collective-permute-start(f32[128,2048]{1,0:T(8,128)} %dynamic-slice_select_fusion), channel_id=1, source_target_pairs={{0,16},{1,17},{10,26},{11,27},{20,4},{21,5},{30,14},{31,15}} | collective-permute-start | bytes 3145736 | tf_op jit(solution)/shard_map/ppermute | solution.py:23
  189.2 44.1 %copy-start.3 = (f32[128,512]{1,0:T(8,128)S(1)}, f32[128,512]{1,0:T(8,128)}, u32[]{:S(2)}) copy-start(f32[128,512]{1,0:T(8,128)} %bitcast_add_fusion.2) | copy-start | bytes 786436
  189.3 12.9 %collective-permute-start.7 = (f32[136,128]{1,0:T(8,128)S(1)}, f32[136,128]{1,0:T(8,128)}, u32[]{:S(2)}, u32[]{:S(2)}) collective-permute-start(f32[136,128]{1,0:T(8,128)S(1)} %add.133), channel_id=1, source_target_pairs={{0,16},{8,24},{16,0},{24,8},{1,17},{9,25},{17,1},{25,9},{2,18},{10... | collective-permute-start | bytes 208904 | tf_op jit(solution)/shard_map/ppermute | solution.py:31
  230.8 6.2 %collective-permute-start.9 = (f32[128,2048]{1,0:T(8,128)S(1)}, f32[128,2048]{1,0:T(8,128)S(1)}, u32[]{:S(2)}, u32[]{:S(2)}) collective-permute-start(f32[128,2048]{1,0:T(8,128)S(1)} %fusion.52), channel_id=1, source_target_pairs={{0,8},{16,24},{1,9},{17,25},{10,2},{26,18},{11,3},{27,19},{20,28},... | collective-permute-start | bytes 3145736 | tf_op jit(solution)/shard_map/ppermute | solution.py:23
  238.1 26.9 %copy-start.1 = (f32[4,128]{1,0:T(4,128)S(1)}, f32[4,128]{1,0:T(4,128)}, u32[]{:S(2)}) copy-start(f32[4,128]{1,0:T(4,128)} %param.18) | copy-start | bytes 6148
Sparse Core Ops, SparseCore 0:
  37.0 17.5 all-gather.2
  132.2 50.8 all-gather.4

commit v7 on v6

--- a/solution.py
+++ b/solution.py
@@ -79,8 +79,6 @@
     blk = width // (n_row * n_col)
     col_part = lax.all_to_all(grads, "col", split_axis=1, concat_axis=0, tiled=True)
     grad_col = lax.all_gather(col_part, "row", axis=0, tiled=True)
-    grad_own = lax.all_to_all(grads, ("row", "col"), split_axis=1, concat_axis=0, tiled=True)
-    grad_own, grad_col = lax.optimization_barrier((grad_own, grad_col))
     nbits = n_col.bit_length() - 1
     letters = "abcdefgh"[:nbits]
     cov_blocks = cov.reshape((2,) * nbits + (cov.shape[0] // n_col, cov.shape[1]))
@@ -88,7 +86,12 @@
         "mk," + letters + "ik->" + letters[::-1] + "mi", grad_col, cov_blocks, precision=mid
     )
     gain_own_t = halving_scatter(partial_t, "col", n_col, col_id)
-    gram_own = jnp.einsum("mk,nk->mn", grad_own, gain_own_t, precision=hi)
+    gain_rows_t = lax.all_gather(gain_own_t, "col", axis=1, tiled=True)
+    factor = n_col // n_row
+    half_t = lax.dynamic_slice_in_dim(gain_rows_t, col_id % factor * col_w, col_w, 1)
+    mine = row_id == col_id // factor
+    gram_part = jnp.einsum("mk,nk->mn", grad_col, half_t, precision=hi)
+    gram_part = jnp.where(mine, gram_part, jnp.zeros_like(gram_part))
     device_id = row_id * n_col + col_id
     slots = lax.dynamic_update_slice_in_dim(
         jnp.zeros((8, m_all), jnp.float32),
@@ -96,16 +99,14 @@
         device_id * frames,
         1,
     )
-    small = jnp.concatenate([gram_own, slots], axis=0)
+    small = jnp.concatenate([gram_part, slots], axis=0)
     small = butterfly_sum(butterfly_sum(small, "col", n_col), "row", n_row)
+    masked = jnp.where(mine, half_t, jnp.zeros_like(half_t))
+    small, masked = lax.optimization_barrier((small, masked))
     gram = small[:m_all] + jnp.diag(noise)
     pred_all = small[m_all]
-    gain_rows_t = lax.all_gather(gain_own_t, "col", axis=1, tiled=True)
     lower = jnp.linalg.cholesky(gram)
-    factor = n_col // n_row
-    half_t = lax.dynamic_slice_in_dim(gain_rows_t, col_id % factor * col_w, col_w, 1)
-    mine = row_id == col_id // factor
-    gain_col_t = broadcast_rows(jnp.where(mine, half_t, jnp.zeros_like(half_t)), n_row, n_col, factor)
+    gain_col_t = broadcast_rows(masked, n_row, n_col, factor)
     white_row = jax.scipy.linalg.solve_triangular(lower, gain_rows_t, lower=True)
     white_col = jax.scipy.linalg.solve_triangular(lower, gain_col_t, lower=True)
     new_cov = cov - jnp.einsum("mi,mj->ij", white_row, white_col, precision=mid)

time: 273 us -> 276 us (1.011)
  waiting for transfers between devices: 117 us -> 125 us
    all_gather x1, waiting for transfers between devices: 31.7 us -> 49 us  [on_device(): gain_rows_t = lax.all_gather(gain_own_t, 'col', axis=1, tiled=True)]
    all_gather x1, waiting for transfers between devices: 2.41 us -> 15.6 us  [on_device(): grad_col = lax.all_gather(col_part, 'row', axis=0, tiled=True)]
    ppermute x5, waiting for transfers between devices: 25.3 us -> 13.8 us  [butterfly_sum(): buf = buf + lax.ppermute(buf, axis, [(i, i ^ bit) for i in range(size)])]
    all_to_all x1 -> x0, waiting for transfers between devices: 10.4 us -> none  [on_device(): lax.all_to_all(grads, ('row', 'col'), split_axis=1, concat_axis=0, tiled=...]
    all_to_all x1 -> x0, starting transfers between devices: 3.6 us -> none  [on_device(): lax.all_to_all(grads, ('row', 'col'), split_axis=1, concat_axis=0, tiled=...]
  transfers between devices with their start and end apart: 13 -> 12, of which waited for: 10 -> 10; matrix products, arithmetic and copies ran while one was open for 14% -> 12% of each run, Pallas kernels for 0% -> 0%
where the time goes in v7:
time: 276 us
  waiting for transfers between devices  125 us (45%)
  matrix products  61.3 us (22%)
  other arithmetic  38.1 us (14%)
  starting transfers between devices  17.6 us (6%)
  blocking collectives  16 us (6%)
  between operations  14.4 us (5%)
  local copies, waits for them, and re-layouts  3.3 us (1%)
    all_gather x1, waiting for transfers between devices, on_device(): gain_rows_t = lax.all_gather(gain_own_t, 'col', axis=1, tiled=True)  49 us
    ppermute x3, waiting for transfers between devices, halving_scatter(): x = keep + lax.ppermute(send, axis, [(i, i ^ bit) for i in range(size)])  46.5 us
    dot_general x1, matrix products, on_device(): new_cov = cov - jnp.einsum('mi,mj->ij', white_row, white_col, precision=mid)  26.9 us
    dot_general x1, matrix products, on_device(): jnp.einsum('mk,' + letters + 'ik->' + letters[::-1] + 'mi', grad_col, cov...  23 us
    all_to_all x1, blocking collectives, on_device(): lax.all_to_all(grads, 'col', split_axis=1, concat_axis=0, tiled=True)  16 us
    all_gather x1, waiting for transfers between devices, on_device(): grad_col = lax.all_gather(col_part, 'row', axis=0, tiled=True)  15.6 us
    ppermute x5, waiting for transfers between devices, butterfly_sum(): buf = buf + lax.ppermute(buf, axis, [(i, i ^ bit) for i in range(size)])  13.8 us
    another operation x3, other arithmetic, on_device(): lower = jnp.linalg.cholesky(gram)  13.2 us
  transfers between devices with their start and end apart: 12, of which 10 were waited for; matrix products, arithmetic and copies ran while one was open for 12% of the time, Pallas kernels for 0%

profile of v7, /device:TPU:0, one launch (start us, length us, event | category | flops | bytes accessed | tf_op | source)
XLA Modules:
  0.0 275.7 jit_solution(6750661937937248524)
XLA Ops:
  7.2 0.7 fusion.28
  7.9 0.9 copy.24
  8.8 5.7 %convert_reduce_fusion = f32[256,256]{1,0:T(8,128)S(1)} fusion(s32[256,32]{1,0:T(8,128)S(1)} %copy.24), kind=kLoop, calls=%fused_computation.1 | loop fusion | flops 6225920 | bytes 294912 | tf_op jit(solution)/shard_map/reduce_sum | solution.py:60
  14.5 1.0 fusion.17
  15.5 1.2 convolution_multiply_fusion.2
  16.7 1.3 fusion.2
  18.1 1.2 multiply_reduce_fusion
  19.2 0.6 fusion
  20.1 16.0 %all_to_all.19 = f32[4,8,2048]{2,0,1:T(4,128)S(1)} all-to-all(f32[4,8,2048]{2,0,1:T(4,128)S(1)} %copy.27), channel_id=1, replica_groups=mesh['row'=4,'col'=8] {'col'}, dimensions={1} | all-to-all | bytes 524288 | tf_op jit(solution)/shard_map/all_to_all | solution.py:80
  36.1 0.8 all_to_all.17
  36.9 0.2 all-gather.5.cloned.1.call-start
  37.1 15.6 %all-gather.3.cloned.1.call-done = f32[128,2048]{1,0:T(8,128)} async-done(((f32[32,2048]{1,0:T(8,128)}), f32[128,2048]{1,0:T(8,128)}) %all-gather.3.cloned.1.call-update) | async-done | bytes 1048592 | tf_op jit(solution)/shard_map/all_gather | solution.py:81
  52.8 23.0 %fusion.5 = f32[128,2,2,2,512]{4,0,3,2,1:T(8,128)S(1)} fusion(f32[2,2,2,512,2048]{4,3,2,1,0:T(8,128)} %bitcast.85, f32[128,2048]{1,0:T(8,128)} %all-gather.3.cloned.1.call-done), kind=kOutput, calls=%fused_computation.17 | convolution fusion | flops 6442450944 | bytes 36700160 | tf_op jit(solution)/shard_map/mk,abcik->cbami/dot_general | solution.py:85
  75.8 1.5 collective-permute-start
  77.4 23.9 %collective-permute-done = f32[2,2,128,512]{3,2,0,1:T(8,128)} collective-permute-done((f32[2,2,128,512]{3,2,0,1:T(8,128)S(1)}, f32[2,2,128,512]{3,2,0,1:T(8,128)}, u32[]{:S(2)}, u32[]{:S(2)}) %collective-permute-start) | collective-permute-done | bytes 1048608 | tf_op jit(solution)/shard_map/ppermute | solution.py:43
  101.3 1.5 bitcast_add_fusion
  102.9 1.6 collective-permute-start.1
  104.4 11.7 %collective-permute-done.1 = f32[2,128,512]{2,1,0:T(8,128)S(1)} collective-permute-done((f32[2,128,512]{2,1,0:T(8,128)S(1)}, f32[2,128,512]{2,1,0:T(8,128)S(1)}, u32[]{:S(2)}, u32[]{:S(2)}) %collective-permute-start.1) | collective-permute-done | bytes 524320 | tf_op jit(solution)/shard_map/ppermute | solution.py:43
  116.3 2.5 collective-permute-start.2
  118.8 10.8 %collective-permute-done.2 = f32[128,512]{1,0:T(8,128)S(1)} collective-permute-done((f32[128,512]{1,0:T(8,128)S(1)}, f32[128,512]{1,0:T(8,128)S(1)}, u32[]{:S(2)}, u32[]{:S(2)}) %collective-permute-start.2) | collective-permute-done | bytes 262176 | tf_op jit(solution)/shard_map/ppermute | solution.py:43
  129.6 0.7 bitcast_add_fusion.2
  130.5 0.2 dynamic_update_slice.3
  130.7 49.0 %all-gather.5.cloned.1.call-done = f32[128,4096]{1,0:T(8,128)} async-done(((f32[128,512]{1,0:T(8,128)}), f32[128,4096]{1,0:T(8,128)}) %all-gather.5.cloned.1.call-update) | async-done | bytes 2097168 | tf_op jit(solution)/shard_map/all_gather | solution.py:89
  179.8 2.4 convolution_select_fusion
  182.2 0.6 collective-permute-start.3
  182.8 3.8 %collective-permute-done.3 = f32[136,128]{1,0:T(8,128)S(1)} collective-permute-done((f32[136,128]{1,0:T(8,128)S(1)}, f32[136,128]{1,0:T(8,128)S(1)}, u32[]{:S(2)}, u32[]{:S(2)}) %collective-permute-start.3) | collective-permute-done | bytes 69664 | tf_op jit(solution)/shard_map/ppermute | solution.py:31
  186.6 1.5 collective-permute-start.4
  188.1 2.8 %collective-permute-done.4 = f32[136,128]{1,0:T(8,128)S(1)} collective-permute-done((f32[136,128]{1,0:T(8,128)S(1)}, f32[136,128]{1,0:T(8,128)S(1)}, u32[]{:S(2)}, u32[]{:S(2)}) %collective-permute-start.4) | collective-permute-done | bytes 69664 | tf_op jit(solution)/shard_map/ppermute | solution.py:31
  191.0 2.0 collective-permute-start.5
  193.0 3.3 %collective-permute-done.5 = f32[136,128]{1,0:T(8,128)S(1)} collective-permute-done((f32[136,128]{1,0:T(8,128)S(1)}, f32[136,128]{1,0:T(8,128)S(1)}, u32[]{:S(2)}, u32[]{:S(2)}) %collective-permute-start.5) | collective-permute-done | bytes 69664 | tf_op jit(solution)/shard_map/ppermute | solution.py:31
  196.3 1.2 collective-permute-done.6
  197.6 1.5 collective-permute-start.7
  199.2 2.7 collective-permute-done.7
  202.0 4.4 %collective-permute-start.8 = (f32[128,2048]{1,0:T(8,128)S(1)}, f32[128,2048]{1,0:T(8,128)}, u32[]{:S(2)}, u32[]{:S(2)}) collective-permute-start(f32[128,2048]{1,0:T(8,128)S(1)} %dynamic-slice_select_fusion), channel_id=1, source_target_pairs={{0,16},{1,17},{10,26},{11,27},{20,4},{21,5},{30,14},{31,15}} | collective-permute-start | bytes 3145736 | tf_op jit(solution)/shard_map/ppermute | solution.py:23
  206.3 0.7 select_add_fusion
  207.0 0.9 copy.29
  208.0 0.7 fusion.24
  208.7 12.5 %cholesky.16 = f32[128,128]{1,0:T(8,128)S(1)} custom-call(f32[128,128]{1,0:T(8,128)} %fusion.24), custom_call_target="Cholesky" | custom-call | tf_op jit(solution)/shard_map/jit(cholesky)/cholesky | solution.py:108
  221.3 0.6 compare_reduce_fusion
  221.9 1.3 fusion.18
  223.2 10.6 %custom-call.16 = f32[1,128,128]{1,2,0:T(8,128)S(1)} custom-call(f32[1,128,128]{2,1,0:T(8,128)} %fusion.18), custom_call_target="InvertDiagBlocksLowerTriangular" | custom-call | tf_op jit(solution)/shard_map/jit(_cho_solve)/triangular_solve | solution.py:113
  233.9 1.4 add.139
  235.3 1.6 collective-permute-start.9
  237.3 0.3 fusion.35
  237.5 1.3 dynamic-slice_add_fusion
  238.9 1.9 fusion.20
  240.9 1.1 fusion.7
  242.0 26.9 %convolution_subtract_fusion = f32[4096,2048]{1,0:T(8,128)} fusion(f32[4096,2048]{1,0:T(8,128)} %param.21, f32[128,4096]{1,0:T(8,128)S(1)} %fusion.20, f32[128,2048]{1,0:T(8,128)S(1)} %fusion.7), kind=kOutput, calls=%fused_computation | convolution fusion | flops 6450839552 | bytes 70254592 | tf_op jit(solution)/shard_map/mi,mj->ij/dot_general | solution.py:112
  (42 shorter events, 1.4 us)
Async XLA Ops:
  7.2 7.3 %copy-start = (f32[4,128]{1,0:T(4,128)S(1)}, f32[4,128]{1,0:T(4,128)}, u32[]{:S(2)}) copy-start(f32[4,128]{1,0:T(4,128)} %param.18) | copy-start | bytes 6148
  7.2 45.6 %all-gather.3.cloned.1.call-start = ((), (), s32[]{:S(2)}) async-start(), calls=%async_computation.1 | async-start | bytes 1310720 | tf_op jit(solution)/shard_map/all_gather | solution.py:81
  36.9 142.9 %all-gather.5.cloned.1.call-start = ((), (), s32[]{:S(2)}) async-start(), calls=%async_computation.2 | async-start | bytes 2359296 | tf_op jit(solution)/shard_map/all_gather | solution.py:89
  75.8 25.5 %collective-permute-start = (f32[2,2,128,512]{3,2,0,1:T(8,128)S(1)}, f32[2,2,128,512]{3,2,0,1:T(8,128)}, u32[]{:S(2)}, u32[]{:S(2)}) collective-permute-start(f32[2,2,128,512]{3,2,0,1:T(8,128)S(1)} %dynamic-slice_bitcast_fusion), channel_id=1, source_target_pairs={{0,1},{1,0},{2,3},{3,2},{4,5},{5,4},{6,7},{7,6},{8,9},{9,8},{10,11... | collective-permute-start | bytes 3145736 | tf_op jit(solution)/shard_map/ppermute | solution.py:43
  102.8 27.6 %copy-start.6 = (s32[256]{0:T(256)S(1)}, s32[256]{0:T(256)}, u32[]{:S(2)}) copy-start(s32[256]{0:T(256)} %param.15) | copy-start | bytes 3076
  102.8 77.0 %copy-start.3 = (f32[128,2048]{1,0:T(8,128)S(1)}, f32[128,2048]{1,0:T(8,128)}, u32[]{:S(2)}) copy-start(f32[128,2048]{1,0:T(8,128)} %all-gather.3.cloned.1.call-done) | copy-start | bytes 3145732
  102.9 13.3 %collective-permute-start.1 = (f32[2,128,512]{2,1,0:T(8,128)S(1)}, f32[2,128,512]{2,1,0:T(8,128)S(1)}, u32[]{:S(2)}, u32[]{:S(2)}) collective-permute-start(f32[2,128,512]{2,1,0:T(8,128)S(1)} %dynamic-slice_bitcast_fusion.1), channel_id=1, source_target_pairs={{0,2},{1,3},{2,0},{3,1},{4,6},{5,7},{6,4},{7,5},{8,10},{9,11},{10,... | collective-permute-start | bytes 1572872 | tf_op jit(solution)/shard_map/ppermute | solution.py:43
  116.3 13.3 %collective-permute-start.2 = (f32[128,512]{1,0:T(8,128)S(1)}, f32[128,512]{1,0:T(8,128)S(1)}, u32[]{:S(2)}, u32[]{:S(2)}) collective-permute-start(f32[128,512]{1,0:T(8,128)S(1)} %dynamic-slice_bitcast_fusion.2), channel_id=1, source_target_pairs={{0,4},{1,5},{2,6},{3,7},{4,0},{5,1},{6,2},{7,3},{8,12},{9,13},{10,... | collective-permute-start | bytes 786440 | tf_op jit(solution)/shard_map/ppermute | solution.py:43
  179.8 19.4 %copy-start.2 = (f32[128,4096]{1,0:T(8,128)S(1)}, f32[128,4096]{1,0:T(8,128)}, u32[]{:S(2)}) copy-start(f32[128,4096]{1,0:T(8,128)} %all-gather.5.cloned.1.call-done) | copy-start | bytes 6291460
  182.2 24.2 %copy-start.5 = (f32[128]{0:T(128)S(1)}, f32[128]{0:T(128)}, u32[]{:S(2)}) copy-start(f32[128]{0:T(128)} %param.20) | copy-start | bytes 1540
  182.2 4.4 %collective-permute-start.3 = (f32[136,128]{1,0:T(8,128)S(1)}, f32[136,128]{1,0:T(8,128)S(1)}, u32[]{:S(2)}, u32[]{:S(2)}) collective-permute-start(f32[136,128]{1,0:T(8,128)S(1)} %pad_maximum_fusion), channel_id=1, source_target_pairs={{0,1},{1,0},{2,3},{3,2},{4,5},{5,4},{6,7},{7,6},{8,9},{9,8},{10,11... | collective-permute-start | bytes 208904 | tf_op jit(solution)/shard_map/ppermute | solution.py:31
  186.6 4.4 %collective-permute-start.4 = (f32[136,128]{1,0:T(8,128)S(1)}, f32[136,128]{1,0:T(8,128)S(1)}, u32[]{:S(2)}, u32[]{:S(2)}) collective-permute-start(f32[136,128]{1,0:T(8,128)S(1)} %fusion.34), channel_id=1, source_target_pairs={{0,2},{1,3},{2,0},{3,1},{4,6},{5,7},{6,4},{7,5},{8,10},{9,11},{10,... | collective-permute-start | bytes 208904 | tf_op jit(solution)/shard_map/ppermute | solution.py:31
  191.0 5.3 %collective-permute-start.5 = (f32[136,128]{1,0:T(8,128)S(1)}, f32[136,128]{1,0:T(8,128)S(1)}, u32[]{:S(2)}, u32[]{:S(2)}) collective-permute-start(f32[136,128]{1,0:T(8,128)S(1)} %add.132), channel_id=1, source_target_pairs={{0,4},{1,5},{2,6},{3,7},{4,0},{5,1},{6,2},{7,3},{8,12},{9,13},{10,... | collective-permute-start | bytes 208904 | tf_op jit(solution)/shard_map/ppermute | solution.py:31
  196.2 1.3 collective-permute-start.6
  197.6 4.4 %collective-permute-start.7 = (f32[136,128]{1,0:T(8,128)S(1)}, f32[136,128]{1,0:T(8,128)S(1)}, u32[]{:S(2)}, u32[]{:S(2)}) collective-permute-start(f32[136,128]{1,0:T(8,128)S(1)} %add.134), channel_id=1, source_target_pairs={{0,16},{8,24},{16,0},{24,8},{1,17},{9,25},{17,1},{25,9},{2,18},{10... | collective-permute-start | bytes 208904 | tf_op jit(solution)/shard_map/ppermute | solution.py:31
  199.2 37.7 %copy-start.7 = (f32[128]{0:T(128)S(1)}, f32[128]{0:T(128)}, u32[]{:S(2)}) copy-start(f32[128]{0:T(128)} %param.19) | copy-start | bytes 1540
  199.2 38.0 %copy-start.4 = (f32[128,512]{1,0:T(8,128)S(1)}, f32[128,512]{1,0:T(8,128)}, u32[]{:S(2)}) copy-start(f32[128,512]{1,0:T(8,128)} %bitcast_add_fusion.2) | copy-start | bytes 786436
  202.0 31.9 %collective-permute-start.8 = (f32[128,2048]{1,0:T(8,128)S(1)}, f32[128,2048]{1,0:T(8,128)}, u32[]{:S(2)}, u32[]{:S(2)}) collective-permute-start(f32[128,2048]{1,0:T(8,128)S(1)} %dynamic-slice_select_fusion), channel_id=1, source_target_pairs={{0,16},{1,17},{10,26},{11,27},{20,4},{21,5},{30,14},{31,15}} | collective-permute-start | bytes 3145736 | tf_op jit(solution)/shard_map/ppermute | solution.py:23
  235.3 5.6 %collective-permute-start.9 = (f32[128,2048]{1,0:T(8,128)S(1)}, f32[128,2048]{1,0:T(8,128)S(1)}, u32[]{:S(2)}, u32[]{:S(2)}) collective-permute-start(f32[128,2048]{1,0:T(8,128)S(1)} %add.139), channel_id=1, source_target_pairs={{0,8},{16,24},{1,9},{17,25},{10,2},{26,18},{11,3},{27,19},{20,28},... | collective-permute-start | bytes 3145736 | tf_op jit(solution)/shard_map/ppermute | solution.py:23
  241.9 26.9 %copy-start.1 = (f32[4,128]{1,0:T(4,128)S(1)}, f32[4,128]{1,0:T(4,128)}, u32[]{:S(2)}) copy-start(f32[4,128]{1,0:T(4,128)} %param.18) | copy-start | bytes 6148
Sparse Core Ops, SparseCore 0:
  37.0 15.7 all-gather.2
  130.5 49.2 all-gather.4

commit v8 on v7

--- a/solution.py
+++ b/solution.py
@@ -44,6 +44,33 @@
     return x
 
 
+def shift_all_to_all(x, axis, size, me):
+    got = [lax.dynamic_index_in_dim(x, me, 1, keepdims=False)]
+    for k in range(1, size):
+        piece = lax.dynamic_index_in_dim(x, (me + size - k) % size, 1, keepdims=False)
+        got.append(lax.ppermute(piece, axis, [(i, (i - k) % size) for i in range(size)]))
+    got = jnp.stack(got, axis=0)
+    both = jnp.concatenate([got, got], axis=0)
+    ordered = lax.dynamic_slice_in_dim(both, (size - me) % size, size, 0)
+    return ordered.reshape((size * x.shape[0],) + x.shape[2:])
+
+
+def doubling_gather(x, axis, size, me):
+    bits = []
+    bit = 1
+    while bit < size:
+        bits.append(bit)
+        bit *= 2
+    rows = x.shape[0]
+    x = x[None]
+    for bit in bits[::-1]:
+        other = lax.ppermute(x, axis, [(i, i ^ bit) for i in range(size)])
+        low = (me // bit) % 2 == 0
+        x = jnp.where(low, jnp.stack([x, other], axis=1), jnp.stack([other, x], axis=1))
+        x = x.reshape((x.shape[0] * 2,) + x.shape[2:])
+    return x.reshape((size * rows,) + x.shape[2:])
+
+
 def on_device(
     atom_feat, types, neighbors, frame_of_atom, weights, type_gain, out_vec, targets, noise, cov
 ):
@@ -77,8 +104,8 @@
     m_all = frames * n_row * n_col
     col_w = width // n_col
     blk = width // (n_row * n_col)
-    col_part = lax.all_to_all(grads, "col", split_axis=1, concat_axis=0, tiled=True)
-    grad_col = lax.all_gather(col_part, "row", axis=0, tiled=True)
+    col_part = shift_all_to_all(grads.reshape(frames, n_col, col_w), "col", n_col, col_id)
+    grad_col = doubling_gather(col_part.reshape(n_col * frames, col_w), "row", n_row, row_id)
     nbits = n_col.bit_length() - 1
     letters = "abcdefgh"[:nbits]
     cov_blocks = cov.reshape((2,) * nbits + (cov.shape[0] // n_col, cov.shape[1]))

time: 276 us -> 272 us (0.986)
  blocking collectives: 16 us -> 0 us
  starting transfers between devices: 17.6 us -> 28.2 us
    all_to_all x1 -> x0, blocking collectives: 16 us -> none  [on_device(): lax.all_to_all(grads, 'col', split_axis=1, concat_axis=0, tiled=True)]
    all_gather x1 -> x0, waiting for transfers between devices: 15.6 us -> none  [on_device(): grad_col = lax.all_gather(col_part, 'row', axis=0, tiled=True)]
    ppermute x0 -> x9, starting transfers between devices: none -> 14.6 us  [the longest x7 13 us: shift_all_to_all(): lax.ppermute(piece, axis, [(i, (i - k) % size) for i in range(size)])]
    ppermute x0 -> x9, waiting for transfers between devices: none -> 12 us  [the longest x2 6.6 us: doubling_gather(): other = lax.ppermute(x, axis, [(i, i ^ bit) for i in range(size)])]
    ppermute x3, starting transfers between devices: 5.59 us -> 1.83 us  [halving_scatter(): x = keep + lax.ppermute(send, axis, [(i, i ^ bit) for i in range(size)])]
    ppermute x3, waiting for transfers between devices: 46.5 us -> 50 us  [halving_scatter(): x = keep + lax.ppermute(send, axis, [(i, i ^ bit) for i in range(size)])]
  transfers between devices with their start and end apart: 12 -> 20, of which waited for: 10 -> 14; matrix products, arithmetic and copies ran while one was open for 12% -> 12% of each run, Pallas kernels for 0% -> 0%
where the time goes in v8:
time: 272 us; the launch traced here: 271 us
  waiting for transfers between devices  124 us (46%)
  matrix products  60.2 us (22%)
  other arithmetic  39.4 us (14%)
  starting transfers between devices  28.2 us (10%)
  between operations  14.8 us (5%)
  local copies, waits for them, and re-layouts  4.96 us (2%)
    ppermute x3, waiting for transfers between devices, halving_scatter(): x = keep + lax.ppermute(send, axis, [(i, i ^ bit) for i in range(size)])  50 us
    all_gather x1, waiting for transfers between devices, on_device(): gain_rows_t = lax.all_gather(gain_own_t, 'col', axis=1, tiled=True)  47.8 us
    dot_general x1, matrix products, on_device(): new_cov = cov - jnp.einsum('mi,mj->ij', white_row, white_col, precision=mid)  26.9 us
    dot_general x1, matrix products, on_device(): jnp.einsum('mk,' + letters + 'ik->' + letters[::-1] + 'mi', grad_col, cov...  22.8 us
    ppermute x5, waiting for transfers between devices, butterfly_sum(): buf = buf + lax.ppermute(buf, axis, [(i, i ^ bit) for i in range(size)])  13.8 us
    another operation x3, other arithmetic, on_device(): lower = jnp.linalg.cholesky(gram)  13.2 us
    ppermute x7, starting transfers between devices, shift_all_to_all(): lax.ppermute(piece, axis, [(i, (i - k) % size) for i in range(size)])  13 us
    another operation x2, other arithmetic, on_device(): coef = jax.scipy.linalg.cho_solve((lower, True), targets - pred_all)  11.9 us
  transfers between devices with their start and end apart: 20, of which 14 were waited for; matrix products, arithmetic and copies ran while one was open for 12% of the time, Pallas kernels for 0%

profile of v8, /device:TPU:0, one launch (start us, length us, event | category | flops | bytes accessed | tf_op | source)
XLA Modules:
  0.0 271.2 jit_solution(7199727040655584454)
XLA Ops:
  8.0 0.9 copy.17
  8.9 5.7 %convert_reduce_fusion = f32[256,256]{1,0:T(8,128)S(1)} fusion(s32[256,32]{1,0:T(8,128)S(1)} %copy.17), kind=kLoop, calls=%fused_computation.1 | loop fusion | flops 6225920 | bytes 294912 | tf_op jit(solution)/shard_map/reduce_sum | solution.py:87
  14.6 1.0 fusion.15
  15.6 1.2 convolution_multiply_fusion.2
  16.8 1.3 fusion.2
  19.5 6.1 %collective-permute-start = (f32[4,2048]{1,0:T(4,128)S(1)}, f32[4,2048]{1,0:T(4,128)S(1)}, u32[]{:S(2)}, u32[]{:S(2)}) collective-permute-start(f32[4,2048]{1,0:T(4,128)S(1)} %bitcast.142), channel_id=1, source_target_pairs={{0,7},{1,0},{2,1},{3,2},{4,3},{5,4},{6,5},{7,6},{8,15},{9,8},{10,9... | collective-permute-start | bytes 98312 | tf_op jit(solution)/shard_map/ppermute | solution.py:51
  26.1 3.0 %collective-permute-start.3 = (f32[4,2048]{1,0:T(4,128)S(1)}, f32[4,2048]{1,0:T(4,128)S(1)}, u32[]{:S(2)}, u32[]{:S(2)}) collective-permute-start(f32[4,2048]{1,0:T(4,128)S(1)} %bitcast.139), channel_id=1, source_target_pairs={{0,4},{1,5},{2,6},{3,7},{4,0},{5,1},{6,2},{7,3},{8,12},{9,13},{10,... | collective-permute-start | bytes 98312 | tf_op jit(solution)/shard_map/ppermute | solution.py:51
  29.3 1.9 collective-permute-start.5
  31.2 1.4 collective-permute-start.6
  32.7 2.3 collective-permute-done.4
  35.0 1.3 collective-permute-done.5
  36.3 1.8 collective-permute-done.6
  38.4 1.6 collective-permute-start.7
  39.9 4.9 %collective-permute-done.7 = f32[1,32,2048]{2,1,0:T(8,128)S(1)} collective-permute-done((f32[1,32,2048]{2,1,0:T(8,128)S(1)}, f32[1,32,2048]{2,1,0:T(8,128)S(1)}, u32[]{:S(2)}, u32[]{:S(2)}) %collective-permute-start.7) | collective-permute-done | bytes 262176 | tf_op jit(solution)/shard_map/ppermute | solution.py:67
  45.1 1.7 collective-permute-done.8
  46.9 22.8 %fusion.33 = f32[128,2,2,2,512]{4,0,3,2,1:T(8,128)S(1)} fusion(f32[128,2048,1,1,1]{1,0,4,3,2:T(8,128)S(1)} %bitcast.133, f32[2,2,2,512,2048]{4,3,2,1,0:T(8,128)} %bitcast.132), kind=kOutput, calls=%fused_computation.99 | convolution fusion | flops 6442450944 | bytes 36700160 | tf_op jit(solution)/shard_map/mk,abcik->cbami/dot_general | solution.py:112
  69.7 1.0 dynamic-slice_bitcast_fusion
  70.7 25.5 %collective-permute-done.9 = f32[2,2,128,512]{3,2,0,1:T(8,128)} collective-permute-done((f32[2,2,128,512]{3,2,0,1:T(8,128)}, f32[2,2,128,512]{3,2,0,1:T(8,128)}, u32[]{:S(2)}, u32[]{:S(2)}) %collective-permute-start.9) | collective-permute-done | bytes 1048608 | tf_op jit(solution)/shard_map/ppermute | solution.py:43
  96.3 1.5 bitcast_add_fusion
  97.7 1.0 copy-done.3
  98.9 13.1 %collective-permute-done.10 = f32[2,128,512]{2,1,0:T(8,128)S(1)} collective-permute-done((f32[2,128,512]{2,1,0:T(8,128)S(1)}, f32[2,128,512]{2,1,0:T(8,128)S(1)}, u32[]{:S(2)}, u32[]{:S(2)}) %collective-permute-start.10) | collective-permute-done | bytes 524320 | tf_op jit(solution)/shard_map/ppermute | solution.py:43
  111.9 1.1 bitcast_add_fusion.1
  113.1 1.8 collective-permute-start.11
  114.9 11.4 %collective-permute-done.11 = f32[128,512]{1,0:T(8,128)S(1)} collective-permute-done((f32[128,512]{1,0:T(8,128)S(1)}, f32[128,512]{1,0:T(8,128)S(1)}, u32[]{:S(2)}, u32[]{:S(2)}) %collective-permute-start.11) | collective-permute-done | bytes 262176 | tf_op jit(solution)/shard_map/ppermute | solution.py:43
  126.3 0.7 bitcast_add_fusion.2
  127.4 47.8 %all-gather.2.cloned.1.call-done = f32[128,4096]{1,0:T(8,128)} async-done(((f32[128,512]{1,0:T(8,128)}), f32[128,4096]{1,0:T(8,128)}) %all-gather.2.cloned.1.call-update) | async-done | bytes 2097168 | tf_op jit(solution)/shard_map/all_gather | solution.py:116
  175.3 2.4 convolution_select_fusion
  178.3 3.8 %collective-permute-done.12 = f32[136,128]{1,0:T(8,128)S(1)} collective-permute-done((f32[136,128]{1,0:T(8,128)S(1)}, f32[136,128]{1,0:T(8,128)S(1)}, u32[]{:S(2)}, u32[]{:S(2)}) %collective-permute-start.12) | collective-permute-done | bytes 69664 | tf_op jit(solution)/shard_map/ppermute | solution.py:31
  182.1 1.5 collective-permute-start.13
  183.6 2.8 %collective-permute-done.13 = f32[136,128]{1,0:T(8,128)S(1)} collective-permute-done((f32[136,128]{1,0:T(8,128)S(1)}, f32[136,128]{1,0:T(8,128)S(1)}, u32[]{:S(2)}, u32[]{:S(2)}) %collective-permute-start.13) | collective-permute-done | bytes 69664 | tf_op jit(solution)/shard_map/ppermute | solution.py:31
  186.5 2.0 collective-permute-start.14
  188.5 3.3 %collective-permute-done.14 = f32[136,128]{1,0:T(8,128)S(1)} collective-permute-done((f32[136,128]{1,0:T(8,128)S(1)}, f32[136,128]{1,0:T(8,128)S(1)}, u32[]{:S(2)}, u32[]{:S(2)}) %collective-permute-start.14) | collective-permute-done | bytes 69664 | tf_op jit(solution)/shard_map/ppermute | solution.py:31
  191.8 1.2 collective-permute-done.15
  193.1 1.5 collective-permute-start.16
  194.8 2.7 %collective-permute-done.16 = f32[136,128]{1,0:T(8,128)S(1)} collective-permute-done((f32[136,128]{1,0:T(8,128)S(1)}, f32[136,128]{1,0:T(8,128)S(1)}, u32[]{:S(2)}, u32[]{:S(2)}) %collective-permute-start.16) | collective-permute-done | bytes 69664 | tf_op jit(solution)/shard_map/ppermute | solution.py:31
  197.5 4.4 %collective-permute-start.17 = (f32[128,2048]{1,0:T(8,128)S(1)}, f32[128,2048]{1,0:T(8,128)}, u32[]{:S(2)}, u32[]{:S(2)}) collective-permute-start(f32[128,2048]{1,0:T(8,128)S(1)} %dynamic-slice_select_fusion), channel_id=1, source_target_pairs={{0,16},{1,17},{10,26},{11,27},{20,4},{21,5},{30,14},{31,15}} | collective-permute-start | bytes 3145736 | tf_op jit(solution)/shard_map/ppermute | solution.py:23
  201.9 0.7 select_add_fusion
  202.6 0.9 copy.21
  203.5 0.7 fusion.22
  204.2 12.5 %cholesky.16 = f32[128,128]{1,0:T(8,128)S(1)} custom-call(f32[128,128]{1,0:T(8,128)} %fusion.22), custom_call_target="Cholesky" | custom-call | tf_op jit(solution)/shard_map/jit(cholesky)/cholesky | solution.py:135
  217.4 1.3 fusion.16
  218.7 10.6 %custom-call.16 = f32[1,128,128]{1,2,0:T(8,128)S(1)} custom-call(f32[1,128,128]{2,1,0:T(8,128)} %fusion.16), custom_call_target="InvertDiagBlocksLowerTriangular" | custom-call | tf_op jit(solution)/shard_map/jit(_cho_solve)/triangular_solve | solution.py:140
  229.4 1.4 add.246
  230.8 1.6 collective-permute-start.18
  233.0 1.3 dynamic-slice_add_fusion
  234.4 1.9 fusion.18
  236.3 1.1 fusion.5
  237.4 26.9 %convolution_subtract_fusion = f32[4096,2048]{1,0:T(8,128)} fusion(f32[4096,2048]{1,0:T(8,128)} %param.21, f32[128,4096]{1,0:T(8,128)S(1)} %fusion.18, f32[128,2048]{1,0:T(8,128)S(1)} %fusion.5), kind=kOutput, calls=%fused_computation | convolution fusion | flops 6450839552 | bytes 70254592 | tf_op jit(solution)/shard_map/mi,mj->ij/dot_general | solution.py:139
  (86 shorter events, 6.1 us)
Async XLA Ops:
  7.2 7.4 %copy-start = (f32[4,128]{1,0:T(4,128)S(1)}, f32[4,128]{1,0:T(4,128)}, u32[]{:S(2)}) copy-start(f32[4,128]{1,0:T(4,128)} %param.18) | copy-start | bytes 6148
  7.2 11.0 %copy-start.5 = (f32[128,128]{1,0:T(8,128)S(1)}, f32[128,128]{1,0:T(8,128)}, u32[]{:S(2)}) copy-start(f32[128,128]{1,0:T(8,128)} %param.16) | copy-start | bytes 196612
  7.2 168.1 %all-gather.2.cloned.1.call-start = ((), (), s32[]{:S(2)}) async-start(), calls=%async_computation | async-start | bytes 2359296 | tf_op jit(solution)/shard_map/all_gather | solution.py:116
  19.5 9.9 %collective-permute-start = (f32[4,2048]{1,0:T(4,128)S(1)}, f32[4,2048]{1,0:T(4,128)S(1)}, u32[]{:S(2)}, u32[]{:S(2)}) collective-permute-start(f32[4,2048]{1,0:T(4,128)S(1)} %bitcast.142), channel_id=1, source_target_pairs={{0,7},{1,0},{2,1},{3,2},{4,3},{5,4},{6,5},{7,6},{8,15},{9,8},{10,9... | collective-permute-start | bytes 98312 | tf_op jit(solution)/shard_map/ppermute | solution.py:51
  25.5 5.7 %collective-permute-start.1 = (f32[4,2048]{1,0:T(4,128)S(1)}, f32[4,2048]{1,0:T(4,128)S(1)}, u32[]{:S(2)}, u32[]{:S(2)}) collective-permute-start(f32[4,2048]{1,0:T(4,128)S(1)} %bitcast.141), channel_id=1, source_target_pairs={{0,6},{1,7},{2,0},{3,1},{4,2},{5,3},{6,4},{7,5},{8,14},{9,15},{10,... | collective-permute-start | bytes 98312 | tf_op jit(solution)/shard_map/ppermute | solution.py:51
  26.0 6.6 %collective-permute-start.2 = (f32[4,2048]{1,0:T(4,128)S(1)}, f32[4,2048]{1,0:T(4,128)S(1)}, u32[]{:S(2)}, u32[]{:S(2)}) collective-permute-start(f32[4,2048]{1,0:T(4,128)S(1)} %bitcast.138), channel_id=1, source_target_pairs={{0,5},{1,6},{2,7},{3,0},{4,1},{5,2},{6,3},{7,4},{8,13},{9,14},{10,... | collective-permute-start | bytes 98312 | tf_op jit(solution)/shard_map/ppermute | solution.py:51
  26.1 6.5 %collective-permute-start.3 = (f32[4,2048]{1,0:T(4,128)S(1)}, f32[4,2048]{1,0:T(4,128)S(1)}, u32[]{:S(2)}, u32[]{:S(2)}) collective-permute-start(f32[4,2048]{1,0:T(4,128)S(1)} %bitcast.139), channel_id=1, source_target_pairs={{0,4},{1,5},{2,6},{3,7},{4,0},{5,1},{6,2},{7,3},{8,12},{9,13},{10,... | collective-permute-start | bytes 98312 | tf_op jit(solution)/shard_map/ppermute | solution.py:51
  29.2 5.8 %collective-permute-start.4 = (f32[4,2048]{1,0:T(4,128)S(1)}, f32[4,2048]{1,0:T(4,128)S(1)}, u32[]{:S(2)}, u32[]{:S(2)}) collective-permute-start(f32[4,2048]{1,0:T(4,128)S(1)} %bitcast.140), channel_id=1, source_target_pairs={{0,3},{1,4},{2,5},{3,6},{4,7},{5,0},{6,1},{7,2},{8,11},{9,12},{10,... | collective-permute-start | bytes 98312 | tf_op jit(solution)/shard_map/ppermute | solution.py:51
  29.3 6.9 %collective-permute-start.5 = (f32[4,2048]{1,0:T(4,128)S(1)}, f32[4,2048]{1,0:T(4,128)S(1)}, u32[]{:S(2)}, u32[]{:S(2)}) collective-permute-start(f32[4,2048]{1,0:T(4,128)S(1)} %bitcast.144), channel_id=1, source_target_pairs={{0,2},{1,3},{2,4},{3,5},{4,6},{5,7},{6,0},{7,1},{8,10},{9,11},{10,... | collective-permute-start | bytes 98312 | tf_op jit(solution)/shard_map/ppermute | solution.py:51
  31.2 6.8 %collective-permute-start.6 = (f32[4,2048]{1,0:T(4,128)S(1)}, f32[4,2048]{1,0:T(4,128)S(1)}, u32[]{:S(2)}, u32[]{:S(2)}) collective-permute-start(f32[4,2048]{1,0:T(4,128)S(1)} %bitcast.143), channel_id=1, source_target_pairs={{0,1},{1,2},{2,3},{3,4},{4,5},{5,6},{6,7},{7,0},{8,9},{9,10},{10,1... | collective-permute-start | bytes 98312 | tf_op jit(solution)/shard_map/ppermute | solution.py:51
  38.4 6.4 %collective-permute-start.7 = (f32[1,32,2048]{2,1,0:T(8,128)S(1)}, f32[1,32,2048]{2,1,0:T(8,128)S(1)}, u32[]{:S(2)}, u32[]{:S(2)}) collective-permute-start(f32[1,32,2048]{2,1,0:T(8,128)S(1)} %broadcast_in_dim_reshape.3), channel_id=1, source_target_pairs={{0,16},{8,24},{16,0},{24,8},{1,17},{9,25},{17,1},{25,9},{2,18},{10... | collective-permute-start | bytes 786440 | tf_op jit(solution)/shard_map/ppermute | solution.py:67
  44.8 2.0 collective-permute-start.8
  70.7 25.5 %collective-permute-start.9 = (f32[2,2,128,512]{3,2,0,1:T(8,128)}, f32[2,2,128,512]{3,2,0,1:T(8,128)}, u32[]{:S(2)}, u32[]{:S(2)}) collective-permute-start(f32[2,2,128,512]{3,2,0,1:T(8,128)} %dynamic-slice_bitcast_fusion), channel_id=1, source_target_pairs={{0,1},{1,0},{2,3},{3,2},{4,5},{5,4},{6,7},{7,6},{8,9},{9,8},{10,11... | collective-permute-start | bytes 3145736 | tf_op jit(solution)/shard_map/ppermute | solution.py:43
  97.7 1.0 copy-start.3
  98.7 28.4 %copy-start.7 = (s32[256]{0:T(256)S(1)}, s32[256]{0:T(256)}, u32[]{:S(2)}) copy-start(s32[256]{0:T(256)} %param.15) | copy-start | bytes 3076
  98.7 13.2 %collective-permute-start.10 = (f32[2,128,512]{2,1,0:T(8,128)S(1)}, f32[2,128,512]{2,1,0:T(8,128)S(1)}, u32[]{:S(2)}, u32[]{:S(2)}) collective-permute-start(f32[2,128,512]{2,1,0:T(8,128)S(1)} %dynamic-slice_bitcast_fusion.1), channel_id=1, source_target_pairs={{0,2},{1,3},{2,0},{3,1},{4,6},{5,7},{6,4},{7,5},{8,10},{9,11},{10,... | collective-permute-start | bytes 1572872 | tf_op jit(solution)/shard_map/ppermute | solution.py:43
  113.1 13.2 %collective-permute-start.11 = (f32[128,512]{1,0:T(8,128)S(1)}, f32[128,512]{1,0:T(8,128)S(1)}, u32[]{:S(2)}, u32[]{:S(2)}) collective-permute-start(f32[128,512]{1,0:T(8,128)S(1)} %dynamic-slice_bitcast_fusion.2), channel_id=1, source_target_pairs={{0,4},{1,5},{2,6},{3,7},{4,0},{5,1},{6,2},{7,3},{8,12},{9,13},{10,... | collective-permute-start | bytes 786440 | tf_op jit(solution)/shard_map/ppermute | solution.py:43
  175.3 19.4 %copy-start.2 = (f32[128,4096]{1,0:T(8,128)S(1)}, f32[128,4096]{1,0:T(8,128)}, u32[]{:S(2)}) copy-start(f32[128,4096]{1,0:T(8,128)} %all-gather.2.cloned.1.call-done) | copy-start | bytes 6291460
  177.7 24.2 %copy-start.6 = (f32[128]{0:T(128)S(1)}, f32[128]{0:T(128)}, u32[]{:S(2)}) copy-start(f32[128]{0:T(128)} %param.20) | copy-start | bytes 1540
  177.7 4.4 %collective-permute-start.12 = (f32[136,128]{1,0:T(8,128)S(1)}, f32[136,128]{1,0:T(8,128)S(1)}, u32[]{:S(2)}, u32[]{:S(2)}) collective-permute-start(f32[136,128]{1,0:T(8,128)S(1)} %pad_maximum_fusion), channel_id=1, source_target_pairs={{0,1},{1,0},{2,3},{3,2},{4,5},{5,4},{6,7},{7,6},{8,9},{9,8},{10,11... | collective-permute-start | bytes 208904 | tf_op jit(solution)/shard_map/ppermute | solution.py:31
  182.1 4.4 %collective-permute-start.13 = (f32[136,128]{1,0:T(8,128)S(1)}, f32[136,128]{1,0:T(8,128)S(1)}, u32[]{:S(2)}, u32[]{:S(2)}) collective-permute-start(f32[136,128]{1,0:T(8,128)S(1)} %fusion.32), channel_id=1, source_target_pairs={{0,2},{1,3},{2,0},{3,1},{4,6},{5,7},{6,4},{7,5},{8,10},{9,11},{10,... | collective-permute-start | bytes 208904 | tf_op jit(solution)/shard_map/ppermute | solution.py:31
  186.5 5.3 %collective-permute-start.14 = (f32[136,128]{1,0:T(8,128)S(1)}, f32[136,128]{1,0:T(8,128)S(1)}, u32[]{:S(2)}, u32[]{:S(2)}) collective-permute-start(f32[136,128]{1,0:T(8,128)S(1)} %add.239), channel_id=1, source_target_pairs={{0,4},{1,5},{2,6},{3,7},{4,0},{5,1},{6,2},{7,3},{8,12},{9,13},{10,... | collective-permute-start | bytes 208904 | tf_op jit(solution)/shard_map/ppermute | solution.py:31
  191.8 1.3 collective-permute-start.15
  193.1 4.4 %collective-permute-start.16 = (f32[136,128]{1,0:T(8,128)S(1)}, f32[136,128]{1,0:T(8,128)S(1)}, u32[]{:S(2)}, u32[]{:S(2)}) collective-permute-start(f32[136,128]{1,0:T(8,128)S(1)} %add.241), channel_id=1, source_target_pairs={{0,16},{8,24},{16,0},{24,8},{1,17},{9,25},{17,1},{25,9},{2,18},{10... | collective-permute-start | bytes 208904 | tf_op jit(solution)/shard_map/ppermute | solution.py:31
  194.7 37.7 %copy-start.8 = (f32[128]{0:T(128)S(1)}, f32[128]{0:T(128)}, u32[]{:S(2)}) copy-start(f32[128]{0:T(128)} %param.19) | copy-start | bytes 1540
  194.7 38.0 %copy-start.4 = (f32[128,512]{1,0:T(8,128)S(1)}, f32[128,512]{1,0:T(8,128)}, u32[]{:S(2)}) copy-start(f32[128,512]{1,0:T(8,128)} %bitcast_add_fusion.2) | copy-start | bytes 786436
  197.5 31.9 %collective-permute-start.17 = (f32[128,2048]{1,0:T(8,128)S(1)}, f32[128,2048]{1,0:T(8,128)}, u32[]{:S(2)}, u32[]{:S(2)}) collective-permute-start(f32[128,2048]{1,0:T(8,128)S(1)} %dynamic-slice_select_fusion), channel_id=1, source_target_pairs={{0,16},{1,17},{10,26},{11,27},{20,4},{21,5},{30,14},{31,15}} | collective-permute-start | bytes 3145736 | tf_op jit(solution)/shard_map/ppermute | solution.py:23
  230.8 5.6 %collective-permute-start.18 = (f32[128,2048]{1,0:T(8,128)S(1)}, f32[128,2048]{1,0:T(8,128)S(1)}, u32[]{:S(2)}, u32[]{:S(2)}) collective-permute-start(f32[128,2048]{1,0:T(8,128)S(1)} %add.246), channel_id=1, source_target_pairs={{0,8},{16,24},{1,9},{17,25},{10,2},{26,18},{11,3},{27,19},{20,28},... | collective-permute-start | bytes 3145736 | tf_op jit(solution)/shard_map/ppermute | solution.py:23
  237.4 26.9 %copy-start.1 = (f32[4,128]{1,0:T(4,128)S(1)}, f32[4,128]{1,0:T(4,128)}, u32[]{:S(2)}) copy-start(f32[4,128]{1,0:T(4,128)} %param.18) | copy-start | bytes 6148
Sparse Core Ops, SparseCore 0:
  127.2 48.0 all-gather.1

commit v9 on v8

--- a/solution.py
+++ b/solution.py
@@ -112,13 +112,18 @@
     partial_t = jnp.einsum(
         "mk," + letters + "ik->" + letters[::-1] + "mi", grad_col, cov_blocks, precision=mid
     )
+    factor = n_col // n_row
+    grad_own = None
+    for t in range(n_row):
+        perm = []
+        for r in range(n_row):
+            for q in range(factor):
+                perm.append((r * n_col + r * factor + q, r * n_col + q * n_row + t))
+        got = lax.ppermute(grad_col[:, t * blk : (t + 1) * blk], ("row", "col"), perm)
+        grad_own = got if grad_own is None else grad_own + got
+    grad_own, partial_t = lax.optimization_barrier((grad_own, partial_t))
     gain_own_t = halving_scatter(partial_t, "col", n_col, col_id)
-    gain_rows_t = lax.all_gather(gain_own_t, "col", axis=1, tiled=True)
-    factor = n_col // n_row
-    half_t = lax.dynamic_slice_in_dim(gain_rows_t, col_id % factor * col_w, col_w, 1)
-    mine = row_id == col_id // factor
-    gram_part = jnp.einsum("mk,nk->mn", grad_col, half_t, precision=hi)
-    gram_part = jnp.where(mine, gram_part, jnp.zeros_like(gram_part))
+    gram_own = jnp.einsum("mk,nk->mn", grad_own, gain_own_t, precision=hi)
     device_id = row_id * n_col + col_id
     slots = lax.dynamic_update_slice_in_dim(
         jnp.zeros((8, m_all), jnp.float32),
@@ -126,10 +131,12 @@
         device_id * frames,
         1,
     )
-    small = jnp.concatenate([gram_part, slots], axis=0)
+    small = jnp.concatenate([gram_own, slots], axis=0)
     small = butterfly_sum(butterfly_sum(small, "col", n_col), "row", n_row)
+    gain_rows_t = lax.all_gather(gain_own_t, "col", axis=1, tiled=True)
+    half_t = lax.dynamic_slice_in_dim(gain_rows_t, col_id % factor * col_w, col_w, 1)
+    mine = row_id == col_id // factor
     masked = jnp.where(mine, half_t, jnp.zeros_like(half_t))
-    small, masked = lax.optimization_barrier((small, masked))
     gram = small[:m_all] + jnp.diag(noise)
     pred_all = small[m_all]
     lower = jnp.linalg.cholesky(gram)

time: 272 us -> 273 us (level)
  waiting for transfers between devices: 124 us -> 118 us
  starting transfers between devices: 28.2 us -> 33.1 us
    ppermute x5, waiting for transfers between devices: 13.8 us -> 30.8 us  [butterfly_sum(): buf = buf + lax.ppermute(buf, axis, [(i, i ^ bit) for i in range(size)])]
    all_gather x1, waiting for transfers between devices: 47.8 us -> 31 us  [on_device(): gain_rows_t = lax.all_gather(gain_own_t, 'col', axis=1, tiled=True)]
    ppermute x0 -> x4, starting transfers between devices: none -> 8.97 us  [on_device(): got = lax.ppermute(grad_col[:, t * blk:(t + 1) * blk], ('row', 'col'), perm)]
    ppermute x3, waiting for transfers between devices: 50 us -> 44.1 us  [halving_scatter(): x = keep + lax.ppermute(send, axis, [(i, i ^ bit) for i in range(size)])]
    ppermute x5, starting transfers between devices: 5.78 us -> 1.52 us  [butterfly_sum(): buf = buf + lax.ppermute(buf, axis, [(i, i ^ bit) for i in range(size)])]
  transfers between devices with their start and end apart: 20 -> 24, of which waited for: 14 -> 13; matrix products, arithmetic and copies ran while one was open for 12% -> 22% of each run, Pallas kernels for 0% -> 0%
where the time goes in v9:
time: 273 us; the launch traced here: 272 us
  waiting for transfers between devices  118 us (43%)
  matrix products  59.8 us (22%)
  other arithmetic  41.5 us (15%)
  starting transfers between devices  33.1 us (12%)
  between operations  14.9 us (5%)
  local copies, waits for them, and re-layouts  4.68 us (2%)
    ppermute x3, waiting for transfers between devices, halving_scatter(): x = keep + lax.ppermute(send, axis, [(i, i ^ bit) for i in range(size)])  44.1 us
    all_gather x1, waiting for transfers between devices, on_device(): gain_rows_t = lax.all_gather(gain_own_t, 'col', axis=1, tiled=True)  31 us
    ppermute x5, waiting for transfers between devices, butterfly_sum(): buf = buf + lax.ppermute(buf, axis, [(i, i ^ bit) for i in range(size)])  30.8 us
    dot_general x1, matrix products, on_device(): new_cov = cov - jnp.einsum('mi,mj->ij', white_row, white_col, precision=mid)  26.9 us
    dot_general x1, matrix products, on_device(): jnp.einsum('mk,' + letters + 'ik->' + letters[::-1] + 'mi', grad_col, cov...  22.7 us
    another operation x3, other arithmetic, on_device(): lower = jnp.linalg.cholesky(gram)  13.2 us
    ppermute x7, starting transfers between devices, shift_all_to_all(): lax.ppermute(piece, axis, [(i, (i - k) % size) for i in range(size)])  12.8 us
    another operation x2, other arithmetic, on_device(): coef = jax.scipy.linalg.cho_solve((lower, True), targets - pred_all)  11.9 us
  transfers between devices with their start and end apart: 24, of which 13 were waited for; matrix products, arithmetic and copies ran while one was open for 22% of the time, Pallas kernels for 0%

profile of v9, /device:TPU:0, one launch (start us, length us, event | category | flops | bytes accessed | tf_op | source)
XLA Modules:
  0.0 272.0 jit_solution(4802588198523209999)
XLA Ops:
  8.0 0.9 copy.16
  8.9 5.7 %convert_reduce_fusion = f32[256,256]{1,0:T(8,128)S(1)} fusion(s32[256,32]{1,0:T(8,128)S(1)} %copy.16), kind=kLoop, calls=%fused_computation.1 | loop fusion | flops 6225920 | bytes 294912 | tf_op jit(solution)/shard_map/reduce_sum | solution.py:87
  14.6 1.0 fusion.14
  15.6 1.2 convolution_multiply_fusion.2
  16.8 1.3 fusion.2
  19.5 6.0 %collective-permute-start = (f32[4,2048]{1,0:T(4,128)S(1)}, f32[4,2048]{1,0:T(4,128)S(1)}, u32[]{:S(2)}, u32[]{:S(2)}) collective-permute-start(f32[4,2048]{1,0:T(4,128)S(1)} %bitcast.141), channel_id=1, source_target_pairs={{0,7},{1,0},{2,1},{3,2},{4,3},{5,4},{6,5},{7,6},{8,15},{9,8},{10,9... | collective-permute-start | bytes 98312 | tf_op jit(solution)/shard_map/ppermute | solution.py:51
  26.1 3.0 %collective-permute-start.3 = (f32[4,2048]{1,0:T(4,128)S(1)}, f32[4,2048]{1,0:T(4,128)S(1)}, u32[]{:S(2)}, u32[]{:S(2)}) collective-permute-start(f32[4,2048]{1,0:T(4,128)S(1)} %bitcast.138), channel_id=1, source_target_pairs={{0,4},{1,5},{2,6},{3,7},{4,0},{5,1},{6,2},{7,3},{8,12},{9,13},{10,... | collective-permute-start | bytes 98312 | tf_op jit(solution)/shard_map/ppermute | solution.py:51
  29.3 1.9 collective-permute-start.5
  31.2 1.2 collective-permute-start.6
  32.5 2.8 %collective-permute-done.4 = f32[4,2048]{1,0:T(4,128)S(1)} collective-permute-done((f32[4,2048]{1,0:T(4,128)S(1)}, f32[4,2048]{1,0:T(4,128)S(1)}, u32[]{:S(2)}, u32[]{:S(2)}) %collective-permute-start.4) | collective-permute-done | bytes 32800 | tf_op jit(solution)/shard_map/ppermute | solution.py:51
  35.3 0.9 collective-permute-done.5
  36.3 1.7 collective-permute-done.6
  38.2 1.6 collective-permute-start.7
  39.7 4.9 %collective-permute-done.7 = f32[1,32,2048]{2,1,0:T(8,128)S(1)} collective-permute-done((f32[1,32,2048]{2,1,0:T(8,128)S(1)}, f32[1,32,2048]{2,1,0:T(8,128)S(1)}, u32[]{:S(2)}, u32[]{:S(2)}) %collective-permute-start.7) | collective-permute-done | bytes 262176 | tf_op jit(solution)/shard_map/ppermute | solution.py:67
  44.9 1.7 collective-permute-done.8
  46.7 1.0 fusion.32
  47.7 1.4 collective-permute-start.10
  49.1 2.0 collective-permute-start.12
  51.1 2.0 collective-permute-start.11
  53.1 3.6 %collective-permute-start.9 = (f32[128,512]{1,0:T(8,128)}, f32[128,512]{1,0:T(8,128)}, u32[]{:S(2)}, u32[]{:S(2)}) collective-permute-start(f32[128,512]{1,0:T(8,128)} %get-tuple-element.21), channel_id=1, source_target_pairs={{0,0},{1,4},{10,8},{11,12},{20,16},{21,20},{30,24},{31,28}} | collective-permute-start | bytes 786440 | tf_op jit(solution)/shard_map/ppermute | solution.py:122
  56.7 22.7 %convolution_bitcast_fusion = f32[2,2,2,128,512]{4,3,0,1,2:T(8,128)S(1)} fusion(f32[128,2048,1,1,1]{1,0,4,3,2:T(8,128)S(1)} %bitcast.133, f32[2,2,2,512,2048]{4,3,2,1,0:T(8,128)} %bitcast.131), kind=kOutput, calls=%fused_computation.3 | convolution fusion | flops 6442450944 | bytes 36700160 | tf_op jit(solution)/shard_map/mk,abcik->cbami/dot_general | solution.py:112
  80.2 1.3 add_add_fusion
  81.9 21.0 %collective-permute-done.13 = f32[2,2,128,512]{3,2,0,1:T(8,128)} collective-permute-done((f32[2,2,128,512]{3,2,0,1:T(8,128)S(1)}, f32[2,2,128,512]{3,2,0,1:T(8,128)}, u32[]{:S(2)}, u32[]{:S(2)}) %collective-permute-start.13) | collective-permute-done | bytes 1048608 | tf_op jit(solution)/shard_map/ppermute | solution.py:43
  102.8 1.5 bitcast_add_fusion
  104.5 12.3 %collective-permute-done.14 = f32[2,128,512]{2,1,0:T(8,128)S(1)} collective-permute-done((f32[2,128,512]{2,1,0:T(8,128)S(1)}, f32[2,128,512]{2,1,0:T(8,128)S(1)}, u32[]{:S(2)}, u32[]{:S(2)}) %collective-permute-start.14) | collective-permute-done | bytes 524320 | tf_op jit(solution)/shard_map/ppermute | solution.py:43
  116.9 2.6 collective-permute-start.15
  119.4 10.9 %collective-permute-done.15 = f32[128,512]{1,0:T(8,128)S(1)} collective-permute-done((f32[128,512]{1,0:T(8,128)S(1)}, f32[128,512]{1,0:T(8,128)S(1)}, u32[]{:S(2)}, u32[]{:S(2)}) %collective-permute-start.15) | collective-permute-done | bytes 262176 | tf_op jit(solution)/shard_map/ppermute | solution.py:43
  130.3 0.7 bitcast_add_fusion.2
  131.5 1.3 fusion.33
  132.8 1.2 collective-permute-start.16
  134.0 3.1 %collective-permute-done.16 = f32[136,128]{1,0:T(8,128)S(1)} collective-permute-done((f32[136,128]{1,0:T(8,128)S(1)}, f32[136,128]{1,0:T(8,128)S(1)}, u32[]{:S(2)}, u32[]{:S(2)}) %collective-permute-start.16) | collective-permute-done | bytes 69664 | tf_op jit(solution)/shard_map/ppermute | solution.py:31
  137.3 6.9 %collective-permute-done.17 = f32[136,128]{1,0:T(8,128)S(1)} collective-permute-done((f32[136,128]{1,0:T(8,128)S(1)}, f32[136,128]{1,0:T(8,128)S(1)}, u32[]{:S(2)}, u32[]{:S(2)}) %collective-permute-start.17) | collective-permute-done | bytes 69664 | tf_op jit(solution)/shard_map/ppermute | solution.py:31
  144.3 7.9 %collective-permute-done.18 = f32[136,128]{1,0:T(8,128)S(1)} collective-permute-done((f32[136,128]{1,0:T(8,128)S(1)}, f32[136,128]{1,0:T(8,128)S(1)}, u32[]{:S(2)}, u32[]{:S(2)}) %collective-permute-start.18) | collective-permute-done | bytes 69664 | tf_op jit(solution)/shard_map/ppermute | solution.py:31
  152.2 31.0 %all-gather.2.cloned.1.call-done = f32[128,4096]{1,0:T(8,128)} async-done(((f32[128,512]{1,0:T(8,128)}), f32[128,4096]{1,0:T(8,128)}) %all-gather.2.cloned.1.call-update) | async-done | bytes 2097168 | tf_op jit(solution)/shard_map/all_gather | solution.py:136
  183.3 2.4 dynamic-slice_select_fusion
  185.7 3.6 %collective-permute-start.21 = (f32[128,2048]{1,0:T(8,128)}, f32[128,2048]{1,0:T(8,128)S(1)}, u32[]{:S(2)}, u32[]{:S(2)}) collective-permute-start(f32[128,2048]{1,0:T(8,128)} %dynamic-slice_select_fusion), channel_id=1, source_target_pairs={{0,16},{1,17},{10,26},{11,27},{20,4},{21,5},{30,14},{31,15}} | collective-permute-start | bytes 3145736 | tf_op jit(solution)/shard_map/ppermute | solution.py:23
  189.5 12.8 %collective-permute-done.20 = f32[136,128]{1,0:T(8,128)} collective-permute-done((f32[136,128]{1,0:T(8,128)S(1)}, f32[136,128]{1,0:T(8,128)}, u32[]{:S(2)}, u32[]{:S(2)}) %collective-permute-start.20) | collective-permute-done | bytes 69664 | tf_op jit(solution)/shard_map/ppermute | solution.py:31
  202.4 0.9 add.253
  204.0 0.9 copy.19
  205.6 12.5 %cholesky.16 = f32[128,128]{1,0:T(8,128)S(1)} custom-call(f32[128,128]{1,0:T(8,128)} %fusion.21), custom_call_target="Cholesky" | custom-call | tf_op jit(solution)/shard_map/jit(cholesky)/cholesky | solution.py:142
  218.8 1.3 fusion.15
  220.1 10.6 %custom-call.16 = f32[1,128,128]{1,2,0:T(8,128)S(1)} custom-call(f32[1,128,128]{2,1,0:T(8,128)} %fusion.15), custom_call_target="InvertDiagBlocksLowerTriangular" | custom-call | tf_op jit(solution)/shard_map/jit(_cho_solve)/triangular_solve | solution.py:147
  230.9 1.6 collective-permute-start.22
  232.5 0.8 convolution_bitcast_fusion.3
  233.8 1.3 dynamic-slice_add_fusion
  235.2 1.9 fusion.17
  237.2 1.1 fusion.5
  238.3 26.9 %convolution_subtract_fusion = f32[4096,2048]{1,0:T(8,128)} fusion(f32[4096,2048]{1,0:T(8,128)} %param.21, f32[128,4096]{1,0:T(8,128)S(1)} %fusion.17, f32[128,2048]{1,0:T(8,128)S(1)} %fusion.5), kind=kOutput, calls=%fused_computation | convolution fusion | flops 6450839552 | bytes 70254592 | tf_op jit(solution)/shard_map/mi,mj->ij/dot_general | solution.py:146
  (94 shorter events, 8.1 us)
Async XLA Ops:
  7.2 7.4 %copy-start = (f32[4,128]{1,0:T(4,128)S(1)}, f32[4,128]{1,0:T(4,128)}, u32[]{:S(2)}) copy-start(f32[4,128]{1,0:T(4,128)} %param.18) | copy-start | bytes 6148
  7.2 11.0 %copy-start.5 = (f32[128,128]{1,0:T(8,128)S(1)}, f32[128,128]{1,0:T(8,128)}, u32[]{:S(2)}) copy-start(f32[128,128]{1,0:T(8,128)} %param.16) | copy-start | bytes 196612
  7.2 176.1 %all-gather.2.cloned.1.call-start = ((), (), s32[]{:S(2)}) async-start(), calls=%async_computation | async-start | bytes 2359296 | tf_op jit(solution)/shard_map/all_gather | solution.py:136
  19.5 9.9 %collective-permute-start = (f32[4,2048]{1,0:T(4,128)S(1)}, f32[4,2048]{1,0:T(4,128)S(1)}, u32[]{:S(2)}, u32[]{:S(2)}) collective-permute-start(f32[4,2048]{1,0:T(4,128)S(1)} %bitcast.141), channel_id=1, source_target_pairs={{0,7},{1,0},{2,1},{3,2},{4,3},{5,4},{6,5},{7,6},{8,15},{9,8},{10,9... | collective-permute-start | bytes 98312 | tf_op jit(solution)/shard_map/ppermute | solution.py:51
  25.5 5.7 %collective-permute-start.1 = (f32[4,2048]{1,0:T(4,128)S(1)}, f32[4,2048]{1,0:T(4,128)S(1)}, u32[]{:S(2)}, u32[]{:S(2)}) collective-permute-start(f32[4,2048]{1,0:T(4,128)S(1)} %bitcast.140), channel_id=1, source_target_pairs={{0,6},{1,7},{2,0},{3,1},{4,2},{5,3},{6,4},{7,5},{8,14},{9,15},{10,... | collective-permute-start | bytes 98312 | tf_op jit(solution)/shard_map/ppermute | solution.py:51
  26.0 6.4 %collective-permute-start.2 = (f32[4,2048]{1,0:T(4,128)S(1)}, f32[4,2048]{1,0:T(4,128)S(1)}, u32[]{:S(2)}, u32[]{:S(2)}) collective-permute-start(f32[4,2048]{1,0:T(4,128)S(1)} %bitcast.137), channel_id=1, source_target_pairs={{0,5},{1,6},{2,7},{3,0},{4,1},{5,2},{6,3},{7,4},{8,13},{9,14},{10,... | collective-permute-start | bytes 98312 | tf_op jit(solution)/shard_map/ppermute | solution.py:51
  26.1 6.3 %collective-permute-start.3 = (f32[4,2048]{1,0:T(4,128)S(1)}, f32[4,2048]{1,0:T(4,128)S(1)}, u32[]{:S(2)}, u32[]{:S(2)}) collective-permute-start(f32[4,2048]{1,0:T(4,128)S(1)} %bitcast.138), channel_id=1, source_target_pairs={{0,4},{1,5},{2,6},{3,7},{4,0},{5,1},{6,2},{7,3},{8,12},{9,13},{10,... | collective-permute-start | bytes 98312 | tf_op jit(solution)/shard_map/ppermute | solution.py:51
  29.2 6.1 %collective-permute-start.4 = (f32[4,2048]{1,0:T(4,128)S(1)}, f32[4,2048]{1,0:T(4,128)S(1)}, u32[]{:S(2)}, u32[]{:S(2)}) collective-permute-start(f32[4,2048]{1,0:T(4,128)S(1)} %bitcast.139), channel_id=1, source_target_pairs={{0,3},{1,4},{2,5},{3,6},{4,7},{5,0},{6,1},{7,2},{8,11},{9,12},{10,... | collective-permute-start | bytes 98312 | tf_op jit(solution)/shard_map/ppermute | solution.py:51
  29.3 6.9 %collective-permute-start.5 = (f32[4,2048]{1,0:T(4,128)S(1)}, f32[4,2048]{1,0:T(4,128)S(1)}, u32[]{:S(2)}, u32[]{:S(2)}) collective-permute-start(f32[4,2048]{1,0:T(4,128)S(1)} %bitcast.143), channel_id=1, source_target_pairs={{0,2},{1,3},{2,4},{3,5},{4,6},{5,7},{6,0},{7,1},{8,10},{9,11},{10,... | collective-permute-start | bytes 98312 | tf_op jit(solution)/shard_map/ppermute | solution.py:51
  31.2 6.7 %collective-permute-start.6 = (f32[4,2048]{1,0:T(4,128)S(1)}, f32[4,2048]{1,0:T(4,128)S(1)}, u32[]{:S(2)}, u32[]{:S(2)}) collective-permute-start(f32[4,2048]{1,0:T(4,128)S(1)} %bitcast.142), channel_id=1, source_target_pairs={{0,1},{1,2},{2,3},{3,4},{4,5},{5,6},{6,7},{7,0},{8,9},{9,10},{10,1... | collective-permute-start | bytes 98312 | tf_op jit(solution)/shard_map/ppermute | solution.py:51
  38.2 6.4 %collective-permute-start.7 = (f32[1,32,2048]{2,1,0:T(8,128)S(1)}, f32[1,32,2048]{2,1,0:T(8,128)S(1)}, u32[]{:S(2)}, u32[]{:S(2)}) collective-permute-start(f32[1,32,2048]{2,1,0:T(8,128)S(1)} %broadcast_in_dim_reshape.3), channel_id=1, source_target_pairs={{0,16},{8,24},{16,0},{24,8},{1,17},{9,25},{17,1},{25,9},{2,18},{10... | collective-permute-start | bytes 786440 | tf_op jit(solution)/shard_map/ppermute | solution.py:67
  44.7 2.0 collective-permute-start.8
  47.7 31.7 %collective-permute-start.10 = (f32[128,512]{1,0:T(8,128)}, f32[128,512]{1,0:T(8,128)S(1)}, u32[]{:S(2)}, u32[]{:S(2)}) collective-permute-start(f32[128,512]{1,0:T(8,128)} %get-tuple-element.18), channel_id=1, source_target_pairs={{0,1},{1,5},{10,9},{11,13},{20,17},{21,21},{30,25},{31,29}} | collective-permute-start | bytes 786440 | tf_op jit(solution)/shard_map/ppermute | solution.py:122
  49.1 30.3 %collective-permute-start.12 = (f32[128,512]{1,0:T(8,128)}, f32[128,512]{1,0:T(8,128)}, u32[]{:S(2)}, u32[]{:S(2)}) collective-permute-start(f32[128,512]{1,0:T(8,128)} %get-tuple-element.19), channel_id=1, source_target_pairs={{0,3},{1,7},{10,11},{11,15},{20,19},{21,23},{30,27},{31,31}} | collective-permute-start | bytes 786440 | tf_op jit(solution)/shard_map/ppermute | solution.py:122
  51.1 28.4 %collective-permute-start.11 = (f32[128,512]{1,0:T(8,128)}, f32[128,512]{1,0:T(8,128)}, u32[]{:S(2)}, u32[]{:S(2)}) collective-permute-start(f32[128,512]{1,0:T(8,128)} %get-tuple-element.20), channel_id=1, source_target_pairs={{0,2},{1,6},{10,10},{11,14},{20,18},{21,22},{30,26},{31,30}} | collective-permute-start | bytes 786440 | tf_op jit(solution)/shard_map/ppermute | solution.py:122
  53.1 27.1 %collective-permute-start.9 = (f32[128,512]{1,0:T(8,128)}, f32[128,512]{1,0:T(8,128)}, u32[]{:S(2)}, u32[]{:S(2)}) collective-permute-start(f32[128,512]{1,0:T(8,128)} %get-tuple-element.21), channel_id=1, source_target_pairs={{0,0},{1,4},{10,8},{11,12},{20,16},{21,20},{30,24},{31,28}} | collective-permute-start | bytes 786440 | tf_op jit(solution)/shard_map/ppermute | solution.py:122
  79.5 0.7 copy-start.4
  81.5 21.3 %collective-permute-start.13 = (f32[2,2,128,512]{3,2,0,1:T(8,128)S(1)}, f32[2,2,128,512]{3,2,0,1:T(8,128)}, u32[]{:S(2)}, u32[]{:S(2)}) collective-permute-start(f32[2,2,128,512]{3,2,0,1:T(8,128)S(1)} %dynamic-slice_bitcast_fusion), channel_id=1, source_target_pairs={{0,1},{1,0},{2,3},{3,2},{4,5},{5,4},{6,7},{7,6},{8,9},{9,8},{10,11... | collective-permute-start | bytes 3145736 | tf_op jit(solution)/shard_map/ppermute | solution.py:43
  104.3 26.8 %copy-start.7 = (s32[256]{0:T(256)S(1)}, s32[256]{0:T(256)}, u32[]{:S(2)}) copy-start(s32[256]{0:T(256)} %param.15) | copy-start | bytes 3076
  104.3 12.4 %collective-permute-start.14 = (f32[2,128,512]{2,1,0:T(8,128)S(1)}, f32[2,128,512]{2,1,0:T(8,128)S(1)}, u32[]{:S(2)}, u32[]{:S(2)}) collective-permute-start(f32[2,128,512]{2,1,0:T(8,128)S(1)} %dynamic-slice_bitcast_fusion.1), channel_id=1, source_target_pairs={{0,2},{1,3},{2,0},{3,1},{4,6},{5,7},{6,4},{7,5},{8,10},{9,11},{10,... | collective-permute-start | bytes 1572872 | tf_op jit(solution)/shard_map/ppermute | solution.py:43
  116.9 13.5 %collective-permute-start.15 = (f32[128,512]{1,0:T(8,128)S(1)}, f32[128,512]{1,0:T(8,128)S(1)}, u32[]{:S(2)}, u32[]{:S(2)}) collective-permute-start(f32[128,512]{1,0:T(8,128)S(1)} %dynamic-slice_bitcast_fusion.2), channel_id=1, source_target_pairs={{0,4},{1,5},{2,6},{3,7},{4,0},{5,1},{6,2},{7,3},{8,12},{9,13},{10,... | collective-permute-start | bytes 786440 | tf_op jit(solution)/shard_map/ppermute | solution.py:43
  131.1 72.2 %copy-start.6 = (f32[128]{0:T(128)S(1)}, f32[128]{0:T(128)}, u32[]{:S(2)}) copy-start(f32[128]{0:T(128)} %param.20) | copy-start | bytes 1540
  132.8 4.4 %collective-permute-start.16 = (f32[136,128]{1,0:T(8,128)S(1)}, f32[136,128]{1,0:T(8,128)S(1)}, u32[]{:S(2)}, u32[]{:S(2)}) collective-permute-start(f32[136,128]{1,0:T(8,128)S(1)} %pad_maximum_fusion), channel_id=1, source_target_pairs={{0,1},{1,0},{2,3},{3,2},{4,5},{5,4},{6,7},{7,6},{8,9},{9,8},{10,11... | collective-permute-start | bytes 208904 | tf_op jit(solution)/shard_map/ppermute | solution.py:31
  137.2 7.0 %collective-permute-start.17 = (f32[136,128]{1,0:T(8,128)S(1)}, f32[136,128]{1,0:T(8,128)S(1)}, u32[]{:S(2)}, u32[]{:S(2)}) collective-permute-start(f32[136,128]{1,0:T(8,128)S(1)} %fusion.31), channel_id=1, source_target_pairs={{0,2},{1,3},{2,0},{3,1},{4,6},{5,7},{6,4},{7,5},{8,10},{9,11},{10,... | collective-permute-start | bytes 208904 | tf_op jit(solution)/shard_map/ppermute | solution.py:31
  144.2 8.0 %collective-permute-start.18 = (f32[136,128]{1,0:T(8,128)S(1)}, f32[136,128]{1,0:T(8,128)S(1)}, u32[]{:S(2)}, u32[]{:S(2)}) collective-permute-start(f32[136,128]{1,0:T(8,128)S(1)} %add.250), channel_id=1, source_target_pairs={{0,4},{1,5},{2,6},{3,7},{4,0},{5,1},{6,2},{7,3},{8,12},{9,13},{10,... | collective-permute-start | bytes 208904 | tf_op jit(solution)/shard_map/ppermute | solution.py:31
  152.2 37.2 %collective-permute-start.19 = (f32[136,128]{1,0:T(8,128)S(1)}, f32[136,128]{1,0:T(8,128)S(1)}, u32[]{:S(2)}, u32[]{:S(2)}) collective-permute-start(f32[136,128]{1,0:T(8,128)S(1)} %add.251), channel_id=1, source_target_pairs={{0,8},{8,0},{16,24},{24,16},{1,9},{9,1},{17,25},{25,17},{2,10},{10... | collective-permute-start | bytes 208904 | tf_op jit(solution)/shard_map/ppermute | solution.py:31
  183.3 47.5 %copy-start.2 = (f32[128,4096]{1,0:T(8,128)S(1)}, f32[128,4096]{1,0:T(8,128)}, u32[]{:S(2)}) copy-start(f32[128,4096]{1,0:T(8,128)} %all-gather.2.cloned.1.call-done) | copy-start | bytes 6291460
  185.7 45.0 %collective-permute-start.21 = (f32[128,2048]{1,0:T(8,128)}, f32[128,2048]{1,0:T(8,128)S(1)}, u32[]{:S(2)}, u32[]{:S(2)}) collective-permute-start(f32[128,2048]{1,0:T(8,128)} %dynamic-slice_select_fusion), channel_id=1, source_target_pairs={{0,16},{1,17},{10,26},{11,27},{20,4},{21,5},{30,14},{31,15}} | collective-permute-start | bytes 3145736 | tf_op jit(solution)/shard_map/ppermute | solution.py:23
  189.4 44.1 %copy-start.3 = (f32[128,512]{1,0:T(8,128)S(1)}, f32[128,512]{1,0:T(8,128)}, u32[]{:S(2)}) copy-start(f32[128,512]{1,0:T(8,128)} %bitcast_add_fusion.2) | copy-start | bytes 786436
  189.4 12.9 %collective-permute-start.20 = (f32[136,128]{1,0:T(8,128)S(1)}, f32[136,128]{1,0:T(8,128)}, u32[]{:S(2)}, u32[]{:S(2)}) collective-permute-start(f32[136,128]{1,0:T(8,128)S(1)} %add.252), channel_id=1, source_target_pairs={{0,16},{8,24},{16,0},{24,8},{1,17},{9,25},{17,1},{25,9},{2,18},{10... | collective-permute-start | bytes 208904 | tf_op jit(solution)/shard_map/ppermute | solution.py:31
  230.9 6.2 %collective-permute-start.22 = (f32[128,2048]{1,0:T(8,128)S(1)}, f32[128,2048]{1,0:T(8,128)S(1)}, u32[]{:S(2)}, u32[]{:S(2)}) collective-permute-start(f32[128,2048]{1,0:T(8,128)S(1)} %fusion.52), channel_id=1, source_target_pairs={{0,8},{16,24},{1,9},{17,25},{10,2},{26,18},{11,3},{27,19},{20,28},... | collective-permute-start | bytes 3145736 | tf_op jit(solution)/shard_map/ppermute | solution.py:23
  238.2 26.9 %copy-start.1 = (f32[4,128]{1,0:T(4,128)S(1)}, f32[4,128]{1,0:T(4,128)}, u32[]{:S(2)}) copy-start(f32[4,128]{1,0:T(4,128)} %param.18) | copy-start | bytes 6148
Sparse Core Ops, SparseCore 0:
  131.2 52.0 all-gather.1

commit v10 on v9

--- a/solution.py
+++ b/solution.py
@@ -137,6 +137,7 @@
     half_t = lax.dynamic_slice_in_dim(gain_rows_t, col_id % factor * col_w, col_w, 1)
     mine = row_id == col_id // factor
     masked = jnp.where(mine, half_t, jnp.zeros_like(half_t))
+    small, masked = lax.optimization_barrier((small, masked))
     gram = small[:m_all] + jnp.diag(noise)
     pred_all = small[m_all]
     lower = jnp.linalg.cholesky(gram)

time: 273 us -> 259 us (0.949)
  waiting for transfers between devices: 118 us -> 103 us
  starting transfers between devices: 33.1 us -> 36.5 us
    ppermute x5, waiting for transfers between devices: 30.8 us -> 21.5 us  [butterfly_sum(): buf = buf + lax.ppermute(buf, axis, [(i, i ^ bit) for i in range(size)])]
    all_gather x1, waiting for transfers between devices: 31 us -> 24.9 us  [on_device(): gain_rows_t = lax.all_gather(gain_own_t, 'col', axis=1, tiled=True)]
  transfers between devices with their start and end apart: 24 -> 24, of which waited for: 13 -> 14; matrix products, arithmetic and copies ran while one was open for 22% -> 22% of each run, Pallas kernels for 0% -> 0%
where the time goes in v10:
time: 259 us; the launch traced here: 258 us
  waiting for transfers between devices  103 us (40%)
  matrix products  59.1 us (23%)
  other arithmetic  40.8 us (16%)
  starting transfers between devices  36.5 us (14%)
  between operations  14.8 us (6%)
  local copies, waits for them, and re-layouts  4.69 us (2%)
    ppermute x3, waiting for transfers between devices, halving_scatter(): x = keep + lax.ppermute(send, axis, [(i, i ^ bit) for i in range(size)])  44.1 us
    dot_general x1, matrix products, on_device(): new_cov = cov - jnp.einsum('mi,mj->ij', white_row, white_col, precision=mid)  26.9 us
    all_gather x1, waiting for transfers between devices, on_device(): gain_rows_t = lax.all_gather(gain_own_t, 'col', axis=1, tiled=True)  24.9 us
    dot_general x1, matrix products, on_device(): jnp.einsum('mk,' + letters + 'ik->' + letters[::-1] + 'mi', grad_col, cov...  22.7 us
    ppermute x5, waiting for transfers between devices, butterfly_sum(): buf = buf + lax.ppermute(buf, axis, [(i, i ^ bit) for i in range(size)])  21.5 us
    another operation x3, other arithmetic, on_device(): lower = jnp.linalg.cholesky(gram)  13.2 us
    ppermute x7, starting transfers between devices, shift_all_to_all(): lax.ppermute(piece, axis, [(i, (i - k) % size) for i in range(size)])  12.8 us
    another operation x2, other arithmetic, on_device(): coef = jax.scipy.linalg.cho_solve((lower, True), targets - pred_all)  11.9 us
  transfers between devices with their start and end apart: 24, of which 14 were waited for; matrix products, arithmetic and copies ran while one was open for 22% of the time, Pallas kernels for 0%

profile of v10, /device:TPU:0, one launch (start us, length us, event | category | flops | bytes accessed | tf_op | source)
XLA Modules:
  0.0 258.4 jit_solution(4925659930275897785)
XLA Ops:
  8.0 0.9 copy.16
  8.9 5.7 %convert_reduce_fusion = f32[256,256]{1,0:T(8,128)S(1)} fusion(s32[256,32]{1,0:T(8,128)S(1)} %copy.16), kind=kLoop, calls=%fused_computation.1 | loop fusion | flops 6225920 | bytes 294912 | tf_op jit(solution)/shard_map/reduce_sum | solution.py:87
  14.6 1.0 fusion.14
  15.6 1.2 convolution_multiply_fusion.2
  16.8 1.3 fusion.2
  19.5 6.0 %collective-permute-start = (f32[4,2048]{1,0:T(4,128)S(1)}, f32[4,2048]{1,0:T(4,128)S(1)}, u32[]{:S(2)}, u32[]{:S(2)}) collective-permute-start(f32[4,2048]{1,0:T(4,128)S(1)} %bitcast.139), channel_id=1, source_target_pairs={{0,7},{1,0},{2,1},{3,2},{4,3},{5,4},{6,5},{7,6},{8,15},{9,8},{10,9... | collective-permute-start | bytes 98312 | tf_op jit(solution)/shard_map/ppermute | solution.py:51
  26.1 3.0 %collective-permute-start.3 = (f32[4,2048]{1,0:T(4,128)S(1)}, f32[4,2048]{1,0:T(4,128)S(1)}, u32[]{:S(2)}, u32[]{:S(2)}) collective-permute-start(f32[4,2048]{1,0:T(4,128)S(1)} %bitcast.136), channel_id=1, source_target_pairs={{0,4},{1,5},{2,6},{3,7},{4,0},{5,1},{6,2},{7,3},{8,12},{9,13},{10,... | collective-permute-start | bytes 98312 | tf_op jit(solution)/shard_map/ppermute | solution.py:51
  29.3 1.9 collective-permute-start.5
  31.2 1.2 collective-permute-start.6
  32.5 2.8 %collective-permute-done.4 = f32[4,2048]{1,0:T(4,128)S(1)} collective-permute-done((f32[4,2048]{1,0:T(4,128)S(1)}, f32[4,2048]{1,0:T(4,128)S(1)}, u32[]{:S(2)}, u32[]{:S(2)}) %collective-permute-start.4) | collective-permute-done | bytes 32800 | tf_op jit(solution)/shard_map/ppermute | solution.py:51
  35.3 0.9 collective-permute-done.5
  36.3 1.7 collective-permute-done.6
  38.2 1.6 collective-permute-start.7
  39.7 4.9 %collective-permute-done.7 = f32[1,32,2048]{2,1,0:T(8,128)S(1)} collective-permute-done((f32[1,32,2048]{2,1,0:T(8,128)S(1)}, f32[1,32,2048]{2,1,0:T(8,128)S(1)}, u32[]{:S(2)}, u32[]{:S(2)}) %collective-permute-start.7) | collective-permute-done | bytes 262176 | tf_op jit(solution)/shard_map/ppermute | solution.py:67
  44.9 1.7 collective-permute-done.8
  46.7 1.0 fusion.31
  47.7 1.4 collective-permute-start.10
  49.1 2.0 collective-permute-start.12
  51.1 2.0 collective-permute-start.11
  53.1 3.6 %collective-permute-start.9 = (f32[128,512]{1,0:T(8,128)}, f32[128,512]{1,0:T(8,128)}, u32[]{:S(2)}, u32[]{:S(2)}) collective-permute-start(f32[128,512]{1,0:T(8,128)} %get-tuple-element.25), channel_id=1, source_target_pairs={{0,0},{1,4},{10,8},{11,12},{20,16},{21,20},{30,24},{31,28}} | collective-permute-start | bytes 786440 | tf_op jit(solution)/shard_map/ppermute | solution.py:122
  56.7 22.7 %convolution_bitcast_fusion = f32[2,2,2,128,512]{4,3,0,1,2:T(8,128)S(1)} fusion(f32[128,2048,1,1,1]{1,0,4,3,2:T(8,128)S(1)} %bitcast.131, f32[2,2,2,512,2048]{4,3,2,1,0:T(8,128)} %bitcast.129), kind=kOutput, calls=%fused_computation.3 | convolution fusion | flops 6442450944 | bytes 36700160 | tf_op jit(solution)/shard_map/mk,abcik->cbami/dot_general | solution.py:112
  80.2 1.3 add_add_fusion
  81.9 20.9 %collective-permute-done.13 = f32[2,2,128,512]{3,2,0,1:T(8,128)} collective-permute-done((f32[2,2,128,512]{3,2,0,1:T(8,128)S(1)}, f32[2,2,128,512]{3,2,0,1:T(8,128)}, u32[]{:S(2)}, u32[]{:S(2)}) %collective-permute-start.13) | collective-permute-done | bytes 1048608 | tf_op jit(solution)/shard_map/ppermute | solution.py:43
  102.8 1.5 bitcast_add_fusion
  104.5 12.3 %collective-permute-done.14 = f32[2,128,512]{2,1,0:T(8,128)S(1)} collective-permute-done((f32[2,128,512]{2,1,0:T(8,128)S(1)}, f32[2,128,512]{2,1,0:T(8,128)S(1)}, u32[]{:S(2)}, u32[]{:S(2)}) %collective-permute-start.14) | collective-permute-done | bytes 524320 | tf_op jit(solution)/shard_map/ppermute | solution.py:43
  116.9 2.6 collective-permute-start.15
  119.4 10.9 %collective-permute-done.15 = f32[128,512]{1,0:T(8,128)S(1)} collective-permute-done((f32[128,512]{1,0:T(8,128)S(1)}, f32[128,512]{1,0:T(8,128)S(1)}, u32[]{:S(2)}, u32[]{:S(2)}) %collective-permute-start.15) | collective-permute-done | bytes 262176 | tf_op jit(solution)/shard_map/ppermute | solution.py:43
  131.5 1.3 fusion.32
  132.8 1.3 collective-permute-start.16
  134.1 3.1 %collective-permute-done.16 = f32[136,128]{1,0:T(8,128)S(1)} collective-permute-done((f32[136,128]{1,0:T(8,128)S(1)}, f32[136,128]{1,0:T(8,128)S(1)}, u32[]{:S(2)}, u32[]{:S(2)}) %collective-permute-start.16) | collective-permute-done | bytes 69664 | tf_op jit(solution)/shard_map/ppermute | solution.py:31
  137.3 6.9 %collective-permute-done.17 = f32[136,128]{1,0:T(8,128)S(1)} collective-permute-done((f32[136,128]{1,0:T(8,128)S(1)}, f32[136,128]{1,0:T(8,128)S(1)}, u32[]{:S(2)}, u32[]{:S(2)}) %collective-permute-start.17) | collective-permute-done | bytes 69664 | tf_op jit(solution)/shard_map/ppermute | solution.py:31
  144.3 7.8 %collective-permute-done.18 = f32[136,128]{1,0:T(8,128)S(1)} collective-permute-done((f32[136,128]{1,0:T(8,128)S(1)}, f32[136,128]{1,0:T(8,128)S(1)}, u32[]{:S(2)}, u32[]{:S(2)}) %collective-permute-start.18) | collective-permute-done | bytes 69664 | tf_op jit(solution)/shard_map/ppermute | solution.py:31
  152.2 1.2 collective-permute-done.19
  153.4 2.4 collective-permute-start.20
  155.9 2.5 collective-permute-done.20
  158.4 24.9 %all-gather.2.cloned.1.call-done = f32[128,4096]{1,0:T(8,128)} async-done(((f32[128,512]{1,0:T(8,128)}), f32[128,4096]{1,0:T(8,128)}) %all-gather.2.cloned.1.call-update) | async-done | bytes 2097168 | tf_op jit(solution)/shard_map/all_gather | solution.py:136
  183.3 1.3 dynamic-slice_select_fusion
  184.6 4.5 %collective-permute-start.21 = (f32[128,2048]{1,0:T(8,128)S(1)}, f32[128,2048]{1,0:T(8,128)}, u32[]{:S(2)}, u32[]{:S(2)}) collective-permute-start(f32[128,2048]{1,0:T(8,128)S(1)} %dynamic-slice_select_fusion), channel_id=1, source_target_pairs={{0,16},{1,17},{10,26},{11,27},{20,4},{21,5},{30,14},{31,15}} | collective-permute-start | bytes 3145736 | tf_op jit(solution)/shard_map/ppermute | solution.py:23
  189.8 0.9 copy.19
  191.5 12.5 %cholesky.16 = f32[128,128]{1,0:T(8,128)S(1)} custom-call(f32[128,128]{1,0:T(8,128)} %fusion.21), custom_call_target="Cholesky" | custom-call | tf_op jit(solution)/shard_map/jit(cholesky)/cholesky | solution.py:143
  204.7 1.3 fusion.15
  206.0 10.6 %custom-call.16 = f32[1,128,128]{1,2,0:T(8,128)S(1)} custom-call(f32[1,128,128]{2,1,0:T(8,128)} %fusion.15), custom_call_target="InvertDiagBlocksLowerTriangular" | custom-call | tf_op jit(solution)/shard_map/jit(_cho_solve)/triangular_solve | solution.py:148
  216.6 1.4 add.258
  218.0 1.6 collective-permute-start.22
  220.3 1.3 dynamic-slice_add_fusion
  221.6 1.9 fusion.17
  223.6 1.1 fusion.5
  224.7 26.9 %convolution_subtract_fusion = f32[4096,2048]{1,0:T(8,128)} fusion(f32[4096,2048]{1,0:T(8,128)} %param.21, f32[128,4096]{1,0:T(8,128)S(1)} %fusion.17, f32[128,2048]{1,0:T(8,128)S(1)} %fusion.5), kind=kOutput, calls=%fused_computation | convolution fusion | flops 6450839552 | bytes 70254592 | tf_op jit(solution)/shard_map/mi,mj->ij/dot_general | solution.py:147
  (96 shorter events, 8.8 us)
Async XLA Ops:
  7.2 7.4 %copy-start = (f32[4,128]{1,0:T(4,128)S(1)}, f32[4,128]{1,0:T(4,128)}, u32[]{:S(2)}) copy-start(f32[4,128]{1,0:T(4,128)} %param.18) | copy-start | bytes 6148
  7.2 11.0 %copy-start.5 = (f32[128,128]{1,0:T(8,128)S(1)}, f32[128,128]{1,0:T(8,128)}, u32[]{:S(2)}) copy-start(f32[128,128]{1,0:T(8,128)} %param.16) | copy-start | bytes 196612
  7.2 176.1 %all-gather.2.cloned.1.call-start = ((), (), s32[]{:S(2)}) async-start(), calls=%async_computation | async-start | bytes 2359296 | tf_op jit(solution)/shard_map/all_gather | solution.py:136
  19.5 9.9 %collective-permute-start = (f32[4,2048]{1,0:T(4,128)S(1)}, f32[4,2048]{1,0:T(4,128)S(1)}, u32[]{:S(2)}, u32[]{:S(2)}) collective-permute-start(f32[4,2048]{1,0:T(4,128)S(1)} %bitcast.139), channel_id=1, source_target_pairs={{0,7},{1,0},{2,1},{3,2},{4,3},{5,4},{6,5},{7,6},{8,15},{9,8},{10,9... | collective-permute-start | bytes 98312 | tf_op jit(solution)/shard_map/ppermute | solution.py:51
  25.5 5.7 %collective-permute-start.1 = (f32[4,2048]{1,0:T(4,128)S(1)}, f32[4,2048]{1,0:T(4,128)S(1)}, u32[]{:S(2)}, u32[]{:S(2)}) collective-permute-start(f32[4,2048]{1,0:T(4,128)S(1)} %bitcast.138), channel_id=1, source_target_pairs={{0,6},{1,7},{2,0},{3,1},{4,2},{5,3},{6,4},{7,5},{8,14},{9,15},{10,... | collective-permute-start | bytes 98312 | tf_op jit(solution)/shard_map/ppermute | solution.py:51
  26.0 6.4 %collective-permute-start.2 = (f32[4,2048]{1,0:T(4,128)S(1)}, f32[4,2048]{1,0:T(4,128)S(1)}, u32[]{:S(2)}, u32[]{:S(2)}) collective-permute-start(f32[4,2048]{1,0:T(4,128)S(1)} %bitcast.135), channel_id=1, source_target_pairs={{0,5},{1,6},{2,7},{3,0},{4,1},{5,2},{6,3},{7,4},{8,13},{9,14},{10,... | collective-permute-start | bytes 98312 | tf_op jit(solution)/shard_map/ppermute | solution.py:51
  26.1 6.3 %collective-permute-start.3 = (f32[4,2048]{1,0:T(4,128)S(1)}, f32[4,2048]{1,0:T(4,128)S(1)}, u32[]{:S(2)}, u32[]{:S(2)}) collective-permute-start(f32[4,2048]{1,0:T(4,128)S(1)} %bitcast.136), channel_id=1, source_target_pairs={{0,4},{1,5},{2,6},{3,7},{4,0},{5,1},{6,2},{7,3},{8,12},{9,13},{10,... | collective-permute-start | bytes 98312 | tf_op jit(solution)/shard_map/ppermute | solution.py:51
  29.2 6.1 %collective-permute-start.4 = (f32[4,2048]{1,0:T(4,128)S(1)}, f32[4,2048]{1,0:T(4,128)S(1)}, u32[]{:S(2)}, u32[]{:S(2)}) collective-permute-start(f32[4,2048]{1,0:T(4,128)S(1)} %bitcast.137), channel_id=1, source_target_pairs={{0,3},{1,4},{2,5},{3,6},{4,7},{5,0},{6,1},{7,2},{8,11},{9,12},{10,... | collective-permute-start | bytes 98312 | tf_op jit(solution)/shard_map/ppermute | solution.py:51
  29.3 6.9 %collective-permute-start.5 = (f32[4,2048]{1,0:T(4,128)S(1)}, f32[4,2048]{1,0:T(4,128)S(1)}, u32[]{:S(2)}, u32[]{:S(2)}) collective-permute-start(f32[4,2048]{1,0:T(4,128)S(1)} %bitcast.141), channel_id=1, source_target_pairs={{0,2},{1,3},{2,4},{3,5},{4,6},{5,7},{6,0},{7,1},{8,10},{9,11},{10,... | collective-permute-start | bytes 98312 | tf_op jit(solution)/shard_map/ppermute | solution.py:51
  31.2 6.7 %collective-permute-start.6 = (f32[4,2048]{1,0:T(4,128)S(1)}, f32[4,2048]{1,0:T(4,128)S(1)}, u32[]{:S(2)}, u32[]{:S(2)}) collective-permute-start(f32[4,2048]{1,0:T(4,128)S(1)} %bitcast.140), channel_id=1, source_target_pairs={{0,1},{1,2},{2,3},{3,4},{4,5},{5,6},{6,7},{7,0},{8,9},{9,10},{10,1... | collective-permute-start | bytes 98312 | tf_op jit(solution)/shard_map/ppermute | solution.py:51
  38.2 6.4 %collective-permute-start.7 = (f32[1,32,2048]{2,1,0:T(8,128)S(1)}, f32[1,32,2048]{2,1,0:T(8,128)S(1)}, u32[]{:S(2)}, u32[]{:S(2)}) collective-permute-start(f32[1,32,2048]{2,1,0:T(8,128)S(1)} %broadcast_in_dim_reshape.3), channel_id=1, source_target_pairs={{0,16},{8,24},{16,0},{24,8},{1,17},{9,25},{17,1},{25,9},{2,18},{10... | collective-permute-start | bytes 786440 | tf_op jit(solution)/shard_map/ppermute | solution.py:67
  44.7 2.0 collective-permute-start.8
  47.7 31.8 %collective-permute-start.10 = (f32[128,512]{1,0:T(8,128)}, f32[128,512]{1,0:T(8,128)S(1)}, u32[]{:S(2)}, u32[]{:S(2)}) collective-permute-start(f32[128,512]{1,0:T(8,128)} %get-tuple-element.22), channel_id=1, source_target_pairs={{0,1},{1,5},{10,9},{11,13},{20,17},{21,21},{30,25},{31,29}} | collective-permute-start | bytes 786440 | tf_op jit(solution)/shard_map/ppermute | solution.py:122
  49.1 30.4 %collective-permute-start.12 = (f32[128,512]{1,0:T(8,128)}, f32[128,512]{1,0:T(8,128)}, u32[]{:S(2)}, u32[]{:S(2)}) collective-permute-start(f32[128,512]{1,0:T(8,128)} %get-tuple-element.23), channel_id=1, source_target_pairs={{0,3},{1,7},{10,11},{11,15},{20,19},{21,23},{30,27},{31,31}} | collective-permute-start | bytes 786440 | tf_op jit(solution)/shard_map/ppermute | solution.py:122
  51.1 28.4 %collective-permute-start.11 = (f32[128,512]{1,0:T(8,128)}, f32[128,512]{1,0:T(8,128)}, u32[]{:S(2)}, u32[]{:S(2)}) collective-permute-start(f32[128,512]{1,0:T(8,128)} %get-tuple-element.24), channel_id=1, source_target_pairs={{0,2},{1,6},{10,10},{11,14},{20,18},{21,22},{30,26},{31,30}} | collective-permute-start | bytes 786440 | tf_op jit(solution)/shard_map/ppermute | solution.py:122
  53.1 27.1 %collective-permute-start.9 = (f32[128,512]{1,0:T(8,128)}, f32[128,512]{1,0:T(8,128)}, u32[]{:S(2)}, u32[]{:S(2)}) collective-permute-start(f32[128,512]{1,0:T(8,128)} %get-tuple-element.25), channel_id=1, source_target_pairs={{0,0},{1,4},{10,8},{11,12},{20,16},{21,20},{30,24},{31,28}} | collective-permute-start | bytes 786440 | tf_op jit(solution)/shard_map/ppermute | solution.py:122
  79.5 0.7 copy-start.4
  81.6 21.3 %collective-permute-start.13 = (f32[2,2,128,512]{3,2,0,1:T(8,128)S(1)}, f32[2,2,128,512]{3,2,0,1:T(8,128)}, u32[]{:S(2)}, u32[]{:S(2)}) collective-permute-start(f32[2,2,128,512]{3,2,0,1:T(8,128)S(1)} %dynamic-slice_bitcast_fusion), channel_id=1, source_target_pairs={{0,1},{1,0},{2,3},{3,2},{4,5},{5,4},{6,7},{7,6},{8,9},{9,8},{10,11... | collective-permute-start | bytes 3145736 | tf_op jit(solution)/shard_map/ppermute | solution.py:43
  104.3 26.8 %copy-start.7 = (s32[256]{0:T(256)S(1)}, s32[256]{0:T(256)}, u32[]{:S(2)}) copy-start(s32[256]{0:T(256)} %param.15) | copy-start | bytes 3076
  104.4 12.4 %collective-permute-start.14 = (f32[2,128,512]{2,1,0:T(8,128)S(1)}, f32[2,128,512]{2,1,0:T(8,128)S(1)}, u32[]{:S(2)}, u32[]{:S(2)}) collective-permute-start(f32[2,128,512]{2,1,0:T(8,128)S(1)} %dynamic-slice_bitcast_fusion.1), channel_id=1, source_target_pairs={{0,2},{1,3},{2,0},{3,1},{4,6},{5,7},{6,4},{7,5},{8,10},{9,11},{10,... | collective-permute-start | bytes 1572872 | tf_op jit(solution)/shard_map/ppermute | solution.py:43
  116.9 13.5 %collective-permute-start.15 = (f32[128,512]{1,0:T(8,128)S(1)}, f32[128,512]{1,0:T(8,128)S(1)}, u32[]{:S(2)}, u32[]{:S(2)}) collective-permute-start(f32[128,512]{1,0:T(8,128)S(1)} %dynamic-slice_bitcast_fusion.2), channel_id=1, source_target_pairs={{0,4},{1,5},{2,6},{3,7},{4,0},{5,1},{6,2},{7,3},{8,12},{9,13},{10,... | collective-permute-start | bytes 786440 | tf_op jit(solution)/shard_map/ppermute | solution.py:43
  131.1 58.0 %copy-start.6 = (f32[128]{0:T(128)S(1)}, f32[128]{0:T(128)}, u32[]{:S(2)}) copy-start(f32[128]{0:T(128)} %param.20) | copy-start | bytes 1540
  132.8 4.4 %collective-permute-start.16 = (f32[136,128]{1,0:T(8,128)S(1)}, f32[136,128]{1,0:T(8,128)S(1)}, u32[]{:S(2)}, u32[]{:S(2)}) collective-permute-start(f32[136,128]{1,0:T(8,128)S(1)} %pad_maximum_fusion), channel_id=1, source_target_pairs={{0,1},{1,0},{2,3},{3,2},{4,5},{5,4},{6,7},{7,6},{8,9},{9,8},{10,11... | collective-permute-start | bytes 208904 | tf_op jit(solution)/shard_map/ppermute | solution.py:31
  137.2 7.0 %collective-permute-start.17 = (f32[136,128]{1,0:T(8,128)S(1)}, f32[136,128]{1,0:T(8,128)S(1)}, u32[]{:S(2)}, u32[]{:S(2)}) collective-permute-start(f32[136,128]{1,0:T(8,128)S(1)} %fusion.30), channel_id=1, source_target_pairs={{0,2},{1,3},{2,0},{3,1},{4,6},{5,7},{6,4},{7,5},{8,10},{9,11},{10,... | collective-permute-start | bytes 208904 | tf_op jit(solution)/shard_map/ppermute | solution.py:31
  144.2 7.9 %collective-permute-start.18 = (f32[136,128]{1,0:T(8,128)S(1)}, f32[136,128]{1,0:T(8,128)S(1)}, u32[]{:S(2)}, u32[]{:S(2)}) collective-permute-start(f32[136,128]{1,0:T(8,128)S(1)} %add.250), channel_id=1, source_target_pairs={{0,4},{1,5},{2,6},{3,7},{4,0},{5,1},{6,2},{7,3},{8,12},{9,13},{10,... | collective-permute-start | bytes 208904 | tf_op jit(solution)/shard_map/ppermute | solution.py:31
  152.1 1.3 collective-permute-start.19
  153.4 4.9 %collective-permute-start.20 = (f32[136,128]{1,0:T(8,128)S(1)}, f32[136,128]{1,0:T(8,128)S(1)}, u32[]{:S(2)}, u32[]{:S(2)}) collective-permute-start(f32[136,128]{1,0:T(8,128)S(1)} %add.252), channel_id=1, source_target_pairs={{0,16},{8,24},{16,0},{24,8},{1,17},{9,25},{17,1},{25,9},{2,18},{10... | collective-permute-start | bytes 208904 | tf_op jit(solution)/shard_map/ppermute | solution.py:31
  184.6 35.1 %copy-start.8 = (f32[128]{0:T(128)S(1)}, f32[128]{0:T(128)}, u32[]{:S(2)}) copy-start(f32[128]{0:T(128)} %param.19) | copy-start | bytes 1540
  184.6 35.4 %copy-start.3 = (f32[128,512]{1,0:T(8,128)S(1)}, f32[128,512]{1,0:T(8,128)}, u32[]{:S(2)}) copy-start(f32[128,512]{1,0:T(8,128)} %bitcast_add_fusion.2) | copy-start | bytes 786436
  184.6 32.0 %collective-permute-start.21 = (f32[128,2048]{1,0:T(8,128)S(1)}, f32[128,2048]{1,0:T(8,128)}, u32[]{:S(2)}, u32[]{:S(2)}) collective-permute-start(f32[128,2048]{1,0:T(8,128)S(1)} %dynamic-slice_select_fusion), channel_id=1, source_target_pairs={{0,16},{1,17},{10,26},{11,27},{20,4},{21,5},{30,14},{31,15}} | collective-permute-start | bytes 3145736 | tf_op jit(solution)/shard_map/ppermute | solution.py:23
  189.1 32.5 %copy-start.2 = (f32[128,4096]{1,0:T(8,128)S(1)}, f32[128,4096]{1,0:T(8,128)}, u32[]{:S(2)}) copy-start(f32[128,4096]{1,0:T(8,128)} %all-gather.2.cloned.1.call-done) | copy-start | bytes 6291460
  218.0 5.6 %collective-permute-start.22 = (f32[128,2048]{1,0:T(8,128)S(1)}, f32[128,2048]{1,0:T(8,128)S(1)}, u32[]{:S(2)}, u32[]{:S(2)}) collective-permute-start(f32[128,2048]{1,0:T(8,128)S(1)} %add.258), channel_id=1, source_target_pairs={{0,8},{16,24},{1,9},{17,25},{10,2},{26,18},{11,3},{27,19},{20,28},... | collective-permute-start | bytes 3145736 | tf_op jit(solution)/shard_map/ppermute | solution.py:23
  224.7 26.9 %copy-start.1 = (f32[4,128]{1,0:T(4,128)S(1)}, f32[4,128]{1,0:T(4,128)}, u32[]{:S(2)}) copy-start(f32[4,128]{1,0:T(4,128)} %param.18) | copy-start | bytes 6148
Sparse Core Ops, SparseCore 0:
  131.2 52.0 all-gather.1

commit v11 on v9

--- a/solution.py
+++ b/solution.py
@@ -134,12 +134,13 @@
     small = jnp.concatenate([gram_own, slots], axis=0)
     small = butterfly_sum(butterfly_sum(small, "col", n_col), "row", n_row)
     gain_rows_t = lax.all_gather(gain_own_t, "col", axis=1, tiled=True)
+    gram = small[:m_all] + jnp.diag(noise)
+    pred_all = small[m_all]
+    lower = jnp.linalg.cholesky(gram)
+    lower, gain_rows_t = lax.optimization_barrier((lower, gain_rows_t))
     half_t = lax.dynamic_slice_in_dim(gain_rows_t, col_id % factor * col_w, col_w, 1)
     mine = row_id == col_id // factor
     masked = jnp.where(mine, half_t, jnp.zeros_like(half_t))
-    gram = small[:m_all] + jnp.diag(noise)
-    pred_all = small[m_all]
-    lower = jnp.linalg.cholesky(gram)
     gain_col_t = broadcast_rows(masked, n_row, n_col, factor)
     white_row = jax.scipy.linalg.solve_triangular(lower, gain_rows_t, lower=True)
     white_col = jax.scipy.linalg.solve_triangular(lower, gain_col_t, lower=True)

time: 273 us -> 244 us (0.89)
  waiting for transfers between devices: 118 us -> 91.6 us
  other arithmetic: 41.5 us -> 38.6 us
    all_gather x1, waiting for transfers between devices: 31 us -> 11.3 us  [on_device(): gain_rows_t = lax.all_gather(gain_own_t, 'col', axis=1, tiled=True)]
    ppermute x5, waiting for transfers between devices: 30.8 us -> 23 us  [butterfly_sum(): buf = buf + lax.ppermute(buf, axis, [(i, i ^ bit) for i in range(size)])]
  transfers between devices with their start and end apart: 24 -> 24, of which waited for: 13 -> 15; matrix products, arithmetic and copies ran while one was open for 22% -> 22% of each run, Pallas kernels for 0% -> 0%
where the time goes in v11:
time: 244 us; the launch traced here: 243 us
  waiting for transfers between devices  91.6 us (38%)
  matrix products  59.4 us (24%)
  other arithmetic  38.6 us (16%)
  starting transfers between devices  34.3 us (14%)
  between operations  14.8 us (6%)
  local copies, waits for them, and re-layouts  4.07 us (2%)
    ppermute x3, waiting for transfers between devices, halving_scatter(): x = keep + lax.ppermute(send, axis, [(i, i ^ bit) for i in range(size)])  44.1 us
    dot_general x1, matrix products, on_device(): new_cov = cov - jnp.einsum('mi,mj->ij', white_row, white_col, precision=mid)  27.1 us
    ppermute x5, waiting for transfers between devices, butterfly_sum(): buf = buf + lax.ppermute(buf, axis, [(i, i ^ bit) for i in range(size)])  23 us
    dot_general x1, matrix products, on_device(): jnp.einsum('mk,' + letters + 'ik->' + letters[::-1] + 'mi', grad_col, cov...  22.7 us
    ppermute x7, starting transfers between devices, shift_all_to_all(): lax.ppermute(piece, axis, [(i, (i - k) % size) for i in range(size)])  12.8 us
    another operation x3, other arithmetic, on_device(): lower = jnp.linalg.cholesky(gram)  12.4 us
    another operation x2, other arithmetic, on_device(): coef = jax.scipy.linalg.cho_solve((lower, True), targets - pred_all)  11.3 us
    all_gather x1, waiting for transfers between devices, on_device(): gain_rows_t = lax.all_gather(gain_own_t, 'col', axis=1, tiled=True)  11.3 us
  transfers between devices with their start and end apart: 24, of which 15 were waited for; matrix products, arithmetic and copies ran while one was open for 22% of the time, Pallas kernels for 0%

profile of v11, /device:TPU:0, one launch (start us, length us, event | category | flops | bytes accessed | tf_op | source)
XLA Modules:
  0.0 242.8 jit_solution(7599102810986948771)
XLA Ops:
  7.3 0.7 fusion.24
  8.0 0.9 copy.16
  8.9 5.7 %convert_reduce_fusion = f32[256,256]{1,0:T(8,128)S(1)} fusion(s32[256,32]{1,0:T(8,128)S(1)} %copy.16), kind=kLoop, calls=%fused_computation.1 | loop fusion | flops 6225920 | bytes 294912 | tf_op jit(solution)/shard_map/reduce_sum | solution.py:87
  14.6 1.0 fusion.14
  15.6 1.2 convolution_multiply_fusion.2
  16.8 1.3 fusion.2
  19.5 6.0 %collective-permute-start = (f32[4,2048]{1,0:T(4,128)S(1)}, f32[4,2048]{1,0:T(4,128)S(1)}, u32[]{:S(2)}, u32[]{:S(2)}) collective-permute-start(f32[4,2048]{1,0:T(4,128)S(1)} %bitcast.141), channel_id=1, source_target_pairs={{0,7},{1,0},{2,1},{3,2},{4,3},{5,4},{6,5},{7,6},{8,15},{9,8},{10,9... | collective-permute-start | bytes 98312 | tf_op jit(solution)/shard_map/ppermute | solution.py:51
  26.1 3.0 %collective-permute-start.3 = (f32[4,2048]{1,0:T(4,128)S(1)}, f32[4,2048]{1,0:T(4,128)S(1)}, u32[]{:S(2)}, u32[]{:S(2)}) collective-permute-start(f32[4,2048]{1,0:T(4,128)S(1)} %bitcast.138), channel_id=1, source_target_pairs={{0,4},{1,5},{2,6},{3,7},{4,0},{5,1},{6,2},{7,3},{8,12},{9,13},{10,... | collective-permute-start | bytes 98312 | tf_op jit(solution)/shard_map/ppermute | solution.py:51
  29.3 1.9 collective-permute-start.5
  31.2 1.2 collective-permute-start.6
  32.5 2.8 %collective-permute-done.4 = f32[4,2048]{1,0:T(4,128)S(1)} collective-permute-done((f32[4,2048]{1,0:T(4,128)S(1)}, f32[4,2048]{1,0:T(4,128)S(1)}, u32[]{:S(2)}, u32[]{:S(2)}) %collective-permute-start.4) | collective-permute-done | bytes 32800 | tf_op jit(solution)/shard_map/ppermute | solution.py:51
  35.3 0.9 collective-permute-done.5
  36.3 1.7 collective-permute-done.6
  38.2 1.6 collective-permute-start.7
  39.7 4.9 %collective-permute-done.7 = f32[1,32,2048]{2,1,0:T(8,128)S(1)} collective-permute-done((f32[1,32,2048]{2,1,0:T(8,128)S(1)}, f32[1,32,2048]{2,1,0:T(8,128)S(1)}, u32[]{:S(2)}, u32[]{:S(2)}) %collective-permute-start.7) | collective-permute-done | bytes 262176 | tf_op jit(solution)/shard_map/ppermute | solution.py:67
  44.9 1.7 collective-permute-done.8
  46.7 1.0 fusion.31
  47.7 1.4 collective-permute-start.10
  49.1 2.0 collective-permute-start.12
  51.1 2.0 collective-permute-start.11
  53.1 3.6 %collective-permute-start.9 = (f32[128,512]{1,0:T(8,128)}, f32[128,512]{1,0:T(8,128)}, u32[]{:S(2)}, u32[]{:S(2)}) collective-permute-start(f32[128,512]{1,0:T(8,128)} %get-tuple-element.25), channel_id=1, source_target_pairs={{0,0},{1,4},{10,8},{11,12},{20,16},{21,20},{30,24},{31,28}} | collective-permute-start | bytes 786440 | tf_op jit(solution)/shard_map/ppermute | solution.py:122
  56.7 22.7 %convolution_bitcast_fusion = f32[2,2,2,128,512]{4,3,0,1,2:T(8,128)S(1)} fusion(f32[128,2048,1,1,1]{1,0,4,3,2:T(8,128)S(1)} %bitcast.133, f32[2,2,2,512,2048]{4,3,2,1,0:T(8,128)} %bitcast.131), kind=kOutput, calls=%fused_computation.3 | convolution fusion | flops 6442450944 | bytes 36700160 | tf_op jit(solution)/shard_map/mk,abcik->cbami/dot_general | solution.py:112
  80.2 1.3 add_add_fusion
  81.9 20.9 %collective-permute-done.13 = f32[2,2,128,512]{3,2,0,1:T(8,128)} collective-permute-done((f32[2,2,128,512]{3,2,0,1:T(8,128)S(1)}, f32[2,2,128,512]{3,2,0,1:T(8,128)}, u32[]{:S(2)}, u32[]{:S(2)}) %collective-permute-start.13) | collective-permute-done | bytes 1048608 | tf_op jit(solution)/shard_map/ppermute | solution.py:43
  102.8 1.5 bitcast_add_fusion
  104.5 12.3 %collective-permute-done.14 = f32[2,128,512]{2,1,0:T(8,128)S(1)} collective-permute-done((f32[2,128,512]{2,1,0:T(8,128)S(1)}, f32[2,128,512]{2,1,0:T(8,128)S(1)}, u32[]{:S(2)}, u32[]{:S(2)}) %collective-permute-start.14) | collective-permute-done | bytes 524320 | tf_op jit(solution)/shard_map/ppermute | solution.py:43
  116.9 2.6 %collective-permute-start.15 = (f32[128,512]{1,0:T(8,128)S(1)}, f32[128,512]{1,0:T(8,128)S(1)}, u32[]{:S(2)}, u32[]{:S(2)}) collective-permute-start(f32[128,512]{1,0:T(8,128)S(1)} %dynamic-slice_bitcast_fusion.2), channel_id=1, source_target_pairs={{0,4},{1,5},{2,6},{3,7},{4,0},{5,1},{6,2},{7,3},{8,12},{9,13},{10,... | collective-permute-start | bytes 786440 | tf_op jit(solution)/shard_map/ppermute | solution.py:43
  119.4 10.9 %collective-permute-done.15 = f32[128,512]{1,0:T(8,128)S(1)} collective-permute-done((f32[128,512]{1,0:T(8,128)S(1)}, f32[128,512]{1,0:T(8,128)S(1)}, u32[]{:S(2)}, u32[]{:S(2)}) %collective-permute-start.15) | collective-permute-done | bytes 262176 | tf_op jit(solution)/shard_map/ppermute | solution.py:43
  130.3 0.7 bitcast_add_fusion.2
  131.7 1.3 fusion.32
  133.0 1.2 collective-permute-start.16
  134.3 3.2 %collective-permute-done.16 = f32[136,128]{1,0:T(8,128)S(1)} collective-permute-done((f32[136,128]{1,0:T(8,128)S(1)}, f32[136,128]{1,0:T(8,128)S(1)}, u32[]{:S(2)}, u32[]{:S(2)}) %collective-permute-start.16) | collective-permute-done | bytes 69664 | tf_op jit(solution)/shard_map/ppermute | solution.py:31
  137.5 7.6 %collective-permute-done.17 = f32[136,128]{1,0:T(8,128)S(1)} collective-permute-done((f32[136,128]{1,0:T(8,128)S(1)}, f32[136,128]{1,0:T(8,128)S(1)}, u32[]{:S(2)}, u32[]{:S(2)}) %collective-permute-start.17) | collective-permute-done | bytes 69664 | tf_op jit(solution)/shard_map/ppermute | solution.py:31
  145.2 8.2 %collective-permute-done.18 = f32[136,128]{1,0:T(8,128)S(1)} collective-permute-done((f32[136,128]{1,0:T(8,128)S(1)}, f32[136,128]{1,0:T(8,128)S(1)}, u32[]{:S(2)}, u32[]{:S(2)}) %collective-permute-start.18) | collective-permute-done | bytes 69664 | tf_op jit(solution)/shard_map/ppermute | solution.py:31
  153.4 1.2 collective-permute-done.19
  154.7 1.5 collective-permute-start.20
  156.2 2.8 %collective-permute-done.20 = f32[136,128]{1,0:T(8,128)S(1)} collective-permute-done((f32[136,128]{1,0:T(8,128)S(1)}, f32[136,128]{1,0:T(8,128)S(1)}, u32[]{:S(2)}, u32[]{:S(2)}) %collective-permute-start.20) | collective-permute-done | bytes 69664 | tf_op jit(solution)/shard_map/ppermute | solution.py:31
  159.4 11.7 %cholesky.16 = f32[128,128]{1,0:T(8,128)S(1)} custom-call(f32[128,128]{1,0:T(8,128)S(1)} %fusion.20), custom_call_target="Cholesky" | custom-call | tf_op jit(solution)/shard_map/jit(cholesky)/cholesky | solution.py:139
  172.4 11.3 %all-gather.2.cloned.1.call-done = f32[128,4096]{1,0:T(8,128)} async-done(((f32[128,512]{1,0:T(8,128)}), f32[128,4096]{1,0:T(8,128)}) %all-gather.2.cloned.1.call-update) | async-done | bytes 2097168 | tf_op jit(solution)/shard_map/all_gather | solution.py:136
  183.7 2.4 %dynamic-slice_select_fusion = f32[128,2048]{1,0:T(8,128)} fusion(f32[128,4096]{1,0:T(8,128)} %all-gather.2.cloned.1.call-done, s32[]{:T(128)S(6)} %select_n.229, pred[]{:T(512)S(6)} %eq.76), kind=kLoop, calls=%fused_computation.20 | loop fusion | flops 262144 | bytes 2097157 | tf_op jit(solution)/shard_map/jit(_where)/select_n | solution.py:143
  186.1 3.5 %collective-permute-start.21 = (f32[128,2048]{1,0:T(8,128)}, f32[128,2048]{1,0:T(8,128)S(1)}, u32[]{:S(2)}, u32[]{:S(2)}) collective-permute-start(f32[128,2048]{1,0:T(8,128)} %dynamic-slice_select_fusion), channel_id=1, source_target_pairs={{0,16},{1,17},{10,26},{11,27},{20,4},{21,5},{30,14},{31,15}} | collective-permute-start | bytes 3145736 | tf_op jit(solution)/shard_map/ppermute | solution.py:23
  190.3 10.6 %custom-call.16 = f32[1,128,128]{1,2,0:T(8,128)S(1)} custom-call(f32[1,128,128]{2,1,0:T(8,128)} %select_bitcast_fusion), custom_call_target="InvertDiagBlocksLowerTriangular" | custom-call | tf_op jit(solution)/shard_map/jit(_cho_solve)/triangular_solve | solution.py:148
  201.0 1.3 collective-permute-done.21
  202.4 1.4 collective-permute-start.22
  204.4 1.3 dynamic-slice_add_fusion
  205.7 1.9 fusion.16
  207.7 1.1 fusion.5
  208.8 27.1 %convolution_subtract_fusion = f32[4096,2048]{1,0:T(8,128)} fusion(f32[4096,2048]{1,0:T(8,128)} %param.21, f32[128,4096]{1,0:T(8,128)S(1)} %fusion.16, f32[128,2048]{1,0:T(8,128)S(1)} %fusion.5), kind=kOutput, calls=%fused_computation | convolution fusion | flops 6450839552 | bytes 70254592 | tf_op jit(solution)/shard_map/mi,mj->ij/dot_general | solution.py:147
  (97 shorter events, 7.9 us)
Async XLA Ops:
  7.2 7.4 %copy-start = (f32[4,128]{1,0:T(4,128)S(1)}, f32[4,128]{1,0:T(4,128)}, u32[]{:S(2)}) copy-start(f32[4,128]{1,0:T(4,128)} %param.18) | copy-start | bytes 6148
  7.2 11.0 %copy-start.5 = (f32[128,128]{1,0:T(8,128)S(1)}, f32[128,128]{1,0:T(8,128)}, u32[]{:S(2)}) copy-start(f32[128,128]{1,0:T(8,128)} %param.16) | copy-start | bytes 196612
  7.2 176.5 %all-gather.2.cloned.1.call-start = ((), (), s32[]{:S(2)}) async-start(), calls=%async_computation | async-start | bytes 2359296 | tf_op jit(solution)/shard_map/all_gather | solution.py:136
  19.5 9.9 %collective-permute-start = (f32[4,2048]{1,0:T(4,128)S(1)}, f32[4,2048]{1,0:T(4,128)S(1)}, u32[]{:S(2)}, u32[]{:S(2)}) collective-permute-start(f32[4,2048]{1,0:T(4,128)S(1)} %bitcast.141), channel_id=1, source_target_pairs={{0,7},{1,0},{2,1},{3,2},{4,3},{5,4},{6,5},{7,6},{8,15},{9,8},{10,9... | collective-permute-start | bytes 98312 | tf_op jit(solution)/shard_map/ppermute | solution.py:51
  25.5 5.7 %collective-permute-start.1 = (f32[4,2048]{1,0:T(4,128)S(1)}, f32[4,2048]{1,0:T(4,128)S(1)}, u32[]{:S(2)}, u32[]{:S(2)}) collective-permute-start(f32[4,2048]{1,0:T(4,128)S(1)} %bitcast.140), channel_id=1, source_target_pairs={{0,6},{1,7},{2,0},{3,1},{4,2},{5,3},{6,4},{7,5},{8,14},{9,15},{10,... | collective-permute-start | bytes 98312 | tf_op jit(solution)/shard_map/ppermute | solution.py:51
  26.0 6.4 %collective-permute-start.2 = (f32[4,2048]{1,0:T(4,128)S(1)}, f32[4,2048]{1,0:T(4,128)S(1)}, u32[]{:S(2)}, u32[]{:S(2)}) collective-permute-start(f32[4,2048]{1,0:T(4,128)S(1)} %bitcast.137), channel_id=1, source_target_pairs={{0,5},{1,6},{2,7},{3,0},{4,1},{5,2},{6,3},{7,4},{8,13},{9,14},{10,... | collective-permute-start | bytes 98312 | tf_op jit(solution)/shard_map/ppermute | solution.py:51
  26.1 6.3 %collective-permute-start.3 = (f32[4,2048]{1,0:T(4,128)S(1)}, f32[4,2048]{1,0:T(4,128)S(1)}, u32[]{:S(2)}, u32[]{:S(2)}) collective-permute-start(f32[4,2048]{1,0:T(4,128)S(1)} %bitcast.138), channel_id=1, source_target_pairs={{0,4},{1,5},{2,6},{3,7},{4,0},{5,1},{6,2},{7,3},{8,12},{9,13},{10,... | collective-permute-start | bytes 98312 | tf_op jit(solution)/shard_map/ppermute | solution.py:51
  29.2 6.1 %collective-permute-start.4 = (f32[4,2048]{1,0:T(4,128)S(1)}, f32[4,2048]{1,0:T(4,128)S(1)}, u32[]{:S(2)}, u32[]{:S(2)}) collective-permute-start(f32[4,2048]{1,0:T(4,128)S(1)} %bitcast.139), channel_id=1, source_target_pairs={{0,3},{1,4},{2,5},{3,6},{4,7},{5,0},{6,1},{7,2},{8,11},{9,12},{10,... | collective-permute-start | bytes 98312 | tf_op jit(solution)/shard_map/ppermute | solution.py:51
  29.3 6.9 %collective-permute-start.5 = (f32[4,2048]{1,0:T(4,128)S(1)}, f32[4,2048]{1,0:T(4,128)S(1)}, u32[]{:S(2)}, u32[]{:S(2)}) collective-permute-start(f32[4,2048]{1,0:T(4,128)S(1)} %bitcast.143), channel_id=1, source_target_pairs={{0,2},{1,3},{2,4},{3,5},{4,6},{5,7},{6,0},{7,1},{8,10},{9,11},{10,... | collective-permute-start | bytes 98312 | tf_op jit(solution)/shard_map/ppermute | solution.py:51
  31.2 6.7 %collective-permute-start.6 = (f32[4,2048]{1,0:T(4,128)S(1)}, f32[4,2048]{1,0:T(4,128)S(1)}, u32[]{:S(2)}, u32[]{:S(2)}) collective-permute-start(f32[4,2048]{1,0:T(4,128)S(1)} %bitcast.142), channel_id=1, source_target_pairs={{0,1},{1,2},{2,3},{3,4},{4,5},{5,6},{6,7},{7,0},{8,9},{9,10},{10,1... | collective-permute-start | bytes 98312 | tf_op jit(solution)/shard_map/ppermute | solution.py:51
  38.2 6.4 %collective-permute-start.7 = (f32[1,32,2048]{2,1,0:T(8,128)S(1)}, f32[1,32,2048]{2,1,0:T(8,128)S(1)}, u32[]{:S(2)}, u32[]{:S(2)}) collective-permute-start(f32[1,32,2048]{2,1,0:T(8,128)S(1)} %broadcast_in_dim_reshape.3), channel_id=1, source_target_pairs={{0,16},{8,24},{16,0},{24,8},{1,17},{9,25},{17,1},{25,9},{2,18},{10... | collective-permute-start | bytes 786440 | tf_op jit(solution)/shard_map/ppermute | solution.py:67
  44.7 2.0 collective-permute-start.8
  47.7 31.8 %collective-permute-start.10 = (f32[128,512]{1,0:T(8,128)}, f32[128,512]{1,0:T(8,128)S(1)}, u32[]{:S(2)}, u32[]{:S(2)}) collective-permute-start(f32[128,512]{1,0:T(8,128)} %get-tuple-element.22), channel_id=1, source_target_pairs={{0,1},{1,5},{10,9},{11,13},{20,17},{21,21},{30,25},{31,29}} | collective-permute-start | bytes 786440 | tf_op jit(solution)/shard_map/ppermute | solution.py:122
  49.1 30.4 %collective-permute-start.12 = (f32[128,512]{1,0:T(8,128)}, f32[128,512]{1,0:T(8,128)}, u32[]{:S(2)}, u32[]{:S(2)}) collective-permute-start(f32[128,512]{1,0:T(8,128)} %get-tuple-element.23), channel_id=1, source_target_pairs={{0,3},{1,7},{10,11},{11,15},{20,19},{21,23},{30,27},{31,31}} | collective-permute-start | bytes 786440 | tf_op jit(solution)/shard_map/ppermute | solution.py:122
  51.1 28.4 %collective-permute-start.11 = (f32[128,512]{1,0:T(8,128)}, f32[128,512]{1,0:T(8,128)}, u32[]{:S(2)}, u32[]{:S(2)}) collective-permute-start(f32[128,512]{1,0:T(8,128)} %get-tuple-element.24), channel_id=1, source_target_pairs={{0,2},{1,6},{10,10},{11,14},{20,18},{21,22},{30,26},{31,30}} | collective-permute-start | bytes 786440 | tf_op jit(solution)/shard_map/ppermute | solution.py:122
  53.1 27.1 %collective-permute-start.9 = (f32[128,512]{1,0:T(8,128)}, f32[128,512]{1,0:T(8,128)}, u32[]{:S(2)}, u32[]{:S(2)}) collective-permute-start(f32[128,512]{1,0:T(8,128)} %get-tuple-element.25), channel_id=1, source_target_pairs={{0,0},{1,4},{10,8},{11,12},{20,16},{21,20},{30,24},{31,28}} | collective-permute-start | bytes 786440 | tf_op jit(solution)/shard_map/ppermute | solution.py:122
  79.5 0.7 copy-start.4
  81.6 21.3 %collective-permute-start.13 = (f32[2,2,128,512]{3,2,0,1:T(8,128)S(1)}, f32[2,2,128,512]{3,2,0,1:T(8,128)}, u32[]{:S(2)}, u32[]{:S(2)}) collective-permute-start(f32[2,2,128,512]{3,2,0,1:T(8,128)S(1)} %dynamic-slice_bitcast_fusion), channel_id=1, source_target_pairs={{0,1},{1,0},{2,3},{3,2},{4,5},{5,4},{6,7},{7,6},{8,9},{9,8},{10,11... | collective-permute-start | bytes 3145736 | tf_op jit(solution)/shard_map/ppermute | solution.py:43
  104.3 26.8 %copy-start.7 = (s32[256]{0:T(256)S(1)}, s32[256]{0:T(256)}, u32[]{:S(2)}) copy-start(s32[256]{0:T(256)} %param.15) | copy-start | bytes 3076
  104.4 12.4 %collective-permute-start.14 = (f32[2,128,512]{2,1,0:T(8,128)S(1)}, f32[2,128,512]{2,1,0:T(8,128)S(1)}, u32[]{:S(2)}, u32[]{:S(2)}) collective-permute-start(f32[2,128,512]{2,1,0:T(8,128)S(1)} %dynamic-slice_bitcast_fusion.1), channel_id=1, source_target_pairs={{0,2},{1,3},{2,0},{3,1},{4,6},{5,7},{6,4},{7,5},{8,10},{9,11},{10,... | collective-permute-start | bytes 1572872 | tf_op jit(solution)/shard_map/ppermute | solution.py:43
  104.5 54.6 %copy-start.6 = (f32[128]{0:T(128)S(1)}, f32[128]{0:T(128)}, u32[]{:S(2)}) copy-start(f32[128]{0:T(128)} %param.20) | copy-start | bytes 1540
  116.9 13.5 %collective-permute-start.15 = (f32[128,512]{1,0:T(8,128)S(1)}, f32[128,512]{1,0:T(8,128)S(1)}, u32[]{:S(2)}, u32[]{:S(2)}) collective-permute-start(f32[128,512]{1,0:T(8,128)S(1)} %dynamic-slice_bitcast_fusion.2), channel_id=1, source_target_pairs={{0,4},{1,5},{2,6},{3,7},{4,0},{5,1},{6,2},{7,3},{8,12},{9,13},{10,... | collective-permute-start | bytes 786440 | tf_op jit(solution)/shard_map/ppermute | solution.py:43
  133.0 4.4 %collective-permute-start.16 = (f32[136,128]{1,0:T(8,128)S(1)}, f32[136,128]{1,0:T(8,128)S(1)}, u32[]{:S(2)}, u32[]{:S(2)}) collective-permute-start(f32[136,128]{1,0:T(8,128)S(1)} %pad_maximum_fusion), channel_id=1, source_target_pairs={{0,1},{1,0},{2,3},{3,2},{4,5},{5,4},{6,7},{7,6},{8,9},{9,8},{10,11... | collective-permute-start | bytes 208904 | tf_op jit(solution)/shard_map/ppermute | solution.py:31
  137.4 7.6 %collective-permute-start.17 = (f32[136,128]{1,0:T(8,128)S(1)}, f32[136,128]{1,0:T(8,128)S(1)}, u32[]{:S(2)}, u32[]{:S(2)}) collective-permute-start(f32[136,128]{1,0:T(8,128)S(1)} %fusion.30), channel_id=1, source_target_pairs={{0,2},{1,3},{2,0},{3,1},{4,6},{5,7},{6,4},{7,5},{8,10},{9,11},{10,... | collective-permute-start | bytes 208904 | tf_op jit(solution)/shard_map/ppermute | solution.py:31
  145.1 8.3 %collective-permute-start.18 = (f32[136,128]{1,0:T(8,128)S(1)}, f32[136,128]{1,0:T(8,128)S(1)}, u32[]{:S(2)}, u32[]{:S(2)}) collective-permute-start(f32[136,128]{1,0:T(8,128)S(1)} %add.250), channel_id=1, source_target_pairs={{0,4},{1,5},{2,6},{3,7},{4,0},{5,1},{6,2},{7,3},{8,12},{9,13},{10,... | collective-permute-start | bytes 208904 | tf_op jit(solution)/shard_map/ppermute | solution.py:31
  153.4 1.3 collective-permute-start.19
  154.7 4.4 %collective-permute-start.20 = (f32[136,128]{1,0:T(8,128)S(1)}, f32[136,128]{1,0:T(8,128)S(1)}, u32[]{:S(2)}, u32[]{:S(2)}) collective-permute-start(f32[136,128]{1,0:T(8,128)S(1)} %add.252), channel_id=1, source_target_pairs={{0,16},{8,24},{16,0},{24,8},{1,17},{9,25},{17,1},{25,9},{2,18},{10... | collective-permute-start | bytes 208904 | tf_op jit(solution)/shard_map/ppermute | solution.py:31
  183.7 18.6 %copy-start.2 = (f32[128,4096]{1,0:T(8,128)S(1)}, f32[128,4096]{1,0:T(8,128)}, u32[]{:S(2)}) copy-start(f32[128,4096]{1,0:T(8,128)} %all-gather.2.cloned.1.call-done) | copy-start | bytes 6291460
  186.1 17.6 %copy-start.8 = (f32[128]{0:T(128)S(1)}, f32[128]{0:T(128)}, u32[]{:S(2)}) copy-start(f32[128]{0:T(128)} %param.19) | copy-start | bytes 1540
  186.1 18.0 %copy-start.3 = (f32[128,512]{1,0:T(8,128)S(1)}, f32[128,512]{1,0:T(8,128)}, u32[]{:S(2)}) copy-start(f32[128,512]{1,0:T(8,128)} %bitcast_add_fusion.2) | copy-start | bytes 786436
  186.1 16.1 %collective-permute-start.21 = (f32[128,2048]{1,0:T(8,128)}, f32[128,2048]{1,0:T(8,128)S(1)}, u32[]{:S(2)}, u32[]{:S(2)}) collective-permute-start(f32[128,2048]{1,0:T(8,128)} %dynamic-slice_select_fusion), channel_id=1, source_target_pairs={{0,16},{1,17},{10,26},{11,27},{20,4},{21,5},{30,14},{31,15}} | collective-permute-start | bytes 3145736 | tf_op jit(solution)/shard_map/ppermute | solution.py:23
  202.4 5.3 %collective-permute-start.22 = (f32[128,2048]{1,0:T(8,128)S(1)}, f32[128,2048]{1,0:T(8,128)S(1)}, u32[]{:S(2)}, u32[]{:S(2)}) collective-permute-start(f32[128,2048]{1,0:T(8,128)S(1)} %fusion.51), channel_id=1, source_target_pairs={{0,8},{16,24},{1,9},{17,25},{10,2},{26,18},{11,3},{27,19},{20,28},... | collective-permute-start | bytes 3145736 | tf_op jit(solution)/shard_map/ppermute | solution.py:23
  208.8 27.2 %copy-start.1 = (f32[4,128]{1,0:T(4,128)S(1)}, f32[4,128]{1,0:T(4,128)}, u32[]{:S(2)}) copy-start(f32[4,128]{1,0:T(4,128)} %param.18) | copy-start | bytes 6148
Sparse Core Ops, SparseCore 0:
  131.2 52.4 all-gather.1

commit v12 on v11

--- a/solution.py
+++ b/solution.py
@@ -33,9 +33,9 @@
     return buf
 
 
-def halving_scatter(x, axis, size, me):
+def halving_scatter(x, axis, size, me, done=0):
     nbits = size.bit_length() - 1
-    for step in range(nbits):
+    for step in range(done, nbits):
         bit = 1 << step
         mine = (me // bit) % 2
         keep = lax.dynamic_index_in_dim(x, mine, 0, keepdims=False)
@@ -109,9 +109,14 @@
     nbits = n_col.bit_length() - 1
     letters = "abcdefgh"[:nbits]
     cov_blocks = cov.reshape((2,) * nbits + (cov.shape[0] // n_col, cov.shape[1]))
-    partial_t = jnp.einsum(
-        "mk," + letters + "ik->" + letters[::-1] + "mi", grad_col, cov_blocks, precision=mid
-    )
+    first = col_id % 2
+    spec = "mk," + letters[:-1] + "ik->" + letters[:-1][::-1] + "mi"
+    send_rows = lax.dynamic_index_in_dim(cov_blocks, 1 - first, nbits - 1, keepdims=False)
+    send_part = jnp.einsum(spec, grad_col, send_rows, precision=mid)
+    got_part = lax.ppermute(send_part, "col", [(i, i ^ 1) for i in range(n_col)])
+    keep_rows = lax.dynamic_index_in_dim(cov_blocks, first, nbits - 1, keepdims=False)
+    keep_part = jnp.einsum(spec, grad_col, keep_rows, precision=mid)
+    partial_t = keep_part + got_part
     factor = n_col // n_row
     grad_own = None
     for t in range(n_row):
@@ -122,7 +127,7 @@
         got = lax.ppermute(grad_col[:, t * blk : (t + 1) * blk], ("row", "col"), perm)
         grad_own = got if grad_own is None else grad_own + got
     grad_own, partial_t = lax.optimization_barrier((grad_own, partial_t))
-    gain_own_t = halving_scatter(partial_t, "col", n_col, col_id)
+    gain_own_t = halving_scatter(partial_t, "col", n_col, col_id, 1)
     gram_own = jnp.einsum("mk,nk->mn", grad_own, gain_own_t, precision=hi)
     device_id = row_id * n_col + col_id
     slots = lax.dynamic_update_slice_in_dim(

time: 244 us -> 239 us (0.980)
  waiting for transfers between devices: 91.6 us -> 85.4 us
  starting transfers between devices: 34.3 us -> 39 us
  other arithmetic: 38.6 us -> 35.7 us
    ppermute x3 -> x2, waiting for transfers between devices: 44.1 us -> 23.6 us  [halving_scatter(): x = keep + lax.ppermute(send, axis, [(i, i ^ bit) for i in range(size)])]
    ppermute x4, waiting for transfers between devices: 0.01 us -> 16.2 us  [on_device(): got = lax.ppermute(grad_col[:, t * blk:(t + 1) * blk], ('row', 'col'), perm)]
    ppermute x5, waiting for transfers between devices: 23 us -> 18.4 us  [butterfly_sum(): buf = buf + lax.ppermute(buf, axis, [(i, i ^ bit) for i in range(size)])]
    ppermute x4, starting transfers between devices: 9 us -> 11.5 us  [on_device(): got = lax.ppermute(grad_col[:, t * blk:(t + 1) * blk], ('row', 'col'), perm)]
    dot_general x1 -> x2, matrix products: 22.7 us -> 20.9 us  [the longest x1 10.6 us: on_device(): keep_part = jnp.einsum(spec, grad_col, keep_rows, precision=mid)]
  transfers between devices with their start and end apart: 24 -> 24, of which waited for: 15 -> 15; matrix products, arithmetic and copies ran while one was open for 22% -> 14% of each run, Pallas kernels for 0% -> 0%
where the time goes in v12:
time: 239 us
  waiting for transfers between devices  85.4 us (36%)
  matrix products  59.8 us (25%)
  starting transfers between devices  39 us (16%)
  other arithmetic  35.7 us (15%)
  between operations  14.8 us (6%)
  local copies, waits for them, and re-layouts  3.81 us (2%)
    dot_general x1, matrix products, on_device(): new_cov = cov - jnp.einsum('mi,mj->ij', white_row, white_col, precision=mid)  26.9 us
    ppermute x2, waiting for transfers between devices, halving_scatter(): x = keep + lax.ppermute(send, axis, [(i, i ^ bit) for i in range(size)])  23.6 us
    ppermute x5, waiting for transfers between devices, butterfly_sum(): buf = buf + lax.ppermute(buf, axis, [(i, i ^ bit) for i in range(size)])  18.4 us
    ppermute x4, waiting for transfers between devices, on_device(): got = lax.ppermute(grad_col[:, t * blk:(t + 1) * blk], ('row', 'col'), perm)  16.2 us
    ppermute x7, starting transfers between devices, shift_all_to_all(): lax.ppermute(piece, axis, [(i, (i - k) % size) for i in range(size)])  12.8 us
    all_gather x1, waiting for transfers between devices, on_device(): gain_rows_t = lax.all_gather(gain_own_t, 'col', axis=1, tiled=True)  12.8 us
    another operation x3, other arithmetic, on_device(): lower = jnp.linalg.cholesky(gram)  12.4 us
    ppermute x4, starting transfers between devices, on_device(): got = lax.ppermute(grad_col[:, t * blk:(t + 1) * blk], ('row', 'col'), perm)  11.5 us
  transfers between devices with their start and end apart: 24, of which 15 were waited for; matrix products, arithmetic and copies ran while one was open for 14% of the time, Pallas kernels for 0%

profile of v12, /device:TPU:0, one launch (start us, length us, event | category | flops | bytes accessed | tf_op | source)
XLA Modules:
  0.0 238.5 jit_solution(6654431291038267993)
XLA Ops:
  8.9 5.7 %convert_reduce_fusion = f32[256,256]{1,0:T(8,128)S(1)} fusion(s32[256,32]{1,0:T(8,128)S(1)} %copy.18), kind=kLoop, calls=%fused_computation.7 | loop fusion | flops 6225920 | bytes 294912 | tf_op jit(solution)/shard_map/reduce_sum | solution.py:87
  14.6 1.0 fusion.29
  15.6 1.2 convolution_multiply_fusion.2
  16.8 1.3 fusion.17
  18.2 1.2 multiply_reduce_fusion
  20.3 6.1 %collective-permute-start = (f32[4,2048]{1,0:T(4,128)S(1)}, f32[4,2048]{1,0:T(4,128)S(1)}, u32[]{:S(2)}, u32[]{:S(2)}) collective-permute-start(f32[4,2048]{1,0:T(4,128)S(1)} %bitcast.159), channel_id=1, source_target_pairs={{0,7},{1,0},{2,1},{3,2},{4,3},{5,4},{6,5},{7,6},{8,15},{9,8},{10,9... | collective-permute-start | bytes 98312 | tf_op jit(solution)/shard_map/ppermute | solution.py:51
  27.0 3.0 %collective-permute-start.3 = (f32[4,2048]{1,0:T(4,128)S(1)}, f32[4,2048]{1,0:T(4,128)S(1)}, u32[]{:S(2)}, u32[]{:S(2)}) collective-permute-start(f32[4,2048]{1,0:T(4,128)S(1)} %bitcast.156), channel_id=1, source_target_pairs={{0,4},{1,5},{2,6},{3,7},{4,0},{5,1},{6,2},{7,3},{8,12},{9,13},{10,... | collective-permute-start | bytes 98312 | tf_op jit(solution)/shard_map/ppermute | solution.py:51
  30.2 1.9 collective-permute-start.5
  32.1 1.2 collective-permute-start.6
  33.3 2.8 %collective-permute-done.4 = f32[4,2048]{1,0:T(4,128)S(1)} collective-permute-done((f32[4,2048]{1,0:T(4,128)S(1)}, f32[4,2048]{1,0:T(4,128)S(1)}, u32[]{:S(2)}, u32[]{:S(2)}) %collective-permute-start.4) | collective-permute-done | bytes 32800 | tf_op jit(solution)/shard_map/ppermute | solution.py:51
  36.1 0.9 collective-permute-done.5
  37.1 1.6 collective-permute-done.6
  39.0 1.6 collective-permute-start.7
  40.6 4.9 %collective-permute-done.7 = f32[1,32,2048]{2,1,0:T(8,128)S(1)} collective-permute-done((f32[1,32,2048]{2,1,0:T(8,128)S(1)}, f32[1,32,2048]{2,1,0:T(8,128)S(1)}, u32[]{:S(2)}, u32[]{:S(2)}) %collective-permute-start.7) | collective-permute-done | bytes 262176 | tf_op jit(solution)/shard_map/ppermute | solution.py:67
  45.7 1.7 collective-permute-done.8
  47.6 10.3 %fusion.12 = f32[2,2,128,512]{2,3,0,1:T(8,128)S(1)} fusion(f32[128,2048,1,1]{1,0,3,2:T(8,128)S(1)} %bitcast.149, f32[2,2,2,512,2048]{4,3,2,1,0:T(8,128)} %bitcast.147, s32[]{:T(128)S(6)} %select_n.219), kind=kOutput, calls=%fused_computation.11 | convolution fusion | flops 3221225472 | bytes 18874372 | tf_op jit(solution)/shard_map/mk,abik->bami/dot_general | solution.py:115
  58.0 1.0 fusion.48
  58.9 4.6 %collective-permute-start.10 = (f32[128,512]{1,0:T(8,128)}, f32[128,512]{1,0:T(8,128)}, u32[]{:S(2)}, u32[]{:S(2)}) collective-permute-start(f32[128,512]{1,0:T(8,128)} %get-tuple-element.22), channel_id=1, source_target_pairs={{0,1},{1,5},{10,9},{11,13},{20,17},{21,21},{30,25},{31,29}} | collective-permute-start | bytes 786440 | tf_op jit(solution)/shard_map/ppermute | solution.py:127
  63.5 2.0 collective-permute-start.12
  65.5 1.3 collective-permute-start.11
  66.8 3.6 %collective-permute-start.9 = (f32[128,512]{1,0:T(8,128)}, f32[128,512]{1,0:T(8,128)}, u32[]{:S(2)}, u32[]{:S(2)}) collective-permute-start(f32[128,512]{1,0:T(8,128)} %get-tuple-element.25), channel_id=1, source_target_pairs={{0,0},{1,4},{10,8},{11,12},{20,16},{21,20},{30,24},{31,28}} | collective-permute-start | bytes 786440 | tf_op jit(solution)/shard_map/ppermute | solution.py:127
  70.4 16.2 %collective-permute-done.10 = f32[128,512]{1,0:T(8,128)} collective-permute-done((f32[128,512]{1,0:T(8,128)}, f32[128,512]{1,0:T(8,128)}, u32[]{:S(2)}, u32[]{:S(2)}) %collective-permute-start.10) | collective-permute-done | bytes 262176 | tf_op jit(solution)/shard_map/ppermute | solution.py:127
  87.4 1.3 add_add_fusion
  88.7 10.6 %fusion.9 = f32[2,2,128,512]{2,3,0,1:T(8,128)S(1)} fusion(f32[2,2,128,512]{2,3,0,1:T(8,128)S(1)} %collective-permute-done.13, f32[128,2048,1,1]{1,0,3,2:T(8,128)S(1)} %bitcast.151, f32[2,2,2,512,2048]{4,3,2,1,0:T(8,128)} %bitcast.148, s32[]{:T(128)S(6)} %select_n.218), kind=kOutput, calls=%fused_computation.10 | convolution fusion | flops 3221487616 | bytes 19922948 | tf_op jit(solution)/shard_map/mk,abik->bami/dot_general | solution.py:118
  99.5 12.4 %collective-permute-done.14 = f32[2,128,512]{1,2,0:T(8,128)S(1)} collective-permute-done((f32[2,128,512]{1,2,0:T(8,128)S(1)}, f32[2,128,512]{1,2,0:T(8,128)S(1)}, u32[]{:S(2)}, u32[]{:S(2)}) %collective-permute-start.14) | collective-permute-done | bytes 524320 | tf_op jit(solution)/shard_map/ppermute | solution.py:43
  111.9 3.2 %collective-permute-start.15 = (f32[128,512]{0,1:T(8,128)S(1)}, f32[128,512]{0,1:T(8,128)S(1)}, u32[]{:S(2)}, u32[]{:S(2)}) collective-permute-start(f32[128,512]{0,1:T(8,128)S(1)} %dynamic-slice_bitcast_fusion.1), channel_id=1, source_target_pairs={{0,4},{1,5},{2,6},{3,7},{4,0},{5,1},{6,2},{7,3},{8,12},{9,13},{10,... | collective-permute-start | bytes 786440 | tf_op jit(solution)/shard_map/ppermute | solution.py:43
  115.1 11.2 %collective-permute-done.15 = f32[128,512]{0,1:T(8,128)S(1)} collective-permute-done((f32[128,512]{0,1:T(8,128)S(1)}, f32[128,512]{0,1:T(8,128)S(1)}, u32[]{:S(2)}, u32[]{:S(2)}) %collective-permute-start.15) | collective-permute-done | bytes 262176 | tf_op jit(solution)/shard_map/ppermute | solution.py:43
  127.5 1.3 fusion.49
  128.9 1.1 collective-permute-start.16
  130.0 3.3 %collective-permute-done.16 = f32[136,128]{1,0:T(8,128)S(1)} collective-permute-done((f32[136,128]{1,0:T(8,128)S(1)}, f32[136,128]{1,0:T(8,128)S(1)}, u32[]{:S(2)}, u32[]{:S(2)}) %collective-permute-start.16) | collective-permute-done | bytes 69664 | tf_op jit(solution)/shard_map/ppermute | solution.py:31
  133.3 4.3 %collective-permute-done.17 = f32[136,128]{1,0:T(8,128)S(1)} collective-permute-done((f32[136,128]{1,0:T(8,128)S(1)}, f32[136,128]{1,0:T(8,128)S(1)}, u32[]{:S(2)}, u32[]{:S(2)}) %collective-permute-start.17) | collective-permute-done | bytes 69664 | tf_op jit(solution)/shard_map/ppermute | solution.py:31
  137.6 1.7 collective-permute-start.18
  139.3 7.1 %collective-permute-done.18 = f32[136,128]{1,0:T(8,128)S(1)} collective-permute-done((f32[136,128]{1,0:T(8,128)S(1)}, f32[136,128]{1,0:T(8,128)S(1)}, u32[]{:S(2)}, u32[]{:S(2)}) %collective-permute-start.18) | collective-permute-done | bytes 69664 | tf_op jit(solution)/shard_map/ppermute | solution.py:31
  146.5 1.2 collective-permute-done.19
  147.8 2.3 collective-permute-start.20
  150.1 2.5 %collective-permute-done.20 = f32[136,128]{1,0:T(8,128)S(1)} collective-permute-done((f32[136,128]{1,0:T(8,128)S(1)}, f32[136,128]{1,0:T(8,128)S(1)}, u32[]{:S(2)}, u32[]{:S(2)}) %collective-permute-start.20) | collective-permute-done | bytes 69664 | tf_op jit(solution)/shard_map/ppermute | solution.py:31
  152.9 11.7 %cholesky.16 = f32[128,128]{1,0:T(8,128)S(1)} custom-call(f32[128,128]{1,0:T(8,128)S(1)} %fusion.35), custom_call_target="Cholesky" | custom-call | tf_op jit(solution)/shard_map/jit(cholesky)/cholesky | solution.py:144
  165.9 12.8 %all-gather.2.cloned.1.call-done = f32[128,4096]{0,1:T(8,128)} async-done(((f32[128,512]{0,1:T(8,128)}), f32[128,4096]{0,1:T(8,128)}) %all-gather.2.cloned.1.call-update) | async-done | bytes 2097168 | tf_op jit(solution)/shard_map/all_gather | solution.py:141
  178.7 1.3 dynamic-slice_select_fusion
  180.0 2.9 %collective-permute-start.21 = (f32[128,2048]{0,1:T(8,128)S(1)}, f32[128,2048]{0,1:T(8,128)S(1)}, u32[]{:S(2)}, u32[]{:S(2)}) collective-permute-start(f32[128,2048]{0,1:T(8,128)S(1)} %dynamic-slice_select_fusion), channel_id=1, source_target_pairs={{0,16},{1,17},{10,26},{11,27},{20,4},{21,5},{30,14},{31,15}} | collective-permute-start | bytes 3145736 | tf_op jit(solution)/shard_map/ppermute | solution.py:23
  182.9 9.8 %custom-call.16 = f32[1,128,128]{1,2,0:T(8,128)S(1)} custom-call(f32[1,128,128]{2,1,0:T(8,128)S(1)} %select_bitcast_fusion), custom_call_target="InvertDiagBlocksLowerTriangular" | custom-call | tf_op jit(solution)/shard_map/jit(_cho_solve)/triangular_solve | solution.py:153
  192.7 2.4 %collective-permute-done.21 = f32[128,2048]{0,1:T(8,128)S(1)} collective-permute-done((f32[128,2048]{0,1:T(8,128)S(1)}, f32[128,2048]{0,1:T(8,128)S(1)}, u32[]{:S(2)}, u32[]{:S(2)}) %collective-permute-start.21) | collective-permute-done | bytes 1048608 | tf_op jit(solution)/shard_map/ppermute | solution.py:23
  195.1 1.4 fusion.68
  196.5 1.6 collective-permute-start.22
  198.8 1.4 dynamic-slice_add_fusion
  200.1 3.5 %fusion.31 = f32[128,4096]{1,0:T(8,128)S(1)} fusion(f32[128,4096]{0,1:T(8,128)} %all-gather.2.cloned.1.call-done, f32[1,128,128]{1,2,0:T(8,128)S(1)} %custom-call.16), kind=kOutput, calls=%fused_computation.48 | convolution fusion | flops 805306368 | bytes 4259840 | tf_op jit(solution)/shard_map/jit(_solve_triangular)/triangular_solve | solution.py:150
  203.7 1.1 fusion.20
  204.8 26.9 %convolution_subtract_fusion = f32[4096,2048]{1,0:T(8,128)} fusion(f32[4096,2048]{1,0:T(8,128)} %param.21, f32[128,4096]{1,0:T(8,128)S(1)} %fusion.31, f32[128,2048]{1,0:T(8,128)S(1)} %fusion.20), kind=kOutput, calls=%fused_computation.6 | convolution fusion | flops 6450839552 | bytes 70254592 | tf_op jit(solution)/shard_map/mi,mj->ij/dot_general | solution.py:152
  (92 shorter events, 8.5 us)
Async XLA Ops:
  7.2 7.4 %copy-start = (f32[4,128]{1,0:T(4,128)S(1)}, f32[4,128]{1,0:T(4,128)}, u32[]{:S(2)}) copy-start(f32[4,128]{1,0:T(4,128)} %param.18) | copy-start | bytes 6148
  7.2 171.5 %all-gather.2.cloned.1.call-start = ((), (), s32[]{:S(2)}) async-start(), calls=%async_computation | async-start | bytes 2359296 | tf_op jit(solution)/shard_map/all_gather | solution.py:141
  20.3 9.9 %collective-permute-start = (f32[4,2048]{1,0:T(4,128)S(1)}, f32[4,2048]{1,0:T(4,128)S(1)}, u32[]{:S(2)}, u32[]{:S(2)}) collective-permute-start(f32[4,2048]{1,0:T(4,128)S(1)} %bitcast.159), channel_id=1, source_target_pairs={{0,7},{1,0},{2,1},{3,2},{4,3},{5,4},{6,5},{7,6},{8,15},{9,8},{10,9... | collective-permute-start | bytes 98312 | tf_op jit(solution)/shard_map/ppermute | solution.py:51
  26.3 5.7 %collective-permute-start.1 = (f32[4,2048]{1,0:T(4,128)S(1)}, f32[4,2048]{1,0:T(4,128)S(1)}, u32[]{:S(2)}, u32[]{:S(2)}) collective-permute-start(f32[4,2048]{1,0:T(4,128)S(1)} %bitcast.158), channel_id=1, source_target_pairs={{0,6},{1,7},{2,0},{3,1},{4,2},{5,3},{6,4},{7,5},{8,14},{9,15},{10,... | collective-permute-start | bytes 98312 | tf_op jit(solution)/shard_map/ppermute | solution.py:51
  26.9 6.4 %collective-permute-start.2 = (f32[4,2048]{1,0:T(4,128)S(1)}, f32[4,2048]{1,0:T(4,128)S(1)}, u32[]{:S(2)}, u32[]{:S(2)}) collective-permute-start(f32[4,2048]{1,0:T(4,128)S(1)} %bitcast.155), channel_id=1, source_target_pairs={{0,5},{1,6},{2,7},{3,0},{4,1},{5,2},{6,3},{7,4},{8,13},{9,14},{10,... | collective-permute-start | bytes 98312 | tf_op jit(solution)/shard_map/ppermute | solution.py:51
  27.0 6.3 %collective-permute-start.3 = (f32[4,2048]{1,0:T(4,128)S(1)}, f32[4,2048]{1,0:T(4,128)S(1)}, u32[]{:S(2)}, u32[]{:S(2)}) collective-permute-start(f32[4,2048]{1,0:T(4,128)S(1)} %bitcast.156), channel_id=1, source_target_pairs={{0,4},{1,5},{2,6},{3,7},{4,0},{5,1},{6,2},{7,3},{8,12},{9,13},{10,... | collective-permute-start | bytes 98312 | tf_op jit(solution)/shard_map/ppermute | solution.py:51
  30.0 6.1 %collective-permute-start.4 = (f32[4,2048]{1,0:T(4,128)S(1)}, f32[4,2048]{1,0:T(4,128)S(1)}, u32[]{:S(2)}, u32[]{:S(2)}) collective-permute-start(f32[4,2048]{1,0:T(4,128)S(1)} %bitcast.157), channel_id=1, source_target_pairs={{0,3},{1,4},{2,5},{3,6},{4,7},{5,0},{6,1},{7,2},{8,11},{9,12},{10,... | collective-permute-start | bytes 98312 | tf_op jit(solution)/shard_map/ppermute | solution.py:51
  30.2 6.9 %collective-permute-start.5 = (f32[4,2048]{1,0:T(4,128)S(1)}, f32[4,2048]{1,0:T(4,128)S(1)}, u32[]{:S(2)}, u32[]{:S(2)}) collective-permute-start(f32[4,2048]{1,0:T(4,128)S(1)} %bitcast.161), channel_id=1, source_target_pairs={{0,2},{1,3},{2,4},{3,5},{4,6},{5,7},{6,0},{7,1},{8,10},{9,11},{10,... | collective-permute-start | bytes 98312 | tf_op jit(solution)/shard_map/ppermute | solution.py:51
  32.1 6.7 %collective-permute-start.6 = (f32[4,2048]{1,0:T(4,128)S(1)}, f32[4,2048]{1,0:T(4,128)S(1)}, u32[]{:S(2)}, u32[]{:S(2)}) collective-permute-start(f32[4,2048]{1,0:T(4,128)S(1)} %bitcast.160), channel_id=1, source_target_pairs={{0,1},{1,2},{2,3},{3,4},{4,5},{5,6},{6,7},{7,0},{8,9},{9,10},{10,1... | collective-permute-start | bytes 98312 | tf_op jit(solution)/shard_map/ppermute | solution.py:51
  39.0 6.4 %collective-permute-start.7 = (f32[1,32,2048]{2,1,0:T(8,128)S(1)}, f32[1,32,2048]{2,1,0:T(8,128)S(1)}, u32[]{:S(2)}, u32[]{:S(2)}) collective-permute-start(f32[1,32,2048]{2,1,0:T(8,128)S(1)} %broadcast_in_dim_reshape.3), channel_id=1, source_target_pairs={{0,16},{8,24},{16,0},{24,8},{1,17},{9,25},{17,1},{25,9},{2,18},{10... | collective-permute-start | bytes 786440 | tf_op jit(solution)/shard_map/ppermute | solution.py:67
  45.5 2.0 collective-permute-start.8
  57.9 30.8 %collective-permute-start.13 = (f32[2,2,128,512]{2,3,0,1:T(8,128)S(1)}, f32[2,2,128,512]{2,3,0,1:T(8,128)S(1)}, u32[]{:S(2)}, u32[]{:S(2)}) collective-permute-start(f32[2,2,128,512]{2,3,0,1:T(8,128)S(1)} %fusion.12), channel_id=1, source_target_pairs={{0,1},{1,0},{2,3},{3,2},{4,5},{5,4},{6,7},{7,6},{8,9},{9,8},{10,11... | collective-permute-start | bytes 3145736 | tf_op jit(solution)/shard_map/ppermute | solution.py:116
  58.9 27.7 %collective-permute-start.10 = (f32[128,512]{1,0:T(8,128)}, f32[128,512]{1,0:T(8,128)}, u32[]{:S(2)}, u32[]{:S(2)}) collective-permute-start(f32[128,512]{1,0:T(8,128)} %get-tuple-element.22), channel_id=1, source_target_pairs={{0,1},{1,5},{10,9},{11,13},{20,17},{21,21},{30,25},{31,29}} | collective-permute-start | bytes 786440 | tf_op jit(solution)/shard_map/ppermute | solution.py:127
  63.5 23.1 %collective-permute-start.12 = (f32[128,512]{1,0:T(8,128)}, f32[128,512]{1,0:T(8,128)}, u32[]{:S(2)}, u32[]{:S(2)}) collective-permute-start(f32[128,512]{1,0:T(8,128)} %get-tuple-element.23), channel_id=1, source_target_pairs={{0,3},{1,7},{10,11},{11,15},{20,19},{21,23},{30,27},{31,31}} | collective-permute-start | bytes 786440 | tf_op jit(solution)/shard_map/ppermute | solution.py:127
  65.5 21.1 %collective-permute-start.11 = (f32[128,512]{1,0:T(8,128)}, f32[128,512]{1,0:T(8,128)S(1)}, u32[]{:S(2)}, u32[]{:S(2)}) collective-permute-start(f32[128,512]{1,0:T(8,128)} %get-tuple-element.24), channel_id=1, source_target_pairs={{0,2},{1,6},{10,10},{11,14},{20,18},{21,22},{30,26},{31,30}} | collective-permute-start | bytes 786440 | tf_op jit(solution)/shard_map/ppermute | solution.py:127
  66.8 20.5 %collective-permute-start.9 = (f32[128,512]{1,0:T(8,128)}, f32[128,512]{1,0:T(8,128)}, u32[]{:S(2)}, u32[]{:S(2)}) collective-permute-start(f32[128,512]{1,0:T(8,128)} %get-tuple-element.25), channel_id=1, source_target_pairs={{0,0},{1,4},{10,8},{11,12},{20,16},{21,20},{30,24},{31,28}} | collective-permute-start | bytes 786440 | tf_op jit(solution)/shard_map/ppermute | solution.py:127
  86.7 0.7 copy-start.3
  88.7 38.5 %copy-start.5 = (s32[256]{0:T(256)S(1)}, s32[256]{0:T(256)}, u32[]{:S(2)}) copy-start(s32[256]{0:T(256)} %param.15) | copy-start | bytes 3076
  88.7 63.9 %copy-start.4 = (f32[128]{0:T(128)S(1)}, f32[128]{0:T(128)}, u32[]{:S(2)}) copy-start(f32[128]{0:T(128)} %param.20) | copy-start | bytes 1540
  99.3 98.8 %copy-start.6 = (f32[128]{0:T(128)S(1)}, f32[128]{0:T(128)}, u32[]{:S(2)}) copy-start(f32[128]{0:T(128)} %param.19) | copy-start | bytes 1540
  99.3 12.5 %collective-permute-start.14 = (f32[2,128,512]{1,2,0:T(8,128)S(1)}, f32[2,128,512]{1,2,0:T(8,128)S(1)}, u32[]{:S(2)}, u32[]{:S(2)}) collective-permute-start(f32[2,128,512]{1,2,0:T(8,128)S(1)} %dynamic-slice_bitcast_fusion), channel_id=1, source_target_pairs={{0,2},{1,3},{2,0},{3,1},{4,6},{5,7},{6,4},{7,5},{8,10},{9,11},{10,... | collective-permute-start | bytes 1572872 | tf_op jit(solution)/shard_map/ppermute | solution.py:43
  111.9 14.4 %collective-permute-start.15 = (f32[128,512]{0,1:T(8,128)S(1)}, f32[128,512]{0,1:T(8,128)S(1)}, u32[]{:S(2)}, u32[]{:S(2)}) collective-permute-start(f32[128,512]{0,1:T(8,128)S(1)} %dynamic-slice_bitcast_fusion.1), channel_id=1, source_target_pairs={{0,4},{1,5},{2,6},{3,7},{4,0},{5,1},{6,2},{7,3},{8,12},{9,13},{10,... | collective-permute-start | bytes 786440 | tf_op jit(solution)/shard_map/ppermute | solution.py:43
  127.1 71.3 %copy-start.2 = (f32[128,512]{0,1:T(8,128)S(1)}, f32[128,512]{0,1:T(8,128)}, u32[]{:S(2)}) copy-start(f32[128,512]{0,1:T(8,128)} %bitcast_add_fusion.1) | copy-start | bytes 786436
  128.9 4.4 %collective-permute-start.16 = (f32[136,128]{1,0:T(8,128)S(1)}, f32[136,128]{1,0:T(8,128)S(1)}, u32[]{:S(2)}, u32[]{:S(2)}) collective-permute-start(f32[136,128]{1,0:T(8,128)S(1)} %pad_maximum_fusion), channel_id=1, source_target_pairs={{0,1},{1,0},{2,3},{3,2},{4,5},{5,4},{6,7},{7,6},{8,9},{9,8},{10,11... | collective-permute-start | bytes 208904 | tf_op jit(solution)/shard_map/ppermute | solution.py:31
  133.2 4.4 %collective-permute-start.17 = (f32[136,128]{1,0:T(8,128)S(1)}, f32[136,128]{1,0:T(8,128)S(1)}, u32[]{:S(2)}, u32[]{:S(2)}) collective-permute-start(f32[136,128]{1,0:T(8,128)S(1)} %fusion.47), channel_id=1, source_target_pairs={{0,2},{1,3},{2,0},{3,1},{4,6},{5,7},{6,4},{7,5},{8,10},{9,11},{10,... | collective-permute-start | bytes 208904 | tf_op jit(solution)/shard_map/ppermute | solution.py:31
  137.6 8.8 %collective-permute-start.18 = (f32[136,128]{1,0:T(8,128)S(1)}, f32[136,128]{1,0:T(8,128)S(1)}, u32[]{:S(2)}, u32[]{:S(2)}) collective-permute-start(f32[136,128]{1,0:T(8,128)S(1)} %add.249), channel_id=1, source_target_pairs={{0,4},{1,5},{2,6},{3,7},{4,0},{5,1},{6,2},{7,3},{8,12},{9,13},{10,... | collective-permute-start | bytes 208904 | tf_op jit(solution)/shard_map/ppermute | solution.py:31
  146.4 1.3 collective-permute-start.19
  147.8 4.8 %collective-permute-start.20 = (f32[136,128]{1,0:T(8,128)S(1)}, f32[136,128]{1,0:T(8,128)S(1)}, u32[]{:S(2)}, u32[]{:S(2)}) collective-permute-start(f32[136,128]{1,0:T(8,128)S(1)} %add.251), channel_id=1, source_target_pairs={{0,16},{8,24},{16,0},{24,8},{1,17},{9,25},{17,1},{25,9},{2,18},{10... | collective-permute-start | bytes 208904 | tf_op jit(solution)/shard_map/ppermute | solution.py:31
  180.0 15.1 %collective-permute-start.21 = (f32[128,2048]{0,1:T(8,128)S(1)}, f32[128,2048]{0,1:T(8,128)S(1)}, u32[]{:S(2)}, u32[]{:S(2)}) collective-permute-start(f32[128,2048]{0,1:T(8,128)S(1)} %dynamic-slice_select_fusion), channel_id=1, source_target_pairs={{0,16},{1,17},{10,26},{11,27},{20,4},{21,5},{30,14},{31,15}} | collective-permute-start | bytes 3145736 | tf_op jit(solution)/shard_map/ppermute | solution.py:23
  196.5 7.2 %collective-permute-start.22 = (f32[128,2048]{0,1:T(8,128)S(1)}, f32[128,2048]{0,1:T(8,128)S(1)}, u32[]{:S(2)}, u32[]{:S(2)}) collective-permute-start(f32[128,2048]{0,1:T(8,128)S(1)} %fusion.68), channel_id=1, source_target_pairs={{0,8},{16,24},{1,9},{17,25},{10,2},{26,18},{11,3},{27,19},{20,28},... | collective-permute-start | bytes 3145736 | tf_op jit(solution)/shard_map/ppermute | solution.py:23
  204.8 26.9 %copy-start.1 = (f32[4,128]{1,0:T(4,128)S(1)}, f32[4,128]{1,0:T(4,128)}, u32[]{:S(2)}) copy-start(f32[4,128]{1,0:T(4,128)} %param.18) | copy-start | bytes 6148
Sparse Core Ops, SparseCore 0:
  127.2 51.3 all-gather.1

commit v13 on v12

--- a/solution.py
+++ b/solution.py
@@ -116,7 +116,7 @@
     got_part = lax.ppermute(send_part, "col", [(i, i ^ 1) for i in range(n_col)])
     keep_rows = lax.dynamic_index_in_dim(cov_blocks, first, nbits - 1, keepdims=False)
     keep_part = jnp.einsum(spec, grad_col, keep_rows, precision=mid)
-    partial_t = keep_part + got_part
+    partial_t = (keep_part, got_part)
     factor = n_col // n_row
     grad_own = None
     for t in range(n_row):
@@ -126,7 +126,8 @@
                 perm.append((r * n_col + r * factor + q, r * n_col + q * n_row + t))
         got = lax.ppermute(grad_col[:, t * blk : (t + 1) * blk], ("row", "col"), perm)
         grad_own = got if grad_own is None else grad_own + got
-    grad_own, partial_t = lax.optimization_barrier((grad_own, partial_t))
+    grad_own, keep_part = lax.optimization_barrier((grad_own, partial_t[0]))
+    partial_t = keep_part + partial_t[1]
     gain_own_t = halving_scatter(partial_t, "col", n_col, col_id, 1)
     gram_own = jnp.einsum("mk,nk->mn", grad_own, gain_own_t, precision=hi)
     device_id = row_id * n_col + col_id

time: 239 us -> 227 us (0.950)
  waiting for transfers between devices: 85.4 us -> 80.3 us
  starting transfers between devices: 39 us -> 34.7 us
    ppermute x4, waiting for transfers between devices: 16.2 us -> 10.8 us  [on_device(): got = lax.ppermute(grad_col[:, t * blk:(t + 1) * blk], ('row', 'col'), perm)]
    ppermute x4, starting transfers between devices: 11.5 us -> 7.35 us  [on_device(): got = lax.ppermute(grad_col[:, t * blk:(t + 1) * blk], ('row', 'col'), perm)]
    ppermute x5, waiting for transfers between devices: 18.4 us -> 21.8 us  [butterfly_sum(): buf = buf + lax.ppermute(buf, axis, [(i, i ^ bit) for i in range(size)])]
  transfers between devices with their start and end apart: 24 -> 24, of which waited for: 15 -> 15; matrix products, arithmetic and copies ran while one was open for 14% -> 18% of each run, Pallas kernels for 0% -> 0%
where the time goes in v13:
time: 227 us; the launch traced here: 226 us
  waiting for transfers between devices  80.3 us (35%)
  matrix products  59.5 us (26%)
  starting transfers between devices  34.7 us (15%)
  other arithmetic  34.7 us (15%)
  between operations  14.9 us (7%)
    dot_general x1, matrix products, on_device(): new_cov = cov - jnp.einsum('mi,mj->ij', white_row, white_col, precision=mid)  26.9 us
    ppermute x2, waiting for transfers between devices, halving_scatter(): x = keep + lax.ppermute(send, axis, [(i, i ^ bit) for i in range(size)])  22.8 us
    ppermute x5, waiting for transfers between devices, butterfly_sum(): buf = buf + lax.ppermute(buf, axis, [(i, i ^ bit) for i in range(size)])  21.8 us
    ppermute x7, starting transfers between devices, shift_all_to_all(): lax.ppermute(piece, axis, [(i, (i - k) % size) for i in range(size)])  12.8 us
    another operation x3, other arithmetic, on_device(): lower = jnp.linalg.cholesky(gram)  12.4 us
    ppermute x4, waiting for transfers between devices, on_device(): got = lax.ppermute(grad_col[:, t * blk:(t + 1) * blk], ('row', 'col'), perm)  10.8 us
    all_gather x1, waiting for transfers between devices, on_device(): gain_rows_t = lax.all_gather(gain_own_t, 'col', axis=1, tiled=True)  10.5 us
    dot_general x1, matrix products, on_device(): send_part = jnp.einsum(spec, grad_col, send_rows, precision=mid)  10.3 us
  transfers between devices with their start and end apart: 24, of which 15 were waited for; matrix products, arithmetic and copies ran while one was open for 18% of the time, Pallas kernels for 0%

profile of v13, /device:TPU:0, one launch (start us, length us, event | category | flops | bytes accessed | tf_op | source)
XLA Modules:
  0.0 226.3 jit_solution(13799073960662249941)
XLA Ops:
  7.3 0.7 fusion.36
  8.0 0.9 copy.18
  8.9 5.7 %convert_reduce_fusion = f32[256,256]{1,0:T(8,128)S(1)} fusion(s32[256,32]{1,0:T(8,128)S(1)} %copy.18), kind=kLoop, calls=%fused_computation.7 | loop fusion | flops 6225920 | bytes 294912 | tf_op jit(solution)/shard_map/reduce_sum | solution.py:87
  14.6 1.0 fusion.26
  15.6 1.2 convolution_multiply_fusion.2
  16.8 1.3 fusion.14
  18.2 1.2 multiply_reduce_fusion
  20.3 6.1 %collective-permute-start = (f32[4,2048]{1,0:T(4,128)S(1)}, f32[4,2048]{1,0:T(4,128)S(1)}, u32[]{:S(2)}, u32[]{:S(2)}) collective-permute-start(f32[4,2048]{1,0:T(4,128)S(1)} %bitcast.155), channel_id=1, source_target_pairs={{0,7},{1,0},{2,1},{3,2},{4,3},{5,4},{6,5},{7,6},{8,15},{9,8},{10,9... | collective-permute-start | bytes 98312 | tf_op jit(solution)/shard_map/ppermute | solution.py:51
  27.0 3.0 %collective-permute-start.3 = (f32[4,2048]{1,0:T(4,128)S(1)}, f32[4,2048]{1,0:T(4,128)S(1)}, u32[]{:S(2)}, u32[]{:S(2)}) collective-permute-start(f32[4,2048]{1,0:T(4,128)S(1)} %bitcast.152), channel_id=1, source_target_pairs={{0,4},{1,5},{2,6},{3,7},{4,0},{5,1},{6,2},{7,3},{8,12},{9,13},{10,... | collective-permute-start | bytes 98312 | tf_op jit(solution)/shard_map/ppermute | solution.py:51
  30.2 1.9 collective-permute-start.5
  32.1 1.2 collective-permute-start.6
  33.3 2.8 %collective-permute-done.4 = f32[4,2048]{1,0:T(4,128)S(1)} collective-permute-done((f32[4,2048]{1,0:T(4,128)S(1)}, f32[4,2048]{1,0:T(4,128)S(1)}, u32[]{:S(2)}, u32[]{:S(2)}) %collective-permute-start.4) | collective-permute-done | bytes 32800 | tf_op jit(solution)/shard_map/ppermute | solution.py:51
  36.1 0.9 collective-permute-done.5
  37.1 1.7 collective-permute-done.6
  39.0 1.6 collective-permute-start.7
  40.6 4.9 %collective-permute-done.7 = f32[1,32,2048]{2,1,0:T(8,128)S(1)} collective-permute-done((f32[1,32,2048]{2,1,0:T(8,128)S(1)}, f32[1,32,2048]{2,1,0:T(8,128)S(1)}, u32[]{:S(2)}, u32[]{:S(2)}) %collective-permute-start.7) | collective-permute-done | bytes 262176 | tf_op jit(solution)/shard_map/ppermute | solution.py:67
  45.7 1.7 collective-permute-done.8
  47.6 10.3 %fusion.9 = f32[2,2,128,512]{2,3,0,1:T(8,128)S(1)} fusion(f32[128,2048,1,1]{1,0,3,2:T(8,128)S(1)} %bitcast.145, f32[2,2,2,512,2048]{4,3,2,1,0:T(8,128)} %bitcast.143, s32[]{:T(128)S(6)} %select_n.219), kind=kOutput, calls=%fused_computation.10 | convolution fusion | flops 3221225472 | bytes 18874372 | tf_op jit(solution)/shard_map/mk,abik->bami/dot_general | solution.py:115
  58.1 3.9 %collective-permute-start.10 = (f32[128,512]{1,0:T(8,128)S(1)}, f32[128,512]{1,0:T(8,128)S(1)}, u32[]{:S(2)}, u32[]{:S(2)}) collective-permute-start(f32[128,512]{1,0:T(8,128)S(1)} %get-tuple-element.22), channel_id=1, source_target_pairs={{0,1},{1,5},{10,9},{11,13},{20,17},{21,21},{30,25},{31,29}} | collective-permute-start | bytes 786440 | tf_op jit(solution)/shard_map/ppermute | solution.py:127
  62.0 1.3 collective-permute-start.12
  63.3 1.3 collective-permute-start.11
  64.6 0.9 collective-permute-start.9
  65.5 10.3 %fusion.6 = f32[2,2,128,512]{2,3,0,1:T(8,128)S(1)} fusion(f32[128,2048,1,1]{1,0,3,2:T(8,128)S(1)} %bitcast.147, f32[2,2,2,512,2048]{4,3,2,1,0:T(8,128)} %bitcast.144, s32[]{:T(128)S(6)} %select_n.218), kind=kOutput, calls=%fused_computation.9 | convolution fusion | flops 3221225472 | bytes 18874372 | tf_op jit(solution)/shard_map/mk,abik->bami/dot_general | solution.py:118
  75.8 10.8 %collective-permute-done.10 = f32[128,512]{1,0:T(8,128)S(1)} collective-permute-done((f32[128,512]{1,0:T(8,128)S(1)}, f32[128,512]{1,0:T(8,128)S(1)}, u32[]{:S(2)}, u32[]{:S(2)}) %collective-permute-start.10) | collective-permute-done | bytes 262176 | tf_op jit(solution)/shard_map/ppermute | solution.py:127
  87.0 12.4 %collective-permute-done.14 = f32[2,128,512]{1,2,0:T(8,128)S(1)} collective-permute-done((f32[2,128,512]{1,2,0:T(8,128)S(1)}, f32[2,128,512]{1,2,0:T(8,128)S(1)}, u32[]{:S(2)}, u32[]{:S(2)}) %collective-permute-start.14) | collective-permute-done | bytes 524320 | tf_op jit(solution)/shard_map/ppermute | solution.py:43
  99.5 4.6 %collective-permute-start.15 = (f32[128,512]{0,1:T(8,128)S(1)}, f32[128,512]{0,1:T(8,128)S(1)}, u32[]{:S(2)}, u32[]{:S(2)}) collective-permute-start(f32[128,512]{0,1:T(8,128)S(1)} %dynamic-slice_bitcast_fusion.1), channel_id=1, source_target_pairs={{0,4},{1,5},{2,6},{3,7},{4,0},{5,1},{6,2},{7,3},{8,12},{9,13},{10,... | collective-permute-start | bytes 786440 | tf_op jit(solution)/shard_map/ppermute | solution.py:43
  104.0 10.5 %collective-permute-done.15 = f32[128,512]{0,1:T(8,128)S(1)} collective-permute-done((f32[128,512]{0,1:T(8,128)S(1)}, f32[128,512]{0,1:T(8,128)S(1)}, u32[]{:S(2)}, u32[]{:S(2)}) %collective-permute-start.15) | collective-permute-done | bytes 262176 | tf_op jit(solution)/shard_map/ppermute | solution.py:43
  114.5 0.7 bitcast_add_fusion.1
  115.6 1.3 fusion.46
  117.5 3.9 %collective-permute-done.16 = f32[136,128]{1,0:T(8,128)S(1)} collective-permute-done((f32[136,128]{1,0:T(8,128)S(1)}, f32[136,128]{1,0:T(8,128)S(1)}, u32[]{:S(2)}, u32[]{:S(2)}) %collective-permute-start.16) | collective-permute-done | bytes 69664 | tf_op jit(solution)/shard_map/ppermute | solution.py:31
  121.5 5.2 %collective-permute-done.17 = f32[136,128]{1,0:T(8,128)S(1)} collective-permute-done((f32[136,128]{1,0:T(8,128)S(1)}, f32[136,128]{1,0:T(8,128)S(1)}, u32[]{:S(2)}, u32[]{:S(2)}) %collective-permute-start.17) | collective-permute-done | bytes 69664 | tf_op jit(solution)/shard_map/ppermute | solution.py:31
  126.7 1.6 collective-permute-start.18
  128.3 8.0 %collective-permute-done.18 = f32[136,128]{1,0:T(8,128)S(1)} collective-permute-done((f32[136,128]{1,0:T(8,128)S(1)}, f32[136,128]{1,0:T(8,128)S(1)}, u32[]{:S(2)}, u32[]{:S(2)}) %collective-permute-start.18) | collective-permute-done | bytes 69664 | tf_op jit(solution)/shard_map/ppermute | solution.py:31
  136.4 1.2 collective-permute-done.19
  137.7 0.9 collective-permute-start.20
  138.6 3.5 %collective-permute-done.20 = f32[136,128]{1,0:T(8,128)S(1)} collective-permute-done((f32[136,128]{1,0:T(8,128)S(1)}, f32[136,128]{1,0:T(8,128)S(1)}, u32[]{:S(2)}, u32[]{:S(2)}) %collective-permute-start.20) | collective-permute-done | bytes 69664 | tf_op jit(solution)/shard_map/ppermute | solution.py:31
  142.3 11.7 %cholesky.16 = f32[128,128]{1,0:T(8,128)S(1)} custom-call(f32[128,128]{1,0:T(8,128)S(1)} %fusion.32), custom_call_target="Cholesky" | custom-call | tf_op jit(solution)/shard_map/jit(cholesky)/cholesky | solution.py:145
  155.4 10.5 %all-gather.2.cloned.1.call-done = f32[128,4096]{0,1:T(8,128)} async-done(((f32[128,512]{0,1:T(8,128)}), f32[128,4096]{0,1:T(8,128)}) %all-gather.2.cloned.1.call-update) | async-done | bytes 2097168 | tf_op jit(solution)/shard_map/all_gather | solution.py:142
  165.9 1.3 dynamic-slice_select_fusion
  167.2 3.5 %collective-permute-start.21 = (f32[128,2048]{0,1:T(8,128)S(1)}, f32[128,2048]{0,1:T(8,128)S(1)}, u32[]{:S(2)}, u32[]{:S(2)}) collective-permute-start(f32[128,2048]{0,1:T(8,128)S(1)} %dynamic-slice_select_fusion), channel_id=1, source_target_pairs={{0,16},{1,17},{10,26},{11,27},{20,4},{21,5},{30,14},{31,15}} | collective-permute-start | bytes 3145736 | tf_op jit(solution)/shard_map/ppermute | solution.py:23
  170.7 9.8 %custom-call.16 = f32[1,128,128]{1,2,0:T(8,128)S(1)} custom-call(f32[1,128,128]{2,1,0:T(8,128)S(1)} %select_bitcast_fusion), custom_call_target="InvertDiagBlocksLowerTriangular" | custom-call | tf_op jit(solution)/shard_map/jit(_cho_solve)/triangular_solve | solution.py:154
  180.5 2.4 %collective-permute-done.21 = f32[128,2048]{0,1:T(8,128)S(1)} collective-permute-done((f32[128,2048]{0,1:T(8,128)S(1)}, f32[128,2048]{0,1:T(8,128)S(1)}, u32[]{:S(2)}, u32[]{:S(2)}) %collective-permute-start.21) | collective-permute-done | bytes 1048608 | tf_op jit(solution)/shard_map/ppermute | solution.py:23
  182.9 1.4 fusion.65
  184.3 1.6 collective-permute-start.22
  186.6 1.4 dynamic-slice_add_fusion
  187.9 3.5 %fusion.28 = f32[128,4096]{1,0:T(8,128)S(1)} fusion(f32[128,4096]{0,1:T(8,128)} %all-gather.2.cloned.1.call-done, f32[1,128,128]{1,2,0:T(8,128)S(1)} %custom-call.16), kind=kOutput, calls=%fused_computation.47 | convolution fusion | flops 805306368 | bytes 4259840 | tf_op jit(solution)/shard_map/jit(_solve_triangular)/triangular_solve | solution.py:151
  191.5 1.1 fusion.17
  192.6 26.9 %convolution_subtract_fusion = f32[4096,2048]{1,0:T(8,128)} fusion(f32[4096,2048]{1,0:T(8,128)} %param.21, f32[128,4096]{1,0:T(8,128)S(1)} %fusion.28, f32[128,2048]{1,0:T(8,128)S(1)} %fusion.17), kind=kOutput, calls=%fused_computation.6 | convolution fusion | flops 6450839552 | bytes 70254592 | tf_op jit(solution)/shard_map/mi,mj->ij/dot_general | solution.py:153
  (91 shorter events, 6.4 us)
Async XLA Ops:
  7.2 7.4 %copy-start = (f32[4,128]{1,0:T(4,128)S(1)}, f32[4,128]{1,0:T(4,128)}, u32[]{:S(2)}) copy-start(f32[4,128]{1,0:T(4,128)} %param.18) | copy-start | bytes 6148
  7.2 158.7 %all-gather.2.cloned.1.call-start = ((), (), s32[]{:S(2)}) async-start(), calls=%async_computation | async-start | bytes 2359296 | tf_op jit(solution)/shard_map/all_gather | solution.py:142
  20.3 9.9 %collective-permute-start = (f32[4,2048]{1,0:T(4,128)S(1)}, f32[4,2048]{1,0:T(4,128)S(1)}, u32[]{:S(2)}, u32[]{:S(2)}) collective-permute-start(f32[4,2048]{1,0:T(4,128)S(1)} %bitcast.155), channel_id=1, source_target_pairs={{0,7},{1,0},{2,1},{3,2},{4,3},{5,4},{6,5},{7,6},{8,15},{9,8},{10,9... | collective-permute-start | bytes 98312 | tf_op jit(solution)/shard_map/ppermute | solution.py:51
  26.3 5.7 %collective-permute-start.1 = (f32[4,2048]{1,0:T(4,128)S(1)}, f32[4,2048]{1,0:T(4,128)S(1)}, u32[]{:S(2)}, u32[]{:S(2)}) collective-permute-start(f32[4,2048]{1,0:T(4,128)S(1)} %bitcast.154), channel_id=1, source_target_pairs={{0,6},{1,7},{2,0},{3,1},{4,2},{5,3},{6,4},{7,5},{8,14},{9,15},{10,... | collective-permute-start | bytes 98312 | tf_op jit(solution)/shard_map/ppermute | solution.py:51
  26.9 6.4 %collective-permute-start.2 = (f32[4,2048]{1,0:T(4,128)S(1)}, f32[4,2048]{1,0:T(4,128)S(1)}, u32[]{:S(2)}, u32[]{:S(2)}) collective-permute-start(f32[4,2048]{1,0:T(4,128)S(1)} %bitcast.151), channel_id=1, source_target_pairs={{0,5},{1,6},{2,7},{3,0},{4,1},{5,2},{6,3},{7,4},{8,13},{9,14},{10,... | collective-permute-start | bytes 98312 | tf_op jit(solution)/shard_map/ppermute | solution.py:51
  27.0 6.3 %collective-permute-start.3 = (f32[4,2048]{1,0:T(4,128)S(1)}, f32[4,2048]{1,0:T(4,128)S(1)}, u32[]{:S(2)}, u32[]{:S(2)}) collective-permute-start(f32[4,2048]{1,0:T(4,128)S(1)} %bitcast.152), channel_id=1, source_target_pairs={{0,4},{1,5},{2,6},{3,7},{4,0},{5,1},{6,2},{7,3},{8,12},{9,13},{10,... | collective-permute-start | bytes 98312 | tf_op jit(solution)/shard_map/ppermute | solution.py:51
  30.0 6.1 %collective-permute-start.4 = (f32[4,2048]{1,0:T(4,128)S(1)}, f32[4,2048]{1,0:T(4,128)S(1)}, u32[]{:S(2)}, u32[]{:S(2)}) collective-permute-start(f32[4,2048]{1,0:T(4,128)S(1)} %bitcast.153), channel_id=1, source_target_pairs={{0,3},{1,4},{2,5},{3,6},{4,7},{5,0},{6,1},{7,2},{8,11},{9,12},{10,... | collective-permute-start | bytes 98312 | tf_op jit(solution)/shard_map/ppermute | solution.py:51
  30.2 6.9 %collective-permute-start.5 = (f32[4,2048]{1,0:T(4,128)S(1)}, f32[4,2048]{1,0:T(4,128)S(1)}, u32[]{:S(2)}, u32[]{:S(2)}) collective-permute-start(f32[4,2048]{1,0:T(4,128)S(1)} %bitcast.157), channel_id=1, source_target_pairs={{0,2},{1,3},{2,4},{3,5},{4,6},{5,7},{6,0},{7,1},{8,10},{9,11},{10,... | collective-permute-start | bytes 98312 | tf_op jit(solution)/shard_map/ppermute | solution.py:51
  32.1 6.7 %collective-permute-start.6 = (f32[4,2048]{1,0:T(4,128)S(1)}, f32[4,2048]{1,0:T(4,128)S(1)}, u32[]{:S(2)}, u32[]{:S(2)}) collective-permute-start(f32[4,2048]{1,0:T(4,128)S(1)} %bitcast.156), channel_id=1, source_target_pairs={{0,1},{1,2},{2,3},{3,4},{4,5},{5,6},{6,7},{7,0},{8,9},{9,10},{10,1... | collective-permute-start | bytes 98312 | tf_op jit(solution)/shard_map/ppermute | solution.py:51
  39.0 6.4 %collective-permute-start.7 = (f32[1,32,2048]{2,1,0:T(8,128)S(1)}, f32[1,32,2048]{2,1,0:T(8,128)S(1)}, u32[]{:S(2)}, u32[]{:S(2)}) collective-permute-start(f32[1,32,2048]{2,1,0:T(8,128)S(1)} %broadcast_in_dim_reshape.3), channel_id=1, source_target_pairs={{0,16},{8,24},{16,0},{24,8},{1,17},{9,25},{17,1},{25,9},{2,18},{10... | collective-permute-start | bytes 786440 | tf_op jit(solution)/shard_map/ppermute | solution.py:67
  45.5 2.0 collective-permute-start.8
  57.9 28.8 %collective-permute-start.13 = (f32[2,2,128,512]{2,3,0,1:T(8,128)S(1)}, f32[2,2,128,512]{2,3,0,1:T(8,128)S(1)}, u32[]{:S(2)}, u32[]{:S(2)}) collective-permute-start(f32[2,2,128,512]{2,3,0,1:T(8,128)S(1)} %fusion.9), channel_id=1, source_target_pairs={{0,1},{1,0},{2,3},{3,2},{4,5},{5,4},{6,7},{7,6},{8,9},{9,8},{10,11... | collective-permute-start | bytes 3145736 | tf_op jit(solution)/shard_map/ppermute | solution.py:116
  58.1 28.5 %collective-permute-start.10 = (f32[128,512]{1,0:T(8,128)S(1)}, f32[128,512]{1,0:T(8,128)S(1)}, u32[]{:S(2)}, u32[]{:S(2)}) collective-permute-start(f32[128,512]{1,0:T(8,128)S(1)} %get-tuple-element.22), channel_id=1, source_target_pairs={{0,1},{1,5},{10,9},{11,13},{20,17},{21,21},{30,25},{31,29}} | collective-permute-start | bytes 786440 | tf_op jit(solution)/shard_map/ppermute | solution.py:127
  62.0 24.6 %collective-permute-start.12 = (f32[128,512]{1,0:T(8,128)S(1)}, f32[128,512]{1,0:T(8,128)S(1)}, u32[]{:S(2)}, u32[]{:S(2)}) collective-permute-start(f32[128,512]{1,0:T(8,128)S(1)} %get-tuple-element.23), channel_id=1, source_target_pairs={{0,3},{1,7},{10,11},{11,15},{20,19},{21,23},{30,27},{31,31}} | collective-permute-start | bytes 786440 | tf_op jit(solution)/shard_map/ppermute | solution.py:127
  63.3 23.3 %collective-permute-start.11 = (f32[128,512]{1,0:T(8,128)S(1)}, f32[128,512]{1,0:T(8,128)S(1)}, u32[]{:S(2)}, u32[]{:S(2)}) collective-permute-start(f32[128,512]{1,0:T(8,128)S(1)} %get-tuple-element.24), channel_id=1, source_target_pairs={{0,2},{1,6},{10,10},{11,14},{20,18},{21,22},{30,26},{31,30}} | collective-permute-start | bytes 786440 | tf_op jit(solution)/shard_map/ppermute | solution.py:127
  64.6 22.0 %collective-permute-start.9 = (f32[128,512]{1,0:T(8,128)S(1)}, f32[128,512]{1,0:T(8,128)S(1)}, u32[]{:S(2)}, u32[]{:S(2)}) collective-permute-start(f32[128,512]{1,0:T(8,128)S(1)} %get-tuple-element.25), channel_id=1, source_target_pairs={{0,0},{1,4},{10,8},{11,12},{20,16},{21,20},{30,24},{31,28}} | collective-permute-start | bytes 786440 | tf_op jit(solution)/shard_map/ppermute | solution.py:127
  75.8 39.5 %copy-start.4 = (s32[256]{0:T(256)S(1)}, s32[256]{0:T(256)}, u32[]{:S(2)}) copy-start(s32[256]{0:T(256)} %param.15) | copy-start | bytes 3076
  75.8 66.3 %copy-start.3 = (f32[128]{0:T(128)S(1)}, f32[128]{0:T(128)}, u32[]{:S(2)}) copy-start(f32[128]{0:T(128)} %param.20) | copy-start | bytes 1540
  75.8 110.1 %copy-start.5 = (f32[128]{0:T(128)S(1)}, f32[128]{0:T(128)}, u32[]{:S(2)}) copy-start(f32[128]{0:T(128)} %param.19) | copy-start | bytes 1540
  86.9 12.5 %collective-permute-start.14 = (f32[2,128,512]{1,2,0:T(8,128)S(1)}, f32[2,128,512]{1,2,0:T(8,128)S(1)}, u32[]{:S(2)}, u32[]{:S(2)}) collective-permute-start(f32[2,128,512]{1,2,0:T(8,128)S(1)} %dynamic-slice_bitcast_fusion), channel_id=1, source_target_pairs={{0,2},{1,3},{2,0},{3,1},{4,6},{5,7},{6,4},{7,5},{8,10},{9,11},{10,... | collective-permute-start | bytes 1572872 | tf_op jit(solution)/shard_map/ppermute | solution.py:43
  99.5 15.0 %collective-permute-start.15 = (f32[128,512]{0,1:T(8,128)S(1)}, f32[128,512]{0,1:T(8,128)S(1)}, u32[]{:S(2)}, u32[]{:S(2)}) collective-permute-start(f32[128,512]{0,1:T(8,128)S(1)} %dynamic-slice_bitcast_fusion.1), channel_id=1, source_target_pairs={{0,4},{1,5},{2,6},{3,7},{4,0},{5,1},{6,2},{7,3},{8,12},{9,13},{10,... | collective-permute-start | bytes 786440 | tf_op jit(solution)/shard_map/ppermute | solution.py:43
  115.2 71.0 %copy-start.2 = (f32[128,512]{0,1:T(8,128)S(1)}, f32[128,512]{0,1:T(8,128)}, u32[]{:S(2)}) copy-start(f32[128,512]{0,1:T(8,128)} %bitcast_add_fusion.1) | copy-start | bytes 786436
  117.0 4.4 %collective-permute-start.16 = (f32[136,128]{1,0:T(8,128)S(1)}, f32[136,128]{1,0:T(8,128)S(1)}, u32[]{:S(2)}, u32[]{:S(2)}) collective-permute-start(f32[136,128]{1,0:T(8,128)S(1)} %pad_maximum_fusion), channel_id=1, source_target_pairs={{0,1},{1,0},{2,3},{3,2},{4,5},{5,4},{6,7},{7,6},{8,9},{9,8},{10,11... | collective-permute-start | bytes 208904 | tf_op jit(solution)/shard_map/ppermute | solution.py:31
  121.4 5.3 %collective-permute-start.17 = (f32[136,128]{1,0:T(8,128)S(1)}, f32[136,128]{1,0:T(8,128)S(1)}, u32[]{:S(2)}, u32[]{:S(2)}) collective-permute-start(f32[136,128]{1,0:T(8,128)S(1)} %fusion.44), channel_id=1, source_target_pairs={{0,2},{1,3},{2,0},{3,1},{4,6},{5,7},{6,4},{7,5},{8,10},{9,11},{10,... | collective-permute-start | bytes 208904 | tf_op jit(solution)/shard_map/ppermute | solution.py:31
  126.7 9.6 %collective-permute-start.18 = (f32[136,128]{1,0:T(8,128)S(1)}, f32[136,128]{1,0:T(8,128)S(1)}, u32[]{:S(2)}, u32[]{:S(2)}) collective-permute-start(f32[136,128]{1,0:T(8,128)S(1)} %add.249), channel_id=1, source_target_pairs={{0,4},{1,5},{2,6},{3,7},{4,0},{5,1},{6,2},{7,3},{8,12},{9,13},{10,... | collective-permute-start | bytes 208904 | tf_op jit(solution)/shard_map/ppermute | solution.py:31
  136.3 1.3 collective-permute-start.19
  137.7 4.4 %collective-permute-start.20 = (f32[136,128]{1,0:T(8,128)S(1)}, f32[136,128]{1,0:T(8,128)S(1)}, u32[]{:S(2)}, u32[]{:S(2)}) collective-permute-start(f32[136,128]{1,0:T(8,128)S(1)} %add.251), channel_id=1, source_target_pairs={{0,16},{8,24},{16,0},{24,8},{1,17},{9,25},{17,1},{25,9},{2,18},{10... | collective-permute-start | bytes 208904 | tf_op jit(solution)/shard_map/ppermute | solution.py:31
  167.2 15.7 %collective-permute-start.21 = (f32[128,2048]{0,1:T(8,128)S(1)}, f32[128,2048]{0,1:T(8,128)S(1)}, u32[]{:S(2)}, u32[]{:S(2)}) collective-permute-start(f32[128,2048]{0,1:T(8,128)S(1)} %dynamic-slice_select_fusion), channel_id=1, source_target_pairs={{0,16},{1,17},{10,26},{11,27},{20,4},{21,5},{30,14},{31,15}} | collective-permute-start | bytes 3145736 | tf_op jit(solution)/shard_map/ppermute | solution.py:23
  184.3 7.2 %collective-permute-start.22 = (f32[128,2048]{0,1:T(8,128)S(1)}, f32[128,2048]{0,1:T(8,128)S(1)}, u32[]{:S(2)}, u32[]{:S(2)}) collective-permute-start(f32[128,2048]{0,1:T(8,128)S(1)} %fusion.65), channel_id=1, source_target_pairs={{0,8},{16,24},{1,9},{17,25},{10,2},{26,18},{11,3},{27,19},{20,28},... | collective-permute-start | bytes 3145736 | tf_op jit(solution)/shard_map/ppermute | solution.py:23
  192.6 26.9 %copy-start.1 = (f32[4,128]{1,0:T(4,128)S(1)}, f32[4,128]{1,0:T(4,128)}, u32[]{:S(2)}) copy-start(f32[4,128]{1,0:T(4,128)} %param.18) | copy-start | bytes 6148
Sparse Core Ops, SparseCore 0:
  115.4 50.4 all-gather.1

commit v14 on v13

--- a/solution.py
+++ b/solution.py
@@ -143,13 +143,14 @@
     gram = small[:m_all] + jnp.diag(noise)
     pred_all = small[m_all]
     lower = jnp.linalg.cholesky(gram)
-    lower, gain_rows_t = lax.optimization_barrier((lower, gain_rows_t))
+    lower_inv = jax.scipy.linalg.solve_triangular(lower, jnp.eye(m_all, dtype=jnp.float32), lower=True)
+    lower, lower_inv, gain_rows_t = lax.optimization_barrier((lower, lower_inv, gain_rows_t))
     half_t = lax.dynamic_slice_in_dim(gain_rows_t, col_id % factor * col_w, col_w, 1)
     mine = row_id == col_id // factor
     masked = jnp.where(mine, half_t, jnp.zeros_like(half_t))
     gain_col_t = broadcast_rows(masked, n_row, n_col, factor)
-    white_row = jax.scipy.linalg.solve_triangular(lower, gain_rows_t, lower=True)
-    white_col = jax.scipy.linalg.solve_triangular(lower, gain_col_t, lower=True)
+    white_row = jnp.dot(lower_inv, gain_rows_t, precision=hi)
+    white_col = jnp.dot(lower_inv, gain_col_t, precision=hi)
     new_cov = cov - jnp.einsum("mi,mj->ij", white_row, white_col, precision=mid)
     coef = jax.scipy.linalg.cho_solve((lower, True), targets - pred_all)
     own_weights = lax.dynamic_slice_in_dim(weights.reshape(-1), device_id * blk, blk, 0)

time: 227 us -> 227 us (level)
  waiting for transfers between devices: 80.3 us -> 70.1 us
  other arithmetic: 34.7 us -> 44.5 us
    another operation x1 -> x3, other arithmetic: 0.69 us -> 11.2 us  [the longest x2 10.5 us: on_device(): jax.scipy.linalg.solve_triangular(lower, jnp.eye(m_all, dtype=jnp.float32...]
    all_gather x1, waiting for transfers between devices: 10.5 us -> 0.46 us  [on_device(): gain_rows_t = lax.all_gather(gain_own_t, 'col', axis=1, tiled=True)]
    dot_general x0 -> x2, matrix products: none -> 4.5 us  [the longest x1 3.51 us: on_device(): white_row = jnp.dot(lower_inv, gain_rows_t, precision=hi)]
    another operation x2 -> x1, matrix products: 4.65 us -> 0.25 us  [on_device(): jax.scipy.linalg.solve_triangular(lower, jnp.eye(m_all, dtype=jnp.float32...]
  transfers between devices with their start and end apart: 24 -> 24, of which waited for: 15 -> 15; matrix products, arithmetic and copies ran while one was open for 18% -> 23% of each run, Pallas kernels for 0% -> 0%
where the time goes in v14:
time: 227 us; the launch traced here: 226 us
  waiting for transfers between devices  70.1 us (31%)
  matrix products  59.6 us (26%)
  other arithmetic  44.5 us (20%)
  starting transfers between devices  34.7 us (15%)
  between operations  14.9 us (7%)
    dot_general x1, matrix products, on_device(): new_cov = cov - jnp.einsum('mi,mj->ij', white_row, white_col, precision=mid)  26.9 us
    ppermute x2, waiting for transfers between devices, halving_scatter(): x = keep + lax.ppermute(send, axis, [(i, i ^ bit) for i in range(size)])  22.8 us
    ppermute x5, waiting for transfers between devices, butterfly_sum(): buf = buf + lax.ppermute(buf, axis, [(i, i ^ bit) for i in range(size)])  21.8 us
    ppermute x7, starting transfers between devices, shift_all_to_all(): lax.ppermute(piece, axis, [(i, (i - k) % size) for i in range(size)])  12.8 us
    another operation x3, other arithmetic, on_device(): lower = jnp.linalg.cholesky(gram)  12.4 us
    ppermute x4, waiting for transfers between devices, on_device(): got = lax.ppermute(grad_col[:, t * blk:(t + 1) * blk], ('row', 'col'), perm)  10.8 us
    another operation x2, other arithmetic, on_device(): jax.scipy.linalg.solve_triangular(lower, jnp.eye(m_all, dtype=jnp.float32...  10.5 us
    dot_general x1, matrix products, on_device(): send_part = jnp.einsum(spec, grad_col, send_rows, precision=mid)  10.3 us
  transfers between devices with their start and end apart: 24, of which 15 were waited for; matrix products, arithmetic and copies ran while one was open for 23% of the time, Pallas kernels for 0%

profile of v14, /device:TPU:0, one launch (start us, length us, event | category | flops | bytes accessed | tf_op | source)
XLA Modules:
  0.0 226.0 jit_solution(8891747541197337779)
XLA Ops:
  7.3 0.7 fusion.35
  8.0 0.9 copy.18
  8.9 5.7 %convert_reduce_fusion = f32[256,256]{1,0:T(8,128)S(1)} fusion(s32[256,32]{1,0:T(8,128)S(1)} %copy.18), kind=kLoop, calls=%fused_computation.7 | loop fusion | flops 6225920 | bytes 294912 | tf_op jit(solution)/shard_map/reduce_sum | solution.py:87
  14.6 1.0 fusion.26
  15.6 1.2 convolution_multiply_fusion.2
  16.8 1.3 fusion.14
  18.2 1.2 multiply_reduce_fusion
  20.3 6.1 %collective-permute-start = (f32[4,2048]{1,0:T(4,128)S(1)}, f32[4,2048]{1,0:T(4,128)S(1)}, u32[]{:S(2)}, u32[]{:S(2)}) collective-permute-start(f32[4,2048]{1,0:T(4,128)S(1)} %bitcast.158), channel_id=1, source_target_pairs={{0,7},{1,0},{2,1},{3,2},{4,3},{5,4},{6,5},{7,6},{8,15},{9,8},{10,9... | collective-permute-start | bytes 98312 | tf_op jit(solution)/shard_map/ppermute | solution.py:51
  27.0 3.0 %collective-permute-start.3 = (f32[4,2048]{1,0:T(4,128)S(1)}, f32[4,2048]{1,0:T(4,128)S(1)}, u32[]{:S(2)}, u32[]{:S(2)}) collective-permute-start(f32[4,2048]{1,0:T(4,128)S(1)} %bitcast.155), channel_id=1, source_target_pairs={{0,4},{1,5},{2,6},{3,7},{4,0},{5,1},{6,2},{7,3},{8,12},{9,13},{10,... | collective-permute-start | bytes 98312 | tf_op jit(solution)/shard_map/ppermute | solution.py:51
  30.2 1.9 collective-permute-start.5
  32.1 1.2 collective-permute-start.6
  33.3 2.8 %collective-permute-done.4 = f32[4,2048]{1,0:T(4,128)S(1)} collective-permute-done((f32[4,2048]{1,0:T(4,128)S(1)}, f32[4,2048]{1,0:T(4,128)S(1)}, u32[]{:S(2)}, u32[]{:S(2)}) %collective-permute-start.4) | collective-permute-done | bytes 32800 | tf_op jit(solution)/shard_map/ppermute | solution.py:51
  36.1 0.9 collective-permute-done.5
  37.1 1.7 collective-permute-done.6
  39.0 1.6 collective-permute-start.7
  40.6 4.9 %collective-permute-done.7 = f32[1,32,2048]{2,1,0:T(8,128)S(1)} collective-permute-done((f32[1,32,2048]{2,1,0:T(8,128)S(1)}, f32[1,32,2048]{2,1,0:T(8,128)S(1)}, u32[]{:S(2)}, u32[]{:S(2)}) %collective-permute-start.7) | collective-permute-done | bytes 262176 | tf_op jit(solution)/shard_map/ppermute | solution.py:67
  45.7 1.7 collective-permute-done.8
  47.6 10.3 %fusion.9 = f32[2,2,128,512]{2,3,0,1:T(8,128)S(1)} fusion(f32[128,2048,1,1]{1,0,3,2:T(8,128)S(1)} %bitcast.148, f32[2,2,2,512,2048]{4,3,2,1,0:T(8,128)} %bitcast.146, s32[]{:T(128)S(6)} %select_n.219), kind=kOutput, calls=%fused_computation.10 | convolution fusion | flops 3221225472 | bytes 18874372 | tf_op jit(solution)/shard_map/mk,abik->bami/dot_general | solution.py:115
  58.1 3.9 %collective-permute-start.10 = (f32[128,512]{1,0:T(8,128)S(1)}, f32[128,512]{1,0:T(8,128)S(1)}, u32[]{:S(2)}, u32[]{:S(2)}) collective-permute-start(f32[128,512]{1,0:T(8,128)S(1)} %get-tuple-element.26), channel_id=1, source_target_pairs={{0,1},{1,5},{10,9},{11,13},{20,17},{21,21},{30,25},{31,29}} | collective-permute-start | bytes 786440 | tf_op jit(solution)/shard_map/ppermute | solution.py:127
  62.0 1.3 collective-permute-start.12
  63.3 1.3 collective-permute-start.11
  64.6 0.9 collective-permute-start.9
  65.5 10.3 %fusion.6 = f32[2,2,128,512]{2,3,0,1:T(8,128)S(1)} fusion(f32[128,2048,1,1]{1,0,3,2:T(8,128)S(1)} %bitcast.150, f32[2,2,2,512,2048]{4,3,2,1,0:T(8,128)} %bitcast.147, s32[]{:T(128)S(6)} %select_n.218), kind=kOutput, calls=%fused_computation.9 | convolution fusion | flops 3221225472 | bytes 18874372 | tf_op jit(solution)/shard_map/mk,abik->bami/dot_general | solution.py:118
  75.8 10.8 %collective-permute-done.10 = f32[128,512]{1,0:T(8,128)S(1)} collective-permute-done((f32[128,512]{1,0:T(8,128)S(1)}, f32[128,512]{1,0:T(8,128)S(1)}, u32[]{:S(2)}, u32[]{:S(2)}) %collective-permute-start.10) | collective-permute-done | bytes 262176 | tf_op jit(solution)/shard_map/ppermute | solution.py:127
  87.0 12.4 %collective-permute-done.14 = f32[2,128,512]{1,2,0:T(8,128)S(1)} collective-permute-done((f32[2,128,512]{1,2,0:T(8,128)S(1)}, f32[2,128,512]{1,2,0:T(8,128)S(1)}, u32[]{:S(2)}, u32[]{:S(2)}) %collective-permute-start.14) | collective-permute-done | bytes 524320 | tf_op jit(solution)/shard_map/ppermute | solution.py:43
  99.5 4.6 %collective-permute-start.15 = (f32[128,512]{0,1:T(8,128)S(1)}, f32[128,512]{0,1:T(8,128)S(1)}, u32[]{:S(2)}, u32[]{:S(2)}) collective-permute-start(f32[128,512]{0,1:T(8,128)S(1)} %dynamic-slice_bitcast_fusion.1), channel_id=1, source_target_pairs={{0,4},{1,5},{2,6},{3,7},{4,0},{5,1},{6,2},{7,3},{8,12},{9,13},{10,... | collective-permute-start | bytes 786440 | tf_op jit(solution)/shard_map/ppermute | solution.py:43
  104.0 10.5 %collective-permute-done.15 = f32[128,512]{0,1:T(8,128)S(1)} collective-permute-done((f32[128,512]{0,1:T(8,128)S(1)}, f32[128,512]{0,1:T(8,128)S(1)}, u32[]{:S(2)}, u32[]{:S(2)}) %collective-permute-start.15) | collective-permute-done | bytes 262176 | tf_op jit(solution)/shard_map/ppermute | solution.py:43
  114.5 0.7 bitcast_add_fusion.1
  115.6 1.3 fusion.45
  117.5 3.9 %collective-permute-done.16 = f32[136,128]{1,0:T(8,128)S(1)} collective-permute-done((f32[136,128]{1,0:T(8,128)S(1)}, f32[136,128]{1,0:T(8,128)S(1)}, u32[]{:S(2)}, u32[]{:S(2)}) %collective-permute-start.16) | collective-permute-done | bytes 69664 | tf_op jit(solution)/shard_map/ppermute | solution.py:31
  121.5 5.2 %collective-permute-done.17 = f32[136,128]{1,0:T(8,128)S(1)} collective-permute-done((f32[136,128]{1,0:T(8,128)S(1)}, f32[136,128]{1,0:T(8,128)S(1)}, u32[]{:S(2)}, u32[]{:S(2)}) %collective-permute-start.17) | collective-permute-done | bytes 69664 | tf_op jit(solution)/shard_map/ppermute | solution.py:31
  126.7 1.6 collective-permute-start.18
  128.3 8.0 %collective-permute-done.18 = f32[136,128]{1,0:T(8,128)S(1)} collective-permute-done((f32[136,128]{1,0:T(8,128)S(1)}, f32[136,128]{1,0:T(8,128)S(1)}, u32[]{:S(2)}, u32[]{:S(2)}) %collective-permute-start.18) | collective-permute-done | bytes 69664 | tf_op jit(solution)/shard_map/ppermute | solution.py:31
  136.4 1.2 collective-permute-done.19
  137.7 0.9 collective-permute-start.20
  138.6 3.5 %collective-permute-done.20 = f32[136,128]{1,0:T(8,128)S(1)} collective-permute-done((f32[136,128]{1,0:T(8,128)S(1)}, f32[136,128]{1,0:T(8,128)S(1)}, u32[]{:S(2)}, u32[]{:S(2)}) %collective-permute-start.20) | collective-permute-done | bytes 69664 | tf_op jit(solution)/shard_map/ppermute | solution.py:31
  142.3 11.7 %cholesky.17 = f32[128,128]{1,0:T(8,128)S(1)} custom-call(f32[128,128]{1,0:T(8,128)S(1)} %fusion.31), custom_call_target="Cholesky" | custom-call | tf_op jit(solution)/shard_map/jit(cholesky)/cholesky | solution.py:145
  155.4 9.8 %custom-call.14 = f32[1,128,128]{1,2,0:T(8,128)S(1)} custom-call(f32[1,128,128]{2,1,0:T(8,128)S(1)} %get-tuple-element.24), custom_call_target="InvertDiagBlocksLowerTriangular" | custom-call | tf_op jit(solution)/shard_map/jit(_solve_triangular)/triangular_solve | solution.py:146
  165.9 1.3 dynamic-slice_select_fusion
  167.2 3.7 %collective-permute-start.21 = (f32[128,2048]{0,1:T(8,128)S(1)}, f32[128,2048]{0,1:T(8,128)S(1)}, u32[]{:S(2)}, u32[]{:S(2)}) collective-permute-start(f32[128,2048]{0,1:T(8,128)S(1)} %dynamic-slice_select_fusion), channel_id=1, source_target_pairs={{0,16},{1,17},{10,26},{11,27},{20,4},{21,5},{30,14},{31,15}} | collective-permute-start | bytes 3145736 | tf_op jit(solution)/shard_map/ppermute | solution.py:23
  170.9 9.8 %custom-call.15 = f32[1,128,128]{1,2,0:T(8,128)S(1)} custom-call(f32[1,128,128]{2,1,0:T(8,128)S(1)} %select_bitcast_fusion), custom_call_target="InvertDiagBlocksLowerTriangular" | custom-call | tf_op jit(solution)/shard_map/jit(_cho_solve)/triangular_solve | solution.py:155
  180.7 2.2 collective-permute-done.21
  182.9 1.4 fusion.67
  184.3 1.4 collective-permute-start.22
  186.4 1.4 dynamic-slice_add_fusion
  187.8 3.5 %fusion.47 = f32[128,4096]{1,0:T(8,128)S(1)} fusion(f32[128,128]{1,0:T(8,128)S(1)} %fusion.29, f32[128,4096]{0,1:T(8,128)} %all-gather.2.cloned.1.call-done), kind=kOutput, calls=%fused_computation.108 | convolution fusion | flops 805306368 | bytes 4259840 | tf_op jit(solution)/shard_map/dot_general | solution.py:152
  191.3 1.0 fusion.17
  192.3 26.9 %convolution_subtract_fusion = f32[4096,2048]{1,0:T(8,128)} fusion(f32[4096,2048]{1,0:T(8,128)} %param.21, f32[128,4096]{1,0:T(8,128)S(1)} %fusion.47, f32[128,2048]{1,0:T(8,128)S(1)} %fusion.17), kind=kOutput, calls=%fused_computation.6 | convolution fusion | flops 6450839552 | bytes 70254592 | tf_op jit(solution)/shard_map/mi,mj->ij/dot_general | solution.py:154
  (93 shorter events, 7.1 us)
Async XLA Ops:
  7.2 7.4 %copy-start = (f32[4,128]{1,0:T(4,128)S(1)}, f32[4,128]{1,0:T(4,128)}, u32[]{:S(2)}) copy-start(f32[4,128]{1,0:T(4,128)} %param.18) | copy-start | bytes 6148
  7.2 158.7 %all-gather.2.cloned.1.call-start = ((), (), s32[]{:S(2)}) async-start(), calls=%async_computation | async-start | bytes 2359296 | tf_op jit(solution)/shard_map/all_gather | solution.py:142
  20.3 9.9 %collective-permute-start = (f32[4,2048]{1,0:T(4,128)S(1)}, f32[4,2048]{1,0:T(4,128)S(1)}, u32[]{:S(2)}, u32[]{:S(2)}) collective-permute-start(f32[4,2048]{1,0:T(4,128)S(1)} %bitcast.158), channel_id=1, source_target_pairs={{0,7},{1,0},{2,1},{3,2},{4,3},{5,4},{6,5},{7,6},{8,15},{9,8},{10,9... | collective-permute-start | bytes 98312 | tf_op jit(solution)/shard_map/ppermute | solution.py:51
  26.3 5.7 %collective-permute-start.1 = (f32[4,2048]{1,0:T(4,128)S(1)}, f32[4,2048]{1,0:T(4,128)S(1)}, u32[]{:S(2)}, u32[]{:S(2)}) collective-permute-start(f32[4,2048]{1,0:T(4,128)S(1)} %bitcast.157), channel_id=1, source_target_pairs={{0,6},{1,7},{2,0},{3,1},{4,2},{5,3},{6,4},{7,5},{8,14},{9,15},{10,... | collective-permute-start | bytes 98312 | tf_op jit(solution)/shard_map/ppermute | solution.py:51
  26.9 6.4 %collective-permute-start.2 = (f32[4,2048]{1,0:T(4,128)S(1)}, f32[4,2048]{1,0:T(4,128)S(1)}, u32[]{:S(2)}, u32[]{:S(2)}) collective-permute-start(f32[4,2048]{1,0:T(4,128)S(1)} %bitcast.154), channel_id=1, source_target_pairs={{0,5},{1,6},{2,7},{3,0},{4,1},{5,2},{6,3},{7,4},{8,13},{9,14},{10,... | collective-permute-start | bytes 98312 | tf_op jit(solution)/shard_map/ppermute | solution.py:51
  27.0 6.3 %collective-permute-start.3 = (f32[4,2048]{1,0:T(4,128)S(1)}, f32[4,2048]{1,0:T(4,128)S(1)}, u32[]{:S(2)}, u32[]{:S(2)}) collective-permute-start(f32[4,2048]{1,0:T(4,128)S(1)} %bitcast.155), channel_id=1, source_target_pairs={{0,4},{1,5},{2,6},{3,7},{4,0},{5,1},{6,2},{7,3},{8,12},{9,13},{10,... | collective-permute-start | bytes 98312 | tf_op jit(solution)/shard_map/ppermute | solution.py:51
  30.0 6.1 %collective-permute-start.4 = (f32[4,2048]{1,0:T(4,128)S(1)}, f32[4,2048]{1,0:T(4,128)S(1)}, u32[]{:S(2)}, u32[]{:S(2)}) collective-permute-start(f32[4,2048]{1,0:T(4,128)S(1)} %bitcast.156), channel_id=1, source_target_pairs={{0,3},{1,4},{2,5},{3,6},{4,7},{5,0},{6,1},{7,2},{8,11},{9,12},{10,... | collective-permute-start | bytes 98312 | tf_op jit(solution)/shard_map/ppermute | solution.py:51
  30.2 6.9 %collective-permute-start.5 = (f32[4,2048]{1,0:T(4,128)S(1)}, f32[4,2048]{1,0:T(4,128)S(1)}, u32[]{:S(2)}, u32[]{:S(2)}) collective-permute-start(f32[4,2048]{1,0:T(4,128)S(1)} %bitcast.160), channel_id=1, source_target_pairs={{0,2},{1,3},{2,4},{3,5},{4,6},{5,7},{6,0},{7,1},{8,10},{9,11},{10,... | collective-permute-start | bytes 98312 | tf_op jit(solution)/shard_map/ppermute | solution.py:51
  32.1 6.7 %collective-permute-start.6 = (f32[4,2048]{1,0:T(4,128)S(1)}, f32[4,2048]{1,0:T(4,128)S(1)}, u32[]{:S(2)}, u32[]{:S(2)}) collective-permute-start(f32[4,2048]{1,0:T(4,128)S(1)} %bitcast.159), channel_id=1, source_target_pairs={{0,1},{1,2},{2,3},{3,4},{4,5},{5,6},{6,7},{7,0},{8,9},{9,10},{10,1... | collective-permute-start | bytes 98312 | tf_op jit(solution)/shard_map/ppermute | solution.py:51
  39.0 6.4 %collective-permute-start.7 = (f32[1,32,2048]{2,1,0:T(8,128)S(1)}, f32[1,32,2048]{2,1,0:T(8,128)S(1)}, u32[]{:S(2)}, u32[]{:S(2)}) collective-permute-start(f32[1,32,2048]{2,1,0:T(8,128)S(1)} %broadcast_in_dim_reshape.3), channel_id=1, source_target_pairs={{0,16},{8,24},{16,0},{24,8},{1,17},{9,25},{17,1},{25,9},{2,18},{10... | collective-permute-start | bytes 786440 | tf_op jit(solution)/shard_map/ppermute | solution.py:67
  45.5 2.0 collective-permute-start.8
  57.9 28.8 %collective-permute-start.13 = (f32[2,2,128,512]{2,3,0,1:T(8,128)S(1)}, f32[2,2,128,512]{2,3,0,1:T(8,128)S(1)}, u32[]{:S(2)}, u32[]{:S(2)}) collective-permute-start(f32[2,2,128,512]{2,3,0,1:T(8,128)S(1)} %fusion.9), channel_id=1, source_target_pairs={{0,1},{1,0},{2,3},{3,2},{4,5},{5,4},{6,7},{7,6},{8,9},{9,8},{10,11... | collective-permute-start | bytes 3145736 | tf_op jit(solution)/shard_map/ppermute | solution.py:116
  58.1 28.5 %collective-permute-start.10 = (f32[128,512]{1,0:T(8,128)S(1)}, f32[128,512]{1,0:T(8,128)S(1)}, u32[]{:S(2)}, u32[]{:S(2)}) collective-permute-start(f32[128,512]{1,0:T(8,128)S(1)} %get-tuple-element.26), channel_id=1, source_target_pairs={{0,1},{1,5},{10,9},{11,13},{20,17},{21,21},{30,25},{31,29}} | collective-permute-start | bytes 786440 | tf_op jit(solution)/shard_map/ppermute | solution.py:127
  62.0 24.6 %collective-permute-start.12 = (f32[128,512]{1,0:T(8,128)S(1)}, f32[128,512]{1,0:T(8,128)S(1)}, u32[]{:S(2)}, u32[]{:S(2)}) collective-permute-start(f32[128,512]{1,0:T(8,128)S(1)} %get-tuple-element.27), channel_id=1, source_target_pairs={{0,3},{1,7},{10,11},{11,15},{20,19},{21,23},{30,27},{31,31}} | collective-permute-start | bytes 786440 | tf_op jit(solution)/shard_map/ppermute | solution.py:127
  63.3 23.3 %collective-permute-start.11 = (f32[128,512]{1,0:T(8,128)S(1)}, f32[128,512]{1,0:T(8,128)S(1)}, u32[]{:S(2)}, u32[]{:S(2)}) collective-permute-start(f32[128,512]{1,0:T(8,128)S(1)} %get-tuple-element.28), channel_id=1, source_target_pairs={{0,2},{1,6},{10,10},{11,14},{20,18},{21,22},{30,26},{31,30}} | collective-permute-start | bytes 786440 | tf_op jit(solution)/shard_map/ppermute | solution.py:127
  64.6 22.0 %collective-permute-start.9 = (f32[128,512]{1,0:T(8,128)S(1)}, f32[128,512]{1,0:T(8,128)S(1)}, u32[]{:S(2)}, u32[]{:S(2)}) collective-permute-start(f32[128,512]{1,0:T(8,128)S(1)} %get-tuple-element.29), channel_id=1, source_target_pairs={{0,0},{1,4},{10,8},{11,12},{20,16},{21,20},{30,24},{31,28}} | collective-permute-start | bytes 786440 | tf_op jit(solution)/shard_map/ppermute | solution.py:127
  75.8 39.5 %copy-start.4 = (s32[256]{0:T(256)S(1)}, s32[256]{0:T(256)}, u32[]{:S(2)}) copy-start(s32[256]{0:T(256)} %param.15) | copy-start | bytes 3076
  75.8 66.3 %copy-start.3 = (f32[128]{0:T(128)S(1)}, f32[128]{0:T(128)}, u32[]{:S(2)}) copy-start(f32[128]{0:T(128)} %param.20) | copy-start | bytes 1540
  75.8 109.9 %copy-start.5 = (f32[128]{0:T(128)S(1)}, f32[128]{0:T(128)}, u32[]{:S(2)}) copy-start(f32[128]{0:T(128)} %param.19) | copy-start | bytes 1540
  86.9 12.5 %collective-permute-start.14 = (f32[2,128,512]{1,2,0:T(8,128)S(1)}, f32[2,128,512]{1,2,0:T(8,128)S(1)}, u32[]{:S(2)}, u32[]{:S(2)}) collective-permute-start(f32[2,128,512]{1,2,0:T(8,128)S(1)} %dynamic-slice_bitcast_fusion), channel_id=1, source_target_pairs={{0,2},{1,3},{2,0},{3,1},{4,6},{5,7},{6,4},{7,5},{8,10},{9,11},{10,... | collective-permute-start | bytes 1572872 | tf_op jit(solution)/shard_map/ppermute | solution.py:43
  99.5 15.0 %collective-permute-start.15 = (f32[128,512]{0,1:T(8,128)S(1)}, f32[128,512]{0,1:T(8,128)S(1)}, u32[]{:S(2)}, u32[]{:S(2)}) collective-permute-start(f32[128,512]{0,1:T(8,128)S(1)} %dynamic-slice_bitcast_fusion.1), channel_id=1, source_target_pairs={{0,4},{1,5},{2,6},{3,7},{4,0},{5,1},{6,2},{7,3},{8,12},{9,13},{10,... | collective-permute-start | bytes 786440 | tf_op jit(solution)/shard_map/ppermute | solution.py:43
  115.2 70.8 %copy-start.2 = (f32[128,512]{0,1:T(8,128)S(1)}, f32[128,512]{0,1:T(8,128)}, u32[]{:S(2)}) copy-start(f32[128,512]{0,1:T(8,128)} %bitcast_add_fusion.1) | copy-start | bytes 786436
  117.0 4.4 %collective-permute-start.16 = (f32[136,128]{1,0:T(8,128)S(1)}, f32[136,128]{1,0:T(8,128)S(1)}, u32[]{:S(2)}, u32[]{:S(2)}) collective-permute-start(f32[136,128]{1,0:T(8,128)S(1)} %pad_maximum_fusion), channel_id=1, source_target_pairs={{0,1},{1,0},{2,3},{3,2},{4,5},{5,4},{6,7},{7,6},{8,9},{9,8},{10,11... | collective-permute-start | bytes 208904 | tf_op jit(solution)/shard_map/ppermute | solution.py:31
  121.4 5.3 %collective-permute-start.17 = (f32[136,128]{1,0:T(8,128)S(1)}, f32[136,128]{1,0:T(8,128)S(1)}, u32[]{:S(2)}, u32[]{:S(2)}) collective-permute-start(f32[136,128]{1,0:T(8,128)S(1)} %fusion.43), channel_id=1, source_target_pairs={{0,2},{1,3},{2,0},{3,1},{4,6},{5,7},{6,4},{7,5},{8,10},{9,11},{10,... | collective-permute-start | bytes 208904 | tf_op jit(solution)/shard_map/ppermute | solution.py:31
  126.7 9.6 %collective-permute-start.18 = (f32[136,128]{1,0:T(8,128)S(1)}, f32[136,128]{1,0:T(8,128)S(1)}, u32[]{:S(2)}, u32[]{:S(2)}) collective-permute-start(f32[136,128]{1,0:T(8,128)S(1)} %add.246), channel_id=1, source_target_pairs={{0,4},{1,5},{2,6},{3,7},{4,0},{5,1},{6,2},{7,3},{8,12},{9,13},{10,... | collective-permute-start | bytes 208904 | tf_op jit(solution)/shard_map/ppermute | solution.py:31
  136.3 1.3 collective-permute-start.19
  137.7 4.4 %collective-permute-start.20 = (f32[136,128]{1,0:T(8,128)S(1)}, f32[136,128]{1,0:T(8,128)S(1)}, u32[]{:S(2)}, u32[]{:S(2)}) collective-permute-start(f32[136,128]{1,0:T(8,128)S(1)} %add.248), channel_id=1, source_target_pairs={{0,16},{8,24},{16,0},{24,8},{1,17},{9,25},{17,1},{25,9},{2,18},{10... | collective-permute-start | bytes 208904 | tf_op jit(solution)/shard_map/ppermute | solution.py:31
  167.2 15.7 %collective-permute-start.21 = (f32[128,2048]{0,1:T(8,128)S(1)}, f32[128,2048]{0,1:T(8,128)S(1)}, u32[]{:S(2)}, u32[]{:S(2)}) collective-permute-start(f32[128,2048]{0,1:T(8,128)S(1)} %dynamic-slice_select_fusion), channel_id=1, source_target_pairs={{0,16},{1,17},{10,26},{11,27},{20,4},{21,5},{30,14},{31,15}} | collective-permute-start | bytes 3145736 | tf_op jit(solution)/shard_map/ppermute | solution.py:23
  184.3 6.9 %collective-permute-start.22 = (f32[128,2048]{0,1:T(8,128)S(1)}, f32[128,2048]{0,1:T(8,128)S(1)}, u32[]{:S(2)}, u32[]{:S(2)}) collective-permute-start(f32[128,2048]{0,1:T(8,128)S(1)} %fusion.67), channel_id=1, source_target_pairs={{0,8},{16,24},{1,9},{17,25},{10,2},{26,18},{11,3},{27,19},{20,28},... | collective-permute-start | bytes 3145736 | tf_op jit(solution)/shard_map/ppermute | solution.py:23
  192.3 26.9 %copy-start.1 = (f32[4,128]{1,0:T(4,128)S(1)}, f32[4,128]{1,0:T(4,128)}, u32[]{:S(2)}) copy-start(f32[4,128]{1,0:T(4,128)} %param.18) | copy-start | bytes 6148
Sparse Core Ops, SparseCore 0:
  115.4 50.4 all-gather.1

commit v15 on v13

--- a/solution.py
+++ b/solution.py
@@ -118,14 +118,13 @@
     keep_part = jnp.einsum(spec, grad_col, keep_rows, precision=mid)
     partial_t = (keep_part, got_part)
     factor = n_col // n_row
-    grad_own = None
-    for t in range(n_row):
-        perm = []
-        for r in range(n_row):
-            for q in range(factor):
-                perm.append((r * n_col + r * factor + q, r * n_col + q * n_row + t))
-        got = lax.ppermute(grad_col[:, t * blk : (t + 1) * blk], ("row", "col"), perm)
-        grad_own = got if grad_own is None else grad_own + got
+    perm = []
+    for r in range(n_row):
+        for q in range(factor):
+            for t in range(n_row):
+                perm.append((t * n_col + r * factor + q, r * n_col + q * n_row + t))
+    own_piece = lax.dynamic_slice_in_dim(grad_col, row_id * blk, blk, 1)
+    grad_own = lax.ppermute(own_piece, ("row", "col"), perm)
     grad_own, keep_part = lax.optimization_barrier((grad_own, partial_t[0]))
     partial_t = keep_part + partial_t[1]
     gain_own_t = halving_scatter(partial_t, "col", n_col, col_id, 1)

time: 227 us -> 229 us (level)
  waiting for transfers between devices: 80.3 us -> 85.8 us
  starting transfers between devices: 34.7 us -> 31.4 us
    ppermute x1, waiting for transfers between devices: 0.01 us -> 15 us  [on_device(): lax.ppermute(send_part, 'col', [(i, i ^ 1) for i in range(n_col)])]
    ppermute x4 -> x1, waiting for transfers between devices: 10.8 us -> 0.01 us  [on_device(): grad_own = lax.ppermute(own_piece, ('row', 'col'), perm)]
    ppermute x4 -> x1, starting transfers between devices: 7.35 us -> 0.86 us  [on_device(): grad_own = lax.ppermute(own_piece, ('row', 'col'), perm)]
    all_gather x1, waiting for transfers between devices: 10.5 us -> 13.7 us  [on_device(): gain_rows_t = lax.all_gather(gain_own_t, 'col', axis=1, tiled=True)]
    ppermute x2, starting transfers between devices: 4.64 us -> 7.65 us  [halving_scatter(): x = keep + lax.ppermute(send, axis, [(i, i ^ bit) for i in range(size)])]
  transfers between devices with their start and end apart: 24 -> 21, of which waited for: 15 -> 15; matrix products, arithmetic and copies ran while one was open for 18% -> 18% of each run, Pallas kernels for 0% -> 0%
where the time goes in v15:
time: 229 us; the launch traced here: 228 us
  waiting for transfers between devices  85.8 us (37%)
  matrix products  59.5 us (26%)
  other arithmetic  34.6 us (15%)
  starting transfers between devices  31.4 us (14%)
  between operations  14.8 us (6%)
    dot_general x1, matrix products, on_device(): new_cov = cov - jnp.einsum('mi,mj->ij', white_row, white_col, precision=mid)  26.9 us
    ppermute x2, waiting for transfers between devices, halving_scatter(): x = keep + lax.ppermute(send, axis, [(i, i ^ bit) for i in range(size)])  22.3 us
    ppermute x5, waiting for transfers between devices, butterfly_sum(): buf = buf + lax.ppermute(buf, axis, [(i, i ^ bit) for i in range(size)])  20.3 us
    ppermute x1, waiting for transfers between devices, on_device(): lax.ppermute(send_part, 'col', [(i, i ^ 1) for i in range(n_col)])  15 us
    all_gather x1, waiting for transfers between devices, on_device(): gain_rows_t = lax.all_gather(gain_own_t, 'col', axis=1, tiled=True)  13.7 us
    ppermute x7, starting transfers between devices, shift_all_to_all(): lax.ppermute(piece, axis, [(i, (i - k) % size) for i in range(size)])  12.8 us
    another operation x3, other arithmetic, on_device(): lower = jnp.linalg.cholesky(gram)  12.4 us
    dot_general x1, matrix products, on_device(): send_part = jnp.einsum(spec, grad_col, send_rows, precision=mid)  10.3 us
  transfers between devices with their start and end apart: 21, of which 15 were waited for; matrix products, arithmetic and copies ran while one was open for 18% of the time, Pallas kernels for 0%

profile of v15, /device:TPU:0, one launch (start us, length us, event | category | flops | bytes accessed | tf_op | source)
XLA Modules:
  0.0 228.3 jit_solution(13592191447796642413)
XLA Ops:
  7.3 0.7 fusion.38
  8.0 0.9 copy.18
  8.9 5.7 %convert_reduce_fusion = f32[256,256]{1,0:T(8,128)S(1)} fusion(s32[256,32]{1,0:T(8,128)S(1)} %copy.18), kind=kLoop, calls=%fused_computation.7 | loop fusion | flops 6225920 | bytes 294912 | tf_op jit(solution)/shard_map/reduce_sum | solution.py:87
  14.6 1.0 fusion.26
  15.6 1.2 convolution_multiply_fusion.2
  16.8 1.3 fusion.14
  18.2 1.2 multiply_reduce_fusion
  20.3 6.1 %collective-permute-start = (f32[4,2048]{1,0:T(4,128)S(1)}, f32[4,2048]{1,0:T(4,128)S(1)}, u32[]{:S(2)}, u32[]{:S(2)}) collective-permute-start(f32[4,2048]{1,0:T(4,128)S(1)} %bitcast.155), channel_id=1, source_target_pairs={{0,7},{1,0},{2,1},{3,2},{4,3},{5,4},{6,5},{7,6},{8,15},{9,8},{10,9... | collective-permute-start | bytes 98312 | tf_op jit(solution)/shard_map/ppermute | solution.py:51
  27.0 3.0 %collective-permute-start.3 = (f32[4,2048]{1,0:T(4,128)S(1)}, f32[4,2048]{1,0:T(4,128)S(1)}, u32[]{:S(2)}, u32[]{:S(2)}) collective-permute-start(f32[4,2048]{1,0:T(4,128)S(1)} %bitcast.152), channel_id=1, source_target_pairs={{0,4},{1,5},{2,6},{3,7},{4,0},{5,1},{6,2},{7,3},{8,12},{9,13},{10,... | collective-permute-start | bytes 98312 | tf_op jit(solution)/shard_map/ppermute | solution.py:51
  30.2 1.9 collective-permute-start.5
  32.1 1.2 collective-permute-start.6
  33.3 2.8 %collective-permute-done.4 = f32[4,2048]{1,0:T(4,128)S(1)} collective-permute-done((f32[4,2048]{1,0:T(4,128)S(1)}, f32[4,2048]{1,0:T(4,128)S(1)}, u32[]{:S(2)}, u32[]{:S(2)}) %collective-permute-start.4) | collective-permute-done | bytes 32800 | tf_op jit(solution)/shard_map/ppermute | solution.py:51
  36.1 0.9 collective-permute-done.5
  37.1 1.7 collective-permute-done.6
  39.0 1.6 collective-permute-start.7
  40.6 4.9 %collective-permute-done.7 = f32[1,32,2048]{2,1,0:T(8,128)S(1)} collective-permute-done((f32[1,32,2048]{2,1,0:T(8,128)S(1)}, f32[1,32,2048]{2,1,0:T(8,128)S(1)}, u32[]{:S(2)}, u32[]{:S(2)}) %collective-permute-start.7) | collective-permute-done | bytes 262176 | tf_op jit(solution)/shard_map/ppermute | solution.py:67
  45.7 1.7 collective-permute-done.8
  47.6 10.3 %fusion.9 = f32[2,2,128,512]{2,3,0,1:T(8,128)S(1)} fusion(f32[128,2048,1,1]{1,0,3,2:T(8,128)S(1)} %bitcast.145, f32[2,2,2,512,2048]{4,3,2,1,0:T(8,128)} %bitcast.143, s32[]{:T(128)S(6)} %select_n.223), kind=kOutput, calls=%fused_computation.10 | convolution fusion | flops 3221225472 | bytes 18874372 | tf_op jit(solution)/shard_map/mk,abik->bami/dot_general | solution.py:115
  58.0 0.9 collective-permute-start.9
  58.9 10.3 %fusion.6 = f32[2,2,128,512]{2,3,0,1:T(8,128)S(1)} fusion(f32[128,2048,1,1]{1,0,3,2:T(8,128)S(1)} %bitcast.147, f32[2,2,2,512,2048]{4,3,2,1,0:T(8,128)} %bitcast.144, s32[]{:T(128)S(6)} %select_n.222), kind=kOutput, calls=%fused_computation.9 | convolution fusion | flops 3221225472 | bytes 18874372 | tf_op jit(solution)/shard_map/mk,abik->bami/dot_general | solution.py:118
  69.2 15.0 %collective-permute-done.10 = f32[2,2,128,512]{2,3,0,1:T(8,128)S(1)} collective-permute-done((f32[2,2,128,512]{2,3,0,1:T(8,128)S(1)}, f32[2,2,128,512]{2,3,0,1:T(8,128)S(1)}, u32[]{:S(2)}, u32[]{:S(2)}) %collective-permute-start.10) | collective-permute-done | bytes 1048608 | tf_op jit(solution)/shard_map/ppermute | solution.py:116
  84.5 2.6 %collective-permute-start.11 = (f32[2,128,512]{1,2,0:T(8,128)S(1)}, f32[2,128,512]{1,2,0:T(8,128)S(1)}, u32[]{:S(2)}, u32[]{:S(2)}) collective-permute-start(f32[2,128,512]{1,2,0:T(8,128)S(1)} %dynamic-slice_bitcast_fusion), channel_id=1, source_target_pairs={{0,2},{1,3},{2,0},{3,1},{4,6},{5,7},{6,4},{7,5},{8,10},{9,11},{10,... | collective-permute-start | bytes 1572872 | tf_op jit(solution)/shard_map/ppermute | solution.py:43
  87.1 11.8 %collective-permute-done.11 = f32[2,128,512]{1,2,0:T(8,128)S(1)} collective-permute-done((f32[2,128,512]{1,2,0:T(8,128)S(1)}, f32[2,128,512]{1,2,0:T(8,128)S(1)}, u32[]{:S(2)}, u32[]{:S(2)}) %collective-permute-start.11) | collective-permute-done | bytes 524320 | tf_op jit(solution)/shard_map/ppermute | solution.py:43
  99.0 5.0 %collective-permute-start.12 = (f32[128,512]{0,1:T(8,128)S(1)}, f32[128,512]{0,1:T(8,128)S(1)}, u32[]{:S(2)}, u32[]{:S(2)}) collective-permute-start(f32[128,512]{0,1:T(8,128)S(1)} %dynamic-slice_bitcast_fusion.1), channel_id=1, source_target_pairs={{0,4},{1,5},{2,6},{3,7},{4,0},{5,1},{6,2},{7,3},{8,12},{9,13},{10,... | collective-permute-start | bytes 786440 | tf_op jit(solution)/shard_map/ppermute | solution.py:43
  104.0 10.5 %collective-permute-done.12 = f32[128,512]{0,1:T(8,128)S(1)} collective-permute-done((f32[128,512]{0,1:T(8,128)S(1)}, f32[128,512]{0,1:T(8,128)S(1)}, u32[]{:S(2)}, u32[]{:S(2)}) %collective-permute-start.12) | collective-permute-done | bytes 262176 | tf_op jit(solution)/shard_map/ppermute | solution.py:43
  114.5 0.7 bitcast_add_fusion.1
  115.7 1.3 fusion.45
  117.1 4.3 %collective-permute-done.13 = f32[136,128]{1,0:T(8,128)S(1)} collective-permute-done((f32[136,128]{1,0:T(8,128)S(1)}, f32[136,128]{1,0:T(8,128)S(1)}, u32[]{:S(2)}, u32[]{:S(2)}) %collective-permute-start.13) | collective-permute-done | bytes 69664 | tf_op jit(solution)/shard_map/ppermute | solution.py:31
  121.5 4.3 %collective-permute-done.14 = f32[136,128]{1,0:T(8,128)S(1)} collective-permute-done((f32[136,128]{1,0:T(8,128)S(1)}, f32[136,128]{1,0:T(8,128)S(1)}, u32[]{:S(2)}, u32[]{:S(2)}) %collective-permute-start.14) | collective-permute-done | bytes 69664 | tf_op jit(solution)/shard_map/ppermute | solution.py:31
  125.8 1.3 collective-permute-start.15
  127.1 7.9 %collective-permute-done.15 = f32[136,128]{1,0:T(8,128)S(1)} collective-permute-done((f32[136,128]{1,0:T(8,128)S(1)}, f32[136,128]{1,0:T(8,128)S(1)}, u32[]{:S(2)}, u32[]{:S(2)}) %collective-permute-start.15) | collective-permute-done | bytes 69664 | tf_op jit(solution)/shard_map/ppermute | solution.py:31
  135.1 1.2 collective-permute-done.16
  136.4 1.9 collective-permute-start.17
  138.2 2.5 %collective-permute-done.17 = f32[136,128]{1,0:T(8,128)S(1)} collective-permute-done((f32[136,128]{1,0:T(8,128)S(1)}, f32[136,128]{1,0:T(8,128)S(1)}, u32[]{:S(2)}, u32[]{:S(2)}) %collective-permute-start.17) | collective-permute-done | bytes 69664 | tf_op jit(solution)/shard_map/ppermute | solution.py:31
  141.0 11.7 %cholesky.16 = f32[128,128]{1,0:T(8,128)S(1)} custom-call(f32[128,128]{1,0:T(8,128)S(1)} %fusion.32), custom_call_target="Cholesky" | custom-call | tf_op jit(solution)/shard_map/jit(cholesky)/cholesky | solution.py:144
  152.8 0.6 compare_reduce_fusion
  153.4 0.7 select_select_fusion
  154.1 13.7 %all-gather.2.cloned.1.call-done = f32[128,4096]{0,1:T(8,128)} async-done(((f32[128,512]{0,1:T(8,128)}), f32[128,4096]{0,1:T(8,128)}) %all-gather.2.cloned.1.call-update) | async-done | bytes 2097168 | tf_op jit(solution)/shard_map/all_gather | solution.py:141
  167.8 1.3 dynamic-slice_select_fusion
  169.1 3.4 %collective-permute-start.18 = (f32[128,2048]{0,1:T(8,128)S(1)}, f32[128,2048]{0,1:T(8,128)S(1)}, u32[]{:S(2)}, u32[]{:S(2)}) collective-permute-start(f32[128,2048]{0,1:T(8,128)S(1)} %dynamic-slice_select_fusion), channel_id=1, source_target_pairs={{0,16},{1,17},{10,26},{11,27},{20,4},{21,5},{30,14},{31,15}} | collective-permute-start | bytes 3145736 | tf_op jit(solution)/shard_map/ppermute | solution.py:23
  172.6 9.8 %custom-call.16 = f32[1,128,128]{1,2,0:T(8,128)S(1)} custom-call(f32[1,128,128]{2,1,0:T(8,128)S(1)} %select_bitcast_fusion), custom_call_target="InvertDiagBlocksLowerTriangular" | custom-call | tf_op jit(solution)/shard_map/jit(_cho_solve)/triangular_solve | solution.py:153
  182.4 2.4 %collective-permute-done.18 = f32[128,2048]{0,1:T(8,128)S(1)} collective-permute-done((f32[128,2048]{0,1:T(8,128)S(1)}, f32[128,2048]{0,1:T(8,128)S(1)}, u32[]{:S(2)}, u32[]{:S(2)}) %collective-permute-start.18) | collective-permute-done | bytes 1048608 | tf_op jit(solution)/shard_map/ppermute | solution.py:23
  184.8 1.4 fusion.64
  186.2 1.6 collective-permute-start.19
  188.5 1.4 dynamic-slice_add_fusion
  189.9 3.5 %fusion.28 = f32[128,4096]{1,0:T(8,128)S(1)} fusion(f32[128,4096]{0,1:T(8,128)} %all-gather.2.cloned.1.call-done, f32[1,128,128]{1,2,0:T(8,128)S(1)} %custom-call.16), kind=kOutput, calls=%fused_computation.46 | convolution fusion | flops 805306368 | bytes 4259840 | tf_op jit(solution)/shard_map/jit(_solve_triangular)/triangular_solve | solution.py:150
  193.4 1.1 fusion.17
  194.5 26.9 %convolution_subtract_fusion = f32[4096,2048]{1,0:T(8,128)} fusion(f32[4096,2048]{1,0:T(8,128)} %param.21, f32[128,4096]{1,0:T(8,128)S(1)} %fusion.28, f32[128,2048]{1,0:T(8,128)S(1)} %fusion.17), kind=kOutput, calls=%fused_computation.6 | convolution fusion | flops 6450839552 | bytes 70254592 | tf_op jit(solution)/shard_map/mi,mj->ij/dot_general | solution.py:152
  (84 shorter events, 4.4 us)
Async XLA Ops:
  7.2 7.4 %copy-start = (f32[4,128]{1,0:T(4,128)S(1)}, f32[4,128]{1,0:T(4,128)}, u32[]{:S(2)}) copy-start(f32[4,128]{1,0:T(4,128)} %param.18) | copy-start | bytes 6148
  7.2 160.7 %all-gather.2.cloned.1.call-start = ((), (), s32[]{:S(2)}) async-start(), calls=%async_computation | async-start | bytes 2359296 | tf_op jit(solution)/shard_map/all_gather | solution.py:141
  20.3 9.9 %collective-permute-start = (f32[4,2048]{1,0:T(4,128)S(1)}, f32[4,2048]{1,0:T(4,128)S(1)}, u32[]{:S(2)}, u32[]{:S(2)}) collective-permute-start(f32[4,2048]{1,0:T(4,128)S(1)} %bitcast.155), channel_id=1, source_target_pairs={{0,7},{1,0},{2,1},{3,2},{4,3},{5,4},{6,5},{7,6},{8,15},{9,8},{10,9... | collective-permute-start | bytes 98312 | tf_op jit(solution)/shard_map/ppermute | solution.py:51
  26.3 5.7 %collective-permute-start.1 = (f32[4,2048]{1,0:T(4,128)S(1)}, f32[4,2048]{1,0:T(4,128)S(1)}, u32[]{:S(2)}, u32[]{:S(2)}) collective-permute-start(f32[4,2048]{1,0:T(4,128)S(1)} %bitcast.154), channel_id=1, source_target_pairs={{0,6},{1,7},{2,0},{3,1},{4,2},{5,3},{6,4},{7,5},{8,14},{9,15},{10,... | collective-permute-start | bytes 98312 | tf_op jit(solution)/shard_map/ppermute | solution.py:51
  26.9 6.4 %collective-permute-start.2 = (f32[4,2048]{1,0:T(4,128)S(1)}, f32[4,2048]{1,0:T(4,128)S(1)}, u32[]{:S(2)}, u32[]{:S(2)}) collective-permute-start(f32[4,2048]{1,0:T(4,128)S(1)} %bitcast.151), channel_id=1, source_target_pairs={{0,5},{1,6},{2,7},{3,0},{4,1},{5,2},{6,3},{7,4},{8,13},{9,14},{10,... | collective-permute-start | bytes 98312 | tf_op jit(solution)/shard_map/ppermute | solution.py:51
  27.0 6.3 %collective-permute-start.3 = (f32[4,2048]{1,0:T(4,128)S(1)}, f32[4,2048]{1,0:T(4,128)S(1)}, u32[]{:S(2)}, u32[]{:S(2)}) collective-permute-start(f32[4,2048]{1,0:T(4,128)S(1)} %bitcast.152), channel_id=1, source_target_pairs={{0,4},{1,5},{2,6},{3,7},{4,0},{5,1},{6,2},{7,3},{8,12},{9,13},{10,... | collective-permute-start | bytes 98312 | tf_op jit(solution)/shard_map/ppermute | solution.py:51
  30.0 6.1 %collective-permute-start.4 = (f32[4,2048]{1,0:T(4,128)S(1)}, f32[4,2048]{1,0:T(4,128)S(1)}, u32[]{:S(2)}, u32[]{:S(2)}) collective-permute-start(f32[4,2048]{1,0:T(4,128)S(1)} %bitcast.153), channel_id=1, source_target_pairs={{0,3},{1,4},{2,5},{3,6},{4,7},{5,0},{6,1},{7,2},{8,11},{9,12},{10,... | collective-permute-start | bytes 98312 | tf_op jit(solution)/shard_map/ppermute | solution.py:51
  30.2 6.9 %collective-permute-start.5 = (f32[4,2048]{1,0:T(4,128)S(1)}, f32[4,2048]{1,0:T(4,128)S(1)}, u32[]{:S(2)}, u32[]{:S(2)}) collective-permute-start(f32[4,2048]{1,0:T(4,128)S(1)} %bitcast.157), channel_id=1, source_target_pairs={{0,2},{1,3},{2,4},{3,5},{4,6},{5,7},{6,0},{7,1},{8,10},{9,11},{10,... | collective-permute-start | bytes 98312 | tf_op jit(solution)/shard_map/ppermute | solution.py:51
  32.1 6.7 %collective-permute-start.6 = (f32[4,2048]{1,0:T(4,128)S(1)}, f32[4,2048]{1,0:T(4,128)S(1)}, u32[]{:S(2)}, u32[]{:S(2)}) collective-permute-start(f32[4,2048]{1,0:T(4,128)S(1)} %bitcast.156), channel_id=1, source_target_pairs={{0,1},{1,2},{2,3},{3,4},{4,5},{5,6},{6,7},{7,0},{8,9},{9,10},{10,1... | collective-permute-start | bytes 98312 | tf_op jit(solution)/shard_map/ppermute | solution.py:51
  39.0 6.4 %collective-permute-start.7 = (f32[1,32,2048]{2,1,0:T(8,128)S(1)}, f32[1,32,2048]{2,1,0:T(8,128)S(1)}, u32[]{:S(2)}, u32[]{:S(2)}) collective-permute-start(f32[1,32,2048]{2,1,0:T(8,128)S(1)} %broadcast_in_dim_reshape.3), channel_id=1, source_target_pairs={{0,16},{8,24},{16,0},{24,8},{1,17},{9,25},{17,1},{25,9},{2,18},{10... | collective-permute-start | bytes 786440 | tf_op jit(solution)/shard_map/ppermute | solution.py:67
  45.5 2.0 collective-permute-start.8
  57.9 26.4 %collective-permute-start.10 = (f32[2,2,128,512]{2,3,0,1:T(8,128)S(1)}, f32[2,2,128,512]{2,3,0,1:T(8,128)S(1)}, u32[]{:S(2)}, u32[]{:S(2)}) collective-permute-start(f32[2,2,128,512]{2,3,0,1:T(8,128)S(1)} %fusion.9), channel_id=1, source_target_pairs={{0,1},{1,0},{2,3},{3,2},{4,5},{5,4},{6,7},{7,6},{8,9},{9,8},{10,11... | collective-permute-start | bytes 3145736 | tf_op jit(solution)/shard_map/ppermute | solution.py:116
  58.0 57.3 %copy-start.4 = (s32[256]{0:T(256)S(1)}, s32[256]{0:T(256)}, u32[]{:S(2)}) copy-start(s32[256]{0:T(256)} %param.15) | copy-start | bytes 3076
  58.0 11.2 %collective-permute-start.9 = (f32[128,512]{1,0:T(8,128)S(1)}, f32[128,512]{1,0:T(8,128)S(1)}, u32[]{:S(2)}, u32[]{:S(2)}) collective-permute-start(f32[128,512]{1,0:T(8,128)S(1)} %constant_dynamic-slice_fusion), channel_id=1, source_target_pairs={{0,0},{8,1},{16,2},{24,3},{1,4},{9,5},{17,6},{25,7},{2,8},{10,9},{... | collective-permute-start | bytes 786440 | tf_op jit(solution)/shard_map/ppermute | solution.py:127
  69.2 71.5 %copy-start.3 = (f32[128]{0:T(128)S(1)}, f32[128]{0:T(128)}, u32[]{:S(2)}) copy-start(f32[128]{0:T(128)} %param.20) | copy-start | bytes 1540
  69.2 118.6 %copy-start.5 = (f32[128]{0:T(128)S(1)}, f32[128]{0:T(128)}, u32[]{:S(2)}) copy-start(f32[128]{0:T(128)} %param.19) | copy-start | bytes 1540
  84.5 14.4 %collective-permute-start.11 = (f32[2,128,512]{1,2,0:T(8,128)S(1)}, f32[2,128,512]{1,2,0:T(8,128)S(1)}, u32[]{:S(2)}, u32[]{:S(2)}) collective-permute-start(f32[2,128,512]{1,2,0:T(8,128)S(1)} %dynamic-slice_bitcast_fusion), channel_id=1, source_target_pairs={{0,2},{1,3},{2,0},{3,1},{4,6},{5,7},{6,4},{7,5},{8,10},{9,11},{10,... | collective-permute-start | bytes 1572872 | tf_op jit(solution)/shard_map/ppermute | solution.py:43
  99.0 15.6 %collective-permute-start.12 = (f32[128,512]{0,1:T(8,128)S(1)}, f32[128,512]{0,1:T(8,128)S(1)}, u32[]{:S(2)}, u32[]{:S(2)}) collective-permute-start(f32[128,512]{0,1:T(8,128)S(1)} %dynamic-slice_bitcast_fusion.1), channel_id=1, source_target_pairs={{0,4},{1,5},{2,6},{3,7},{4,0},{5,1},{6,2},{7,3},{8,12},{9,13},{10,... | collective-permute-start | bytes 786440 | tf_op jit(solution)/shard_map/ppermute | solution.py:43
  115.3 72.9 %copy-start.2 = (f32[128,512]{0,1:T(8,128)S(1)}, f32[128,512]{0,1:T(8,128)}, u32[]{:S(2)}) copy-start(f32[128,512]{0,1:T(8,128)} %bitcast_add_fusion.1) | copy-start | bytes 786436
  117.0 4.4 %collective-permute-start.13 = (f32[136,128]{1,0:T(8,128)S(1)}, f32[136,128]{1,0:T(8,128)S(1)}, u32[]{:S(2)}, u32[]{:S(2)}) collective-permute-start(f32[136,128]{1,0:T(8,128)S(1)} %pad_maximum_fusion), channel_id=1, source_target_pairs={{0,1},{1,0},{2,3},{3,2},{4,5},{5,4},{6,7},{7,6},{8,9},{9,8},{10,11... | collective-permute-start | bytes 208904 | tf_op jit(solution)/shard_map/ppermute | solution.py:31
  121.4 4.4 %collective-permute-start.14 = (f32[136,128]{1,0:T(8,128)S(1)}, f32[136,128]{1,0:T(8,128)S(1)}, u32[]{:S(2)}, u32[]{:S(2)}) collective-permute-start(f32[136,128]{1,0:T(8,128)S(1)} %fusion.44), channel_id=1, source_target_pairs={{0,2},{1,3},{2,0},{3,1},{4,6},{5,7},{6,4},{7,5},{8,10},{9,11},{10,... | collective-permute-start | bytes 208904 | tf_op jit(solution)/shard_map/ppermute | solution.py:31
  125.8 9.2 %collective-permute-start.15 = (f32[136,128]{1,0:T(8,128)S(1)}, f32[136,128]{1,0:T(8,128)S(1)}, u32[]{:S(2)}, u32[]{:S(2)}) collective-permute-start(f32[136,128]{1,0:T(8,128)S(1)} %add.241), channel_id=1, source_target_pairs={{0,4},{1,5},{2,6},{3,7},{4,0},{5,1},{6,2},{7,3},{8,12},{9,13},{10,... | collective-permute-start | bytes 208904 | tf_op jit(solution)/shard_map/ppermute | solution.py:31
  135.0 1.3 collective-permute-start.16
  136.4 4.4 %collective-permute-start.17 = (f32[136,128]{1,0:T(8,128)S(1)}, f32[136,128]{1,0:T(8,128)S(1)}, u32[]{:S(2)}, u32[]{:S(2)}) collective-permute-start(f32[136,128]{1,0:T(8,128)S(1)} %add.243), channel_id=1, source_target_pairs={{0,16},{8,24},{16,0},{24,8},{1,17},{9,25},{17,1},{25,9},{2,18},{10... | collective-permute-start | bytes 208904 | tf_op jit(solution)/shard_map/ppermute | solution.py:31
  169.1 15.7 %collective-permute-start.18 = (f32[128,2048]{0,1:T(8,128)S(1)}, f32[128,2048]{0,1:T(8,128)S(1)}, u32[]{:S(2)}, u32[]{:S(2)}) collective-permute-start(f32[128,2048]{0,1:T(8,128)S(1)} %dynamic-slice_select_fusion), channel_id=1, source_target_pairs={{0,16},{1,17},{10,26},{11,27},{20,4},{21,5},{30,14},{31,15}} | collective-permute-start | bytes 3145736 | tf_op jit(solution)/shard_map/ppermute | solution.py:23
  186.2 7.2 %collective-permute-start.19 = (f32[128,2048]{0,1:T(8,128)S(1)}, f32[128,2048]{0,1:T(8,128)S(1)}, u32[]{:S(2)}, u32[]{:S(2)}) collective-permute-start(f32[128,2048]{0,1:T(8,128)S(1)} %fusion.64), channel_id=1, source_target_pairs={{0,8},{16,24},{1,9},{17,25},{10,2},{26,18},{11,3},{27,19},{20,28},... | collective-permute-start | bytes 3145736 | tf_op jit(solution)/shard_map/ppermute | solution.py:23
  194.5 26.9 %copy-start.1 = (f32[4,128]{1,0:T(4,128)S(1)}, f32[4,128]{1,0:T(4,128)}, u32[]{:S(2)}) copy-start(f32[4,128]{1,0:T(4,128)} %param.18) | copy-start | bytes 6148
Sparse Core Ops, SparseCore 0:
  115.4 52.3 all-gather.1

commit v16 on v13

--- a/solution.py
+++ b/solution.py
@@ -85,7 +85,7 @@
     row_out = jnp.dot(onehot_type, out_vec, precision=hi)
     scaled = atom_feat * row_gain
     counts = jnp.sum(
-        (neighbors[:, :, None] == jnp.arange(atoms)[None, None, :]).astype(jnp.float32), axis=1
+        (neighbors.T[:, :, None] == jnp.arange(atoms)[None, None, :]).astype(jnp.float32), axis=0
     )
     near_sum = jnp.dot(counts, scaled, precision=hi)
     desc = jnp.tanh(atom_feat + near_sum / nbrs)

time: 227 us -> 222 us (0.978)
  other arithmetic: 34.7 us -> 31.6 us
    reduce_sum x1, other arithmetic: 5.69 us -> 2.55 us  [on_device(): jnp.sum((neighbors.T[:, :, None] == jnp.arange(atoms)[None, None, :]).ast...]
  transfers between devices with their start and end apart: 24 -> 24, of which waited for: 15 -> 15; matrix products, arithmetic and copies ran while one was open for 18% -> 19% of each run, Pallas kernels for 0% -> 0%
where the time goes in v16:
time: 222 us
  waiting for transfers between devices  80.3 us (36%)
  matrix products  59.5 us (27%)
  starting transfers between devices  34.1 us (15%)
  other arithmetic  31.6 us (14%)
  between operations  14.9 us (7%)
    dot_general x1, matrix products, on_device(): new_cov = cov - jnp.einsum('mi,mj->ij', white_row, white_col, precision=mid)  26.9 us
    ppermute x2, waiting for transfers between devices, halving_scatter(): x = keep + lax.ppermute(send, axis, [(i, i ^ bit) for i in range(size)])  22.8 us
    ppermute x5, waiting for transfers between devices, butterfly_sum(): buf = buf + lax.ppermute(buf, axis, [(i, i ^ bit) for i in range(size)])  21.8 us
    ppermute x7, starting transfers between devices, shift_all_to_all(): lax.ppermute(piece, axis, [(i, (i - k) % size) for i in range(size)])  12.8 us
    another operation x3, other arithmetic, on_device(): lower = jnp.linalg.cholesky(gram)  12.4 us
    ppermute x4, waiting for transfers between devices, on_device(): got = lax.ppermute(grad_col[:, t * blk:(t + 1) * blk], ('row', 'col'), perm)  10.8 us
    all_gather x1, waiting for transfers between devices, on_device(): gain_rows_t = lax.all_gather(gain_own_t, 'col', axis=1, tiled=True)  10.5 us
    dot_general x1, matrix products, on_device(): send_part = jnp.einsum(spec, grad_col, send_rows, precision=mid)  10.3 us
  transfers between devices with their start and end apart: 24, of which 15 were waited for; matrix products, arithmetic and copies ran while one was open for 19% of the time, Pallas kernels for 0%

profile of v16, /device:TPU:0, one launch (start us, length us, event | category | flops | bytes accessed | tf_op | source)
XLA Modules:
  0.0 221.7 jit_solution(3396074872382856743)
XLA Ops:
  7.3 0.7 fusion.36
  8.0 2.5 %convert_reduce_fusion = f32[256,256]{1,0:T(8,128)S(1)} fusion(s32[32,256]{1,0:T(8,128)} %bitcast.152), kind=kLoop, calls=%fused_computation.7 | loop fusion | flops 6225920 | bytes 294912 | tf_op jit(solution)/shard_map/reduce_sum | solution.py:87
  10.6 1.0 fusion.26
  11.6 1.2 convolution_multiply_fusion.2
  12.8 1.3 fusion.14
  14.2 1.2 multiply_reduce_fusion
  16.3 6.1 %collective-permute-start = (f32[4,2048]{1,0:T(4,128)S(1)}, f32[4,2048]{1,0:T(4,128)S(1)}, u32[]{:S(2)}, u32[]{:S(2)}) collective-permute-start(f32[4,2048]{1,0:T(4,128)S(1)} %bitcast.157), channel_id=1, source_target_pairs={{0,7},{1,0},{2,1},{3,2},{4,3},{5,4},{6,5},{7,6},{8,15},{9,8},{10,9... | collective-permute-start | bytes 98312 | tf_op jit(solution)/shard_map/ppermute | solution.py:51
  23.0 3.0 %collective-permute-start.3 = (f32[4,2048]{1,0:T(4,128)S(1)}, f32[4,2048]{1,0:T(4,128)S(1)}, u32[]{:S(2)}, u32[]{:S(2)}) collective-permute-start(f32[4,2048]{1,0:T(4,128)S(1)} %bitcast.154), channel_id=1, source_target_pairs={{0,4},{1,5},{2,6},{3,7},{4,0},{5,1},{6,2},{7,3},{8,12},{9,13},{10,... | collective-permute-start | bytes 98312 | tf_op jit(solution)/shard_map/ppermute | solution.py:51
  26.2 1.9 collective-permute-start.5
  28.1 1.2 collective-permute-start.6
  29.3 2.8 %collective-permute-done.4 = f32[4,2048]{1,0:T(4,128)S(1)} collective-permute-done((f32[4,2048]{1,0:T(4,128)S(1)}, f32[4,2048]{1,0:T(4,128)S(1)}, u32[]{:S(2)}, u32[]{:S(2)}) %collective-permute-start.4) | collective-permute-done | bytes 32800 | tf_op jit(solution)/shard_map/ppermute | solution.py:51
  32.1 0.9 collective-permute-done.5
  33.1 1.6 collective-permute-done.6
  35.0 1.6 collective-permute-start.7
  36.6 4.9 %collective-permute-done.7 = f32[1,32,2048]{2,1,0:T(8,128)S(1)} collective-permute-done((f32[1,32,2048]{2,1,0:T(8,128)S(1)}, f32[1,32,2048]{2,1,0:T(8,128)S(1)}, u32[]{:S(2)}, u32[]{:S(2)}) %collective-permute-start.7) | collective-permute-done | bytes 262176 | tf_op jit(solution)/shard_map/ppermute | solution.py:67
  41.7 1.7 collective-permute-done.8
  43.6 10.3 %fusion.9 = f32[2,2,128,512]{2,3,0,1:T(8,128)S(1)} fusion(f32[128,2048,1,1]{1,0,3,2:T(8,128)S(1)} %bitcast.146, f32[2,2,2,512,2048]{4,3,2,1,0:T(8,128)} %bitcast.144, s32[]{:T(128)S(6)} %select_n.219), kind=kOutput, calls=%fused_computation.10 | convolution fusion | flops 3221225472 | bytes 18874372 | tf_op jit(solution)/shard_map/mk,abik->bami/dot_general | solution.py:115
  54.1 3.9 %collective-permute-start.10 = (f32[128,512]{1,0:T(8,128)S(1)}, f32[128,512]{1,0:T(8,128)S(1)}, u32[]{:S(2)}, u32[]{:S(2)}) collective-permute-start(f32[128,512]{1,0:T(8,128)S(1)} %get-tuple-element.22), channel_id=1, source_target_pairs={{0,1},{1,5},{10,9},{11,13},{20,17},{21,21},{30,25},{31,29}} | collective-permute-start | bytes 786440 | tf_op jit(solution)/shard_map/ppermute | solution.py:127
  58.0 1.3 collective-permute-start.12
  59.3 1.3 collective-permute-start.11
  60.6 0.9 collective-permute-start.9
  61.5 10.3 %fusion.6 = f32[2,2,128,512]{2,3,0,1:T(8,128)S(1)} fusion(f32[128,2048,1,1]{1,0,3,2:T(8,128)S(1)} %bitcast.148, f32[2,2,2,512,2048]{4,3,2,1,0:T(8,128)} %bitcast.145, s32[]{:T(128)S(6)} %select_n.218), kind=kOutput, calls=%fused_computation.9 | convolution fusion | flops 3221225472 | bytes 18874372 | tf_op jit(solution)/shard_map/mk,abik->bami/dot_general | solution.py:118
  71.8 10.8 %collective-permute-done.10 = f32[128,512]{1,0:T(8,128)S(1)} collective-permute-done((f32[128,512]{1,0:T(8,128)S(1)}, f32[128,512]{1,0:T(8,128)S(1)}, u32[]{:S(2)}, u32[]{:S(2)}) %collective-permute-start.10) | collective-permute-done | bytes 262176 | tf_op jit(solution)/shard_map/ppermute | solution.py:127
  83.0 12.4 %collective-permute-done.14 = f32[2,128,512]{1,2,0:T(8,128)S(1)} collective-permute-done((f32[2,128,512]{1,2,0:T(8,128)S(1)}, f32[2,128,512]{1,2,0:T(8,128)S(1)}, u32[]{:S(2)}, u32[]{:S(2)}) %collective-permute-start.14) | collective-permute-done | bytes 524320 | tf_op jit(solution)/shard_map/ppermute | solution.py:43
  95.5 4.6 %collective-permute-start.15 = (f32[128,512]{0,1:T(8,128)S(1)}, f32[128,512]{0,1:T(8,128)S(1)}, u32[]{:S(2)}, u32[]{:S(2)}) collective-permute-start(f32[128,512]{0,1:T(8,128)S(1)} %dynamic-slice_bitcast_fusion.1), channel_id=1, source_target_pairs={{0,4},{1,5},{2,6},{3,7},{4,0},{5,1},{6,2},{7,3},{8,12},{9,13},{10,... | collective-permute-start | bytes 786440 | tf_op jit(solution)/shard_map/ppermute | solution.py:43
  100.0 10.5 %collective-permute-done.15 = f32[128,512]{0,1:T(8,128)S(1)} collective-permute-done((f32[128,512]{0,1:T(8,128)S(1)}, f32[128,512]{0,1:T(8,128)S(1)}, u32[]{:S(2)}, u32[]{:S(2)}) %collective-permute-start.15) | collective-permute-done | bytes 262176 | tf_op jit(solution)/shard_map/ppermute | solution.py:43
  110.5 0.7 bitcast_add_fusion.1
  111.6 1.3 fusion.46
  113.5 3.8 %collective-permute-done.16 = f32[136,128]{1,0:T(8,128)S(1)} collective-permute-done((f32[136,128]{1,0:T(8,128)S(1)}, f32[136,128]{1,0:T(8,128)S(1)}, u32[]{:S(2)}, u32[]{:S(2)}) %collective-permute-start.16) | collective-permute-done | bytes 69664 | tf_op jit(solution)/shard_map/ppermute | solution.py:31
  117.5 5.2 %collective-permute-done.17 = f32[136,128]{1,0:T(8,128)S(1)} collective-permute-done((f32[136,128]{1,0:T(8,128)S(1)}, f32[136,128]{1,0:T(8,128)S(1)}, u32[]{:S(2)}, u32[]{:S(2)}) %collective-permute-start.17) | collective-permute-done | bytes 69664 | tf_op jit(solution)/shard_map/ppermute | solution.py:31
  122.7 1.6 collective-permute-start.18
  124.3 8.0 %collective-permute-done.18 = f32[136,128]{1,0:T(8,128)S(1)} collective-permute-done((f32[136,128]{1,0:T(8,128)S(1)}, f32[136,128]{1,0:T(8,128)S(1)}, u32[]{:S(2)}, u32[]{:S(2)}) %collective-permute-start.18) | collective-permute-done | bytes 69664 | tf_op jit(solution)/shard_map/ppermute | solution.py:31
  132.4 1.2 collective-permute-done.19
  133.7 0.9 collective-permute-start.20
  134.6 3.5 %collective-permute-done.20 = f32[136,128]{1,0:T(8,128)S(1)} collective-permute-done((f32[136,128]{1,0:T(8,128)S(1)}, f32[136,128]{1,0:T(8,128)S(1)}, u32[]{:S(2)}, u32[]{:S(2)}) %collective-permute-start.20) | collective-permute-done | bytes 69664 | tf_op jit(solution)/shard_map/ppermute | solution.py:31
  138.3 11.7 %cholesky.16 = f32[128,128]{1,0:T(8,128)S(1)} custom-call(f32[128,128]{1,0:T(8,128)S(1)} %fusion.32), custom_call_target="Cholesky" | custom-call | tf_op jit(solution)/shard_map/jit(cholesky)/cholesky | solution.py:145
  150.7 0.7 select_select_fusion
  151.4 10.5 %all-gather.2.cloned.1.call-done = f32[128,4096]{0,1:T(8,128)} async-done(((f32[128,512]{0,1:T(8,128)}), f32[128,4096]{0,1:T(8,128)}) %all-gather.2.cloned.1.call-update) | async-done | bytes 2097168 | tf_op jit(solution)/shard_map/all_gather | solution.py:142
  161.9 1.3 dynamic-slice_select_fusion
  163.2 2.8 %collective-permute-start.21 = (f32[128,2048]{0,1:T(8,128)S(1)}, f32[128,2048]{0,1:T(8,128)S(1)}, u32[]{:S(2)}, u32[]{:S(2)}) collective-permute-start(f32[128,2048]{0,1:T(8,128)S(1)} %dynamic-slice_select_fusion), channel_id=1, source_target_pairs={{0,16},{1,17},{10,26},{11,27},{20,4},{21,5},{30,14},{31,15}} | collective-permute-start | bytes 3145736 | tf_op jit(solution)/shard_map/ppermute | solution.py:23
  166.1 9.8 %custom-call.16 = f32[1,128,128]{1,2,0:T(8,128)S(1)} custom-call(f32[1,128,128]{2,1,0:T(8,128)S(1)} %select_bitcast_fusion), custom_call_target="InvertDiagBlocksLowerTriangular" | custom-call | tf_op jit(solution)/shard_map/jit(_cho_solve)/triangular_solve | solution.py:154
  175.9 2.4 %collective-permute-done.21 = f32[128,2048]{0,1:T(8,128)S(1)} collective-permute-done((f32[128,2048]{0,1:T(8,128)S(1)}, f32[128,2048]{0,1:T(8,128)S(1)}, u32[]{:S(2)}, u32[]{:S(2)}) %collective-permute-start.21) | collective-permute-done | bytes 1048608 | tf_op jit(solution)/shard_map/ppermute | solution.py:23
  178.3 1.4 fusion.65
  179.7 1.6 collective-permute-start.22
  182.0 1.4 dynamic-slice_add_fusion
  183.3 3.5 %fusion.28 = f32[128,4096]{1,0:T(8,128)S(1)} fusion(f32[128,4096]{0,1:T(8,128)} %all-gather.2.cloned.1.call-done, f32[1,128,128]{1,2,0:T(8,128)S(1)} %custom-call.16), kind=kOutput, calls=%fused_computation.47 | convolution fusion | flops 805306368 | bytes 4259840 | tf_op jit(solution)/shard_map/jit(_solve_triangular)/triangular_solve | solution.py:151
  186.9 1.1 fusion.17
  188.0 26.9 %convolution_subtract_fusion = f32[4096,2048]{1,0:T(8,128)} fusion(f32[4096,2048]{1,0:T(8,128)} %param.21, f32[128,4096]{1,0:T(8,128)S(1)} %fusion.28, f32[128,2048]{1,0:T(8,128)S(1)} %fusion.17), kind=kOutput, calls=%fused_computation.6 | convolution fusion | flops 6450839552 | bytes 70254592 | tf_op jit(solution)/shard_map/mi,mj->ij/dot_general | solution.py:153
  (90 shorter events, 5.7 us)
Async XLA Ops:
  7.2 3.4 %copy-start = (f32[4,128]{1,0:T(4,128)S(1)}, f32[4,128]{1,0:T(4,128)}, u32[]{:S(2)}) copy-start(f32[4,128]{1,0:T(4,128)} %param.18) | copy-start | bytes 6148
  7.2 154.7 %all-gather.2.cloned.1.call-start = ((), (), s32[]{:S(2)}) async-start(), calls=%async_computation | async-start | bytes 2359296 | tf_op jit(solution)/shard_map/all_gather | solution.py:142
  16.3 9.9 %collective-permute-start = (f32[4,2048]{1,0:T(4,128)S(1)}, f32[4,2048]{1,0:T(4,128)S(1)}, u32[]{:S(2)}, u32[]{:S(2)}) collective-permute-start(f32[4,2048]{1,0:T(4,128)S(1)} %bitcast.157), channel_id=1, source_target_pairs={{0,7},{1,0},{2,1},{3,2},{4,3},{5,4},{6,5},{7,6},{8,15},{9,8},{10,9... | collective-permute-start | bytes 98312 | tf_op jit(solution)/shard_map/ppermute | solution.py:51
  22.4 5.7 %collective-permute-start.1 = (f32[4,2048]{1,0:T(4,128)S(1)}, f32[4,2048]{1,0:T(4,128)S(1)}, u32[]{:S(2)}, u32[]{:S(2)}) collective-permute-start(f32[4,2048]{1,0:T(4,128)S(1)} %bitcast.156), channel_id=1, source_target_pairs={{0,6},{1,7},{2,0},{3,1},{4,2},{5,3},{6,4},{7,5},{8,14},{9,15},{10,... | collective-permute-start | bytes 98312 | tf_op jit(solution)/shard_map/ppermute | solution.py:51
  22.9 6.4 %collective-permute-start.2 = (f32[4,2048]{1,0:T(4,128)S(1)}, f32[4,2048]{1,0:T(4,128)S(1)}, u32[]{:S(2)}, u32[]{:S(2)}) collective-permute-start(f32[4,2048]{1,0:T(4,128)S(1)} %bitcast.153), channel_id=1, source_target_pairs={{0,5},{1,6},{2,7},{3,0},{4,1},{5,2},{6,3},{7,4},{8,13},{9,14},{10,... | collective-permute-start | bytes 98312 | tf_op jit(solution)/shard_map/ppermute | solution.py:51
  23.0 6.3 %collective-permute-start.3 = (f32[4,2048]{1,0:T(4,128)S(1)}, f32[4,2048]{1,0:T(4,128)S(1)}, u32[]{:S(2)}, u32[]{:S(2)}) collective-permute-start(f32[4,2048]{1,0:T(4,128)S(1)} %bitcast.154), channel_id=1, source_target_pairs={{0,4},{1,5},{2,6},{3,7},{4,0},{5,1},{6,2},{7,3},{8,12},{9,13},{10,... | collective-permute-start | bytes 98312 | tf_op jit(solution)/shard_map/ppermute | solution.py:51
  26.0 6.1 %collective-permute-start.4 = (f32[4,2048]{1,0:T(4,128)S(1)}, f32[4,2048]{1,0:T(4,128)S(1)}, u32[]{:S(2)}, u32[]{:S(2)}) collective-permute-start(f32[4,2048]{1,0:T(4,128)S(1)} %bitcast.155), channel_id=1, source_target_pairs={{0,3},{1,4},{2,5},{3,6},{4,7},{5,0},{6,1},{7,2},{8,11},{9,12},{10,... | collective-permute-start | bytes 98312 | tf_op jit(solution)/shard_map/ppermute | solution.py:51
  26.2 6.9 %collective-permute-start.5 = (f32[4,2048]{1,0:T(4,128)S(1)}, f32[4,2048]{1,0:T(4,128)S(1)}, u32[]{:S(2)}, u32[]{:S(2)}) collective-permute-start(f32[4,2048]{1,0:T(4,128)S(1)} %bitcast.159), channel_id=1, source_target_pairs={{0,2},{1,3},{2,4},{3,5},{4,6},{5,7},{6,0},{7,1},{8,10},{9,11},{10,... | collective-permute-start | bytes 98312 | tf_op jit(solution)/shard_map/ppermute | solution.py:51
  28.1 6.7 %collective-permute-start.6 = (f32[4,2048]{1,0:T(4,128)S(1)}, f32[4,2048]{1,0:T(4,128)S(1)}, u32[]{:S(2)}, u32[]{:S(2)}) collective-permute-start(f32[4,2048]{1,0:T(4,128)S(1)} %bitcast.158), channel_id=1, source_target_pairs={{0,1},{1,2},{2,3},{3,4},{4,5},{5,6},{6,7},{7,0},{8,9},{9,10},{10,1... | collective-permute-start | bytes 98312 | tf_op jit(solution)/shard_map/ppermute | solution.py:51
  35.0 6.4 %collective-permute-start.7 = (f32[1,32,2048]{2,1,0:T(8,128)S(1)}, f32[1,32,2048]{2,1,0:T(8,128)S(1)}, u32[]{:S(2)}, u32[]{:S(2)}) collective-permute-start(f32[1,32,2048]{2,1,0:T(8,128)S(1)} %broadcast_in_dim_reshape.3), channel_id=1, source_target_pairs={{0,16},{8,24},{16,0},{24,8},{1,17},{9,25},{17,1},{25,9},{2,18},{10... | collective-permute-start | bytes 786440 | tf_op jit(solution)/shard_map/ppermute | solution.py:67
  41.5 2.0 collective-permute-start.8
  53.9 28.8 %collective-permute-start.13 = (f32[2,2,128,512]{2,3,0,1:T(8,128)S(1)}, f32[2,2,128,512]{2,3,0,1:T(8,128)S(1)}, u32[]{:S(2)}, u32[]{:S(2)}) collective-permute-start(f32[2,2,128,512]{2,3,0,1:T(8,128)S(1)} %fusion.9), channel_id=1, source_target_pairs={{0,1},{1,0},{2,3},{3,2},{4,5},{5,4},{6,7},{7,6},{8,9},{9,8},{10,11... | collective-permute-start | bytes 3145736 | tf_op jit(solution)/shard_map/ppermute | solution.py:116
  54.1 28.5 %collective-permute-start.10 = (f32[128,512]{1,0:T(8,128)S(1)}, f32[128,512]{1,0:T(8,128)S(1)}, u32[]{:S(2)}, u32[]{:S(2)}) collective-permute-start(f32[128,512]{1,0:T(8,128)S(1)} %get-tuple-element.22), channel_id=1, source_target_pairs={{0,1},{1,5},{10,9},{11,13},{20,17},{21,21},{30,25},{31,29}} | collective-permute-start | bytes 786440 | tf_op jit(solution)/shard_map/ppermute | solution.py:127
  58.0 24.6 %collective-permute-start.12 = (f32[128,512]{1,0:T(8,128)S(1)}, f32[128,512]{1,0:T(8,128)S(1)}, u32[]{:S(2)}, u32[]{:S(2)}) collective-permute-start(f32[128,512]{1,0:T(8,128)S(1)} %get-tuple-element.23), channel_id=1, source_target_pairs={{0,3},{1,7},{10,11},{11,15},{20,19},{21,23},{30,27},{31,31}} | collective-permute-start | bytes 786440 | tf_op jit(solution)/shard_map/ppermute | solution.py:127
  59.3 23.3 %collective-permute-start.11 = (f32[128,512]{1,0:T(8,128)S(1)}, f32[128,512]{1,0:T(8,128)S(1)}, u32[]{:S(2)}, u32[]{:S(2)}) collective-permute-start(f32[128,512]{1,0:T(8,128)S(1)} %get-tuple-element.24), channel_id=1, source_target_pairs={{0,2},{1,6},{10,10},{11,14},{20,18},{21,22},{30,26},{31,30}} | collective-permute-start | bytes 786440 | tf_op jit(solution)/shard_map/ppermute | solution.py:127
  60.6 22.0 %collective-permute-start.9 = (f32[128,512]{1,0:T(8,128)S(1)}, f32[128,512]{1,0:T(8,128)S(1)}, u32[]{:S(2)}, u32[]{:S(2)}) collective-permute-start(f32[128,512]{1,0:T(8,128)S(1)} %get-tuple-element.25), channel_id=1, source_target_pairs={{0,0},{1,4},{10,8},{11,12},{20,16},{21,20},{30,24},{31,28}} | collective-permute-start | bytes 786440 | tf_op jit(solution)/shard_map/ppermute | solution.py:127
  71.8 39.5 %copy-start.4 = (s32[256]{0:T(256)S(1)}, s32[256]{0:T(256)}, u32[]{:S(2)}) copy-start(s32[256]{0:T(256)} %param.15) | copy-start | bytes 3076
  71.8 66.3 %copy-start.3 = (f32[128]{0:T(128)S(1)}, f32[128]{0:T(128)}, u32[]{:S(2)}) copy-start(f32[128]{0:T(128)} %param.20) | copy-start | bytes 1540
  71.8 109.5 %copy-start.5 = (f32[128]{0:T(128)S(1)}, f32[128]{0:T(128)}, u32[]{:S(2)}) copy-start(f32[128]{0:T(128)} %param.19) | copy-start | bytes 1540
  82.9 12.5 %collective-permute-start.14 = (f32[2,128,512]{1,2,0:T(8,128)S(1)}, f32[2,128,512]{1,2,0:T(8,128)S(1)}, u32[]{:S(2)}, u32[]{:S(2)}) collective-permute-start(f32[2,128,512]{1,2,0:T(8,128)S(1)} %dynamic-slice_bitcast_fusion), channel_id=1, source_target_pairs={{0,2},{1,3},{2,0},{3,1},{4,6},{5,7},{6,4},{7,5},{8,10},{9,11},{10,... | collective-permute-start | bytes 1572872 | tf_op jit(solution)/shard_map/ppermute | solution.py:43
  95.5 15.0 %collective-permute-start.15 = (f32[128,512]{0,1:T(8,128)S(1)}, f32[128,512]{0,1:T(8,128)S(1)}, u32[]{:S(2)}, u32[]{:S(2)}) collective-permute-start(f32[128,512]{0,1:T(8,128)S(1)} %dynamic-slice_bitcast_fusion.1), channel_id=1, source_target_pairs={{0,4},{1,5},{2,6},{3,7},{4,0},{5,1},{6,2},{7,3},{8,12},{9,13},{10,... | collective-permute-start | bytes 786440 | tf_op jit(solution)/shard_map/ppermute | solution.py:43
  111.3 70.4 %copy-start.2 = (f32[128,512]{0,1:T(8,128)S(1)}, f32[128,512]{0,1:T(8,128)}, u32[]{:S(2)}) copy-start(f32[128,512]{0,1:T(8,128)} %bitcast_add_fusion.1) | copy-start | bytes 786436
  113.0 4.4 %collective-permute-start.16 = (f32[136,128]{1,0:T(8,128)S(1)}, f32[136,128]{1,0:T(8,128)S(1)}, u32[]{:S(2)}, u32[]{:S(2)}) collective-permute-start(f32[136,128]{1,0:T(8,128)S(1)} %pad_maximum_fusion), channel_id=1, source_target_pairs={{0,1},{1,0},{2,3},{3,2},{4,5},{5,4},{6,7},{7,6},{8,9},{9,8},{10,11... | collective-permute-start | bytes 208904 | tf_op jit(solution)/shard_map/ppermute | solution.py:31
  117.4 5.3 %collective-permute-start.17 = (f32[136,128]{1,0:T(8,128)S(1)}, f32[136,128]{1,0:T(8,128)S(1)}, u32[]{:S(2)}, u32[]{:S(2)}) collective-permute-start(f32[136,128]{1,0:T(8,128)S(1)} %fusion.44), channel_id=1, source_target_pairs={{0,2},{1,3},{2,0},{3,1},{4,6},{5,7},{6,4},{7,5},{8,10},{9,11},{10,... | collective-permute-start | bytes 208904 | tf_op jit(solution)/shard_map/ppermute | solution.py:31
  122.7 9.6 %collective-permute-start.18 = (f32[136,128]{1,0:T(8,128)S(1)}, f32[136,128]{1,0:T(8,128)S(1)}, u32[]{:S(2)}, u32[]{:S(2)}) collective-permute-start(f32[136,128]{1,0:T(8,128)S(1)} %add.249), channel_id=1, source_target_pairs={{0,4},{1,5},{2,6},{3,7},{4,0},{5,1},{6,2},{7,3},{8,12},{9,13},{10,... | collective-permute-start | bytes 208904 | tf_op jit(solution)/shard_map/ppermute | solution.py:31
  132.3 1.3 collective-permute-start.19
  133.7 4.4 %collective-permute-start.20 = (f32[136,128]{1,0:T(8,128)S(1)}, f32[136,128]{1,0:T(8,128)S(1)}, u32[]{:S(2)}, u32[]{:S(2)}) collective-permute-start(f32[136,128]{1,0:T(8,128)S(1)} %add.251), channel_id=1, source_target_pairs={{0,16},{8,24},{16,0},{24,8},{1,17},{9,25},{17,1},{25,9},{2,18},{10... | collective-permute-start | bytes 208904 | tf_op jit(solution)/shard_map/ppermute | solution.py:31
  163.2 15.1 %collective-permute-start.21 = (f32[128,2048]{0,1:T(8,128)S(1)}, f32[128,2048]{0,1:T(8,128)S(1)}, u32[]{:S(2)}, u32[]{:S(2)}) collective-permute-start(f32[128,2048]{0,1:T(8,128)S(1)} %dynamic-slice_select_fusion), channel_id=1, source_target_pairs={{0,16},{1,17},{10,26},{11,27},{20,4},{21,5},{30,14},{31,15}} | collective-permute-start | bytes 3145736 | tf_op jit(solution)/shard_map/ppermute | solution.py:23
  179.7 7.2 %collective-permute-start.22 = (f32[128,2048]{0,1:T(8,128)S(1)}, f32[128,2048]{0,1:T(8,128)S(1)}, u32[]{:S(2)}, u32[]{:S(2)}) collective-permute-start(f32[128,2048]{0,1:T(8,128)S(1)} %fusion.65), channel_id=1, source_target_pairs={{0,8},{16,24},{1,9},{17,25},{10,2},{26,18},{11,3},{27,19},{20,28},... | collective-permute-start | bytes 3145736 | tf_op jit(solution)/shard_map/ppermute | solution.py:23
  188.0 26.9 %copy-start.1 = (f32[4,128]{1,0:T(4,128)S(1)}, f32[4,128]{1,0:T(4,128)}, u32[]{:S(2)}) copy-start(f32[4,128]{1,0:T(4,128)} %param.18) | copy-start | bytes 6148
Sparse Core Ops, SparseCore 0:
  111.4 50.4 all-gather.1
